TPU v7x, 128 devices: a whole 4x4x4 slice. The times are simulated.
128 devices in a mesh: tm: 32 (over y, x, core), space: 4 (over z).
Axes of the slice: x: 4, y: 4, z: 4, core: 2. Of those that a mesh axis runs over, the one named last changes fastest.
Arguments:
- fields: bfloat16 [1024, 8, 32, 256], P('tm', None, 'space'), may hold values from -6 to 6
- conv_in: bfloat16 [64, 8, 3, 3], replicated, may hold values from -0.75 to 0.75
- conv_mid: bfloat16 [128, 64, 3, 3], replicated, may hold values from -0.25 to 0.25
- obs_gain: bfloat16 [8, 64, 128, 256], P('space'), may hold values from -0.0014648438 to 0.0014648438
- transition: float32 [256, 256], replicated, as said below
- back_gain: float32 [256, 256], replicated, as said below
- retain: float32 [1024, 256], P('tm'), may hold values from 0.5 to 1.03
Outputs:
- filtered: float32 [1024, 256], P(('tm', 'space'))
- smoothed: float32 [1024, 256], P(('tm', 'space'))
Inputs may be any that keep to these rules, and one draw needn't show every extreme that they name: The spectral norm of transition is below one. The spectral norm of back_gain is below one.
All inputs are finite; a program needn't handle non-finite values.
Results may differ from a plain program's by a relative error of at most 0.0045.
Values may be sent and summed in bfloat16 or wider, within the bound.
No kernel may reach another device: no remote copies, remote signals or barrier semaphores. Data moves between devices by JAX's collectives and lax.ppermute only.
A program may use at most 192 MiB of HBM per device.

v0:
```python
import jax
import jax.numpy as jnp
from jax import lax
from jax.sharding import PartitionSpec as P

precise = lax.Precision.HIGHEST
FLAT = ("tm", "space")


def dot(a, b):
    return jnp.dot(a, b, precision=precise)


def shift_down(value, axis, steps, count):
    return lax.ppermute(value, axis, [(i, i + steps) for i in range(count - steps)])


def shift_up(value, axis, steps, count):
    return lax.ppermute(value, axis, [(i + steps, i) for i in range(count - steps)])


def conv_stride(images, kernel, layout_out):
    return lax.conv_general_dilated(
        images,
        kernel,
        (2, 2),
        ((0, 0), (1, 1)),
        dimension_numbers=("NCHW", "OIHW", layout_out),
        preferred_element_type=jnp.float32,
    )


def encode(fields, conv_in, conv_mid, obs_gain, bands):
    band = lax.axis_index("space")
    edge = fields[:, :, -3:, :]
    flat = edge.reshape(edge.shape[0] * edge.shape[1], edge.shape[2] * edge.shape[3])
    above = shift_down(flat, "space", 1, bands).reshape(edge.shape)
    hidden = conv_stride(jnp.concatenate([above, fields], axis=2), conv_in, "NCHW")
    hidden = jax.nn.silu(hidden).astype(jnp.bfloat16)
    row = lax.broadcasted_iota(jnp.int32, hidden.shape, 2)
    hidden = jnp.where((row == 0) & (band == 0), jnp.zeros_like(hidden), hidden)
    encoded = conv_stride(hidden, conv_mid, "NHWC")
    encoded = jax.nn.silu(encoded).astype(jnp.bfloat16)
    return jnp.einsum("shwc,hwcm->sm", encoded, obs_gain, preferred_element_type=jnp.float32)


def sum_bands(partial, bands):
    got = [lax.ppermute(partial, "space", [(i, (i + d) % bands) for i in range(bands)]) for d in (1, 2, 3)]
    return (partial + got[1]) + (got[2] + got[0])


def exclusive_scan(mats, vecs, axis, count):
    mat1 = shift_down(mats, axis, 1, count)
    mat2 = shift_down(mats, axis, 2, count)
    vec1 = shift_down(vecs, axis, 1, count)
    vec2 = shift_down(vecs, axis, 2, count)
    carry = vec1 + dot(mat1, vec2)
    gain = dot(mat1, mat2)
    stride = 2
    while stride < count:
        more = stride * 2 < count
        got = shift_down(carry, axis, stride, count)
        if more:
            got_gain = shift_down(gain, axis, stride, count)
        carry = carry + dot(gain, got)
        if more:
            gain = dot(gain, got_gain)
        stride *= 2
    return carry


def suffix_scan(heads, step_power, axis, count):
    got1 = shift_up(heads, axis, 1, count)
    got2 = shift_up(heads, axis, 2, count)
    entering = got1 + dot(step_power, got2)
    jump = dot(step_power, step_power)
    stride = 2
    while stride < count:
        got = shift_up(entering, axis, stride, count)
        entering = entering + dot(jump, got)
        if stride * 2 < count:
            jump = dot(jump, jump)
        stride *= 2
    return entering


def per_device(fields, conv_in, conv_mid, obs_gain, transition, back_gain, retain):
    bands = lax.axis_size("space")
    blocks = lax.axis_size("tm")
    band = lax.axis_index("space")
    hours = fields.shape[0] // bands
    modes = transition.shape[0]
    gates = retain.reshape(bands, hours, modes)
    transition_t = transition.T

    phis = gates[:, 0, :, None] * transition[None]
    for i in range(1, hours):
        phis = gates[:, i, :, None] * jnp.einsum("ab,sbc->sac", transition, phis, precision=precise)
    block_phi = phis[0]
    for s in range(1, bands):
        block_phi = dot(phis[s], block_phi)

    partial = encode(fields, conv_in, conv_mid, obs_gain, bands)
    increments = sum_bands(partial, bands).reshape(bands, hours, modes)

    state = increments[:, 0]
    local = [state]
    for i in range(1, hours):
        state = gates[:, i] * dot(state, transition_t) + increments[:, i]
        local.append(state)
    local = jnp.stack(local, axis=1)
    ends = local[:, -1]
    block_sum = ends[0]
    for s in range(1, bands):
        block_sum = dot(phis[s], block_sum) + ends[s]

    carry = exclusive_scan(block_phi, block_sum, "tm", blocks)
    starts = [carry]
    for s in range(bands - 1):
        starts.append(dot(phis[s], starts[-1]) + ends[s])
    state = jnp.stack(starts)
    filtered = []
    for i in range(hours):
        state = gates[:, i] * dot(state, transition_t) + increments[:, i]
        filtered.append(state)
    filtered = jnp.stack(filtered, axis=1)

    powers = [jnp.eye(modes, dtype=jnp.float32), back_gain]
    while len(powers) <= hours:
        top = powers[-1]
        more = jnp.einsum("ab,sbc->sac", top, jnp.stack(powers[1:]), precision=precise)
        powers.extend(list(more))
    powers = powers[: hours + 1]
    step = powers[hours]
    joined_t = dot(back_gain, transition).T
    stacked = jnp.concatenate([p.T for p in powers[:hours]], axis=0)
    sources = filtered - jnp.einsum("sia,ab->sib", filtered, joined_t, precision=precise)
    padded = jnp.concatenate([sources, jnp.zeros_like(sources)], axis=1)
    hankel = jnp.concatenate([padded[:, d : d + hours] for d in range(hours)], axis=2)
    inner = dot(hankel.reshape(bands * hours, hours * modes), stacked).reshape(bands, hours, modes)
    heads = inner[:, 0]
    block_head = heads[bands - 1]
    for s in range(bands - 2, -1, -1):
        block_head = heads[s] + dot(step, block_head)
    block_step = step
    reach = 1
    while reach < bands:
        block_step = dot(block_step, block_step)
        reach *= 2

    is_last = lax.axis_index("tm") == blocks - 1
    boundary = dot(transition, filtered[bands - 1, hours - 1])
    block_head = block_head + jnp.where(is_last, dot(block_step, boundary), 0.0)
    entering = suffix_scan(block_head, block_step, "tm", blocks)
    entering = jnp.where(is_last, boundary, entering)

    inputs = [entering]
    for s in range(bands - 1, 0, -1):
        inputs.insert(0, heads[s] + dot(step, inputs[0]))
    mine = lax.dynamic_index_in_dim(jnp.stack(inputs), band, 0, False)
    tails = jnp.concatenate([powers[hours - i].T for i in range(hours)], axis=1)
    smoothed = lax.dynamic_index_in_dim(inner, band, 0, False) + dot(mine[None, :], tails).reshape(hours, modes)
    return lax.dynamic_index_in_dim(filtered, band, 0, False), smoothed


def solution(mesh):
    placed = (
        P("tm", None, "space", None),
        P(),
        P(),
        P("space", None, None, None),
        P(),
        P(),
        P("tm", None),
    )
    return jax.shard_map(
        per_device,
        mesh=mesh,
        in_specs=placed,
        out_specs=(P(FLAT, None), P(FLAT, None)),
        check_vma=False,
    )
```

profile of v0, /device:TPU:14, one launch (start us, length us, event | category | flops | bytes accessed | tf_op | source)
XLA Modules:
  0.0 170.6 jit_solution(723586542328869064)
XLA Ops:
  0.7 1.1 copy.84
  1.8 1.1 fusion.130
  3.0 2.0 %fusion.23 = f32[4,256,256]{1,2,0:T(8,128)S(1)} fusion(f32[256,256]{0,1:T(8,128)S(1)} %copy.84, f32[4,256]{1,0:T(4,128)S(1)} %get-tuple-element.59, f32[4,256]{1,0:T(4,128)S(1)} %get-tuple-element.52, f32[256,256]{1,0:T(8,128)} %param.11), kind=kOutput, calls=%fused_computation.29 | convolution fusion | flops 805830656 | bytes 1581056 | tf_op jit(solution)/shard_map/ab,sbc->sac/dot_general | solution.py:98
  5.0 1.0 fusion.22
  6.1 1.0 fusion.21
  7.1 1.0 fusion.20
  8.2 1.0 fusion.19
  9.2 1.0 fusion.18
  10.3 1.0 fusion.17
  12.5 1.3 fusion.74
  13.8 1.9 %collective-permute-start.5 = (f32[256,256]{1,0:T(8,128)}, f32[256,256]{1,0:T(8,128)}, u32[]{:S(2)}, u32[]{:S(2)}) collective-permute-start(f32[256,256]{1,0:T(8,128)} %fusion.74), channel_id=1, source_target_pairs={{0,4},{4,8},{8,12},{12,16},{16,20},{20,24},{24,28},{28,32},{32,36}... | collective-permute-start | bytes 786440 | tf_op jit(solution)/shard_map/ppermute | solution.py:15
  15.7 3.4 %collective-permute-start.7 = (f32[256,256]{1,0:T(8,128)}, f32[256,256]{1,0:T(8,128)}, u32[]{:S(2)}, u32[]{:S(2)}) collective-permute-start(f32[256,256]{1,0:T(8,128)} %fusion.74), channel_id=1, source_target_pairs={{0,8},{4,12},{8,16},{12,20},{16,24},{20,28},{24,32},{28,36},{32,40... | collective-permute-start | bytes 786440 | tf_op jit(solution)/shard_map/ppermute | solution.py:15
  19.5 0.8 copy.129
  20.3 4.6 %collective-permute-start = (bf16[256,768]{1,0:T(8,128)(2,1)}, bf16[256,768]{1,0:T(8,128)(2,1)}, u32[]{:S(2)}, u32[]{:S(2)}) collective-permute-start(bf16[256,768]{1,0:T(8,128)(2,1)} %bitcast.151), channel_id=1, source_target_pairs={{0,1},{1,2},{2,3},{4,5},{5,6},{6,7},{8,9},{9,10},{10,11},{12,13},{... | collective-permute-start | bytes 1179656 | tf_op jit(solution)/shard_map/ppermute | solution.py:15
  26.5 1.3 constant_dynamic-update-slice_fusion.16
  28.4 1.0 convolution_bitcast_fusion
  30.7 0.9 bitcast_dynamic-update-slice_fusion
  33.9 1.1 fusion.149
  34.9 5.2 %copy.86 = bf16[32,8,8,256]{0,1,3,2:T(8,128)(2,1)} copy(bf16[32,8,8,256]{3,2,1,0:T(8,128)(2,1)} %param.7) | data formatting | bytes 2097152 | tf_op args[0]
  40.6 0.9 fusion.84
  41.5 2.2 %reshape.51 = bf16[32,8,3,256]{3,2,1,0:T(4,128)(2,1)} reshape(bf16[256,768]{1,0:T(8,128)(2,1)} %collective-permute-done) | data formatting | bytes 786432 | tf_op jit(solution)/shard_map/reshape | solution.py:37
  43.7 3.0 %copy.85 = bf16[32,8,3,256]{0,1,3,2:T(8,128)(2,1)} copy(bf16[32,8,3,256]{3,2,1,0:T(4,128)(2,1)} %reshape.51) | data formatting | bytes 786432 | tf_op jit(solution)/shard_map/reshape | solution.py:37
  46.7 9.4 %fusion.4 = f32[32,2,64,128]{3,0,2,1:T(8,128)} fusion(bf16[128,64,3,3]{0,1,3,2:T(8,128)(2,1)S(1)} %copy-done, pred[5]{0:T(512)(128)(4,1)} %compare_and_fusion, bf16[64,8,3,3]{0,1,3,2:T(8,128)(2,1)} %param.8, bf16[32,8,8,256]{0,1,3,2:T(8,128)(2,1)} %copy.86, bf16[32,8,3,256]{0,1,3,2:T(8,128)(2,1)} %copy.85), kind=kOutput, calls=%fused_computation.5 | convolution fusion | flops 799834112 | bytes 3695621 | tf_op jit(solution)/shard_map/conv_general_dilated | solution.py:23
  56.1 5.3 %convolution_bitcast_fusion.3 = f32[32,256]{1,0:T(8,128)S(1)} fusion(bf16[2,64,128,256]{3,2,1,0:T(8,128)(2,1)} %param.10, f32[32,2,64,128]{3,0,2,1:T(8,128)} %fusion.4), kind=kOutput, calls=%fused_computation.33 | convolution fusion | flops 271056896 | bytes 10518528 | tf_op jit(solution)/shard_map/shwc,hwcm->sm/dot_general | solution.py:44
  61.5 1.2 collective-permute-start.2
  62.7 1.1 collective-permute-start.3
  63.8 3.0 %collective-permute-start.1 = (f32[32,256]{1,0:T(8,128)S(1)}, f32[32,256]{1,0:T(8,128)S(1)}, u32[]{:S(2)}, u32[]{:S(2)}) collective-permute-start(f32[32,256]{1,0:T(8,128)S(1)} %convolution_bitcast_fusion.3), channel_id=1, source_target_pairs={{0,2},{1,3},{2,0},{3,1},{4,6},{5,7},{6,4},{7,5},{8,10},{9,11},{10,... | collective-permute-start | bytes 98312 | tf_op jit(solution)/shard_map/ppermute | solution.py:48
  66.8 0.9 fusion.82
  68.1 1.4 collective-permute-done.1
  73.3 3.4 %collective-permute-start.6 = (f32[256]{0:T(256)S(1)}, f32[256]{0:T(256)S(1)}, u32[]{:S(2)}, u32[]{:S(2)}) collective-permute-start(f32[256]{0:T(256)S(1)} %add.157), channel_id=1, source_target_pairs={{0,8},{4,12},{8,16},{12,20},{16,24},{20,28},{24,32},{28,36},{32,40... | collective-permute-start | bytes 3080 | tf_op jit(solution)/shard_map/ppermute | solution.py:15
  76.8 1.4 fusion.133
  78.2 3.2 %collective-permute-start.9 = (f32[256,256]{1,0:T(8,128)S(1)}, f32[256,256]{1,0:T(8,128)S(1)}, u32[]{:S(2)}, u32[]{:S(2)}) collective-permute-start(f32[256,256]{1,0:T(8,128)S(1)} %fusion.133), channel_id=1, source_target_pairs={{0,8},{4,12},{8,16},{12,20},{16,24},{20,28},{24,32},{28,36},{32,40... | collective-permute-start | bytes 786440 | tf_op jit(solution)/shard_map/ppermute | solution.py:15
  81.5 1.9 %collective-permute-start.4 = (f32[256]{0:T(256)S(1)}, f32[256]{0:T(256)S(1)}, u32[]{:S(2)}, u32[]{:S(2)}) collective-permute-start(f32[256]{0:T(256)S(1)} %add.157), channel_id=1, source_target_pairs={{0,4},{4,8},{8,12},{12,16},{16,20},{20,24},{24,28},{28,32},{32,36}... | collective-permute-start | bytes 3080 | tf_op jit(solution)/shard_map/ppermute | solution.py:15
  83.4 1.2 fusion.132
  84.7 2.1 %collective-permute-done.4 = f32[256]{0:T(256)S(1)} collective-permute-done((f32[256]{0:T(256)S(1)}, f32[256]{0:T(256)S(1)}, u32[]{:S(2)}, u32[]{:S(2)}) %collective-permute-start.4) | collective-permute-done | bytes 1056 | tf_op jit(solution)/shard_map/ppermute | solution.py:15
  86.8 4.9 %collective-permute-start.8 = (f32[256]{0:T(256)S(1)}, f32[256]{0:T(256)S(1)}, u32[]{:S(2)}, u32[]{:S(2)}) collective-permute-start(f32[256]{0:T(256)S(1)} %add.158), channel_id=1, source_target_pairs={{0,8},{4,12},{8,16},{12,20},{16,24},{20,28},{24,32},{28,36},{32,40... | collective-permute-start | bytes 3080 | tf_op jit(solution)/shard_map/ppermute | solution.py:15
  91.6 0.9 fusion.80
  93.2 3.7 %collective-permute-start.10 = (f32[256]{0:T(256)S(1)}, f32[256]{0:T(256)S(1)}, u32[]{:S(2)}, u32[]{:S(2)}) collective-permute-start(f32[256]{0:T(256)S(1)} %add.159), channel_id=1, source_target_pairs={{0,16},{4,20},{8,24},{12,28},{16,32},{20,36},{24,40},{28,44},{32,4... | collective-permute-start | bytes 3080 | tf_op jit(solution)/shard_map/ppermute | solution.py:15
  97.3 4.4 %collective-permute-start.11 = (f32[256,256]{1,0:T(8,128)S(1)}, f32[256,256]{1,0:T(8,128)S(1)}, u32[]{:S(2)}, u32[]{:S(2)}) collective-permute-start(f32[256,256]{1,0:T(8,128)S(1)} %fusion.135), channel_id=1, source_target_pairs={{0,16},{4,20},{8,24},{12,28},{16,32},{20,36},{24,40},{28,44},{32,4... | collective-permute-start | bytes 786440 | tf_op jit(solution)/shard_map/ppermute | solution.py:15
  103.3 1.9 %collective-permute-start.12 = (f32[256]{0:T(256)}, f32[256]{0:T(256)}, u32[]{:S(2)}, u32[]{:S(2)}) collective-permute-start(f32[256]{0:T(256)} %add.160), channel_id=1, source_target_pairs={{0,32},{4,36},{8,40},{12,44},{16,48},{20,52},{24,56},{28,60},{32,6... | collective-permute-start | bytes 3080 | tf_op jit(solution)/shard_map/ppermute | solution.py:15
  105.2 1.8 %collective-permute-done.11 = f32[256,256]{1,0:T(8,128)S(1)} collective-permute-done((f32[256,256]{1,0:T(8,128)S(1)}, f32[256,256]{1,0:T(8,128)S(1)}, u32[]{:S(2)}, u32[]{:S(2)}) %collective-permute-start.11) | collective-permute-done | bytes 262176 | tf_op jit(solution)/shard_map/ppermute | solution.py:15
  107.0 1.1 fusion.137
  108.1 3.2 %collective-permute-start.13 = (f32[256,256]{1,0:T(8,128)}, f32[256,256]{1,0:T(8,128)}, u32[]{:S(2)}, u32[]{:S(2)}) collective-permute-start(f32[256,256]{1,0:T(8,128)} %fusion.137), channel_id=1, source_target_pairs={{0,32},{4,36},{8,40},{12,44},{16,48},{20,52},{24,56},{28,60},{32,6... | collective-permute-start | bytes 786440 | tf_op jit(solution)/shard_map/ppermute | solution.py:15
  111.3 1.1 convolution_bitcast_fusion.2
  112.5 1.2 fusion.138
  113.8 0.7 add.161
  114.5 1.3 collective-permute-start.14
  115.8 0.9 collective-permute-done.13
  116.7 1.4 fusion.139
  118.7 0.8 add.163
  123.9 1.3 fusion.15
  126.6 5.4 %collective-permute-start.16 = (f32[256]{0:T(256)S(1)}, f32[256]{0:T(256)S(1)}, u32[]{:S(2)}, u32[]{:S(2)}) collective-permute-start(f32[256]{0:T(256)S(1)} %select_add_fusion), channel_id=1, source_target_pairs={{8,0},{12,4},{16,8},{20,12},{24,16},{28,20},{32,24},{36,28},{40,32... | collective-permute-start | bytes 3080 | tf_op jit(solution)/shard_map/ppermute | solution.py:19
  132.8 1.9 %collective-permute-start.15 = (f32[256]{0:T(256)S(1)}, f32[256]{0:T(256)S(1)}, u32[]{:S(2)}, u32[]{:S(2)}) collective-permute-start(f32[256]{0:T(256)S(1)} %select_add_fusion), channel_id=1, source_target_pairs={{4,0},{8,4},{12,8},{16,12},{20,16},{24,20},{28,24},{32,28},{36,32}... | collective-permute-start | bytes 3080 | tf_op jit(solution)/shard_map/ppermute | solution.py:19
  134.7 2.3 %collective-permute-done.16 = f32[256]{0:T(256)S(1)} collective-permute-done((f32[256]{0:T(256)S(1)}, f32[256]{0:T(256)S(1)}, u32[]{:S(2)}, u32[]{:S(2)}) %collective-permute-start.16) | collective-permute-done | bytes 1056 | tf_op jit(solution)/shard_map/ppermute | solution.py:19
  137.4 1.9 %collective-permute-start.17 = (f32[256]{0:T(256)S(1)}, f32[256]{0:T(256)S(1)}, u32[]{:S(2)}, u32[]{:S(2)}) collective-permute-start(f32[256]{0:T(256)S(1)} %add.179), channel_id=1, source_target_pairs={{8,0},{12,4},{16,8},{20,12},{24,16},{28,20},{32,24},{36,28},{40,32... | collective-permute-start | bytes 3080 | tf_op jit(solution)/shard_map/ppermute | solution.py:19
  140.0 4.9 %collective-permute-done.17 = f32[256]{0:T(256)S(1)} collective-permute-done((f32[256]{0:T(256)S(1)}, f32[256]{0:T(256)S(1)}, u32[]{:S(2)}, u32[]{:S(2)}) %collective-permute-start.17) | collective-permute-done | bytes 1056 | tf_op jit(solution)/shard_map/ppermute | solution.py:19
  145.2 2.0 %collective-permute-start.18 = (f32[256]{0:T(256)S(1)}, f32[256]{0:T(256)S(1)}, u32[]{:S(2)}, u32[]{:S(2)}) collective-permute-start(f32[256]{0:T(256)S(1)} %add.180), channel_id=1, source_target_pairs={{16,0},{20,4},{24,8},{28,12},{32,16},{36,20},{40,24},{44,28},{48,3... | collective-permute-start | bytes 3080 | tf_op jit(solution)/shard_map/ppermute | solution.py:19
  147.2 0.8 bitcast_dynamic-update-slice_fusion.3
  148.0 5.2 %collective-permute-done.18 = f32[256]{0:T(256)S(1)} collective-permute-done((f32[256]{0:T(256)S(1)}, f32[256]{0:T(256)S(1)}, u32[]{:S(2)}, u32[]{:S(2)}) %collective-permute-start.18) | collective-permute-done | bytes 1056 | tf_op jit(solution)/shard_map/ppermute | solution.py:19
  153.4 2.4 %collective-permute-start.19 = (f32[256]{0:T(256)S(1)}, f32[256]{0:T(256)S(1)}, u32[]{:S(2)}, u32[]{:S(2)}) collective-permute-start(f32[256]{0:T(256)S(1)} %add.181), channel_id=1, source_target_pairs={{32,0},{36,4},{40,8},{44,12},{48,16},{52,20},{56,24},{60,28},{64,3... | collective-permute-start | bytes 3080 | tf_op jit(solution)/shard_map/ppermute | solution.py:19
  155.8 3.1 %collective-permute-done.19 = f32[256]{0:T(256)S(1)} collective-permute-done((f32[256]{0:T(256)S(1)}, f32[256]{0:T(256)S(1)}, u32[]{:S(2)}, u32[]{:S(2)}) %collective-permute-start.19) | collective-permute-done | bytes 1056 | tf_op jit(solution)/shard_map/ppermute | solution.py:19
  159.2 1.3 collective-permute-start.20
  161.2 5.0 %collective-permute-done.20 = f32[256]{0:T(256)S(1)} collective-permute-done((f32[256]{0:T(256)S(1)}, f32[256]{0:T(256)S(1)}, u32[]{:S(2)}, u32[]{:S(2)}) %collective-permute-start.20) | collective-permute-done | bytes 1056 | tf_op jit(solution)/shard_map/ppermute | solution.py:19
  167.3 2.7 %fusion.12 = f32[1,8,256]{2,0,1:T(1,128)S(1)} fusion(f32[32,8,8,256]{3,2,1,0:T(8,128)} %bitcast.147, s32[]{:T(128)S(6)} %select_n.26, f32[1,256]{1,0:T(1,128)S(1)} %bitcast.452, f32[1,256]{1,0:T(1,128)S(1)} %bitcast.465, f32[1,256]{1,0:T(1,128)S(1)} %bitcast.449, f32[1,256]{1,0:T(1,128)S(1)} %bitcast.445), kind=kOutput, calls=%fused_computation.9 | convolution fusion | flops 6292224 | bytes 2109444 | tf_op jit(solution)/shard_map/dot_general | solution.py:11
  (221 shorter events, 25.6 us)
Async XLA Ops:
  0.6 46.1 %copy-start = (bf16[128,64,3,3]{0,1,3,2:T(8,128)(2,1)S(1)}, bf16[128,64,3,3]{0,1,3,2:T(8,128)(2,1)}, u32[]{:S(2)}) copy-start(bf16[128,64,3,3]{0,1,3,2:T(8,128)(2,1)} %param.9) | copy-start | bytes 442372
  10.2 8.9 %copy-start.12 = (bf16[32,8,8,256]{3,2,1,0:T(8,128)(2,1)S(1)}, bf16[32,8,8,256]{3,2,1,0:T(8,128)(2,1)}, u32[]{:S(2)}) copy-start(bf16[32,8,8,256]{3,2,1,0:T(8,128)(2,1)} %param.7) | copy-start | bytes 3145732
  11.9 13.7 %copy-start.9 = (f32[256,256]{1,0:T(8,128)S(1)}, f32[256,256]{1,0:T(8,128)}, u32[]{:S(2)}) copy-start(f32[256,256]{1,0:T(8,128)} %param.12) | copy-start | bytes 786436
  13.8 62.9 %collective-permute-start.5 = (f32[256,256]{1,0:T(8,128)}, f32[256,256]{1,0:T(8,128)}, u32[]{:S(2)}, u32[]{:S(2)}) collective-permute-start(f32[256,256]{1,0:T(8,128)} %fusion.74), channel_id=1, source_target_pairs={{0,4},{4,8},{8,12},{12,16},{16,20},{20,24},{24,28},{28,32},{32,36}... | collective-permute-start | bytes 786440 | tf_op jit(solution)/shard_map/ppermute | solution.py:15
  15.7 61.0 %collective-permute-start.7 = (f32[256,256]{1,0:T(8,128)}, f32[256,256]{1,0:T(8,128)}, u32[]{:S(2)}, u32[]{:S(2)}) collective-permute-start(f32[256,256]{1,0:T(8,128)} %fusion.74), channel_id=1, source_target_pairs={{0,8},{4,12},{8,16},{12,20},{16,24},{20,28},{24,32},{28,36},{32,40... | collective-permute-start | bytes 786440 | tf_op jit(solution)/shard_map/ppermute | solution.py:15
  20.3 21.2 %collective-permute-start = (bf16[256,768]{1,0:T(8,128)(2,1)}, bf16[256,768]{1,0:T(8,128)(2,1)}, u32[]{:S(2)}, u32[]{:S(2)}) collective-permute-start(bf16[256,768]{1,0:T(8,128)(2,1)} %bitcast.151), channel_id=1, source_target_pairs={{0,1},{1,2},{2,3},{4,5},{5,6},{6,7},{8,9},{9,10},{10,11},{12,13},{... | collective-permute-start | bytes 1179656 | tf_op jit(solution)/shard_map/ppermute | solution.py:15
  56.1 13.5 %copy-start.34 = (f32[4,1,256]{2,1,0:T(1,128)S(1)}, f32[4,1,256]{2,1,0:T(1,128)}, u32[]{:S(2)}) copy-start(f32[4,1,256]{2,1,0:T(1,128)} %copy-done.33) | copy-start | bytes 12292
  56.1 13.9 %copy-start.31 = (f32[4,1,256]{2,1,0:T(1,128)S(1)}, f32[4,1,256]{2,1,0:T(1,128)}, u32[]{:S(2)}) copy-start(f32[4,1,256]{2,1,0:T(1,128)} %copy-done.30) | copy-start | bytes 12292
  56.1 14.2 %copy-start.28 = (f32[4,1,256]{2,1,0:T(1,128)S(1)}, f32[4,1,256]{2,1,0:T(1,128)}, u32[]{:S(2)}) copy-start(f32[4,1,256]{2,1,0:T(1,128)} %copy-done.27) | copy-start | bytes 12292
  56.1 14.5 %copy-start.25 = (f32[4,1,256]{2,1,0:T(1,128)S(1)}, f32[4,1,256]{2,1,0:T(1,128)}, u32[]{:S(2)}) copy-start(f32[4,1,256]{2,1,0:T(1,128)} %copy-done.24) | copy-start | bytes 12292
  61.5 9.5 %copy-start.22 = (f32[4,1,256]{2,1,0:T(1,128)S(1)}, f32[4,1,256]{2,1,0:T(1,128)}, u32[]{:S(2)}) copy-start(f32[4,1,256]{2,1,0:T(1,128)} %copy-done.21) | copy-start | bytes 12292
  61.5 9.8 %copy-start.19 = (f32[4,1,256]{2,1,0:T(1,128)S(1)}, f32[4,1,256]{2,1,0:T(1,128)}, u32[]{:S(2)}) copy-start(f32[4,1,256]{2,1,0:T(1,128)} %copy-done.18) | copy-start | bytes 12292
  61.5 10.1 %copy-start.16 = (f32[4,1,256]{2,1,0:T(1,128)S(1)}, f32[4,1,256]{2,1,0:T(1,128)}, u32[]{:S(2)}) copy-start(f32[4,1,256]{2,1,0:T(1,128)} %copy-done.15) | copy-start | bytes 12292
  61.5 6.2 %collective-permute-start.2 = (f32[32,256]{1,0:T(8,128)S(1)}, f32[32,256]{1,0:T(8,128)S(1)}, u32[]{:S(2)}, u32[]{:S(2)}) collective-permute-start(f32[32,256]{1,0:T(8,128)S(1)} %convolution_bitcast_fusion.3), channel_id=1, source_target_pairs={{0,3},{1,0},{2,1},{3,2},{4,7},{5,4},{6,5},{7,6},{8,11},{9,8},{10,9... | collective-permute-start | bytes 98312 | tf_op jit(solution)/shard_map/ppermute | solution.py:48
  62.7 5.4 %collective-permute-start.3 = (f32[32,256]{1,0:T(8,128)S(1)}, f32[32,256]{1,0:T(8,128)S(1)}, u32[]{:S(2)}, u32[]{:S(2)}) collective-permute-start(f32[32,256]{1,0:T(8,128)S(1)} %convolution_bitcast_fusion.3), channel_id=1, source_target_pairs={{0,1},{1,2},{2,3},{3,0},{4,5},{5,6},{6,7},{7,4},{8,9},{9,10},{10,1... | collective-permute-start | bytes 98312 | tf_op jit(solution)/shard_map/ppermute | solution.py:48
  63.8 5.7 %collective-permute-start.1 = (f32[32,256]{1,0:T(8,128)S(1)}, f32[32,256]{1,0:T(8,128)S(1)}, u32[]{:S(2)}, u32[]{:S(2)}) collective-permute-start(f32[32,256]{1,0:T(8,128)S(1)} %convolution_bitcast_fusion.3), channel_id=1, source_target_pairs={{0,2},{1,3},{2,0},{3,1},{4,6},{5,7},{6,4},{7,5},{8,10},{9,11},{10,... | collective-permute-start | bytes 98312 | tf_op jit(solution)/shard_map/ppermute | solution.py:48
  69.6 8.6 %copy-start.38 = (f32[4,1,256]{2,1,0:T(1,128)}, f32[4,1,256]{2,1,0:T(1,128)S(1)}, u32[]{:S(2)}) copy-start(f32[4,1,256]{2,1,0:T(1,128)S(1)} %get-tuple-element.13) | copy-start | bytes 12292
  69.6 11.9 %copy-start.40 = (f32[4,1,256]{2,1,0:T(1,128)}, f32[4,1,256]{2,1,0:T(1,128)S(1)}, u32[]{:S(2)}) copy-start(f32[4,1,256]{2,1,0:T(1,128)S(1)} %get-tuple-element.14) | copy-start | bytes 12292
  69.6 13.8 %copy-start.42 = (f32[4,1,256]{2,1,0:T(1,128)}, f32[4,1,256]{2,1,0:T(1,128)S(1)}, u32[]{:S(2)}) copy-start(f32[4,1,256]{2,1,0:T(1,128)S(1)} %get-tuple-element.15) | copy-start | bytes 12292
  69.6 13.8 %copy-start.44 = (f32[4,1,256]{2,1,0:T(1,128)}, f32[4,1,256]{2,1,0:T(1,128)S(1)}, u32[]{:S(2)}) copy-start(f32[4,1,256]{2,1,0:T(1,128)S(1)} %get-tuple-element.16) | copy-start | bytes 12292
  69.6 13.8 %copy-start.46 = (f32[4,1,256]{2,1,0:T(1,128)}, f32[4,1,256]{2,1,0:T(1,128)S(1)}, u32[]{:S(2)}) copy-start(f32[4,1,256]{2,1,0:T(1,128)S(1)} %get-tuple-element.17) | copy-start | bytes 12292
  69.6 15.1 %copy-start.48 = (f32[4,1,256]{2,1,0:T(1,128)}, f32[4,1,256]{2,1,0:T(1,128)S(1)}, u32[]{:S(2)}) copy-start(f32[4,1,256]{2,1,0:T(1,128)S(1)} %get-tuple-element.18) | copy-start | bytes 12292
  69.6 17.1 %copy-start.50 = (f32[4,1,256]{2,1,0:T(1,128)}, f32[4,1,256]{2,1,0:T(1,128)S(1)}, u32[]{:S(2)}) copy-start(f32[4,1,256]{2,1,0:T(1,128)S(1)} %get-tuple-element.19) | copy-start | bytes 12292
  71.6 30.1 %copy-start.3 = (f32[2,256,256]{1,2,0:T(8,128)S(1)}, f32[2,256,256]{1,2,0:T(8,128)}, u32[]{:S(2)}) copy-start(f32[2,256,256]{1,2,0:T(8,128)} %copy-done.2) | copy-start | bytes 1572868
  72.8 13.9 %copy-start.54 = (f32[1,256]{1,0:T(1,128)}, f32[1,256]{1,0:T(1,128)S(1)}, u32[]{:S(2)}) copy-start(f32[1,256]{1,0:T(1,128)S(1)} %get-tuple-element.30) | copy-start | bytes 3076
  72.8 13.9 %copy-start.56 = (f32[1,256]{1,0:T(1,128)}, f32[1,256]{1,0:T(1,128)S(1)}, u32[]{:S(2)}) copy-start(f32[1,256]{1,0:T(1,128)S(1)} %get-tuple-element.31) | copy-start | bytes 3076
  73.3 10.1 %collective-permute-start.6 = (f32[256]{0:T(256)S(1)}, f32[256]{0:T(256)S(1)}, u32[]{:S(2)}, u32[]{:S(2)}) collective-permute-start(f32[256]{0:T(256)S(1)} %add.157), channel_id=1, source_target_pairs={{0,8},{4,12},{8,16},{12,20},{16,24},{20,28},{24,32},{28,36},{32,40... | collective-permute-start | bytes 3080 | tf_op jit(solution)/shard_map/ppermute | solution.py:15
  78.2 33.1 %copy-start.10 = (f32[256,256]{1,0:T(8,128)S(1)}, f32[256,256]{1,0:T(8,128)}, u32[]{:S(2)}) copy-start(f32[256,256]{1,0:T(8,128)} %param.12) | copy-start | bytes 786436
  78.2 18.7 %collective-permute-start.9 = (f32[256,256]{1,0:T(8,128)S(1)}, f32[256,256]{1,0:T(8,128)S(1)}, u32[]{:S(2)}, u32[]{:S(2)}) collective-permute-start(f32[256,256]{1,0:T(8,128)S(1)} %fusion.133), channel_id=1, source_target_pairs={{0,8},{4,12},{8,16},{12,20},{16,24},{20,28},{24,32},{28,36},{32,40... | collective-permute-start | bytes 786440 | tf_op jit(solution)/shard_map/ppermute | solution.py:15
  81.5 5.3 %collective-permute-start.4 = (f32[256]{0:T(256)S(1)}, f32[256]{0:T(256)S(1)}, u32[]{:S(2)}, u32[]{:S(2)}) collective-permute-start(f32[256]{0:T(256)S(1)} %add.157), channel_id=1, source_target_pairs={{0,4},{4,8},{8,12},{12,16},{16,20},{20,24},{24,28},{28,32},{32,36}... | collective-permute-start | bytes 3080 | tf_op jit(solution)/shard_map/ppermute | solution.py:15
  86.8 6.1 %collective-permute-start.8 = (f32[256]{0:T(256)S(1)}, f32[256]{0:T(256)S(1)}, u32[]{:S(2)}, u32[]{:S(2)}) collective-permute-start(f32[256]{0:T(256)S(1)} %add.158), channel_id=1, source_target_pairs={{0,8},{4,12},{8,16},{12,20},{16,24},{20,28},{24,32},{28,36},{32,40... | collective-permute-start | bytes 3080 | tf_op jit(solution)/shard_map/ppermute | solution.py:15
  93.2 9.3 %collective-permute-start.10 = (f32[256]{0:T(256)S(1)}, f32[256]{0:T(256)S(1)}, u32[]{:S(2)}, u32[]{:S(2)}) collective-permute-start(f32[256]{0:T(256)S(1)} %add.159), channel_id=1, source_target_pairs={{0,16},{4,20},{8,24},{12,28},{16,32},{20,36},{24,40},{28,44},{32,4... | collective-permute-start | bytes 3080 | tf_op jit(solution)/shard_map/ppermute | solution.py:15
  97.3 9.8 %collective-permute-start.11 = (f32[256,256]{1,0:T(8,128)S(1)}, f32[256,256]{1,0:T(8,128)S(1)}, u32[]{:S(2)}, u32[]{:S(2)}) collective-permute-start(f32[256,256]{1,0:T(8,128)S(1)} %fusion.135), channel_id=1, source_target_pairs={{0,16},{4,20},{8,24},{12,28},{16,32},{20,36},{24,40},{28,44},{32,4... | collective-permute-start | bytes 786440 | tf_op jit(solution)/shard_map/ppermute | solution.py:15
  103.3 9.2 %collective-permute-start.12 = (f32[256]{0:T(256)}, f32[256]{0:T(256)}, u32[]{:S(2)}, u32[]{:S(2)}) collective-permute-start(f32[256]{0:T(256)} %add.160), channel_id=1, source_target_pairs={{0,32},{4,36},{8,40},{12,44},{16,48},{20,52},{24,56},{28,60},{32,6... | collective-permute-start | bytes 3080 | tf_op jit(solution)/shard_map/ppermute | solution.py:15
  108.1 8.6 %collective-permute-start.13 = (f32[256,256]{1,0:T(8,128)}, f32[256,256]{1,0:T(8,128)}, u32[]{:S(2)}, u32[]{:S(2)}) collective-permute-start(f32[256,256]{1,0:T(8,128)} %fusion.137), channel_id=1, source_target_pairs={{0,32},{4,36},{8,40},{12,44},{16,48},{20,52},{24,56},{28,60},{32,6... | collective-permute-start | bytes 786440 | tf_op jit(solution)/shard_map/ppermute | solution.py:15
  112.4 8.2 %copy-start.55 = (f32[1,256]{1,0:T(1,128)S(1)}, f32[1,256]{1,0:T(1,128)}, u32[]{:S(2)}) copy-start(f32[1,256]{1,0:T(1,128)} %copy-done.54) | copy-start | bytes 3076
  112.4 8.2 %copy-start.51 = (f32[4,1,256]{2,1,0:T(1,128)S(1)}, f32[4,1,256]{2,1,0:T(1,128)}, u32[]{:S(2)}) copy-start(f32[4,1,256]{2,1,0:T(1,128)} %copy-done.50) | copy-start | bytes 12292
  112.4 8.2 %copy-start.53 = (f32[4,1,256]{2,1,0:T(1,128)S(1)}, f32[4,1,256]{2,1,0:T(1,128)}, u32[]{:S(2)}) copy-start(f32[4,1,256]{2,1,0:T(1,128)} %copy-done.52) | copy-start | bytes 12292
  112.4 8.6 %copy-start.35 = (f32[4,1,256]{2,1,0:T(1,128)S(1)}, f32[4,1,256]{2,1,0:T(1,128)}, u32[]{:S(2)}) copy-start(f32[4,1,256]{2,1,0:T(1,128)} %copy-done.33) | copy-start | bytes 12292
  112.4 8.6 %copy-start.49 = (f32[4,1,256]{2,1,0:T(1,128)S(1)}, f32[4,1,256]{2,1,0:T(1,128)}, u32[]{:S(2)}) copy-start(f32[4,1,256]{2,1,0:T(1,128)} %copy-done.48) | copy-start | bytes 12292
  112.4 8.9 %copy-start.32 = (f32[4,1,256]{2,1,0:T(1,128)S(1)}, f32[4,1,256]{2,1,0:T(1,128)}, u32[]{:S(2)}) copy-start(f32[4,1,256]{2,1,0:T(1,128)} %copy-done.30) | copy-start | bytes 12292
  112.4 8.9 %copy-start.47 = (f32[4,1,256]{2,1,0:T(1,128)S(1)}, f32[4,1,256]{2,1,0:T(1,128)}, u32[]{:S(2)}) copy-start(f32[4,1,256]{2,1,0:T(1,128)} %copy-done.46) | copy-start | bytes 12292
  112.4 9.2 %copy-start.29 = (f32[4,1,256]{2,1,0:T(1,128)S(1)}, f32[4,1,256]{2,1,0:T(1,128)}, u32[]{:S(2)}) copy-start(f32[4,1,256]{2,1,0:T(1,128)} %copy-done.27) | copy-start | bytes 12292
  112.4 9.2 %copy-start.45 = (f32[4,1,256]{2,1,0:T(1,128)S(1)}, f32[4,1,256]{2,1,0:T(1,128)}, u32[]{:S(2)}) copy-start(f32[4,1,256]{2,1,0:T(1,128)} %copy-done.44) | copy-start | bytes 12292
  112.4 9.5 %copy-start.26 = (f32[4,1,256]{2,1,0:T(1,128)S(1)}, f32[4,1,256]{2,1,0:T(1,128)}, u32[]{:S(2)}) copy-start(f32[4,1,256]{2,1,0:T(1,128)} %copy-done.24) | copy-start | bytes 12292
  112.5 9.5 %copy-start.43 = (f32[4,1,256]{2,1,0:T(1,128)S(1)}, f32[4,1,256]{2,1,0:T(1,128)}, u32[]{:S(2)}) copy-start(f32[4,1,256]{2,1,0:T(1,128)} %copy-done.42) | copy-start | bytes 12292
  112.5 9.9 %copy-start.23 = (f32[4,1,256]{2,1,0:T(1,128)S(1)}, f32[4,1,256]{2,1,0:T(1,128)}, u32[]{:S(2)}) copy-start(f32[4,1,256]{2,1,0:T(1,128)} %copy-done.21) | copy-start | bytes 12292
  112.5 9.9 %copy-start.41 = (f32[4,1,256]{2,1,0:T(1,128)S(1)}, f32[4,1,256]{2,1,0:T(1,128)}, u32[]{:S(2)}) copy-start(f32[4,1,256]{2,1,0:T(1,128)} %copy-done.40) | copy-start | bytes 12292
  112.5 10.2 %copy-start.20 = (f32[4,1,256]{2,1,0:T(1,128)S(1)}, f32[4,1,256]{2,1,0:T(1,128)}, u32[]{:S(2)}) copy-start(f32[4,1,256]{2,1,0:T(1,128)} %copy-done.18) | copy-start | bytes 12292
  112.5 10.2 %copy-start.39 = (f32[4,1,256]{2,1,0:T(1,128)S(1)}, f32[4,1,256]{2,1,0:T(1,128)}, u32[]{:S(2)}) copy-start(f32[4,1,256]{2,1,0:T(1,128)} %copy-done.38) | copy-start | bytes 12292
  112.5 10.5 %copy-start.17 = (f32[4,1,256]{2,1,0:T(1,128)S(1)}, f32[4,1,256]{2,1,0:T(1,128)}, u32[]{:S(2)}) copy-start(f32[4,1,256]{2,1,0:T(1,128)} %copy-done.15) | copy-start | bytes 12292
  112.5 10.5 %copy-start.37 = (f32[4,1,256]{2,1,0:T(1,128)S(1)}, f32[4,1,256]{2,1,0:T(1,128)}, u32[]{:S(2)}) copy-start(f32[4,1,256]{2,1,0:T(1,128)} %copy-done.36) | copy-start | bytes 12292
  113.8 9.6 %copy-start.14 = (f32[256,256,1]{1,0,2:T(8,128)S(1)}, f32[256,256,1]{1,0,2:T(8,128)}, u32[]{:S(2)}) copy-start(f32[256,256,1]{1,0,2:T(8,128)} %convolution_bitcast_fusion.2) | copy-start | bytes 786436
  114.5 3.6 %collective-permute-start.14 = (f32[256]{0:T(256)S(1)}, f32[256]{0:T(256)S(1)}, u32[]{:S(2)}, u32[]{:S(2)}) collective-permute-start(f32[256]{0:T(256)S(1)} %add.161), channel_id=1, source_target_pairs={{0,64},{4,68},{8,72},{12,76},{16,80},{20,84},{24,88},{28,92},{32,9... | collective-permute-start | bytes 3080 | tf_op jit(solution)/shard_map/ppermute | solution.py:15
  123.7 8.3 %copy-start.4 = (f32[2,256,256]{1,2,0:T(8,128)S(1)}, f32[2,256,256]{1,2,0:T(8,128)}, u32[]{:S(2)}) copy-start(f32[2,256,256]{1,2,0:T(8,128)} %copy-done.2) | copy-start | bytes 1572868
  123.9 21.1 %copy-start.8 = (f32[256,256]{1,0:T(8,128)S(1)}, f32[256,256]{1,0:T(8,128)}, u32[]{:S(2)}) copy-start(f32[256,256]{1,0:T(8,128)} %copy-done.7) | copy-start | bytes 786436
  125.2 27.9 %copy-start.6 = (f32[256,256]{1,0:T(8,128)S(1)}, f32[256,256]{1,0:T(8,128)}, u32[]{:S(2)}) copy-start(f32[256,256]{1,0:T(8,128)} %copy-done.5) | copy-start | bytes 786436
  125.2 41.0 %copy-start.13 = (f32[256,256]{1,0:T(8,128)S(1)}, f32[256,256]{1,0:T(8,128)}, u32[]{:S(2)}) copy-start(f32[256,256]{1,0:T(8,128)} %fusion.149) | copy-start | bytes 786436
  126.6 10.4 %collective-permute-start.16 = (f32[256]{0:T(256)S(1)}, f32[256]{0:T(256)S(1)}, u32[]{:S(2)}, u32[]{:S(2)}) collective-permute-start(f32[256]{0:T(256)S(1)} %select_add_fusion), channel_id=1, source_target_pairs={{8,0},{12,4},{16,8},{20,12},{24,16},{28,20},{32,24},{36,28},{40,32... | collective-permute-start | bytes 3080 | tf_op jit(solution)/shard_map/ppermute | solution.py:19
  132.8 4.5 %collective-permute-start.15 = (f32[256]{0:T(256)S(1)}, f32[256]{0:T(256)S(1)}, u32[]{:S(2)}, u32[]{:S(2)}) collective-permute-start(f32[256]{0:T(256)S(1)} %select_add_fusion), channel_id=1, source_target_pairs={{4,0},{8,4},{12,8},{16,12},{20,16},{24,20},{28,24},{32,28},{36,32}... | collective-permute-start | bytes 3080 | tf_op jit(solution)/shard_map/ppermute | solution.py:19
  137.4 7.6 %collective-permute-start.17 = (f32[256]{0:T(256)S(1)}, f32[256]{0:T(256)S(1)}, u32[]{:S(2)}, u32[]{:S(2)}) collective-permute-start(f32[256]{0:T(256)S(1)} %add.179), channel_id=1, source_target_pairs={{8,0},{12,4},{16,8},{20,12},{24,16},{28,20},{32,24},{36,28},{40,32... | collective-permute-start | bytes 3080 | tf_op jit(solution)/shard_map/ppermute | solution.py:19
  145.2 7.9 %collective-permute-start.18 = (f32[256]{0:T(256)S(1)}, f32[256]{0:T(256)S(1)}, u32[]{:S(2)}, u32[]{:S(2)}) collective-permute-start(f32[256]{0:T(256)S(1)} %add.180), channel_id=1, source_target_pairs={{16,0},{20,4},{24,8},{28,12},{32,16},{36,20},{40,24},{44,28},{48,3... | collective-permute-start | bytes 3080 | tf_op jit(solution)/shard_map/ppermute | solution.py:19
  153.4 5.5 %collective-permute-start.19 = (f32[256]{0:T(256)S(1)}, f32[256]{0:T(256)S(1)}, u32[]{:S(2)}, u32[]{:S(2)}) collective-permute-start(f32[256]{0:T(256)S(1)} %add.181), channel_id=1, source_target_pairs={{32,0},{36,4},{40,8},{44,12},{48,16},{52,20},{56,24},{60,28},{64,3... | collective-permute-start | bytes 3080 | tf_op jit(solution)/shard_map/ppermute | solution.py:19
  159.2 7.0 %collective-permute-start.20 = (f32[256]{0:T(256)S(1)}, f32[256]{0:T(256)S(1)}, u32[]{:S(2)}, u32[]{:S(2)}) collective-permute-start(f32[256]{0:T(256)S(1)} %add.182), channel_id=1, source_target_pairs={{64,0},{68,4},{72,8},{76,12},{80,16},{84,20},{88,24},{92,28},{96,3... | collective-permute-start | bytes 3080 | tf_op jit(solution)/shard_map/ppermute | solution.py:19
  (14 other events, 50.2 us)
where the time goes:
time: 172 us; the launch traced here: 171 us
  starting transfers between devices  58.1 us (34%)
  matrix products  53.2 us (31%)
  waiting for transfers between devices  27.5 us (16%)
  local copies, waits for them, and re-layouts  24.9 us (14%)
  other arithmetic  4.89 us (3%)
  between operations  2.06 us (1%)
    ppermute x12, starting transfers between devices, shift_down(): lax.ppermute(value, axis, [(i, i + steps) for i in range(count - steps)])  37.9 us
    dot_general x55, matrix products, dot(): return jnp.dot(a, b, precision=precise)  27.1 us
    ppermute x6, waiting for transfers between devices, shift_up(): lax.ppermute(value, axis, [(i + steps, i) for i in range(count - steps)])  20.5 us
    unnamed x135, local copies, waits for them, and re-layouts  17.1 us
    ppermute x6, starting transfers between devices, shift_up(): lax.ppermute(value, axis, [(i + steps, i) for i in range(count - steps)])  15 us
    conv_general_dilated x1, matrix products, conv_stride(): lax.conv_general_dilated(images, kernel, (2, 2), ((0, 0), (1, 1)), dimens...  9.39 us
    dot_general x7, matrix products, per_device(): jnp.einsum('ab,sbc->sac', transition, phis, precision=precise)  8.11 us
    dot_general x1, matrix products, encode(): jnp.einsum('shwc,hwcm->sm', encoded, obs_gain, preferred_element_type=jnp...  5.35 us
  transfers between devices with their start and end apart: 21, of which 11 were waited for; matrix products, arithmetic and copies ran while one was open for 32% of the time, Pallas kernels for 0%

commit v1 on v0

--- a/solution.py
+++ b/solution.py
@@ -49,22 +49,26 @@
     return (partial + got[1]) + (got[2] + got[0])
 
 
-def exclusive_scan(mats, vecs, axis, count):
+def scan_gains(mats, axis, count):
     mat1 = shift_down(mats, axis, 1, count)
     mat2 = shift_down(mats, axis, 2, count)
+    gains = [dot(mat1, mat2)]
+    stride = 2
+    while stride * 2 < count:
+        got_gain = shift_down(gains[-1], axis, stride, count)
+        gains.append(dot(gains[-1], got_gain))
+        stride *= 2
+    return mat1, gains
+
+
+def scan_carry(mat1, gains, vecs, axis, count):
     vec1 = shift_down(vecs, axis, 1, count)
     vec2 = shift_down(vecs, axis, 2, count)
     carry = vec1 + dot(mat1, vec2)
-    gain = dot(mat1, mat2)
     stride = 2
-    while stride < count:
-        more = stride * 2 < count
+    for gain in gains:
         got = shift_down(carry, axis, stride, count)
-        if more:
-            got_gain = shift_down(gain, axis, stride, count)
         carry = carry + dot(gain, got)
-        if more:
-            gain = dot(gain, got_gain)
         stride *= 2
     return carry
 
@@ -100,7 +104,9 @@
     for s in range(1, bands):
         block_phi = dot(phis[s], block_phi)
 
+    mat1, gains = scan_gains(block_phi, "tm", blocks)
     partial = encode(fields, conv_in, conv_mid, obs_gain, bands)
+    (mat1, gains), partial = lax.optimization_barrier(((mat1, gains), partial))
     increments = sum_bands(partial, bands).reshape(bands, hours, modes)
 
     state = increments[:, 0]
@@ -114,7 +120,7 @@
     for s in range(1, bands):
         block_sum = dot(phis[s], block_sum) + ends[s]
 
-    carry = exclusive_scan(block_phi, block_sum, "tm", blocks)
+    carry = scan_carry(mat1, gains, block_sum, "tm", blocks)
     starts = [carry]
     for s in range(bands - 1):
         starts.append(dot(phis[s], starts[-1]) + ends[s])

time: 172 us -> 188 us (1.093)
  matrix products: 53.2 us -> 62.3 us
  waiting for transfers between devices: 27.5 us -> 34.3 us
    dot_general x55, matrix products: 27.1 us -> 36.3 us  [dot(): return jnp.dot(a, b, precision=precise)]
    ppermute x6, waiting for transfers between devices: 20.5 us -> 24.4 us  [shift_up(): lax.ppermute(value, axis, [(i + steps, i) for i in range(count - steps)])]
    ppermute x12, waiting for transfers between devices: 5.16 us -> 8.52 us  [shift_down(): lax.ppermute(value, axis, [(i, i + steps) for i in range(count - steps)])]
    unnamed x135 -> x115, local copies, waits for them, and re-layouts: 17.1 us -> 17.1 us
  transfers between devices with their start and end apart: 21 -> 21, of which waited for: 11 -> 12; matrix products, arithmetic and copies ran while one was open for 32% -> 27% of each run, Pallas kernels for 0% -> 0%
where the time goes in v1:
time: 188 us; the launch traced here: 187 us
  matrix products  62.3 us (33%)
  starting transfers between devices  57.8 us (31%)
  waiting for transfers between devices  34.3 us (18%)
  local copies, waits for them, and re-layouts  24.8 us (13%)
  other arithmetic  5.4 us (3%)
  between operations  1.99 us (1%)
    ppermute x12, starting transfers between devices, shift_down(): lax.ppermute(value, axis, [(i, i + steps) for i in range(count - steps)])  39.6 us
    dot_general x55, matrix products, dot(): return jnp.dot(a, b, precision=precise)  36.3 us
    ppermute x6, waiting for transfers between devices, shift_up(): lax.ppermute(value, axis, [(i + steps, i) for i in range(count - steps)])  24.4 us
    unnamed x115, local copies, waits for them, and re-layouts  17.1 us
    ppermute x6, starting transfers between devices, shift_up(): lax.ppermute(value, axis, [(i + steps, i) for i in range(count - steps)])  13.3 us
    conv_general_dilated x1, matrix products, conv_stride(): lax.conv_general_dilated(images, kernel, (2, 2), ((0, 0), (1, 1)), dimens...  9.42 us
    ppermute x12, waiting for transfers between devices, shift_down(): lax.ppermute(value, axis, [(i, i + steps) for i in range(count - steps)])  8.52 us
    dot_general x7, matrix products, per_device(): jnp.einsum('ab,sbc->sac', transition, phis, precision=precise)  8.1 us
  transfers between devices with their start and end apart: 21, of which 12 were waited for; matrix products, arithmetic and copies ran while one was open for 27% of the time, Pallas kernels for 0%

profile of v1, /device:TPU:14, one launch (start us, length us, event | category | flops | bytes accessed | tf_op | source)
XLA Modules:
  0.0 186.7 jit_solution(11947761721854296596)
XLA Ops:
  0.7 1.1 copy.84
  1.8 1.1 fusion.130
  3.0 2.0 %fusion.23 = f32[4,256,256]{1,2,0:T(8,128)S(1)} fusion(f32[256,256]{0,1:T(8,128)S(1)} %copy.84, f32[4,256]{1,0:T(4,128)S(1)} %get-tuple-element.71, f32[4,256]{1,0:T(4,128)S(1)} %get-tuple-element.64, f32[256,256]{1,0:T(8,128)} %param.11), kind=kOutput, calls=%fused_computation.29 | convolution fusion | flops 805830656 | bytes 1581056 | tf_op jit(solution)/shard_map/ab,sbc->sac/dot_general | solution.py:102
  5.0 1.0 fusion.22
  6.1 1.0 fusion.21
  7.1 1.0 fusion.20
  8.2 1.0 fusion.19
  9.2 1.0 fusion.18
  10.3 1.0 fusion.17
  12.5 1.3 fusion.75
  13.8 1.9 %collective-permute-start = (f32[256,256]{1,0:T(8,128)}, f32[256,256]{1,0:T(8,128)}, u32[]{:S(2)}, u32[]{:S(2)}) collective-permute-start(f32[256,256]{1,0:T(8,128)} %fusion.75), channel_id=1, source_target_pairs={{0,4},{4,8},{8,12},{12,16},{16,20},{20,24},{24,28},{28,32},{32,36}... | collective-permute-start | bytes 786440 | tf_op jit(solution)/shard_map/ppermute | solution.py:15
  15.7 3.4 %collective-permute-start.1 = (f32[256,256]{1,0:T(8,128)}, f32[256,256]{1,0:T(8,128)}, u32[]{:S(2)}, u32[]{:S(2)}) collective-permute-start(f32[256,256]{1,0:T(8,128)} %fusion.75), channel_id=1, source_target_pairs={{0,8},{4,12},{8,16},{12,20},{16,24},{20,28},{24,32},{28,36},{32,40... | collective-permute-start | bytes 786440 | tf_op jit(solution)/shard_map/ppermute | solution.py:15
  20.2 4.6 %collective-permute-start.5 = (bf16[256,768]{1,0:T(8,128)(2,1)}, bf16[256,768]{1,0:T(8,128)(2,1)}, u32[]{:S(2)}, u32[]{:S(2)}) collective-permute-start(bf16[256,768]{1,0:T(8,128)(2,1)} %bitcast.151), channel_id=1, source_target_pairs={{0,1},{1,2},{2,3},{4,5},{5,6},{6,7},{8,9},{9,10},{10,11},{12,13},{... | collective-permute-start | bytes 1179656 | tf_op jit(solution)/shard_map/ppermute | solution.py:15
  26.4 1.3 constant_dynamic-update-slice_fusion.16
  30.7 1.1 fusion.145
  32.5 1.4 fusion.147
  34.0 2.1 %fusion.132 = f32[256,256]{1,0:T(8,128)} fusion(f32[256,256]{1,0:T(8,128)} %collective-permute-done, f32[256,256]{1,0:T(8,128)} %collective-permute-done.1), kind=kOutput, calls=%fused_computation.224 | convolution fusion | flops 201326592 | bytes 786432 | tf_op jit(solution)/shard_map/dot_general | solution.py:11
  36.1 3.4 %collective-permute-start.2 = (f32[256,256]{1,0:T(8,128)}, f32[256,256]{1,0:T(8,128)}, u32[]{:S(2)}, u32[]{:S(2)}) collective-permute-start(f32[256,256]{1,0:T(8,128)} %fusion.132), channel_id=1, source_target_pairs={{0,8},{4,12},{8,16},{12,20},{16,24},{20,28},{24,32},{28,36},{32,40... | collective-permute-start | bytes 786440 | tf_op jit(solution)/shard_map/ppermute | solution.py:15
  40.0 5.1 %copy.86 = bf16[32,8,8,256]{0,1,3,2:T(8,128)(2,1)} copy(bf16[32,8,8,256]{3,2,1,0:T(8,128)(2,1)} %param.7) | data formatting | bytes 2097152 | tf_op args[0]
  45.1 1.8 bitcast_dynamic-update-slice_fusion
  47.0 2.1 %reshape.51 = bf16[32,8,3,256]{3,2,1,0:T(4,128)(2,1)} reshape(bf16[256,768]{1,0:T(8,128)(2,1)} %collective-permute-done.5) | data formatting | bytes 786432 | tf_op jit(solution)/shard_map/reshape | solution.py:37
  49.1 3.0 %copy.85 = bf16[32,8,3,256]{0,1,3,2:T(8,128)(2,1)} copy(bf16[32,8,3,256]{3,2,1,0:T(4,128)(2,1)} %reshape.51) | data formatting | bytes 786432 | tf_op jit(solution)/shard_map/reshape | solution.py:37
  52.1 2.1 %fusion.133 = f32[256,256]{1,0:T(8,128)} fusion(f32[256,256]{1,0:T(8,128)} %fusion.132, f32[256,256]{1,0:T(8,128)} %collective-permute-done.2), kind=kOutput, calls=%fused_computation.225 | convolution fusion | flops 201326592 | bytes 786432 | tf_op jit(solution)/shard_map/dot_general | solution.py:11
  54.2 4.0 %collective-permute-start.3 = (f32[256,256]{1,0:T(8,128)}, f32[256,256]{1,0:T(8,128)}, u32[]{:S(2)}, u32[]{:S(2)}) collective-permute-start(f32[256,256]{1,0:T(8,128)} %fusion.133), channel_id=1, source_target_pairs={{0,16},{4,20},{8,24},{12,28},{16,32},{20,36},{24,40},{28,44},{32,4... | collective-permute-start | bytes 786440 | tf_op jit(solution)/shard_map/ppermute | solution.py:15
  58.3 9.4 %fusion.4 = f32[32,2,64,128]{3,0,2,1:T(8,128)} fusion(bf16[128,64,3,3]{0,1,3,2:T(8,128)(2,1)S(1)} %copy-done, pred[5]{0:T(512)(128)(4,1)} %compare_and_fusion, bf16[64,8,3,3]{0,1,3,2:T(8,128)(2,1)} %param.8, bf16[32,8,8,256]{0,1,3,2:T(8,128)(2,1)} %copy.86, bf16[32,8,3,256]{0,1,3,2:T(8,128)(2,1)} %copy.85), kind=kOutput, calls=%fused_computation.5 | convolution fusion | flops 799834112 | bytes 3695621 | tf_op jit(solution)/shard_map/conv_general_dilated | solution.py:23
  67.7 1.4 fusion.134
  69.1 3.4 %collective-permute-start.4 = (f32[256,256]{1,0:T(8,128)S(1)}, f32[256,256]{1,0:T(8,128)S(1)}, u32[]{:S(2)}, u32[]{:S(2)}) collective-permute-start(f32[256,256]{1,0:T(8,128)S(1)} %fusion.134), channel_id=1, source_target_pairs={{0,32},{4,36},{8,40},{12,44},{16,48},{20,52},{24,56},{28,60},{32,6... | collective-permute-start | bytes 786440 | tf_op jit(solution)/shard_map/ppermute | solution.py:15
  72.5 5.3 %convolution_bitcast_fusion.3 = f32[32,256]{1,0:T(8,128)S(1)} fusion(bf16[2,64,128,256]{3,2,1,0:T(8,128)(2,1)} %param.10, f32[32,2,64,128]{3,0,2,1:T(8,128)} %fusion.4), kind=kOutput, calls=%fused_computation.33 | convolution fusion | flops 271056896 | bytes 10518528 | tf_op jit(solution)/shard_map/shwc,hwcm->sm/dot_general | solution.py:44
  77.9 1.5 collective-permute-done.4
  79.4 1.1 fusion.135
  80.5 1.2 collective-permute-start.7
  82.5 3.0 %collective-permute-start.6 = (f32[32,256]{1,0:T(8,128)S(1)}, f32[32,256]{1,0:T(8,128)S(1)}, u32[]{:S(2)}, u32[]{:S(2)}) collective-permute-start(f32[32,256]{1,0:T(8,128)S(1)} %convolution_bitcast_fusion.3), channel_id=1, source_target_pairs={{0,2},{1,3},{2,0},{3,1},{4,6},{5,7},{6,4},{7,5},{8,10},{9,11},{10,... | collective-permute-start | bytes 98312 | tf_op jit(solution)/shard_map/ppermute | solution.py:48
  85.5 1.1 fusion.149
  86.8 1.2 collective-permute-done.6
  91.7 4.0 %collective-permute-start.10 = (f32[256]{0:T(256)S(1)}, f32[256]{0:T(256)S(1)}, u32[]{:S(2)}, u32[]{:S(2)}) collective-permute-start(f32[256]{0:T(256)S(1)} %add.157), channel_id=1, source_target_pairs={{0,8},{4,12},{8,16},{12,20},{16,24},{20,28},{24,32},{28,36},{32,40... | collective-permute-start | bytes 3080 | tf_op jit(solution)/shard_map/ppermute | solution.py:15
  96.7 1.9 %collective-permute-start.9 = (f32[256]{0:T(256)S(1)}, f32[256]{0:T(256)S(1)}, u32[]{:S(2)}, u32[]{:S(2)}) collective-permute-start(f32[256]{0:T(256)S(1)} %add.157), channel_id=1, source_target_pairs={{0,4},{4,8},{8,12},{12,16},{16,20},{20,24},{24,28},{28,32},{32,36}... | collective-permute-start | bytes 3080 | tf_op jit(solution)/shard_map/ppermute | solution.py:15
  98.6 1.2 fusion.136
  99.8 1.7 collective-permute-done.9
  101.5 4.9 %collective-permute-start.11 = (f32[256]{0:T(256)S(1)}, f32[256]{0:T(256)S(1)}, u32[]{:S(2)}, u32[]{:S(2)}) collective-permute-start(f32[256]{0:T(256)S(1)} %add.158), channel_id=1, source_target_pairs={{0,8},{4,12},{8,16},{12,20},{16,24},{20,28},{24,32},{28,36},{32,40... | collective-permute-start | bytes 3080 | tf_op jit(solution)/shard_map/ppermute | solution.py:15
  107.7 1.2 fusion.137
  109.0 3.6 %collective-permute-start.12 = (f32[256]{0:T(256)S(1)}, f32[256]{0:T(256)S(1)}, u32[]{:S(2)}, u32[]{:S(2)}) collective-permute-start(f32[256]{0:T(256)S(1)} %add.159), channel_id=1, source_target_pairs={{0,16},{4,20},{8,24},{12,28},{16,32},{20,36},{24,40},{28,44},{32,4... | collective-permute-start | bytes 3080 | tf_op jit(solution)/shard_map/ppermute | solution.py:15
  113.5 2.5 %collective-permute-done.12 = f32[256]{0:T(256)S(1)} collective-permute-done((f32[256]{0:T(256)S(1)}, f32[256]{0:T(256)S(1)}, u32[]{:S(2)}, u32[]{:S(2)}) %collective-permute-start.12) | collective-permute-done | bytes 1056 | tf_op jit(solution)/shard_map/ppermute | solution.py:15
  116.0 1.2 fusion.138
  117.2 2.2 %collective-permute-start.13 = (f32[256]{0:T(256)S(1)}, f32[256]{0:T(256)S(1)}, u32[]{:S(2)}, u32[]{:S(2)}) collective-permute-start(f32[256]{0:T(256)S(1)} %add.160), channel_id=1, source_target_pairs={{0,32},{4,36},{8,40},{12,44},{16,48},{20,52},{24,56},{28,60},{32,6... | collective-permute-start | bytes 3080 | tf_op jit(solution)/shard_map/ppermute | solution.py:15
  120.2 2.5 %collective-permute-done.13 = f32[256]{0:T(256)S(1)} collective-permute-done((f32[256]{0:T(256)S(1)}, f32[256]{0:T(256)S(1)}, u32[]{:S(2)}, u32[]{:S(2)}) %collective-permute-start.13) | collective-permute-done | bytes 1056 | tf_op jit(solution)/shard_map/ppermute | solution.py:15
  123.6 2.2 %collective-permute-start.14 = (f32[256]{0:T(256)}, f32[256]{0:T(256)}, u32[]{:S(2)}, u32[]{:S(2)}) collective-permute-start(f32[256]{0:T(256)} %add.161), channel_id=1, source_target_pairs={{0,64},{4,68},{8,72},{12,76},{16,80},{20,84},{24,88},{28,92},{32,9... | collective-permute-start | bytes 3080 | tf_op jit(solution)/shard_map/ppermute | solution.py:15
  125.7 1.1 convolution_bitcast_fusion.2
  126.9 1.4 fusion.140
  132.6 1.1 constant_dynamic-update-slice_fusion.6
  133.7 1.0 constant_dynamic-update-slice_fusion.5
  134.8 1.0 constant_dynamic-update-slice_fusion.4
  137.7 1.3 fusion.15
  140.4 4.2 %collective-permute-start.16 = (f32[256]{0:T(256)S(1)}, f32[256]{0:T(256)S(1)}, u32[]{:S(2)}, u32[]{:S(2)}) collective-permute-start(f32[256]{0:T(256)S(1)} %select_add_fusion), channel_id=1, source_target_pairs={{8,0},{12,4},{16,8},{20,12},{24,16},{28,20},{32,24},{36,28},{40,32... | collective-permute-start | bytes 3080 | tf_op jit(solution)/shard_map/ppermute | solution.py:19
  145.4 1.9 %collective-permute-start.15 = (f32[256]{0:T(256)S(1)}, f32[256]{0:T(256)S(1)}, u32[]{:S(2)}, u32[]{:S(2)}) collective-permute-start(f32[256]{0:T(256)S(1)} %select_add_fusion), channel_id=1, source_target_pairs={{4,0},{8,4},{12,8},{16,12},{20,16},{24,20},{28,24},{32,28},{36,32}... | collective-permute-start | bytes 3080 | tf_op jit(solution)/shard_map/ppermute | solution.py:19
  147.3 5.8 %collective-permute-done.16 = f32[256]{0:T(256)S(1)} collective-permute-done((f32[256]{0:T(256)S(1)}, f32[256]{0:T(256)S(1)}, u32[]{:S(2)}, u32[]{:S(2)}) %collective-permute-start.16) | collective-permute-done | bytes 1056 | tf_op jit(solution)/shard_map/ppermute | solution.py:19
  153.5 1.9 %collective-permute-start.17 = (f32[256]{0:T(256)S(1)}, f32[256]{0:T(256)S(1)}, u32[]{:S(2)}, u32[]{:S(2)}) collective-permute-start(f32[256]{0:T(256)S(1)} %add.179), channel_id=1, source_target_pairs={{8,0},{12,4},{16,8},{20,12},{24,16},{28,20},{32,24},{36,28},{40,32... | collective-permute-start | bytes 3080 | tf_op jit(solution)/shard_map/ppermute | solution.py:19
  156.2 4.9 %collective-permute-done.17 = f32[256]{0:T(256)S(1)} collective-permute-done((f32[256]{0:T(256)S(1)}, f32[256]{0:T(256)S(1)}, u32[]{:S(2)}, u32[]{:S(2)}) %collective-permute-start.17) | collective-permute-done | bytes 1056 | tf_op jit(solution)/shard_map/ppermute | solution.py:19
  161.3 2.0 %collective-permute-start.18 = (f32[256]{0:T(256)S(1)}, f32[256]{0:T(256)S(1)}, u32[]{:S(2)}, u32[]{:S(2)}) collective-permute-start(f32[256]{0:T(256)S(1)} %add.180), channel_id=1, source_target_pairs={{16,0},{20,4},{24,8},{28,12},{32,16},{36,20},{40,24},{44,28},{48,3... | collective-permute-start | bytes 3080 | tf_op jit(solution)/shard_map/ppermute | solution.py:19
  164.1 5.2 %collective-permute-done.18 = f32[256]{0:T(256)S(1)} collective-permute-done((f32[256]{0:T(256)S(1)}, f32[256]{0:T(256)S(1)}, u32[]{:S(2)}, u32[]{:S(2)}) %collective-permute-start.18) | collective-permute-done | bytes 1056 | tf_op jit(solution)/shard_map/ppermute | solution.py:19
  169.5 2.0 %collective-permute-start.19 = (f32[256]{0:T(256)S(1)}, f32[256]{0:T(256)S(1)}, u32[]{:S(2)}, u32[]{:S(2)}) collective-permute-start(f32[256]{0:T(256)S(1)} %add.181), channel_id=1, source_target_pairs={{32,0},{36,4},{40,8},{44,12},{48,16},{52,20},{56,24},{60,28},{64,3... | collective-permute-start | bytes 3080 | tf_op jit(solution)/shard_map/ppermute | solution.py:19
  171.5 3.5 %collective-permute-done.19 = f32[256]{0:T(256)S(1)} collective-permute-done((f32[256]{0:T(256)S(1)}, f32[256]{0:T(256)S(1)}, u32[]{:S(2)}, u32[]{:S(2)}) %collective-permute-start.19) | collective-permute-done | bytes 1056 | tf_op jit(solution)/shard_map/ppermute | solution.py:19
  175.3 1.3 collective-permute-start.20
  177.3 5.0 %collective-permute-done.20 = f32[256]{0:T(256)S(1)} collective-permute-done((f32[256]{0:T(256)S(1)}, f32[256]{0:T(256)S(1)}, u32[]{:S(2)}, u32[]{:S(2)}) %collective-permute-start.20) | collective-permute-done | bytes 1056 | tf_op jit(solution)/shard_map/ppermute | solution.py:19
  183.4 2.7 %fusion.12 = f32[1,8,256]{2,0,1:T(1,128)S(1)} fusion(f32[32,8,8,256]{3,2,1,0:T(8,128)} %bitcast.147, s32[]{:T(128)S(6)} %select_n.26, f32[1,256]{1,0:T(1,128)S(1)} %bitcast.452, f32[1,256]{1,0:T(1,128)S(1)} %bitcast.465, f32[1,256]{1,0:T(1,128)S(1)} %bitcast.449, f32[1,256]{1,0:T(1,128)S(1)} %bitcast.445), kind=kOutput, calls=%fused_computation.9 | convolution fusion | flops 6292224 | bytes 2109444 | tf_op jit(solution)/shard_map/dot_general | solution.py:11
  (201 shorter events, 30.7 us)
Async XLA Ops:
  0.6 57.6 %copy-start = (bf16[128,64,3,3]{0,1,3,2:T(8,128)(2,1)S(1)}, bf16[128,64,3,3]{0,1,3,2:T(8,128)(2,1)}, u32[]{:S(2)}) copy-start(bf16[128,64,3,3]{0,1,3,2:T(8,128)(2,1)} %param.9) | copy-start | bytes 442372
  0.6 4.4 %copy-start.1 = (f32[256,256]{1,0:T(8,128)S(1)}, f32[256,256]{1,0:T(8,128)}, u32[]{:S(2)}) copy-start(f32[256,256]{1,0:T(8,128)} %param.11) | copy-start | bytes 786436
  2.9 2.1 %copy-start.14 = (f32[4,1,256]{2,1,0:T(1,128)}, f32[4,1,256]{2,1,0:T(1,128)S(1)}, u32[]{:S(2)}) copy-start(f32[4,1,256]{2,1,0:T(1,128)S(1)} %get-tuple-element.32) | copy-start | bytes 12292
  2.9 4.2 %copy-start.23 = (f32[4,1,256]{2,1,0:T(1,128)}, f32[4,1,256]{2,1,0:T(1,128)S(1)}, u32[]{:S(2)}) copy-start(f32[4,1,256]{2,1,0:T(1,128)S(1)} %get-tuple-element.35) | copy-start | bytes 12292
  2.9 4.2 %copy-start.26 = (f32[4,1,256]{2,1,0:T(1,128)}, f32[4,1,256]{2,1,0:T(1,128)S(1)}, u32[]{:S(2)}) copy-start(f32[4,1,256]{2,1,0:T(1,128)S(1)} %get-tuple-element.34) | copy-start | bytes 12292
  3.0 5.2 %copy-start.17 = (f32[4,1,256]{2,1,0:T(1,128)}, f32[4,1,256]{2,1,0:T(1,128)S(1)}, u32[]{:S(2)}) copy-start(f32[4,1,256]{2,1,0:T(1,128)S(1)} %get-tuple-element.37) | copy-start | bytes 12292
  3.0 5.2 %copy-start.20 = (f32[4,1,256]{2,1,0:T(1,128)}, f32[4,1,256]{2,1,0:T(1,128)S(1)}, u32[]{:S(2)}) copy-start(f32[4,1,256]{2,1,0:T(1,128)S(1)} %get-tuple-element.36) | copy-start | bytes 12292
  10.2 8.9 %copy-start.11 = (bf16[32,8,8,256]{3,2,1,0:T(8,128)(2,1)S(1)}, bf16[32,8,8,256]{3,2,1,0:T(8,128)(2,1)}, u32[]{:S(2)}) copy-start(bf16[32,8,8,256]{3,2,1,0:T(8,128)(2,1)} %param.7) | copy-start | bytes 3145732
  11.9 13.7 %copy-start.8 = (f32[256,256]{1,0:T(8,128)S(1)}, f32[256,256]{1,0:T(8,128)}, u32[]{:S(2)}) copy-start(f32[256,256]{1,0:T(8,128)} %param.12) | copy-start | bytes 786436
  13.8 20.2 %collective-permute-start = (f32[256,256]{1,0:T(8,128)}, f32[256,256]{1,0:T(8,128)}, u32[]{:S(2)}, u32[]{:S(2)}) collective-permute-start(f32[256,256]{1,0:T(8,128)} %fusion.75), channel_id=1, source_target_pairs={{0,4},{4,8},{8,12},{12,16},{16,20},{20,24},{24,28},{28,32},{32,36}... | collective-permute-start | bytes 786440 | tf_op jit(solution)/shard_map/ppermute | solution.py:15
  15.7 18.3 %collective-permute-start.1 = (f32[256,256]{1,0:T(8,128)}, f32[256,256]{1,0:T(8,128)}, u32[]{:S(2)}, u32[]{:S(2)}) collective-permute-start(f32[256,256]{1,0:T(8,128)} %fusion.75), channel_id=1, source_target_pairs={{0,8},{4,12},{8,16},{12,20},{16,24},{20,28},{24,32},{28,36},{32,40... | collective-permute-start | bytes 786440 | tf_op jit(solution)/shard_map/ppermute | solution.py:15
  20.2 26.7 %collective-permute-start.5 = (bf16[256,768]{1,0:T(8,128)(2,1)}, bf16[256,768]{1,0:T(8,128)(2,1)}, u32[]{:S(2)}, u32[]{:S(2)}) collective-permute-start(bf16[256,768]{1,0:T(8,128)(2,1)} %bitcast.151), channel_id=1, source_target_pairs={{0,1},{1,2},{2,3},{4,5},{5,6},{6,7},{8,9},{9,10},{10,11},{12,13},{... | collective-permute-start | bytes 1179656 | tf_op jit(solution)/shard_map/ppermute | solution.py:15
  28.3 3.5 %copy-start.2 = (f32[2,256,256]{1,2,0:T(8,128)}, f32[2,256,256]{1,2,0:T(8,128)S(1)}, u32[]{:S(2)}) copy-start(f32[2,256,256]{1,2,0:T(8,128)S(1)} %convolution_bitcast_fusion.1) | copy-start | bytes 1572868
  36.1 16.0 %collective-permute-start.2 = (f32[256,256]{1,0:T(8,128)}, f32[256,256]{1,0:T(8,128)}, u32[]{:S(2)}, u32[]{:S(2)}) collective-permute-start(f32[256,256]{1,0:T(8,128)} %fusion.132), channel_id=1, source_target_pairs={{0,8},{4,12},{8,16},{12,20},{16,24},{20,28},{24,32},{28,36},{32,40... | collective-permute-start | bytes 786440 | tf_op jit(solution)/shard_map/ppermute | solution.py:15
  54.2 13.5 %collective-permute-start.3 = (f32[256,256]{1,0:T(8,128)}, f32[256,256]{1,0:T(8,128)}, u32[]{:S(2)}, u32[]{:S(2)}) collective-permute-start(f32[256,256]{1,0:T(8,128)} %fusion.133), channel_id=1, source_target_pairs={{0,16},{4,20},{8,24},{12,28},{16,32},{20,36},{24,40},{28,44},{32,4... | collective-permute-start | bytes 786440 | tf_op jit(solution)/shard_map/ppermute | solution.py:15
  69.1 19.0 %copy-start.31 = (f32[4,1,256]{2,1,0:T(1,128)S(1)}, f32[4,1,256]{2,1,0:T(1,128)}, u32[]{:S(2)}) copy-start(f32[4,1,256]{2,1,0:T(1,128)} %copy-done.30) | copy-start | bytes 12292
  69.1 19.3 %copy-start.29 = (f32[4,1,256]{2,1,0:T(1,128)S(1)}, f32[4,1,256]{2,1,0:T(1,128)}, u32[]{:S(2)}) copy-start(f32[4,1,256]{2,1,0:T(1,128)} %copy-done.28) | copy-start | bytes 12292
  69.1 10.3 %collective-permute-start.4 = (f32[256,256]{1,0:T(8,128)S(1)}, f32[256,256]{1,0:T(8,128)S(1)}, u32[]{:S(2)}, u32[]{:S(2)}) collective-permute-start(f32[256,256]{1,0:T(8,128)S(1)} %fusion.134), channel_id=1, source_target_pairs={{0,32},{4,36},{8,40},{12,44},{16,48},{20,52},{24,56},{28,60},{32,6... | collective-permute-start | bytes 786440 | tf_op jit(solution)/shard_map/ppermute | solution.py:15
  77.9 10.8 %copy-start.27 = (f32[4,1,256]{2,1,0:T(1,128)S(1)}, f32[4,1,256]{2,1,0:T(1,128)}, u32[]{:S(2)}) copy-start(f32[4,1,256]{2,1,0:T(1,128)} %copy-done.26) | copy-start | bytes 12292
  77.9 11.2 %copy-start.24 = (f32[4,1,256]{2,1,0:T(1,128)S(1)}, f32[4,1,256]{2,1,0:T(1,128)}, u32[]{:S(2)}) copy-start(f32[4,1,256]{2,1,0:T(1,128)} %copy-done.23) | copy-start | bytes 12292
  77.9 11.5 %copy-start.21 = (f32[4,1,256]{2,1,0:T(1,128)S(1)}, f32[4,1,256]{2,1,0:T(1,128)}, u32[]{:S(2)}) copy-start(f32[4,1,256]{2,1,0:T(1,128)} %copy-done.20) | copy-start | bytes 12292
  77.9 11.8 %copy-start.18 = (f32[4,1,256]{2,1,0:T(1,128)S(1)}, f32[4,1,256]{2,1,0:T(1,128)}, u32[]{:S(2)}) copy-start(f32[4,1,256]{2,1,0:T(1,128)} %copy-done.17) | copy-start | bytes 12292
  77.9 12.1 %copy-start.15 = (f32[4,1,256]{2,1,0:T(1,128)S(1)}, f32[4,1,256]{2,1,0:T(1,128)}, u32[]{:S(2)}) copy-start(f32[4,1,256]{2,1,0:T(1,128)} %copy-done.14) | copy-start | bytes 12292
  80.5 6.1 %collective-permute-start.7 = (f32[32,256]{1,0:T(8,128)S(1)}, f32[32,256]{1,0:T(8,128)S(1)}, u32[]{:S(2)}, u32[]{:S(2)}) collective-permute-start(f32[32,256]{1,0:T(8,128)S(1)} %convolution_bitcast_fusion.3), channel_id=1, source_target_pairs={{0,3},{1,0},{2,1},{3,2},{4,7},{5,4},{6,5},{7,6},{8,11},{9,8},{10,9... | collective-permute-start | bytes 98312 | tf_op jit(solution)/shard_map/ppermute | solution.py:48
  81.7 5.1 %collective-permute-start.8 = (f32[32,256]{1,0:T(8,128)S(1)}, f32[32,256]{1,0:T(8,128)S(1)}, u32[]{:S(2)}, u32[]{:S(2)}) collective-permute-start(f32[32,256]{1,0:T(8,128)S(1)} %convolution_bitcast_fusion.3), channel_id=1, source_target_pairs={{0,1},{1,2},{2,3},{3,0},{4,5},{5,6},{6,7},{7,4},{8,9},{9,10},{10,1... | collective-permute-start | bytes 98312 | tf_op jit(solution)/shard_map/ppermute | solution.py:48
  82.5 5.4 %collective-permute-start.6 = (f32[32,256]{1,0:T(8,128)S(1)}, f32[32,256]{1,0:T(8,128)S(1)}, u32[]{:S(2)}, u32[]{:S(2)}) collective-permute-start(f32[32,256]{1,0:T(8,128)S(1)} %convolution_bitcast_fusion.3), channel_id=1, source_target_pairs={{0,2},{1,3},{2,0},{3,1},{4,6},{5,7},{6,4},{7,5},{8,10},{9,11},{10,... | collective-permute-start | bytes 98312 | tf_op jit(solution)/shard_map/ppermute | solution.py:48
  88.0 19.3 %copy-start.32 = (f32[4,1,256]{2,1,0:T(1,128)}, f32[4,1,256]{2,1,0:T(1,128)S(1)}, u32[]{:S(2)}) copy-start(f32[4,1,256]{2,1,0:T(1,128)S(1)} %get-tuple-element.24) | copy-start | bytes 12292
  88.0 19.3 %copy-start.34 = (f32[4,1,256]{2,1,0:T(1,128)}, f32[4,1,256]{2,1,0:T(1,128)S(1)}, u32[]{:S(2)}) copy-start(f32[4,1,256]{2,1,0:T(1,128)S(1)} %get-tuple-element.25) | copy-start | bytes 12292
  88.0 19.3 %copy-start.36 = (f32[4,1,256]{2,1,0:T(1,128)}, f32[4,1,256]{2,1,0:T(1,128)S(1)}, u32[]{:S(2)}) copy-start(f32[4,1,256]{2,1,0:T(1,128)S(1)} %get-tuple-element.26) | copy-start | bytes 12292
  88.0 19.3 %copy-start.38 = (f32[4,1,256]{2,1,0:T(1,128)}, f32[4,1,256]{2,1,0:T(1,128)S(1)}, u32[]{:S(2)}) copy-start(f32[4,1,256]{2,1,0:T(1,128)S(1)} %get-tuple-element.27) | copy-start | bytes 12292
  88.0 19.3 %copy-start.40 = (f32[4,1,256]{2,1,0:T(1,128)}, f32[4,1,256]{2,1,0:T(1,128)S(1)}, u32[]{:S(2)}) copy-start(f32[4,1,256]{2,1,0:T(1,128)S(1)} %get-tuple-element.28) | copy-start | bytes 12292
  88.0 19.3 %copy-start.41 = (f32[4,1,256]{2,1,0:T(1,128)}, f32[4,1,256]{2,1,0:T(1,128)S(1)}, u32[]{:S(2)}) copy-start(f32[4,1,256]{2,1,0:T(1,128)S(1)} %get-tuple-element.29) | copy-start | bytes 12292
  88.0 19.3 %copy-start.42 = (f32[4,1,256]{2,1,0:T(1,128)}, f32[4,1,256]{2,1,0:T(1,128)S(1)}, u32[]{:S(2)}) copy-start(f32[4,1,256]{2,1,0:T(1,128)S(1)} %get-tuple-element.30) | copy-start | bytes 12292
  88.0 19.3 %copy-start.43 = (f32[4,1,256]{2,1,0:T(1,128)}, f32[4,1,256]{2,1,0:T(1,128)S(1)}, u32[]{:S(2)}) copy-start(f32[4,1,256]{2,1,0:T(1,128)S(1)} %get-tuple-element.31) | copy-start | bytes 12292
  91.2 4.5 %copy-start.45 = (f32[1,256]{1,0:T(1,128)}, f32[1,256]{1,0:T(1,128)S(1)}, u32[]{:S(2)}) copy-start(f32[1,256]{1,0:T(1,128)S(1)} %get-tuple-element.42) | copy-start | bytes 3076
  91.2 4.5 %copy-start.46 = (f32[1,256]{1,0:T(1,128)}, f32[1,256]{1,0:T(1,128)S(1)}, u32[]{:S(2)}) copy-start(f32[1,256]{1,0:T(1,128)S(1)} %get-tuple-element.43) | copy-start | bytes 3076
  91.2 28.2 %copy-start.3 = (f32[2,256,256]{1,2,0:T(8,128)S(1)}, f32[2,256,256]{1,2,0:T(8,128)}, u32[]{:S(2)}) copy-start(f32[2,256,256]{1,2,0:T(8,128)} %copy-done.2) | copy-start | bytes 1572868
  91.7 6.9 %collective-permute-start.10 = (f32[256]{0:T(256)S(1)}, f32[256]{0:T(256)S(1)}, u32[]{:S(2)}, u32[]{:S(2)}) collective-permute-start(f32[256]{0:T(256)S(1)} %add.157), channel_id=1, source_target_pairs={{0,8},{4,12},{8,16},{12,20},{16,24},{20,28},{24,32},{28,36},{32,40... | collective-permute-start | bytes 3080 | tf_op jit(solution)/shard_map/ppermute | solution.py:15
  95.8 30.0 %copy-start.9 = (f32[256,256]{1,0:T(8,128)S(1)}, f32[256,256]{1,0:T(8,128)}, u32[]{:S(2)}) copy-start(f32[256,256]{1,0:T(8,128)} %param.12) | copy-start | bytes 786436
  96.7 4.9 %collective-permute-start.9 = (f32[256]{0:T(256)S(1)}, f32[256]{0:T(256)S(1)}, u32[]{:S(2)}, u32[]{:S(2)}) collective-permute-start(f32[256]{0:T(256)S(1)} %add.157), channel_id=1, source_target_pairs={{0,4},{4,8},{8,12},{12,16},{16,20},{20,24},{24,28},{28,32},{32,36}... | collective-permute-start | bytes 3080 | tf_op jit(solution)/shard_map/ppermute | solution.py:15
  101.5 6.2 %collective-permute-start.11 = (f32[256]{0:T(256)S(1)}, f32[256]{0:T(256)S(1)}, u32[]{:S(2)}, u32[]{:S(2)}) collective-permute-start(f32[256]{0:T(256)S(1)} %add.158), channel_id=1, source_target_pairs={{0,8},{4,12},{8,16},{12,20},{16,24},{20,28},{24,32},{28,36},{32,40... | collective-permute-start | bytes 3080 | tf_op jit(solution)/shard_map/ppermute | solution.py:15
  109.0 7.0 %collective-permute-start.12 = (f32[256]{0:T(256)S(1)}, f32[256]{0:T(256)S(1)}, u32[]{:S(2)}, u32[]{:S(2)}) collective-permute-start(f32[256]{0:T(256)S(1)} %add.159), channel_id=1, source_target_pairs={{0,16},{4,20},{8,24},{12,28},{16,32},{20,36},{24,40},{28,44},{32,4... | collective-permute-start | bytes 3080 | tf_op jit(solution)/shard_map/ppermute | solution.py:15
  117.2 5.5 %collective-permute-start.13 = (f32[256]{0:T(256)S(1)}, f32[256]{0:T(256)S(1)}, u32[]{:S(2)}, u32[]{:S(2)}) collective-permute-start(f32[256]{0:T(256)S(1)} %add.160), channel_id=1, source_target_pairs={{0,32},{4,36},{8,40},{12,44},{16,48},{20,52},{24,56},{28,60},{32,6... | collective-permute-start | bytes 3080 | tf_op jit(solution)/shard_map/ppermute | solution.py:15
  123.6 3.3 %collective-permute-start.14 = (f32[256]{0:T(256)}, f32[256]{0:T(256)}, u32[]{:S(2)}, u32[]{:S(2)}) collective-permute-start(f32[256]{0:T(256)} %add.161), channel_id=1, source_target_pairs={{0,64},{4,68},{8,72},{12,76},{16,80},{20,84},{24,88},{28,92},{32,9... | collective-permute-start | bytes 3080 | tf_op jit(solution)/shard_map/ppermute | solution.py:15
  126.8 9.0 %copy-start.25 = (f32[4,1,256]{2,1,0:T(1,128)S(1)}, f32[4,1,256]{2,1,0:T(1,128)}, u32[]{:S(2)}) copy-start(f32[4,1,256]{2,1,0:T(1,128)} %copy-done.23) | copy-start | bytes 12292
  126.8 9.0 %copy-start.39 = (f32[4,1,256]{2,1,0:T(1,128)S(1)}, f32[4,1,256]{2,1,0:T(1,128)}, u32[]{:S(2)}) copy-start(f32[4,1,256]{2,1,0:T(1,128)} %copy-done.38) | copy-start | bytes 12292
  126.8 9.3 %copy-start.22 = (f32[4,1,256]{2,1,0:T(1,128)S(1)}, f32[4,1,256]{2,1,0:T(1,128)}, u32[]{:S(2)}) copy-start(f32[4,1,256]{2,1,0:T(1,128)} %copy-done.20) | copy-start | bytes 12292
  126.8 9.3 %copy-start.37 = (f32[4,1,256]{2,1,0:T(1,128)S(1)}, f32[4,1,256]{2,1,0:T(1,128)}, u32[]{:S(2)}) copy-start(f32[4,1,256]{2,1,0:T(1,128)} %copy-done.36) | copy-start | bytes 12292
  126.8 9.6 %copy-start.19 = (f32[4,1,256]{2,1,0:T(1,128)S(1)}, f32[4,1,256]{2,1,0:T(1,128)}, u32[]{:S(2)}) copy-start(f32[4,1,256]{2,1,0:T(1,128)} %copy-done.17) | copy-start | bytes 12292
  126.9 9.6 %copy-start.35 = (f32[4,1,256]{2,1,0:T(1,128)S(1)}, f32[4,1,256]{2,1,0:T(1,128)}, u32[]{:S(2)}) copy-start(f32[4,1,256]{2,1,0:T(1,128)} %copy-done.34) | copy-start | bytes 12292
  126.9 10.0 %copy-start.16 = (f32[4,1,256]{2,1,0:T(1,128)S(1)}, f32[4,1,256]{2,1,0:T(1,128)}, u32[]{:S(2)}) copy-start(f32[4,1,256]{2,1,0:T(1,128)} %copy-done.14) | copy-start | bytes 12292
  126.9 10.0 %copy-start.33 = (f32[4,1,256]{2,1,0:T(1,128)S(1)}, f32[4,1,256]{2,1,0:T(1,128)}, u32[]{:S(2)}) copy-start(f32[4,1,256]{2,1,0:T(1,128)} %copy-done.32) | copy-start | bytes 12292
  126.9 10.3 %copy-start.13 = (f32[256,256,1]{1,0,2:T(8,128)S(1)}, f32[256,256,1]{1,0,2:T(8,128)}, u32[]{:S(2)}) copy-start(f32[256,256,1]{1,0,2:T(8,128)} %convolution_bitcast_fusion.2) | copy-start | bytes 786436
  126.9 10.8 %copy-start.10 = (f32[2048,256]{1,0:T(8,128)S(1)}, f32[2048,256]{1,0:T(8,128)}, u32[]{:S(2)}) copy-start(f32[2048,256]{1,0:T(8,128)} %get-tuple-element.15) | copy-start | bytes 6291460
  137.5 7.1 %copy-start.4 = (f32[2,256,256]{1,2,0:T(8,128)S(1)}, f32[2,256,256]{1,2,0:T(8,128)}, u32[]{:S(2)}) copy-start(f32[2,256,256]{1,2,0:T(8,128)} %copy-done.2) | copy-start | bytes 1572868
  137.7 23.4 %copy-start.7 = (f32[256,256]{1,0:T(8,128)S(1)}, f32[256,256]{1,0:T(8,128)}, u32[]{:S(2)}) copy-start(f32[256,256]{1,0:T(8,128)} %copy-done.6) | copy-start | bytes 786436
  139.0 30.3 %copy-start.5 = (f32[256,256]{1,0:T(8,128)S(1)}, f32[256,256]{1,0:T(8,128)}, u32[]{:S(2)}) copy-start(f32[256,256]{1,0:T(8,128)} %fusion.145) | copy-start | bytes 786436
  139.0 43.3 %copy-start.12 = (f32[256,256]{1,0:T(8,128)S(1)}, f32[256,256]{1,0:T(8,128)}, u32[]{:S(2)}) copy-start(f32[256,256]{1,0:T(8,128)} %fusion.149) | copy-start | bytes 786436
  140.4 12.7 %collective-permute-start.16 = (f32[256]{0:T(256)S(1)}, f32[256]{0:T(256)S(1)}, u32[]{:S(2)}, u32[]{:S(2)}) collective-permute-start(f32[256]{0:T(256)S(1)} %select_add_fusion), channel_id=1, source_target_pairs={{8,0},{12,4},{16,8},{20,12},{24,16},{28,20},{32,24},{36,28},{40,32... | collective-permute-start | bytes 3080 | tf_op jit(solution)/shard_map/ppermute | solution.py:19
  145.4 8.0 %collective-permute-start.15 = (f32[256]{0:T(256)S(1)}, f32[256]{0:T(256)S(1)}, u32[]{:S(2)}, u32[]{:S(2)}) collective-permute-start(f32[256]{0:T(256)S(1)} %select_add_fusion), channel_id=1, source_target_pairs={{4,0},{8,4},{12,8},{16,12},{20,16},{24,20},{28,24},{32,28},{36,32}... | collective-permute-start | bytes 3080 | tf_op jit(solution)/shard_map/ppermute | solution.py:19
  153.5 7.6 %collective-permute-start.17 = (f32[256]{0:T(256)S(1)}, f32[256]{0:T(256)S(1)}, u32[]{:S(2)}, u32[]{:S(2)}) collective-permute-start(f32[256]{0:T(256)S(1)} %add.179), channel_id=1, source_target_pairs={{8,0},{12,4},{16,8},{20,12},{24,16},{28,20},{32,24},{36,28},{40,32... | collective-permute-start | bytes 3080 | tf_op jit(solution)/shard_map/ppermute | solution.py:19
  161.3 7.9 %collective-permute-start.18 = (f32[256]{0:T(256)S(1)}, f32[256]{0:T(256)S(1)}, u32[]{:S(2)}, u32[]{:S(2)}) collective-permute-start(f32[256]{0:T(256)S(1)} %add.180), channel_id=1, source_target_pairs={{16,0},{20,4},{24,8},{28,12},{32,16},{36,20},{40,24},{44,28},{48,3... | collective-permute-start | bytes 3080 | tf_op jit(solution)/shard_map/ppermute | solution.py:19
  169.5 5.5 %collective-permute-start.19 = (f32[256]{0:T(256)S(1)}, f32[256]{0:T(256)S(1)}, u32[]{:S(2)}, u32[]{:S(2)}) collective-permute-start(f32[256]{0:T(256)S(1)} %add.181), channel_id=1, source_target_pairs={{32,0},{36,4},{40,8},{44,12},{48,16},{52,20},{56,24},{60,28},{64,3... | collective-permute-start | bytes 3080 | tf_op jit(solution)/shard_map/ppermute | solution.py:19
  175.3 7.0 %collective-permute-start.20 = (f32[256]{0:T(256)S(1)}, f32[256]{0:T(256)S(1)}, u32[]{:S(2)}, u32[]{:S(2)}) collective-permute-start(f32[256]{0:T(256)S(1)} %add.182), channel_id=1, source_target_pairs={{64,0},{68,4},{72,8},{76,12},{80,16},{84,20},{88,24},{92,28},{96,3... | collective-permute-start | bytes 3080 | tf_op jit(solution)/shard_map/ppermute | solution.py:19
  (4 other events, 8.1 us)

commit v2 on v0

--- a/solution.py
+++ b/solution.py
@@ -30,11 +30,14 @@
     )
 
 
-def encode(fields, conv_in, conv_mid, obs_gain, bands):
-    band = lax.axis_index("space")
+def halo(fields, bands):
     edge = fields[:, :, -3:, :]
     flat = edge.reshape(edge.shape[0] * edge.shape[1], edge.shape[2] * edge.shape[3])
-    above = shift_down(flat, "space", 1, bands).reshape(edge.shape)
+    return shift_down(flat, "space", 1, bands).reshape(edge.shape)
+
+
+def encode(fields, above, conv_in, conv_mid, obs_gain, bands):
+    band = lax.axis_index("space")
     hidden = conv_stride(jnp.concatenate([above, fields], axis=2), conv_in, "NCHW")
     hidden = jax.nn.silu(hidden).astype(jnp.bfloat16)
     row = lax.broadcasted_iota(jnp.int32, hidden.shape, 2)
@@ -100,7 +103,9 @@
     for s in range(1, bands):
         block_phi = dot(phis[s], block_phi)
 
-    partial = encode(fields, conv_in, conv_mid, obs_gain, bands)
+    above = halo(fields, bands)
+    above, block_phi = lax.optimization_barrier((above, block_phi))
+    partial = encode(fields, above, conv_in, conv_mid, obs_gain, bands)
     increments = sum_bands(partial, bands).reshape(bands, hours, modes)
 
     state = increments[:, 0]

time: 172 us -> 167 us (0.971)
  starting transfers between devices: 58.1 us -> 52.7 us
  waiting for transfers between devices: 27.5 us -> 31.4 us
  matrix products: 53.2 us -> 50.4 us
    ppermute x6, starting transfers between devices: 15 us -> 11.1 us  [shift_up(): lax.ppermute(value, axis, [(i + steps, i) for i in range(count - steps)])]
    ppermute x6, waiting for transfers between devices: 20.5 us -> 23.9 us  [shift_up(): lax.ppermute(value, axis, [(i + steps, i) for i in range(count - steps)])]
    reshape x2 -> x1, local copies, waits for them, and re-layouts: 5.2 us -> 2.14 us  [halo(): return shift_down(flat, 'space', 1, bands).reshape(edge.shape)]
    optimization_barrier x0 -> x1, local copies, waits for them, and re-layouts: none -> 3.03 us  [per_device(): above, block_phi = lax.optimization_barrier((above, block_phi))]
    ppermute x12, waiting for transfers between devices: 5.16 us -> 7.54 us  [shift_down(): lax.ppermute(value, axis, [(i, i + steps) for i in range(count - steps)])]
    ppermute x3, waiting for transfers between devices: 1.86 us -> 0.01 us  [sum_bands(): lax.ppermute(partial, 'space', [(i, (i + d) % bands) for i in range(bands)])]
    dot_general x55, matrix products: 27.1 us -> 25.3 us  [dot(): return jnp.dot(a, b, precision=precise)]
    unnamed x135 -> x137, local copies, waits for them, and re-layouts: 17.1 us -> 17.6 us
  transfers between devices with their start and end apart: 21 -> 21, of which waited for: 11 -> 9; matrix products, arithmetic and copies ran while one was open for 32% -> 26% of each run, Pallas kernels for 0% -> 0%
where the time goes in v2:
time: 167 us; the launch traced here: 166 us
  starting transfers between devices  52.7 us (32%)
  matrix products  50.4 us (30%)
  waiting for transfers between devices  31.4 us (19%)
  local copies, waits for them, and re-layouts  24.3 us (15%)
  other arithmetic  4.96 us (3%)
  between operations  2.08 us (1%)
    ppermute x12, starting transfers between devices, shift_down(): lax.ppermute(value, axis, [(i, i + steps) for i in range(count - steps)])  36.7 us
    dot_general x55, matrix products, dot(): return jnp.dot(a, b, precision=precise)  25.3 us
    ppermute x6, waiting for transfers between devices, shift_up(): lax.ppermute(value, axis, [(i + steps, i) for i in range(count - steps)])  23.9 us
    unnamed x137, local copies, waits for them, and re-layouts  17.6 us
    ppermute x6, starting transfers between devices, shift_up(): lax.ppermute(value, axis, [(i + steps, i) for i in range(count - steps)])  11.1 us
    conv_general_dilated x1, matrix products, conv_stride(): lax.conv_general_dilated(images, kernel, (2, 2), ((0, 0), (1, 1)), dimens...  9.38 us
    ppermute x12, waiting for transfers between devices, shift_down(): lax.ppermute(value, axis, [(i, i + steps) for i in range(count - steps)])  7.54 us
    dot_general x7, matrix products, per_device(): jnp.einsum('ab,sbc->sac', transition, phis, precision=precise)  7.16 us
  transfers between devices with their start and end apart: 21, of which 9 were waited for; matrix products, arithmetic and copies ran while one was open for 26% of the time, Pallas kernels for 0%

profile of v2, /device:TPU:14, one launch (start us, length us, event | category | flops | bytes accessed | tf_op | source)
XLA Modules:
  0.0 165.9 jit_solution(147564301350248971)
XLA Ops:
  0.7 1.6 slice_bitcast_fusion
  2.3 0.8 copy.129
  3.1 4.6 %collective-permute-start = (bf16[256,768]{1,0:T(8,128)(2,1)}, bf16[256,768]{1,0:T(8,128)(2,1)}, u32[]{:S(2)}, u32[]{:S(2)}) collective-permute-start(bf16[256,768]{1,0:T(8,128)(2,1)} %bitcast.151), channel_id=1, source_target_pairs={{0,1},{1,2},{2,3},{4,5},{5,6},{6,7},{8,9},{9,10},{10,11},{12,13},{... | collective-permute-start | bytes 1179656 | tf_op jit(solution)/shard_map/ppermute | solution.py:15
  8.7 1.0 fusion.23
  9.7 1.0 fusion.22
  10.8 1.0 fusion.21
  11.8 1.0 fusion.20
  12.9 1.0 fusion.19
  13.9 1.0 fusion.18
  15.0 1.0 fusion.17
  17.2 1.3 fusion.75
  18.6 0.8 bitcast_dynamic-update-slice_fusion.4
  19.4 1.3 constant_dynamic-update-slice_fusion.16
  21.3 1.0 convolution_bitcast_fusion
  22.3 0.8 fusion.59
  24.6 1.1 fusion.149
  26.5 5.1 %copy.86 = bf16[32,8,8,256]{0,1,3,2:T(8,128)(2,1)} copy(bf16[32,8,8,256]{3,2,1,0:T(8,128)(2,1)} %param.7) | data formatting | bytes 2097152 | tf_op args[0]
  32.1 1.8 %bitcast_dynamic-update-slice_fusion = (f32[256,2048]{1,0:T(8,128)}, f32[2048,256]{1,0:T(8,128)}) fusion(f32[4,256,256]{1,2,0:T(8,128)S(1)} %convolution_bitcast_fusion, f32[2048,256]{1,0:T(8,128)} %fusion.79, f32[2,256,256]{1,2,0:T(8,128)} %copy-done.2), kind=kLoop, calls=%fused_computation.85 | loop fusion | bytes 1048576
  33.9 2.1 %reshape.51 = bf16[32,8,3,256]{3,2,1,0:T(4,128)(2,1)} reshape(bf16[256,768]{1,0:T(8,128)(2,1)} %collective-permute-done) | data formatting | bytes 786432 | tf_op jit(solution)/shard_map/reshape | solution.py:36
  36.1 3.0 %copy.85 = bf16[32,8,3,256]{0,1,3,2:T(8,128)(2,1)} copy(bf16[32,8,3,256]{3,2,1,0:T(4,128)(2,1)} %reshape.51) | data formatting | bytes 786432 | tf_op jit(solution)/shard_map/optimization_barrier | solution.py:107
  39.1 9.4 %fusion.4 = f32[32,2,64,128]{3,0,2,1:T(8,128)} fusion(bf16[128,64,3,3]{0,1,3,2:T(8,128)(2,1)S(1)} %copy-done, pred[5]{0:T(512)(128)(4,1)} %compare_and_fusion, bf16[64,8,3,3]{0,1,3,2:T(8,128)(2,1)} %param.8, bf16[32,8,8,256]{0,1,3,2:T(8,128)(2,1)} %copy.86, bf16[32,8,3,256]{0,1,3,2:T(8,128)(2,1)} %copy.85), kind=kOutput, calls=%fused_computation.5 | convolution fusion | flops 799834112 | bytes 3695621 | tf_op jit(solution)/shard_map/conv_general_dilated | solution.py:23
  48.5 5.4 %convolution_bitcast_fusion.3 = f32[32,256]{1,0:T(8,128)S(1)} fusion(bf16[2,64,128,256]{3,2,1,0:T(8,128)(2,1)} %param.10, f32[32,2,64,128]{3,0,2,1:T(8,128)} %fusion.4), kind=kOutput, calls=%fused_computation.33 | convolution fusion | flops 271056896 | bytes 10518528 | tf_op jit(solution)/shard_map/shwc,hwcm->sm/dot_general | solution.py:47
  53.9 0.8 collective-permute-start.2
  54.7 1.3 collective-permute-start.3
  56.0 2.8 %collective-permute-start.1 = (f32[32,256]{1,0:T(8,128)S(1)}, f32[32,256]{1,0:T(8,128)S(1)}, u32[]{:S(2)}, u32[]{:S(2)}) collective-permute-start(f32[32,256]{1,0:T(8,128)S(1)} %convolution_bitcast_fusion.3), channel_id=1, source_target_pairs={{0,2},{1,3},{2,0},{3,1},{4,6},{5,7},{6,4},{7,5},{8,10},{9,11},{10,... | collective-permute-start | bytes 98312 | tf_op jit(solution)/shard_map/ppermute | solution.py:51
  58.8 0.9 fusion.84
  59.7 1.9 %collective-permute-start.5 = (f32[256,256]{1,0:T(8,128)S(1)}, f32[256,256]{1,0:T(8,128)S(1)}, u32[]{:S(2)}, u32[]{:S(2)}) collective-permute-start(f32[256,256]{1,0:T(8,128)S(1)} %copy-done.14), channel_id=1, source_target_pairs={{0,4},{4,8},{8,12},{12,16},{16,20},{20,24},{24,28},{28,32},{32,36}... | collective-permute-start | bytes 786440 | tf_op jit(solution)/shard_map/ppermute | solution.py:15
  61.6 3.6 %collective-permute-start.7 = (f32[256,256]{1,0:T(8,128)S(1)}, f32[256,256]{1,0:T(8,128)S(1)}, u32[]{:S(2)}, u32[]{:S(2)}) collective-permute-start(f32[256,256]{1,0:T(8,128)S(1)} %copy-done.14), channel_id=1, source_target_pairs={{0,8},{4,12},{8,16},{12,20},{16,24},{20,28},{24,32},{28,36},{32,40... | collective-permute-start | bytes 786440 | tf_op jit(solution)/shard_map/ppermute | solution.py:15
  69.1 3.4 %collective-permute-start.6 = (f32[256]{0:T(256)S(1)}, f32[256]{0:T(256)S(1)}, u32[]{:S(2)}, u32[]{:S(2)}) collective-permute-start(f32[256]{0:T(256)S(1)} %add.157), channel_id=1, source_target_pairs={{0,8},{4,12},{8,16},{12,20},{16,24},{20,28},{24,32},{28,36},{32,40... | collective-permute-start | bytes 3080 | tf_op jit(solution)/shard_map/ppermute | solution.py:15
  72.5 0.9 fusion.82
  73.4 2.9 %collective-permute-start.4 = (f32[256]{0:T(256)S(1)}, f32[256]{0:T(256)S(1)}, u32[]{:S(2)}, u32[]{:S(2)}) collective-permute-start(f32[256]{0:T(256)S(1)} %add.157), channel_id=1, source_target_pairs={{0,4},{4,8},{8,12},{12,16},{16,20},{20,24},{24,28},{28,32},{32,36}... | collective-permute-start | bytes 3080 | tf_op jit(solution)/shard_map/ppermute | solution.py:15
  76.6 1.7 %collective-permute-done.4 = f32[256]{0:T(256)S(1)} collective-permute-done((f32[256]{0:T(256)S(1)}, f32[256]{0:T(256)S(1)}, u32[]{:S(2)}, u32[]{:S(2)}) %collective-permute-start.4) | collective-permute-done | bytes 1056 | tf_op jit(solution)/shard_map/ppermute | solution.py:15
  78.2 5.6 %collective-permute-start.8 = (f32[256]{0:T(256)S(1)}, f32[256]{0:T(256)S(1)}, u32[]{:S(2)}, u32[]{:S(2)}) collective-permute-start(f32[256]{0:T(256)S(1)} %add.158), channel_id=1, source_target_pairs={{0,8},{4,12},{8,16},{12,20},{16,24},{20,28},{24,32},{28,36},{32,40... | collective-permute-start | bytes 3080 | tf_op jit(solution)/shard_map/ppermute | solution.py:15
  84.3 1.9 %collective-permute-start.9 = (f32[256,256]{1,0:T(8,128)S(1)}, f32[256,256]{1,0:T(8,128)S(1)}, u32[]{:S(2)}, u32[]{:S(2)}) collective-permute-start(f32[256,256]{1,0:T(8,128)S(1)} %fusion.133), channel_id=1, source_target_pairs={{0,8},{4,12},{8,16},{12,20},{16,24},{20,28},{24,32},{28,36},{32,40... | collective-permute-start | bytes 786440 | tf_op jit(solution)/shard_map/ppermute | solution.py:15
  86.3 0.9 fusion.80
  87.4 3.2 %collective-permute-start.10 = (f32[256]{0:T(256)S(1)}, f32[256]{0:T(256)S(1)}, u32[]{:S(2)}, u32[]{:S(2)}) collective-permute-start(f32[256]{0:T(256)S(1)} %add.159), channel_id=1, source_target_pairs={{0,16},{4,20},{8,24},{12,28},{16,32},{20,36},{24,40},{28,44},{32,4... | collective-permute-start | bytes 3080 | tf_op jit(solution)/shard_map/ppermute | solution.py:15
  90.6 2.0 %collective-permute-done.9 = f32[256,256]{1,0:T(8,128)S(1)} collective-permute-done((f32[256,256]{1,0:T(8,128)S(1)}, f32[256,256]{1,0:T(8,128)S(1)}, u32[]{:S(2)}, u32[]{:S(2)}) %collective-permute-start.9) | collective-permute-done | bytes 262176 | tf_op jit(solution)/shard_map/ppermute | solution.py:15
  93.0 2.9 %collective-permute-start.11 = (f32[256,256]{1,0:T(8,128)S(1)}, f32[256,256]{1,0:T(8,128)S(1)}, u32[]{:S(2)}, u32[]{:S(2)}) collective-permute-start(f32[256,256]{1,0:T(8,128)S(1)} %fusion.135), channel_id=1, source_target_pairs={{0,16},{4,20},{8,24},{12,28},{16,32},{20,36},{24,40},{28,44},{32,4... | collective-permute-start | bytes 786440 | tf_op jit(solution)/shard_map/ppermute | solution.py:15
  97.6 2.1 %collective-permute-start.12 = (f32[256]{0:T(256)}, f32[256]{0:T(256)}, u32[]{:S(2)}, u32[]{:S(2)}) collective-permute-start(f32[256]{0:T(256)} %add.160), channel_id=1, source_target_pairs={{0,32},{4,36},{8,40},{12,44},{16,48},{20,52},{24,56},{28,60},{32,6... | collective-permute-start | bytes 3080 | tf_op jit(solution)/shard_map/ppermute | solution.py:15
  99.8 3.0 %collective-permute-done.11 = f32[256,256]{1,0:T(8,128)S(1)} collective-permute-done((f32[256,256]{1,0:T(8,128)S(1)}, f32[256,256]{1,0:T(8,128)S(1)}, u32[]{:S(2)}, u32[]{:S(2)}) %collective-permute-start.11) | collective-permute-done | bytes 262176 | tf_op jit(solution)/shard_map/ppermute | solution.py:15
  102.8 1.1 fusion.137
  103.9 3.2 %collective-permute-start.13 = (f32[256,256]{1,0:T(8,128)}, f32[256,256]{1,0:T(8,128)}, u32[]{:S(2)}, u32[]{:S(2)}) collective-permute-start(f32[256,256]{1,0:T(8,128)} %fusion.137), channel_id=1, source_target_pairs={{0,32},{4,36},{8,40},{12,44},{16,48},{20,52},{24,56},{28,60},{32,6... | collective-permute-start | bytes 786440 | tf_op jit(solution)/shard_map/ppermute | solution.py:15
  107.0 1.1 convolution_bitcast_fusion.2
  108.3 1.2 fusion.138
  109.5 0.8 add.161
  110.3 1.3 collective-permute-start.14
  111.6 0.8 collective-permute-done.13
  112.4 1.4 fusion.139
  114.4 0.7 add.163
  119.6 1.3 fusion.15
  122.4 1.9 %collective-permute-start.16 = (f32[256]{0:T(256)S(1)}, f32[256]{0:T(256)S(1)}, u32[]{:S(2)}, u32[]{:S(2)}) collective-permute-start(f32[256]{0:T(256)S(1)} %select_add_fusion), channel_id=1, source_target_pairs={{8,0},{12,4},{16,8},{20,12},{24,16},{28,20},{32,24},{36,28},{40,32... | collective-permute-start | bytes 3080 | tf_op jit(solution)/shard_map/ppermute | solution.py:19
  124.3 0.8 fusion.78
  125.1 1.9 %collective-permute-start.15 = (f32[256]{0:T(256)S(1)}, f32[256]{0:T(256)S(1)}, u32[]{:S(2)}, u32[]{:S(2)}) collective-permute-start(f32[256]{0:T(256)S(1)} %select_add_fusion), channel_id=1, source_target_pairs={{4,0},{8,4},{12,8},{16,12},{20,16},{24,20},{28,24},{32,28},{36,32}... | collective-permute-start | bytes 3080 | tf_op jit(solution)/shard_map/ppermute | solution.py:19
  127.0 5.2 %collective-permute-done.16 = f32[256]{0:T(256)S(1)} collective-permute-done((f32[256]{0:T(256)S(1)}, f32[256]{0:T(256)S(1)}, u32[]{:S(2)}, u32[]{:S(2)}) %collective-permute-start.16) | collective-permute-done | bytes 1056 | tf_op jit(solution)/shard_map/ppermute | solution.py:19
  132.6 1.9 %collective-permute-start.17 = (f32[256]{0:T(256)S(1)}, f32[256]{0:T(256)S(1)}, u32[]{:S(2)}, u32[]{:S(2)}) collective-permute-start(f32[256]{0:T(256)S(1)} %add.179), channel_id=1, source_target_pairs={{8,0},{12,4},{16,8},{20,12},{24,16},{28,20},{32,24},{36,28},{40,32... | collective-permute-start | bytes 3080 | tf_op jit(solution)/shard_map/ppermute | solution.py:19
  134.5 0.8 constant_dynamic-update-slice_fusion.17
  135.3 4.9 %collective-permute-done.17 = f32[256]{0:T(256)S(1)} collective-permute-done((f32[256]{0:T(256)S(1)}, f32[256]{0:T(256)S(1)}, u32[]{:S(2)}, u32[]{:S(2)}) %collective-permute-start.17) | collective-permute-done | bytes 1056 | tf_op jit(solution)/shard_map/ppermute | solution.py:19
  140.5 2.0 %collective-permute-start.18 = (f32[256]{0:T(256)S(1)}, f32[256]{0:T(256)S(1)}, u32[]{:S(2)}, u32[]{:S(2)}) collective-permute-start(f32[256]{0:T(256)S(1)} %add.180), channel_id=1, source_target_pairs={{16,0},{20,4},{24,8},{28,12},{32,16},{36,20},{40,24},{44,28},{48,3... | collective-permute-start | bytes 3080 | tf_op jit(solution)/shard_map/ppermute | solution.py:19
  143.2 5.2 %collective-permute-done.18 = f32[256]{0:T(256)S(1)} collective-permute-done((f32[256]{0:T(256)S(1)}, f32[256]{0:T(256)S(1)}, u32[]{:S(2)}, u32[]{:S(2)}) %collective-permute-start.18) | collective-permute-done | bytes 1056 | tf_op jit(solution)/shard_map/ppermute | solution.py:19
  148.7 2.0 %collective-permute-start.19 = (f32[256]{0:T(256)S(1)}, f32[256]{0:T(256)S(1)}, u32[]{:S(2)}, u32[]{:S(2)}) collective-permute-start(f32[256]{0:T(256)S(1)} %add.181), channel_id=1, source_target_pairs={{32,0},{36,4},{40,8},{44,12},{48,16},{52,20},{56,24},{60,28},{64,3... | collective-permute-start | bytes 3080 | tf_op jit(solution)/shard_map/ppermute | solution.py:19
  150.7 3.5 %collective-permute-done.19 = f32[256]{0:T(256)S(1)} collective-permute-done((f32[256]{0:T(256)S(1)}, f32[256]{0:T(256)S(1)}, u32[]{:S(2)}, u32[]{:S(2)}) %collective-permute-start.19) | collective-permute-done | bytes 1056 | tf_op jit(solution)/shard_map/ppermute | solution.py:19
  154.5 1.3 collective-permute-start.20
  156.4 5.0 %collective-permute-done.20 = f32[256]{0:T(256)S(1)} collective-permute-done((f32[256]{0:T(256)S(1)}, f32[256]{0:T(256)S(1)}, u32[]{:S(2)}, u32[]{:S(2)}) %collective-permute-start.20) | collective-permute-done | bytes 1056 | tf_op jit(solution)/shard_map/ppermute | solution.py:19
  162.5 2.7 %fusion.12 = f32[1,8,256]{2,0,1:T(1,128)S(1)} fusion(f32[32,8,8,256]{3,2,1,0:T(8,128)} %bitcast.147, s32[]{:T(128)S(6)} %select_n.26, f32[1,256]{1,0:T(1,128)S(1)} %bitcast.452, f32[1,256]{1,0:T(1,128)S(1)} %bitcast.464, f32[1,256]{1,0:T(1,128)S(1)} %bitcast.449, f32[1,256]{1,0:T(1,128)S(1)} %bitcast.445), kind=kOutput, calls=%fused_computation.9 | convolution fusion | flops 6292224 | bytes 2109444 | tf_op jit(solution)/shard_map/dot_general | solution.py:11
  (223 shorter events, 22.6 us)
Async XLA Ops:
  0.6 38.5 %copy-start = (bf16[128,64,3,3]{0,1,3,2:T(8,128)(2,1)S(1)}, bf16[128,64,3,3]{0,1,3,2:T(8,128)(2,1)}, u32[]{:S(2)}) copy-start(bf16[128,64,3,3]{0,1,3,2:T(8,128)(2,1)} %param.9) | copy-start | bytes 442372
  0.7 7.9 %copy-start.54 = (f32[32,256]{1,0:T(8,128)S(1)}, f32[32,256]{1,0:T(8,128)}, u32[]{:S(2)}) copy-start(f32[32,256]{1,0:T(8,128)} %param.13) | copy-start | bytes 98308
  3.1 30.9 %collective-permute-start = (bf16[256,768]{1,0:T(8,128)(2,1)}, bf16[256,768]{1,0:T(8,128)(2,1)}, u32[]{:S(2)}, u32[]{:S(2)}) collective-permute-start(bf16[256,768]{1,0:T(8,128)(2,1)} %bitcast.151), channel_id=1, source_target_pairs={{0,1},{1,2},{2,3},{4,5},{5,6},{6,7},{8,9},{9,10},{10,11},{12,13},{... | collective-permute-start | bytes 1179656 | tf_op jit(solution)/shard_map/ppermute | solution.py:15
  48.5 11.2 %copy-start.14 = (f32[256,256]{1,0:T(8,128)S(1)}, f32[256,256]{1,0:T(8,128)}, u32[]{:S(2)}) copy-start(f32[256,256]{1,0:T(8,128)} %fusion.75) | copy-start | bytes 786436
  48.5 16.9 %copy-start.34 = (f32[4,1,256]{2,1,0:T(1,128)S(1)}, f32[4,1,256]{2,1,0:T(1,128)}, u32[]{:S(2)}) copy-start(f32[4,1,256]{2,1,0:T(1,128)} %copy-done.33) | copy-start | bytes 12292
  48.5 17.3 %copy-start.31 = (f32[4,1,256]{2,1,0:T(1,128)S(1)}, f32[4,1,256]{2,1,0:T(1,128)}, u32[]{:S(2)}) copy-start(f32[4,1,256]{2,1,0:T(1,128)} %copy-done.30) | copy-start | bytes 12292
  48.5 17.6 %copy-start.28 = (f32[4,1,256]{2,1,0:T(1,128)S(1)}, f32[4,1,256]{2,1,0:T(1,128)}, u32[]{:S(2)}) copy-start(f32[4,1,256]{2,1,0:T(1,128)} %copy-done.27) | copy-start | bytes 12292
  53.9 12.5 %copy-start.25 = (f32[4,1,256]{2,1,0:T(1,128)S(1)}, f32[4,1,256]{2,1,0:T(1,128)}, u32[]{:S(2)}) copy-start(f32[4,1,256]{2,1,0:T(1,128)} %copy-done.24) | copy-start | bytes 12292
  53.9 12.9 %copy-start.22 = (f32[4,1,256]{2,1,0:T(1,128)S(1)}, f32[4,1,256]{2,1,0:T(1,128)}, u32[]{:S(2)}) copy-start(f32[4,1,256]{2,1,0:T(1,128)} %copy-done.21) | copy-start | bytes 12292
  53.9 13.2 %copy-start.19 = (f32[4,1,256]{2,1,0:T(1,128)S(1)}, f32[4,1,256]{2,1,0:T(1,128)}, u32[]{:S(2)}) copy-start(f32[4,1,256]{2,1,0:T(1,128)} %copy-done.18) | copy-start | bytes 12292
  53.9 13.5 %copy-start.16 = (f32[4,1,256]{2,1,0:T(1,128)S(1)}, f32[4,1,256]{2,1,0:T(1,128)}, u32[]{:S(2)}) copy-start(f32[4,1,256]{2,1,0:T(1,128)} %copy-done.15) | copy-start | bytes 12292
  53.9 11.3 %collective-permute-start.2 = (f32[32,256]{1,0:T(8,128)S(1)}, f32[32,256]{1,0:T(8,128)S(1)}, u32[]{:S(2)}, u32[]{:S(2)}) collective-permute-start(f32[32,256]{1,0:T(8,128)S(1)} %convolution_bitcast_fusion.3), channel_id=1, source_target_pairs={{0,3},{1,0},{2,1},{3,2},{4,7},{5,4},{6,5},{7,6},{8,11},{9,8},{10,9... | collective-permute-start | bytes 98312 | tf_op jit(solution)/shard_map/ppermute | solution.py:51
  54.7 10.5 %collective-permute-start.3 = (f32[32,256]{1,0:T(8,128)S(1)}, f32[32,256]{1,0:T(8,128)S(1)}, u32[]{:S(2)}, u32[]{:S(2)}) collective-permute-start(f32[32,256]{1,0:T(8,128)S(1)} %convolution_bitcast_fusion.3), channel_id=1, source_target_pairs={{0,1},{1,2},{2,3},{3,0},{4,5},{5,6},{6,7},{7,4},{8,9},{9,10},{10,1... | collective-permute-start | bytes 98312 | tf_op jit(solution)/shard_map/ppermute | solution.py:51
  56.0 9.3 %collective-permute-start.1 = (f32[32,256]{1,0:T(8,128)S(1)}, f32[32,256]{1,0:T(8,128)S(1)}, u32[]{:S(2)}, u32[]{:S(2)}) collective-permute-start(f32[32,256]{1,0:T(8,128)S(1)} %convolution_bitcast_fusion.3), channel_id=1, source_target_pairs={{0,2},{1,3},{2,0},{3,1},{4,6},{5,7},{6,4},{7,5},{8,10},{9,11},{10,... | collective-permute-start | bytes 98312 | tf_op jit(solution)/shard_map/ppermute | solution.py:51
  59.7 16.6 %collective-permute-start.5 = (f32[256,256]{1,0:T(8,128)S(1)}, f32[256,256]{1,0:T(8,128)S(1)}, u32[]{:S(2)}, u32[]{:S(2)}) collective-permute-start(f32[256,256]{1,0:T(8,128)S(1)} %copy-done.14), channel_id=1, source_target_pairs={{0,4},{4,8},{8,12},{12,16},{16,20},{20,24},{24,28},{28,32},{32,36}... | collective-permute-start | bytes 786440 | tf_op jit(solution)/shard_map/ppermute | solution.py:15
  61.6 22.3 %collective-permute-start.7 = (f32[256,256]{1,0:T(8,128)S(1)}, f32[256,256]{1,0:T(8,128)S(1)}, u32[]{:S(2)}, u32[]{:S(2)}) collective-permute-start(f32[256,256]{1,0:T(8,128)S(1)} %copy-done.14), channel_id=1, source_target_pairs={{0,8},{4,12},{8,16},{12,20},{16,24},{20,28},{24,32},{28,36},{32,40... | collective-permute-start | bytes 786440 | tf_op jit(solution)/shard_map/ppermute | solution.py:15
  65.3 18.9 %copy-start.36 = (f32[4,1,256]{2,1,0:T(1,128)}, f32[4,1,256]{2,1,0:T(1,128)S(1)}, u32[]{:S(2)}) copy-start(f32[4,1,256]{2,1,0:T(1,128)S(1)} %get-tuple-element.16) | copy-start | bytes 12292
  65.3 18.9 %copy-start.38 = (f32[4,1,256]{2,1,0:T(1,128)}, f32[4,1,256]{2,1,0:T(1,128)S(1)}, u32[]{:S(2)}) copy-start(f32[4,1,256]{2,1,0:T(1,128)S(1)} %get-tuple-element.17) | copy-start | bytes 12292
  65.3 18.9 %copy-start.40 = (f32[4,1,256]{2,1,0:T(1,128)}, f32[4,1,256]{2,1,0:T(1,128)S(1)}, u32[]{:S(2)}) copy-start(f32[4,1,256]{2,1,0:T(1,128)S(1)} %get-tuple-element.18) | copy-start | bytes 12292
  65.4 18.9 %copy-start.42 = (f32[4,1,256]{2,1,0:T(1,128)}, f32[4,1,256]{2,1,0:T(1,128)S(1)}, u32[]{:S(2)}) copy-start(f32[4,1,256]{2,1,0:T(1,128)S(1)} %get-tuple-element.19) | copy-start | bytes 12292
  65.4 18.9 %copy-start.44 = (f32[4,1,256]{2,1,0:T(1,128)}, f32[4,1,256]{2,1,0:T(1,128)S(1)}, u32[]{:S(2)}) copy-start(f32[4,1,256]{2,1,0:T(1,128)S(1)} %get-tuple-element.20) | copy-start | bytes 12292
  65.4 18.9 %copy-start.46 = (f32[4,1,256]{2,1,0:T(1,128)}, f32[4,1,256]{2,1,0:T(1,128)S(1)}, u32[]{:S(2)}) copy-start(f32[4,1,256]{2,1,0:T(1,128)S(1)} %get-tuple-element.21) | copy-start | bytes 12292
  65.4 18.9 %copy-start.48 = (f32[4,1,256]{2,1,0:T(1,128)}, f32[4,1,256]{2,1,0:T(1,128)S(1)}, u32[]{:S(2)}) copy-start(f32[4,1,256]{2,1,0:T(1,128)S(1)} %get-tuple-element.22) | copy-start | bytes 12292
  65.4 18.9 %copy-start.50 = (f32[4,1,256]{2,1,0:T(1,128)}, f32[4,1,256]{2,1,0:T(1,128)S(1)}, u32[]{:S(2)}) copy-start(f32[4,1,256]{2,1,0:T(1,128)S(1)} %get-tuple-element.23) | copy-start | bytes 12292
  68.6 17.7 %copy-start.55 = (f32[1,256]{1,0:T(1,128)}, f32[1,256]{1,0:T(1,128)S(1)}, u32[]{:S(2)}) copy-start(f32[1,256]{1,0:T(1,128)S(1)} %get-tuple-element.34) | copy-start | bytes 3076
  68.6 17.7 %copy-start.57 = (f32[1,256]{1,0:T(1,128)}, f32[1,256]{1,0:T(1,128)S(1)}, u32[]{:S(2)}) copy-start(f32[1,256]{1,0:T(1,128)S(1)} %get-tuple-element.35) | copy-start | bytes 3076
  68.8 27.1 %copy-start.3 = (f32[2,256,256]{1,2,0:T(8,128)S(1)}, f32[2,256,256]{1,2,0:T(8,128)}, u32[]{:S(2)}) copy-start(f32[2,256,256]{1,2,0:T(8,128)} %copy-done.2) | copy-start | bytes 1572868
  69.1 7.2 %collective-permute-start.6 = (f32[256]{0:T(256)S(1)}, f32[256]{0:T(256)S(1)}, u32[]{:S(2)}, u32[]{:S(2)}) collective-permute-start(f32[256]{0:T(256)S(1)} %add.157), channel_id=1, source_target_pairs={{0,8},{4,12},{8,16},{12,20},{16,24},{20,28},{24,32},{28,36},{32,40... | collective-permute-start | bytes 3080 | tf_op jit(solution)/shard_map/ppermute | solution.py:15
  73.4 4.9 %collective-permute-start.4 = (f32[256]{0:T(256)S(1)}, f32[256]{0:T(256)S(1)}, u32[]{:S(2)}, u32[]{:S(2)}) collective-permute-start(f32[256]{0:T(256)S(1)} %add.157), channel_id=1, source_target_pairs={{0,4},{4,8},{8,12},{12,16},{16,20},{20,24},{24,28},{28,32},{32,36}... | collective-permute-start | bytes 3080 | tf_op jit(solution)/shard_map/ppermute | solution.py:15
  78.2 28.8 %copy-start.10 = (f32[256,256]{1,0:T(8,128)S(1)}, f32[256,256]{1,0:T(8,128)}, u32[]{:S(2)}) copy-start(f32[256,256]{1,0:T(8,128)} %param.12) | copy-start | bytes 786436
  78.2 8.9 %collective-permute-start.8 = (f32[256]{0:T(256)S(1)}, f32[256]{0:T(256)S(1)}, u32[]{:S(2)}, u32[]{:S(2)}) collective-permute-start(f32[256]{0:T(256)S(1)} %add.158), channel_id=1, source_target_pairs={{0,8},{4,12},{8,16},{12,20},{16,24},{20,28},{24,32},{28,36},{32,40... | collective-permute-start | bytes 3080 | tf_op jit(solution)/shard_map/ppermute | solution.py:15
  84.3 8.3 %collective-permute-start.9 = (f32[256,256]{1,0:T(8,128)S(1)}, f32[256,256]{1,0:T(8,128)S(1)}, u32[]{:S(2)}, u32[]{:S(2)}) collective-permute-start(f32[256,256]{1,0:T(8,128)S(1)} %fusion.133), channel_id=1, source_target_pairs={{0,8},{4,12},{8,16},{12,20},{16,24},{20,28},{24,32},{28,36},{32,40... | collective-permute-start | bytes 786440 | tf_op jit(solution)/shard_map/ppermute | solution.py:15
  87.4 9.3 %collective-permute-start.10 = (f32[256]{0:T(256)S(1)}, f32[256]{0:T(256)S(1)}, u32[]{:S(2)}, u32[]{:S(2)}) collective-permute-start(f32[256]{0:T(256)S(1)} %add.159), channel_id=1, source_target_pairs={{0,16},{4,20},{8,24},{12,28},{16,32},{20,36},{24,40},{28,44},{32,4... | collective-permute-start | bytes 3080 | tf_op jit(solution)/shard_map/ppermute | solution.py:15
  93.0 9.8 %collective-permute-start.11 = (f32[256,256]{1,0:T(8,128)S(1)}, f32[256,256]{1,0:T(8,128)S(1)}, u32[]{:S(2)}, u32[]{:S(2)}) collective-permute-start(f32[256,256]{1,0:T(8,128)S(1)} %fusion.135), channel_id=1, source_target_pairs={{0,16},{4,20},{8,24},{12,28},{16,32},{20,36},{24,40},{28,44},{32,4... | collective-permute-start | bytes 786440 | tf_op jit(solution)/shard_map/ppermute | solution.py:15
  97.6 10.7 %collective-permute-start.12 = (f32[256]{0:T(256)}, f32[256]{0:T(256)}, u32[]{:S(2)}, u32[]{:S(2)}) collective-permute-start(f32[256]{0:T(256)} %add.160), channel_id=1, source_target_pairs={{0,32},{4,36},{8,40},{12,44},{16,48},{20,52},{24,56},{28,60},{32,6... | collective-permute-start | bytes 3080 | tf_op jit(solution)/shard_map/ppermute | solution.py:15
  103.9 8.6 %collective-permute-start.13 = (f32[256,256]{1,0:T(8,128)}, f32[256,256]{1,0:T(8,128)}, u32[]{:S(2)}, u32[]{:S(2)}) collective-permute-start(f32[256,256]{1,0:T(8,128)} %fusion.137), channel_id=1, source_target_pairs={{0,32},{4,36},{8,40},{12,44},{16,48},{20,52},{24,56},{28,60},{32,6... | collective-permute-start | bytes 786440 | tf_op jit(solution)/shard_map/ppermute | solution.py:15
  108.1 8.2 %copy-start.56 = (f32[1,256]{1,0:T(1,128)S(1)}, f32[1,256]{1,0:T(1,128)}, u32[]{:S(2)}) copy-start(f32[1,256]{1,0:T(1,128)} %copy-done.55) | copy-start | bytes 3076
  108.1 8.2 %copy-start.51 = (f32[4,1,256]{2,1,0:T(1,128)S(1)}, f32[4,1,256]{2,1,0:T(1,128)}, u32[]{:S(2)}) copy-start(f32[4,1,256]{2,1,0:T(1,128)} %copy-done.50) | copy-start | bytes 12292
  108.1 8.2 %copy-start.53 = (f32[4,1,256]{2,1,0:T(1,128)S(1)}, f32[4,1,256]{2,1,0:T(1,128)}, u32[]{:S(2)}) copy-start(f32[4,1,256]{2,1,0:T(1,128)} %copy-done.52) | copy-start | bytes 12292
  108.1 8.5 %copy-start.35 = (f32[4,1,256]{2,1,0:T(1,128)S(1)}, f32[4,1,256]{2,1,0:T(1,128)}, u32[]{:S(2)}) copy-start(f32[4,1,256]{2,1,0:T(1,128)} %copy-done.33) | copy-start | bytes 12292
  108.1 8.5 %copy-start.49 = (f32[4,1,256]{2,1,0:T(1,128)S(1)}, f32[4,1,256]{2,1,0:T(1,128)}, u32[]{:S(2)}) copy-start(f32[4,1,256]{2,1,0:T(1,128)} %copy-done.48) | copy-start | bytes 12292
  108.2 8.9 %copy-start.32 = (f32[4,1,256]{2,1,0:T(1,128)S(1)}, f32[4,1,256]{2,1,0:T(1,128)}, u32[]{:S(2)}) copy-start(f32[4,1,256]{2,1,0:T(1,128)} %copy-done.30) | copy-start | bytes 12292
  108.2 8.9 %copy-start.47 = (f32[4,1,256]{2,1,0:T(1,128)S(1)}, f32[4,1,256]{2,1,0:T(1,128)}, u32[]{:S(2)}) copy-start(f32[4,1,256]{2,1,0:T(1,128)} %copy-done.46) | copy-start | bytes 12292
  108.2 9.2 %copy-start.29 = (f32[4,1,256]{2,1,0:T(1,128)S(1)}, f32[4,1,256]{2,1,0:T(1,128)}, u32[]{:S(2)}) copy-start(f32[4,1,256]{2,1,0:T(1,128)} %copy-done.27) | copy-start | bytes 12292
  108.2 9.2 %copy-start.45 = (f32[4,1,256]{2,1,0:T(1,128)S(1)}, f32[4,1,256]{2,1,0:T(1,128)}, u32[]{:S(2)}) copy-start(f32[4,1,256]{2,1,0:T(1,128)} %copy-done.44) | copy-start | bytes 12292
  108.2 9.5 %copy-start.26 = (f32[4,1,256]{2,1,0:T(1,128)S(1)}, f32[4,1,256]{2,1,0:T(1,128)}, u32[]{:S(2)}) copy-start(f32[4,1,256]{2,1,0:T(1,128)} %copy-done.24) | copy-start | bytes 12292
  108.2 9.5 %copy-start.43 = (f32[4,1,256]{2,1,0:T(1,128)S(1)}, f32[4,1,256]{2,1,0:T(1,128)}, u32[]{:S(2)}) copy-start(f32[4,1,256]{2,1,0:T(1,128)} %copy-done.42) | copy-start | bytes 12292
  108.2 9.9 %copy-start.23 = (f32[4,1,256]{2,1,0:T(1,128)S(1)}, f32[4,1,256]{2,1,0:T(1,128)}, u32[]{:S(2)}) copy-start(f32[4,1,256]{2,1,0:T(1,128)} %copy-done.21) | copy-start | bytes 12292
  108.2 9.9 %copy-start.41 = (f32[4,1,256]{2,1,0:T(1,128)S(1)}, f32[4,1,256]{2,1,0:T(1,128)}, u32[]{:S(2)}) copy-start(f32[4,1,256]{2,1,0:T(1,128)} %copy-done.40) | copy-start | bytes 12292
  108.2 10.2 %copy-start.20 = (f32[4,1,256]{2,1,0:T(1,128)S(1)}, f32[4,1,256]{2,1,0:T(1,128)}, u32[]{:S(2)}) copy-start(f32[4,1,256]{2,1,0:T(1,128)} %copy-done.18) | copy-start | bytes 12292
  108.2 10.2 %copy-start.39 = (f32[4,1,256]{2,1,0:T(1,128)S(1)}, f32[4,1,256]{2,1,0:T(1,128)}, u32[]{:S(2)}) copy-start(f32[4,1,256]{2,1,0:T(1,128)} %copy-done.38) | copy-start | bytes 12292
  108.3 10.5 %copy-start.17 = (f32[4,1,256]{2,1,0:T(1,128)S(1)}, f32[4,1,256]{2,1,0:T(1,128)}, u32[]{:S(2)}) copy-start(f32[4,1,256]{2,1,0:T(1,128)} %copy-done.15) | copy-start | bytes 12292
  108.3 10.5 %copy-start.37 = (f32[4,1,256]{2,1,0:T(1,128)S(1)}, f32[4,1,256]{2,1,0:T(1,128)}, u32[]{:S(2)}) copy-start(f32[4,1,256]{2,1,0:T(1,128)} %copy-done.36) | copy-start | bytes 12292
  109.5 9.6 %copy-start.13 = (f32[256,256,1]{1,0,2:T(8,128)S(1)}, f32[256,256,1]{1,0,2:T(8,128)}, u32[]{:S(2)}) copy-start(f32[256,256,1]{1,0,2:T(8,128)} %convolution_bitcast_fusion.2) | copy-start | bytes 786436
  110.3 3.6 %collective-permute-start.14 = (f32[256]{0:T(256)S(1)}, f32[256]{0:T(256)S(1)}, u32[]{:S(2)}, u32[]{:S(2)}) collective-permute-start(f32[256]{0:T(256)S(1)} %add.161), channel_id=1, source_target_pairs={{0,64},{4,68},{8,72},{12,76},{16,80},{20,84},{24,88},{28,92},{32,9... | collective-permute-start | bytes 3080 | tf_op jit(solution)/shard_map/ppermute | solution.py:15
  119.6 20.6 %copy-start.8 = (f32[256,256]{1,0:T(8,128)S(1)}, f32[256,256]{1,0:T(8,128)}, u32[]{:S(2)}) copy-start(f32[256,256]{1,0:T(8,128)} %copy-done.7) | copy-start | bytes 786436
  120.9 27.5 %copy-start.6 = (f32[256,256]{1,0:T(8,128)S(1)}, f32[256,256]{1,0:T(8,128)}, u32[]{:S(2)}) copy-start(f32[256,256]{1,0:T(8,128)} %copy-done.5) | copy-start | bytes 786436
  120.9 40.5 %copy-start.12 = (f32[256,256]{1,0:T(8,128)S(1)}, f32[256,256]{1,0:T(8,128)}, u32[]{:S(2)}) copy-start(f32[256,256]{1,0:T(8,128)} %fusion.149) | copy-start | bytes 786436
  122.4 9.9 %collective-permute-start.16 = (f32[256]{0:T(256)S(1)}, f32[256]{0:T(256)S(1)}, u32[]{:S(2)}, u32[]{:S(2)}) collective-permute-start(f32[256]{0:T(256)S(1)} %select_add_fusion), channel_id=1, source_target_pairs={{8,0},{12,4},{16,8},{20,12},{24,16},{28,20},{32,24},{36,28},{40,32... | collective-permute-start | bytes 3080 | tf_op jit(solution)/shard_map/ppermute | solution.py:19
  125.1 7.4 %collective-permute-start.15 = (f32[256]{0:T(256)S(1)}, f32[256]{0:T(256)S(1)}, u32[]{:S(2)}, u32[]{:S(2)}) collective-permute-start(f32[256]{0:T(256)S(1)} %select_add_fusion), channel_id=1, source_target_pairs={{4,0},{8,4},{12,8},{16,12},{20,16},{24,20},{28,24},{32,28},{36,32}... | collective-permute-start | bytes 3080 | tf_op jit(solution)/shard_map/ppermute | solution.py:19
  132.6 7.6 %collective-permute-start.17 = (f32[256]{0:T(256)S(1)}, f32[256]{0:T(256)S(1)}, u32[]{:S(2)}, u32[]{:S(2)}) collective-permute-start(f32[256]{0:T(256)S(1)} %add.179), channel_id=1, source_target_pairs={{8,0},{12,4},{16,8},{20,12},{24,16},{28,20},{32,24},{36,28},{40,32... | collective-permute-start | bytes 3080 | tf_op jit(solution)/shard_map/ppermute | solution.py:19
  140.5 7.9 %collective-permute-start.18 = (f32[256]{0:T(256)S(1)}, f32[256]{0:T(256)S(1)}, u32[]{:S(2)}, u32[]{:S(2)}) collective-permute-start(f32[256]{0:T(256)S(1)} %add.180), channel_id=1, source_target_pairs={{16,0},{20,4},{24,8},{28,12},{32,16},{36,20},{40,24},{44,28},{48,3... | collective-permute-start | bytes 3080 | tf_op jit(solution)/shard_map/ppermute | solution.py:19
  148.7 5.5 %collective-permute-start.19 = (f32[256]{0:T(256)S(1)}, f32[256]{0:T(256)S(1)}, u32[]{:S(2)}, u32[]{:S(2)}) collective-permute-start(f32[256]{0:T(256)S(1)} %add.181), channel_id=1, source_target_pairs={{32,0},{36,4},{40,8},{44,12},{48,16},{52,20},{56,24},{60,28},{64,3... | collective-permute-start | bytes 3080 | tf_op jit(solution)/shard_map/ppermute | solution.py:19
  154.5 7.0 %collective-permute-start.20 = (f32[256]{0:T(256)S(1)}, f32[256]{0:T(256)S(1)}, u32[]{:S(2)}, u32[]{:S(2)}) collective-permute-start(f32[256]{0:T(256)S(1)} %add.182), channel_id=1, source_target_pairs={{64,0},{68,4},{72,8},{76,12},{80,16},{84,20},{88,24},{92,28},{96,3... | collective-permute-start | bytes 3080 | tf_op jit(solution)/shard_map/ppermute | solution.py:19
  (15 other events, 50.6 us)

commit v3 on v2

--- a/solution.py
+++ b/solution.py
@@ -31,9 +31,7 @@
 
 
 def halo(fields, bands):
-    edge = fields[:, :, -3:, :]
-    flat = edge.reshape(edge.shape[0] * edge.shape[1], edge.shape[2] * edge.shape[3])
-    return shift_down(flat, "space", 1, bands).reshape(edge.shape)
+    return shift_down(fields[:, :, -3:, :], "space", 1, bands)
 
 
 def encode(fields, above, conv_in, conv_mid, obs_gain, bands):

time: 167 us -> 164 us (0.982)
  local copies, waits for them, and re-layouts: 24.3 us -> 22.1 us
    reshape x1 -> x0, local copies, waits for them, and re-layouts: 2.14 us -> none  [halo(): return shift_down(flat, 'space', 1, bands).reshape(edge.shape)]
    unnamed x137 -> x136, local copies, waits for them, and re-layouts: 17.6 us -> 16.1 us
where the time goes in v3:
time: 164 us
  starting transfers between devices  52.7 us (32%)
  matrix products  50.4 us (31%)
  waiting for transfers between devices  31.5 us (19%)
  local copies, waits for them, and re-layouts  22.1 us (13%)
  other arithmetic  4.96 us (3%)
  between operations  2.08 us (1%)
    ppermute x12, starting transfers between devices, shift_down(): lax.ppermute(value, axis, [(i, i + steps) for i in range(count - steps)])  36.7 us
    dot_general x55, matrix products, dot(): return jnp.dot(a, b, precision=precise)  25.3 us
    ppermute x6, waiting for transfers between devices, shift_up(): lax.ppermute(value, axis, [(i + steps, i) for i in range(count - steps)])  23.9 us
    unnamed x136, local copies, waits for them, and re-layouts  16.1 us
    ppermute x6, starting transfers between devices, shift_up(): lax.ppermute(value, axis, [(i + steps, i) for i in range(count - steps)])  11 us
    conv_general_dilated x1, matrix products, conv_stride(): lax.conv_general_dilated(images, kernel, (2, 2), ((0, 0), (1, 1)), dimens...  9.38 us
    ppermute x12, waiting for transfers between devices, shift_down(): lax.ppermute(value, axis, [(i, i + steps) for i in range(count - steps)])  7.56 us
    dot_general x7, matrix products, per_device(): jnp.einsum('ab,sbc->sac', transition, phis, precision=precise)  7.15 us
  transfers between devices with their start and end apart: 21, of which 9 were waited for; matrix products, arithmetic and copies ran while one was open for 26% of the time, Pallas kernels for 0%

profile of v3, /device:TPU:14, one launch (start us, length us, event | category | flops | bytes accessed | tf_op | source)
XLA Modules:
  0.0 163.7 jit_solution(7560083417581954423)
XLA Ops:
  0.7 1.6 slice.168
  2.3 0.8 copy.122
  3.1 4.6 %collective-permute-start = (bf16[32,8,3,256]{3,1,2,0:T(8,128)(2,1)}, bf16[32,8,3,256]{3,1,2,0:T(8,128)(2,1)}, u32[]{:S(2)}, u32[]{:S(2)}) collective-permute-start(bf16[32,8,3,256]{3,1,2,0:T(8,128)(2,1)} %copy.122), channel_id=1, source_target_pairs={{0,1},{1,2},{2,3},{4,5},{5,6},{6,7},{8,9},{9,10},{10,11},{12,13},{... | collective-permute-start | bytes 1179656 | tf_op jit(solution)/shard_map/ppermute | solution.py:15
  8.7 1.0 fusion.23
  9.7 1.0 fusion.22
  10.8 1.0 fusion.21
  11.8 1.0 fusion.20
  12.9 1.0 fusion.19
  13.9 1.0 fusion.18
  15.0 1.0 fusion.17
  17.2 1.3 fusion.75
  18.6 0.8 bitcast_dynamic-update-slice_fusion.4
  19.4 1.3 constant_dynamic-update-slice_fusion.16
  21.3 1.0 convolution_bitcast_fusion
  22.3 0.8 fusion.59
  24.6 1.1 fusion.149
  26.5 5.1 %copy.88 = bf16[32,8,8,256]{0,1,3,2:T(8,128)(2,1)} copy(bf16[32,8,8,256]{3,2,1,0:T(8,128)(2,1)} %param.7) | data formatting | bytes 2097152 | tf_op args[0]
  32.1 1.8 %bitcast_dynamic-update-slice_fusion = (f32[256,2048]{1,0:T(8,128)}, f32[2048,256]{1,0:T(8,128)}) fusion(f32[4,256,256]{1,2,0:T(8,128)S(1)} %convolution_bitcast_fusion, f32[2048,256]{1,0:T(8,128)} %fusion.79, f32[2,256,256]{1,2,0:T(8,128)} %copy-done.2), kind=kLoop, calls=%fused_computation.84 | loop fusion | bytes 1048576
  33.9 2.9 %copy.87 = bf16[32,8,3,256]{0,1,3,2:T(8,128)(2,1)} copy(bf16[32,8,3,256]{3,1,2,0:T(8,128)(2,1)} %collective-permute-done) | data formatting | bytes 786432 | tf_op jit(solution)/shard_map/optimization_barrier | solution.py:105
  36.9 9.4 %fusion.4 = f32[32,2,64,128]{3,0,2,1:T(8,128)} fusion(bf16[128,64,3,3]{0,1,3,2:T(8,128)(2,1)S(1)} %copy-done, pred[5]{0:T(512)(128)(4,1)} %compare_and_fusion, bf16[64,8,3,3]{0,1,3,2:T(8,128)(2,1)} %param.8, bf16[32,8,8,256]{0,1,3,2:T(8,128)(2,1)} %copy.88, bf16[32,8,3,256]{0,1,3,2:T(8,128)(2,1)} %copy.87), kind=kOutput, calls=%fused_computation.5 | convolution fusion | flops 799834112 | bytes 3695621 | tf_op jit(solution)/shard_map/conv_general_dilated | solution.py:23
  46.3 5.4 %convolution_bitcast_fusion.3 = f32[32,256]{1,0:T(8,128)S(1)} fusion(bf16[2,64,128,256]{3,2,1,0:T(8,128)(2,1)} %param.10, f32[32,2,64,128]{3,0,2,1:T(8,128)} %fusion.4), kind=kOutput, calls=%fused_computation.33 | convolution fusion | flops 271056896 | bytes 10518528 | tf_op jit(solution)/shard_map/shwc,hwcm->sm/dot_general | solution.py:45
  51.7 0.8 collective-permute-start.2
  52.5 1.3 collective-permute-start.3
  53.8 2.9 %collective-permute-start.1 = (f32[32,256]{1,0:T(8,128)S(1)}, f32[32,256]{1,0:T(8,128)S(1)}, u32[]{:S(2)}, u32[]{:S(2)}) collective-permute-start(f32[32,256]{1,0:T(8,128)S(1)} %convolution_bitcast_fusion.3), channel_id=1, source_target_pairs={{0,2},{1,3},{2,0},{3,1},{4,6},{5,7},{6,4},{7,5},{8,10},{9,11},{10,... | collective-permute-start | bytes 98312 | tf_op jit(solution)/shard_map/ppermute | solution.py:49
  56.6 0.9 fusion.84
  57.5 1.9 %collective-permute-start.5 = (f32[256,256]{1,0:T(8,128)S(1)}, f32[256,256]{1,0:T(8,128)S(1)}, u32[]{:S(2)}, u32[]{:S(2)}) collective-permute-start(f32[256,256]{1,0:T(8,128)S(1)} %copy-done.14), channel_id=1, source_target_pairs={{0,4},{4,8},{8,12},{12,16},{16,20},{20,24},{24,28},{28,32},{32,36}... | collective-permute-start | bytes 786440 | tf_op jit(solution)/shard_map/ppermute | solution.py:15
  59.4 3.4 %collective-permute-start.7 = (f32[256,256]{1,0:T(8,128)S(1)}, f32[256,256]{1,0:T(8,128)S(1)}, u32[]{:S(2)}, u32[]{:S(2)}) collective-permute-start(f32[256,256]{1,0:T(8,128)S(1)} %copy-done.14), channel_id=1, source_target_pairs={{0,8},{4,12},{8,16},{12,20},{16,24},{20,28},{24,32},{28,36},{32,40... | collective-permute-start | bytes 786440 | tf_op jit(solution)/shard_map/ppermute | solution.py:15
  66.6 3.4 %collective-permute-start.6 = (f32[256]{0:T(256)S(1)}, f32[256]{0:T(256)S(1)}, u32[]{:S(2)}, u32[]{:S(2)}) collective-permute-start(f32[256]{0:T(256)S(1)} %add.157), channel_id=1, source_target_pairs={{0,8},{4,12},{8,16},{12,20},{16,24},{20,28},{24,32},{28,36},{32,40... | collective-permute-start | bytes 3080 | tf_op jit(solution)/shard_map/ppermute | solution.py:15
  70.1 0.9 fusion.82
  70.9 2.9 %collective-permute-start.4 = (f32[256]{0:T(256)S(1)}, f32[256]{0:T(256)S(1)}, u32[]{:S(2)}, u32[]{:S(2)}) collective-permute-start(f32[256]{0:T(256)S(1)} %add.157), channel_id=1, source_target_pairs={{0,4},{4,8},{8,12},{12,16},{16,20},{20,24},{24,28},{28,32},{32,36}... | collective-permute-start | bytes 3080 | tf_op jit(solution)/shard_map/ppermute | solution.py:15
  74.2 1.6 collective-permute-done.4
  75.8 5.9 %collective-permute-start.8 = (f32[256]{0:T(256)S(1)}, f32[256]{0:T(256)S(1)}, u32[]{:S(2)}, u32[]{:S(2)}) collective-permute-start(f32[256]{0:T(256)S(1)} %add.158), channel_id=1, source_target_pairs={{0,8},{4,12},{8,16},{12,20},{16,24},{20,28},{24,32},{28,36},{32,40... | collective-permute-start | bytes 3080 | tf_op jit(solution)/shard_map/ppermute | solution.py:15
  82.2 1.9 %collective-permute-start.9 = (f32[256,256]{1,0:T(8,128)S(1)}, f32[256,256]{1,0:T(8,128)S(1)}, u32[]{:S(2)}, u32[]{:S(2)}) collective-permute-start(f32[256,256]{1,0:T(8,128)S(1)} %fusion.133), channel_id=1, source_target_pairs={{0,8},{4,12},{8,16},{12,20},{16,24},{20,28},{24,32},{28,36},{32,40... | collective-permute-start | bytes 786440 | tf_op jit(solution)/shard_map/ppermute | solution.py:15
  84.1 0.9 fusion.80
  85.2 3.1 %collective-permute-start.10 = (f32[256]{0:T(256)S(1)}, f32[256]{0:T(256)S(1)}, u32[]{:S(2)}, u32[]{:S(2)}) collective-permute-start(f32[256]{0:T(256)S(1)} %add.159), channel_id=1, source_target_pairs={{0,16},{4,20},{8,24},{12,28},{16,32},{20,36},{24,40},{28,44},{32,4... | collective-permute-start | bytes 3080 | tf_op jit(solution)/shard_map/ppermute | solution.py:15
  88.4 2.0 %collective-permute-done.9 = f32[256,256]{1,0:T(8,128)S(1)} collective-permute-done((f32[256,256]{1,0:T(8,128)S(1)}, f32[256,256]{1,0:T(8,128)S(1)}, u32[]{:S(2)}, u32[]{:S(2)}) %collective-permute-start.9) | collective-permute-done | bytes 262176 | tf_op jit(solution)/shard_map/ppermute | solution.py:15
  90.8 2.9 %collective-permute-start.11 = (f32[256,256]{1,0:T(8,128)S(1)}, f32[256,256]{1,0:T(8,128)S(1)}, u32[]{:S(2)}, u32[]{:S(2)}) collective-permute-start(f32[256,256]{1,0:T(8,128)S(1)} %fusion.135), channel_id=1, source_target_pairs={{0,16},{4,20},{8,24},{12,28},{16,32},{20,36},{24,40},{28,44},{32,4... | collective-permute-start | bytes 786440 | tf_op jit(solution)/shard_map/ppermute | solution.py:15
  95.4 2.1 %collective-permute-start.12 = (f32[256]{0:T(256)}, f32[256]{0:T(256)}, u32[]{:S(2)}, u32[]{:S(2)}) collective-permute-start(f32[256]{0:T(256)} %add.160), channel_id=1, source_target_pairs={{0,32},{4,36},{8,40},{12,44},{16,48},{20,52},{24,56},{28,60},{32,6... | collective-permute-start | bytes 3080 | tf_op jit(solution)/shard_map/ppermute | solution.py:15
  97.6 3.0 %collective-permute-done.11 = f32[256,256]{1,0:T(8,128)S(1)} collective-permute-done((f32[256,256]{1,0:T(8,128)S(1)}, f32[256,256]{1,0:T(8,128)S(1)}, u32[]{:S(2)}, u32[]{:S(2)}) %collective-permute-start.11) | collective-permute-done | bytes 262176 | tf_op jit(solution)/shard_map/ppermute | solution.py:15
  100.6 1.1 fusion.137
  101.7 3.2 %collective-permute-start.13 = (f32[256,256]{1,0:T(8,128)}, f32[256,256]{1,0:T(8,128)}, u32[]{:S(2)}, u32[]{:S(2)}) collective-permute-start(f32[256,256]{1,0:T(8,128)} %fusion.137), channel_id=1, source_target_pairs={{0,32},{4,36},{8,40},{12,44},{16,48},{20,52},{24,56},{28,60},{32,6... | collective-permute-start | bytes 786440 | tf_op jit(solution)/shard_map/ppermute | solution.py:15
  104.8 1.1 convolution_bitcast_fusion.2
  106.1 1.2 fusion.138
  107.3 0.8 add.161
  108.1 1.3 collective-permute-start.14
  109.4 0.9 collective-permute-done.13
  110.2 1.4 fusion.139
  112.2 0.7 add.163
  117.4 1.3 fusion.15
  120.2 1.9 %collective-permute-start.16 = (f32[256]{0:T(256)S(1)}, f32[256]{0:T(256)S(1)}, u32[]{:S(2)}, u32[]{:S(2)}) collective-permute-start(f32[256]{0:T(256)S(1)} %select_add_fusion), channel_id=1, source_target_pairs={{8,0},{12,4},{16,8},{20,12},{24,16},{28,20},{32,24},{36,28},{40,32... | collective-permute-start | bytes 3080 | tf_op jit(solution)/shard_map/ppermute | solution.py:19
  122.1 0.8 fusion.78
  122.9 1.9 %collective-permute-start.15 = (f32[256]{0:T(256)S(1)}, f32[256]{0:T(256)S(1)}, u32[]{:S(2)}, u32[]{:S(2)}) collective-permute-start(f32[256]{0:T(256)S(1)} %select_add_fusion), channel_id=1, source_target_pairs={{4,0},{8,4},{12,8},{16,12},{20,16},{24,20},{28,24},{32,28},{36,32}... | collective-permute-start | bytes 3080 | tf_op jit(solution)/shard_map/ppermute | solution.py:19
  124.8 5.3 %collective-permute-done.16 = f32[256]{0:T(256)S(1)} collective-permute-done((f32[256]{0:T(256)S(1)}, f32[256]{0:T(256)S(1)}, u32[]{:S(2)}, u32[]{:S(2)}) %collective-permute-start.16) | collective-permute-done | bytes 1056 | tf_op jit(solution)/shard_map/ppermute | solution.py:19
  130.4 1.9 %collective-permute-start.17 = (f32[256]{0:T(256)S(1)}, f32[256]{0:T(256)S(1)}, u32[]{:S(2)}, u32[]{:S(2)}) collective-permute-start(f32[256]{0:T(256)S(1)} %add.179), channel_id=1, source_target_pairs={{8,0},{12,4},{16,8},{20,12},{24,16},{28,20},{32,24},{36,28},{40,32... | collective-permute-start | bytes 3080 | tf_op jit(solution)/shard_map/ppermute | solution.py:19
  132.3 0.8 constant_dynamic-update-slice_fusion.17
  133.1 4.9 %collective-permute-done.17 = f32[256]{0:T(256)S(1)} collective-permute-done((f32[256]{0:T(256)S(1)}, f32[256]{0:T(256)S(1)}, u32[]{:S(2)}, u32[]{:S(2)}) %collective-permute-start.17) | collective-permute-done | bytes 1056 | tf_op jit(solution)/shard_map/ppermute | solution.py:19
  138.3 2.0 %collective-permute-start.18 = (f32[256]{0:T(256)S(1)}, f32[256]{0:T(256)S(1)}, u32[]{:S(2)}, u32[]{:S(2)}) collective-permute-start(f32[256]{0:T(256)S(1)} %add.180), channel_id=1, source_target_pairs={{16,0},{20,4},{24,8},{28,12},{32,16},{36,20},{40,24},{44,28},{48,3... | collective-permute-start | bytes 3080 | tf_op jit(solution)/shard_map/ppermute | solution.py:19
  140.2 0.7 bitcast_dynamic-update-slice_fusion.3
  141.0 5.2 %collective-permute-done.18 = f32[256]{0:T(256)S(1)} collective-permute-done((f32[256]{0:T(256)S(1)}, f32[256]{0:T(256)S(1)}, u32[]{:S(2)}, u32[]{:S(2)}) %collective-permute-start.18) | collective-permute-done | bytes 1056 | tf_op jit(solution)/shard_map/ppermute | solution.py:19
  146.5 2.0 %collective-permute-start.19 = (f32[256]{0:T(256)S(1)}, f32[256]{0:T(256)S(1)}, u32[]{:S(2)}, u32[]{:S(2)}) collective-permute-start(f32[256]{0:T(256)S(1)} %add.181), channel_id=1, source_target_pairs={{32,0},{36,4},{40,8},{44,12},{48,16},{52,20},{56,24},{60,28},{64,3... | collective-permute-start | bytes 3080 | tf_op jit(solution)/shard_map/ppermute | solution.py:19
  148.5 3.5 %collective-permute-done.19 = f32[256]{0:T(256)S(1)} collective-permute-done((f32[256]{0:T(256)S(1)}, f32[256]{0:T(256)S(1)}, u32[]{:S(2)}, u32[]{:S(2)}) %collective-permute-start.19) | collective-permute-done | bytes 1056 | tf_op jit(solution)/shard_map/ppermute | solution.py:19
  152.3 1.3 collective-permute-start.20
  154.2 5.0 %collective-permute-done.20 = f32[256]{0:T(256)S(1)} collective-permute-done((f32[256]{0:T(256)S(1)}, f32[256]{0:T(256)S(1)}, u32[]{:S(2)}, u32[]{:S(2)}) %collective-permute-start.20) | collective-permute-done | bytes 1056 | tf_op jit(solution)/shard_map/ppermute | solution.py:19
  160.4 2.7 %fusion.12 = f32[1,8,256]{2,0,1:T(1,128)S(1)} fusion(f32[32,8,8,256]{3,2,1,0:T(8,128)} %bitcast.147, s32[]{:T(128)S(6)} %select_n.26, f32[1,256]{1,0:T(1,128)S(1)} %bitcast.448, f32[1,256]{1,0:T(1,128)S(1)} %bitcast.460, f32[1,256]{1,0:T(1,128)S(1)} %bitcast.445, f32[1,256]{1,0:T(1,128)S(1)} %bitcast.441), kind=kOutput, calls=%fused_computation.9 | convolution fusion | flops 6292224 | bytes 2109444 | tf_op jit(solution)/shard_map/dot_general | solution.py:11
  (222 shorter events, 21.9 us)
Async XLA Ops:
  0.6 36.2 %copy-start = (bf16[128,64,3,3]{0,1,3,2:T(8,128)(2,1)S(1)}, bf16[128,64,3,3]{0,1,3,2:T(8,128)(2,1)}, u32[]{:S(2)}) copy-start(bf16[128,64,3,3]{0,1,3,2:T(8,128)(2,1)} %param.9) | copy-start | bytes 442372
  0.7 7.9 %copy-start.54 = (f32[32,256]{1,0:T(8,128)S(1)}, f32[32,256]{1,0:T(8,128)}, u32[]{:S(2)}) copy-start(f32[32,256]{1,0:T(8,128)} %param.13) | copy-start | bytes 98308
  3.1 30.8 %collective-permute-start = (bf16[32,8,3,256]{3,1,2,0:T(8,128)(2,1)}, bf16[32,8,3,256]{3,1,2,0:T(8,128)(2,1)}, u32[]{:S(2)}, u32[]{:S(2)}) collective-permute-start(bf16[32,8,3,256]{3,1,2,0:T(8,128)(2,1)} %copy.122), channel_id=1, source_target_pairs={{0,1},{1,2},{2,3},{4,5},{5,6},{6,7},{8,9},{9,10},{10,11},{12,13},{... | collective-permute-start | bytes 1179656 | tf_op jit(solution)/shard_map/ppermute | solution.py:15
  46.2 11.3 %copy-start.14 = (f32[256,256]{1,0:T(8,128)S(1)}, f32[256,256]{1,0:T(8,128)}, u32[]{:S(2)}) copy-start(f32[256,256]{1,0:T(8,128)} %fusion.75) | copy-start | bytes 786436
  46.2 16.8 %copy-start.34 = (f32[4,1,256]{2,1,0:T(1,128)S(1)}, f32[4,1,256]{2,1,0:T(1,128)}, u32[]{:S(2)}) copy-start(f32[4,1,256]{2,1,0:T(1,128)} %copy-done.33) | copy-start | bytes 12292
  46.2 17.1 %copy-start.31 = (f32[4,1,256]{2,1,0:T(1,128)S(1)}, f32[4,1,256]{2,1,0:T(1,128)}, u32[]{:S(2)}) copy-start(f32[4,1,256]{2,1,0:T(1,128)} %copy-done.30) | copy-start | bytes 12292
  46.2 17.4 %copy-start.28 = (f32[4,1,256]{2,1,0:T(1,128)S(1)}, f32[4,1,256]{2,1,0:T(1,128)}, u32[]{:S(2)}) copy-start(f32[4,1,256]{2,1,0:T(1,128)} %copy-done.27) | copy-start | bytes 12292
  51.6 12.4 %copy-start.25 = (f32[4,1,256]{2,1,0:T(1,128)S(1)}, f32[4,1,256]{2,1,0:T(1,128)}, u32[]{:S(2)}) copy-start(f32[4,1,256]{2,1,0:T(1,128)} %copy-done.24) | copy-start | bytes 12292
  51.6 12.7 %copy-start.22 = (f32[4,1,256]{2,1,0:T(1,128)S(1)}, f32[4,1,256]{2,1,0:T(1,128)}, u32[]{:S(2)}) copy-start(f32[4,1,256]{2,1,0:T(1,128)} %copy-done.21) | copy-start | bytes 12292
  51.7 13.0 %copy-start.19 = (f32[4,1,256]{2,1,0:T(1,128)S(1)}, f32[4,1,256]{2,1,0:T(1,128)}, u32[]{:S(2)}) copy-start(f32[4,1,256]{2,1,0:T(1,128)} %copy-done.18) | copy-start | bytes 12292
  51.7 13.3 %copy-start.16 = (f32[4,1,256]{2,1,0:T(1,128)S(1)}, f32[4,1,256]{2,1,0:T(1,128)}, u32[]{:S(2)}) copy-start(f32[4,1,256]{2,1,0:T(1,128)} %copy-done.15) | copy-start | bytes 12292
  51.7 11.1 %collective-permute-start.2 = (f32[32,256]{1,0:T(8,128)S(1)}, f32[32,256]{1,0:T(8,128)S(1)}, u32[]{:S(2)}, u32[]{:S(2)}) collective-permute-start(f32[32,256]{1,0:T(8,128)S(1)} %convolution_bitcast_fusion.3), channel_id=1, source_target_pairs={{0,3},{1,0},{2,1},{3,2},{4,7},{5,4},{6,5},{7,6},{8,11},{9,8},{10,9... | collective-permute-start | bytes 98312 | tf_op jit(solution)/shard_map/ppermute | solution.py:49
  52.5 10.3 %collective-permute-start.3 = (f32[32,256]{1,0:T(8,128)S(1)}, f32[32,256]{1,0:T(8,128)S(1)}, u32[]{:S(2)}, u32[]{:S(2)}) collective-permute-start(f32[32,256]{1,0:T(8,128)S(1)} %convolution_bitcast_fusion.3), channel_id=1, source_target_pairs={{0,1},{1,2},{2,3},{3,0},{4,5},{5,6},{6,7},{7,4},{8,9},{9,10},{10,1... | collective-permute-start | bytes 98312 | tf_op jit(solution)/shard_map/ppermute | solution.py:49
  53.8 9.1 %collective-permute-start.1 = (f32[32,256]{1,0:T(8,128)S(1)}, f32[32,256]{1,0:T(8,128)S(1)}, u32[]{:S(2)}, u32[]{:S(2)}) collective-permute-start(f32[32,256]{1,0:T(8,128)S(1)} %convolution_bitcast_fusion.3), channel_id=1, source_target_pairs={{0,2},{1,3},{2,0},{3,1},{4,6},{5,7},{6,4},{7,5},{8,10},{9,11},{10,... | collective-permute-start | bytes 98312 | tf_op jit(solution)/shard_map/ppermute | solution.py:49
  57.5 16.4 %collective-permute-start.5 = (f32[256,256]{1,0:T(8,128)S(1)}, f32[256,256]{1,0:T(8,128)S(1)}, u32[]{:S(2)}, u32[]{:S(2)}) collective-permute-start(f32[256,256]{1,0:T(8,128)S(1)} %copy-done.14), channel_id=1, source_target_pairs={{0,4},{4,8},{8,12},{12,16},{16,20},{20,24},{24,28},{28,32},{32,36}... | collective-permute-start | bytes 786440 | tf_op jit(solution)/shard_map/ppermute | solution.py:15
  59.4 22.3 %collective-permute-start.7 = (f32[256,256]{1,0:T(8,128)S(1)}, f32[256,256]{1,0:T(8,128)S(1)}, u32[]{:S(2)}, u32[]{:S(2)}) collective-permute-start(f32[256,256]{1,0:T(8,128)S(1)} %copy-done.14), channel_id=1, source_target_pairs={{0,8},{4,12},{8,16},{12,20},{16,24},{20,28},{24,32},{28,36},{32,40... | collective-permute-start | bytes 786440 | tf_op jit(solution)/shard_map/ppermute | solution.py:15
  62.9 19.2 %copy-start.36 = (f32[4,1,256]{2,1,0:T(1,128)}, f32[4,1,256]{2,1,0:T(1,128)S(1)}, u32[]{:S(2)}) copy-start(f32[4,1,256]{2,1,0:T(1,128)S(1)} %get-tuple-element.16) | copy-start | bytes 12292
  62.9 19.2 %copy-start.38 = (f32[4,1,256]{2,1,0:T(1,128)}, f32[4,1,256]{2,1,0:T(1,128)S(1)}, u32[]{:S(2)}) copy-start(f32[4,1,256]{2,1,0:T(1,128)S(1)} %get-tuple-element.17) | copy-start | bytes 12292
  62.9 19.2 %copy-start.40 = (f32[4,1,256]{2,1,0:T(1,128)}, f32[4,1,256]{2,1,0:T(1,128)S(1)}, u32[]{:S(2)}) copy-start(f32[4,1,256]{2,1,0:T(1,128)S(1)} %get-tuple-element.18) | copy-start | bytes 12292
  62.9 19.2 %copy-start.42 = (f32[4,1,256]{2,1,0:T(1,128)}, f32[4,1,256]{2,1,0:T(1,128)S(1)}, u32[]{:S(2)}) copy-start(f32[4,1,256]{2,1,0:T(1,128)S(1)} %get-tuple-element.19) | copy-start | bytes 12292
  62.9 19.2 %copy-start.44 = (f32[4,1,256]{2,1,0:T(1,128)}, f32[4,1,256]{2,1,0:T(1,128)S(1)}, u32[]{:S(2)}) copy-start(f32[4,1,256]{2,1,0:T(1,128)S(1)} %get-tuple-element.20) | copy-start | bytes 12292
  63.0 19.2 %copy-start.46 = (f32[4,1,256]{2,1,0:T(1,128)}, f32[4,1,256]{2,1,0:T(1,128)S(1)}, u32[]{:S(2)}) copy-start(f32[4,1,256]{2,1,0:T(1,128)S(1)} %get-tuple-element.21) | copy-start | bytes 12292
  63.0 19.2 %copy-start.48 = (f32[4,1,256]{2,1,0:T(1,128)}, f32[4,1,256]{2,1,0:T(1,128)S(1)}, u32[]{:S(2)}) copy-start(f32[4,1,256]{2,1,0:T(1,128)S(1)} %get-tuple-element.22) | copy-start | bytes 12292
  63.0 19.2 %copy-start.50 = (f32[4,1,256]{2,1,0:T(1,128)}, f32[4,1,256]{2,1,0:T(1,128)S(1)}, u32[]{:S(2)}) copy-start(f32[4,1,256]{2,1,0:T(1,128)S(1)} %get-tuple-element.23) | copy-start | bytes 12292
  66.2 17.9 %copy-start.55 = (f32[1,256]{1,0:T(1,128)}, f32[1,256]{1,0:T(1,128)S(1)}, u32[]{:S(2)}) copy-start(f32[1,256]{1,0:T(1,128)S(1)} %get-tuple-element.34) | copy-start | bytes 3076
  66.2 17.9 %copy-start.57 = (f32[1,256]{1,0:T(1,128)}, f32[1,256]{1,0:T(1,128)S(1)}, u32[]{:S(2)}) copy-start(f32[1,256]{1,0:T(1,128)S(1)} %get-tuple-element.35) | copy-start | bytes 3076
  66.4 27.4 %copy-start.3 = (f32[2,256,256]{1,2,0:T(8,128)S(1)}, f32[2,256,256]{1,2,0:T(8,128)}, u32[]{:S(2)}) copy-start(f32[2,256,256]{1,2,0:T(8,128)} %copy-done.2) | copy-start | bytes 1572868
  66.6 7.2 %collective-permute-start.6 = (f32[256]{0:T(256)S(1)}, f32[256]{0:T(256)S(1)}, u32[]{:S(2)}, u32[]{:S(2)}) collective-permute-start(f32[256]{0:T(256)S(1)} %add.157), channel_id=1, source_target_pairs={{0,8},{4,12},{8,16},{12,20},{16,24},{20,28},{24,32},{28,36},{32,40... | collective-permute-start | bytes 3080 | tf_op jit(solution)/shard_map/ppermute | solution.py:15
  70.9 4.9 %collective-permute-start.4 = (f32[256]{0:T(256)S(1)}, f32[256]{0:T(256)S(1)}, u32[]{:S(2)}, u32[]{:S(2)}) collective-permute-start(f32[256]{0:T(256)S(1)} %add.157), channel_id=1, source_target_pairs={{0,4},{4,8},{8,12},{12,16},{16,20},{20,24},{24,28},{28,32},{32,36}... | collective-permute-start | bytes 3080 | tf_op jit(solution)/shard_map/ppermute | solution.py:15
  75.8 29.0 %copy-start.10 = (f32[256,256]{1,0:T(8,128)S(1)}, f32[256,256]{1,0:T(8,128)}, u32[]{:S(2)}) copy-start(f32[256,256]{1,0:T(8,128)} %param.12) | copy-start | bytes 786436
  75.8 9.2 %collective-permute-start.8 = (f32[256]{0:T(256)S(1)}, f32[256]{0:T(256)S(1)}, u32[]{:S(2)}, u32[]{:S(2)}) collective-permute-start(f32[256]{0:T(256)S(1)} %add.158), channel_id=1, source_target_pairs={{0,8},{4,12},{8,16},{12,20},{16,24},{20,28},{24,32},{28,36},{32,40... | collective-permute-start | bytes 3080 | tf_op jit(solution)/shard_map/ppermute | solution.py:15
  82.2 8.3 %collective-permute-start.9 = (f32[256,256]{1,0:T(8,128)S(1)}, f32[256,256]{1,0:T(8,128)S(1)}, u32[]{:S(2)}, u32[]{:S(2)}) collective-permute-start(f32[256,256]{1,0:T(8,128)S(1)} %fusion.133), channel_id=1, source_target_pairs={{0,8},{4,12},{8,16},{12,20},{16,24},{20,28},{24,32},{28,36},{32,40... | collective-permute-start | bytes 786440 | tf_op jit(solution)/shard_map/ppermute | solution.py:15
  85.2 9.3 %collective-permute-start.10 = (f32[256]{0:T(256)S(1)}, f32[256]{0:T(256)S(1)}, u32[]{:S(2)}, u32[]{:S(2)}) collective-permute-start(f32[256]{0:T(256)S(1)} %add.159), channel_id=1, source_target_pairs={{0,16},{4,20},{8,24},{12,28},{16,32},{20,36},{24,40},{28,44},{32,4... | collective-permute-start | bytes 3080 | tf_op jit(solution)/shard_map/ppermute | solution.py:15
  90.8 9.8 %collective-permute-start.11 = (f32[256,256]{1,0:T(8,128)S(1)}, f32[256,256]{1,0:T(8,128)S(1)}, u32[]{:S(2)}, u32[]{:S(2)}) collective-permute-start(f32[256,256]{1,0:T(8,128)S(1)} %fusion.135), channel_id=1, source_target_pairs={{0,16},{4,20},{8,24},{12,28},{16,32},{20,36},{24,40},{28,44},{32,4... | collective-permute-start | bytes 786440 | tf_op jit(solution)/shard_map/ppermute | solution.py:15
  95.4 10.7 %collective-permute-start.12 = (f32[256]{0:T(256)}, f32[256]{0:T(256)}, u32[]{:S(2)}, u32[]{:S(2)}) collective-permute-start(f32[256]{0:T(256)} %add.160), channel_id=1, source_target_pairs={{0,32},{4,36},{8,40},{12,44},{16,48},{20,52},{24,56},{28,60},{32,6... | collective-permute-start | bytes 3080 | tf_op jit(solution)/shard_map/ppermute | solution.py:15
  101.7 8.6 %collective-permute-start.13 = (f32[256,256]{1,0:T(8,128)}, f32[256,256]{1,0:T(8,128)}, u32[]{:S(2)}, u32[]{:S(2)}) collective-permute-start(f32[256,256]{1,0:T(8,128)} %fusion.137), channel_id=1, source_target_pairs={{0,32},{4,36},{8,40},{12,44},{16,48},{20,52},{24,56},{28,60},{32,6... | collective-permute-start | bytes 786440 | tf_op jit(solution)/shard_map/ppermute | solution.py:15
  105.9 8.2 %copy-start.56 = (f32[1,256]{1,0:T(1,128)S(1)}, f32[1,256]{1,0:T(1,128)}, u32[]{:S(2)}) copy-start(f32[1,256]{1,0:T(1,128)} %copy-done.55) | copy-start | bytes 3076
  105.9 8.2 %copy-start.51 = (f32[4,1,256]{2,1,0:T(1,128)S(1)}, f32[4,1,256]{2,1,0:T(1,128)}, u32[]{:S(2)}) copy-start(f32[4,1,256]{2,1,0:T(1,128)} %copy-done.50) | copy-start | bytes 12292
  105.9 8.2 %copy-start.53 = (f32[4,1,256]{2,1,0:T(1,128)S(1)}, f32[4,1,256]{2,1,0:T(1,128)}, u32[]{:S(2)}) copy-start(f32[4,1,256]{2,1,0:T(1,128)} %copy-done.52) | copy-start | bytes 12292
  105.9 8.6 %copy-start.35 = (f32[4,1,256]{2,1,0:T(1,128)S(1)}, f32[4,1,256]{2,1,0:T(1,128)}, u32[]{:S(2)}) copy-start(f32[4,1,256]{2,1,0:T(1,128)} %copy-done.33) | copy-start | bytes 12292
  105.9 8.6 %copy-start.49 = (f32[4,1,256]{2,1,0:T(1,128)S(1)}, f32[4,1,256]{2,1,0:T(1,128)}, u32[]{:S(2)}) copy-start(f32[4,1,256]{2,1,0:T(1,128)} %copy-done.48) | copy-start | bytes 12292
  106.0 8.9 %copy-start.32 = (f32[4,1,256]{2,1,0:T(1,128)S(1)}, f32[4,1,256]{2,1,0:T(1,128)}, u32[]{:S(2)}) copy-start(f32[4,1,256]{2,1,0:T(1,128)} %copy-done.30) | copy-start | bytes 12292
  106.0 8.9 %copy-start.47 = (f32[4,1,256]{2,1,0:T(1,128)S(1)}, f32[4,1,256]{2,1,0:T(1,128)}, u32[]{:S(2)}) copy-start(f32[4,1,256]{2,1,0:T(1,128)} %copy-done.46) | copy-start | bytes 12292
  106.0 9.2 %copy-start.29 = (f32[4,1,256]{2,1,0:T(1,128)S(1)}, f32[4,1,256]{2,1,0:T(1,128)}, u32[]{:S(2)}) copy-start(f32[4,1,256]{2,1,0:T(1,128)} %copy-done.27) | copy-start | bytes 12292
  106.0 9.2 %copy-start.45 = (f32[4,1,256]{2,1,0:T(1,128)S(1)}, f32[4,1,256]{2,1,0:T(1,128)}, u32[]{:S(2)}) copy-start(f32[4,1,256]{2,1,0:T(1,128)} %copy-done.44) | copy-start | bytes 12292
  106.0 9.5 %copy-start.26 = (f32[4,1,256]{2,1,0:T(1,128)S(1)}, f32[4,1,256]{2,1,0:T(1,128)}, u32[]{:S(2)}) copy-start(f32[4,1,256]{2,1,0:T(1,128)} %copy-done.24) | copy-start | bytes 12292
  106.0 9.5 %copy-start.43 = (f32[4,1,256]{2,1,0:T(1,128)S(1)}, f32[4,1,256]{2,1,0:T(1,128)}, u32[]{:S(2)}) copy-start(f32[4,1,256]{2,1,0:T(1,128)} %copy-done.42) | copy-start | bytes 12292
  106.0 9.9 %copy-start.23 = (f32[4,1,256]{2,1,0:T(1,128)S(1)}, f32[4,1,256]{2,1,0:T(1,128)}, u32[]{:S(2)}) copy-start(f32[4,1,256]{2,1,0:T(1,128)} %copy-done.21) | copy-start | bytes 12292
  106.0 9.9 %copy-start.41 = (f32[4,1,256]{2,1,0:T(1,128)S(1)}, f32[4,1,256]{2,1,0:T(1,128)}, u32[]{:S(2)}) copy-start(f32[4,1,256]{2,1,0:T(1,128)} %copy-done.40) | copy-start | bytes 12292
  106.0 10.2 %copy-start.20 = (f32[4,1,256]{2,1,0:T(1,128)S(1)}, f32[4,1,256]{2,1,0:T(1,128)}, u32[]{:S(2)}) copy-start(f32[4,1,256]{2,1,0:T(1,128)} %copy-done.18) | copy-start | bytes 12292
  106.0 10.2 %copy-start.39 = (f32[4,1,256]{2,1,0:T(1,128)S(1)}, f32[4,1,256]{2,1,0:T(1,128)}, u32[]{:S(2)}) copy-start(f32[4,1,256]{2,1,0:T(1,128)} %copy-done.38) | copy-start | bytes 12292
  106.1 10.5 %copy-start.17 = (f32[4,1,256]{2,1,0:T(1,128)S(1)}, f32[4,1,256]{2,1,0:T(1,128)}, u32[]{:S(2)}) copy-start(f32[4,1,256]{2,1,0:T(1,128)} %copy-done.15) | copy-start | bytes 12292
  106.1 10.5 %copy-start.37 = (f32[4,1,256]{2,1,0:T(1,128)S(1)}, f32[4,1,256]{2,1,0:T(1,128)}, u32[]{:S(2)}) copy-start(f32[4,1,256]{2,1,0:T(1,128)} %copy-done.36) | copy-start | bytes 12292
  107.3 9.6 %copy-start.13 = (f32[256,256,1]{1,0,2:T(8,128)S(1)}, f32[256,256,1]{1,0,2:T(8,128)}, u32[]{:S(2)}) copy-start(f32[256,256,1]{1,0,2:T(8,128)} %convolution_bitcast_fusion.2) | copy-start | bytes 786436
  108.1 3.6 %collective-permute-start.14 = (f32[256]{0:T(256)S(1)}, f32[256]{0:T(256)S(1)}, u32[]{:S(2)}, u32[]{:S(2)}) collective-permute-start(f32[256]{0:T(256)S(1)} %add.161), channel_id=1, source_target_pairs={{0,64},{4,68},{8,72},{12,76},{16,80},{20,84},{24,88},{28,92},{32,9... | collective-permute-start | bytes 3080 | tf_op jit(solution)/shard_map/ppermute | solution.py:15
  117.4 20.6 %copy-start.8 = (f32[256,256]{1,0:T(8,128)S(1)}, f32[256,256]{1,0:T(8,128)}, u32[]{:S(2)}) copy-start(f32[256,256]{1,0:T(8,128)} %copy-done.7) | copy-start | bytes 786436
  118.7 27.5 %copy-start.6 = (f32[256,256]{1,0:T(8,128)S(1)}, f32[256,256]{1,0:T(8,128)}, u32[]{:S(2)}) copy-start(f32[256,256]{1,0:T(8,128)} %copy-done.5) | copy-start | bytes 786436
  118.7 40.5 %copy-start.12 = (f32[256,256]{1,0:T(8,128)S(1)}, f32[256,256]{1,0:T(8,128)}, u32[]{:S(2)}) copy-start(f32[256,256]{1,0:T(8,128)} %fusion.149) | copy-start | bytes 786436
  120.2 9.9 %collective-permute-start.16 = (f32[256]{0:T(256)S(1)}, f32[256]{0:T(256)S(1)}, u32[]{:S(2)}, u32[]{:S(2)}) collective-permute-start(f32[256]{0:T(256)S(1)} %select_add_fusion), channel_id=1, source_target_pairs={{8,0},{12,4},{16,8},{20,12},{24,16},{28,20},{32,24},{36,28},{40,32... | collective-permute-start | bytes 3080 | tf_op jit(solution)/shard_map/ppermute | solution.py:19
  122.9 7.5 %collective-permute-start.15 = (f32[256]{0:T(256)S(1)}, f32[256]{0:T(256)S(1)}, u32[]{:S(2)}, u32[]{:S(2)}) collective-permute-start(f32[256]{0:T(256)S(1)} %select_add_fusion), channel_id=1, source_target_pairs={{4,0},{8,4},{12,8},{16,12},{20,16},{24,20},{28,24},{32,28},{36,32}... | collective-permute-start | bytes 3080 | tf_op jit(solution)/shard_map/ppermute | solution.py:19
  130.4 7.6 %collective-permute-start.17 = (f32[256]{0:T(256)S(1)}, f32[256]{0:T(256)S(1)}, u32[]{:S(2)}, u32[]{:S(2)}) collective-permute-start(f32[256]{0:T(256)S(1)} %add.179), channel_id=1, source_target_pairs={{8,0},{12,4},{16,8},{20,12},{24,16},{28,20},{32,24},{36,28},{40,32... | collective-permute-start | bytes 3080 | tf_op jit(solution)/shard_map/ppermute | solution.py:19
  138.3 7.9 %collective-permute-start.18 = (f32[256]{0:T(256)S(1)}, f32[256]{0:T(256)S(1)}, u32[]{:S(2)}, u32[]{:S(2)}) collective-permute-start(f32[256]{0:T(256)S(1)} %add.180), channel_id=1, source_target_pairs={{16,0},{20,4},{24,8},{28,12},{32,16},{36,20},{40,24},{44,28},{48,3... | collective-permute-start | bytes 3080 | tf_op jit(solution)/shard_map/ppermute | solution.py:19
  146.5 5.5 %collective-permute-start.19 = (f32[256]{0:T(256)S(1)}, f32[256]{0:T(256)S(1)}, u32[]{:S(2)}, u32[]{:S(2)}) collective-permute-start(f32[256]{0:T(256)S(1)} %add.181), channel_id=1, source_target_pairs={{32,0},{36,4},{40,8},{44,12},{48,16},{52,20},{56,24},{60,28},{64,3... | collective-permute-start | bytes 3080 | tf_op jit(solution)/shard_map/ppermute | solution.py:19
  152.3 7.0 %collective-permute-start.20 = (f32[256]{0:T(256)S(1)}, f32[256]{0:T(256)S(1)}, u32[]{:S(2)}, u32[]{:S(2)}) collective-permute-start(f32[256]{0:T(256)S(1)} %add.182), channel_id=1, source_target_pairs={{64,0},{68,4},{72,8},{76,12},{80,16},{84,20},{88,24},{92,28},{96,3... | collective-permute-start | bytes 3080 | tf_op jit(solution)/shard_map/ppermute | solution.py:19
  (15 other events, 50.6 us)

commit v4 on v3

--- a/solution.py
+++ b/solution.py
@@ -4,11 +4,16 @@
 from jax.sharding import PartitionSpec as P
 
 precise = lax.Precision.HIGHEST
+product = lax.Precision.HIGH
 FLAT = ("tm", "space")
 
 
 def dot(a, b):
     return jnp.dot(a, b, precision=precise)
+
+
+def mat(a, b):
+    return jnp.dot(a, b, precision=product)
 
 
 def shift_down(value, axis, steps, count):
@@ -56,7 +61,7 @@
     vec1 = shift_down(vecs, axis, 1, count)
     vec2 = shift_down(vecs, axis, 2, count)
     carry = vec1 + dot(mat1, vec2)
-    gain = dot(mat1, mat2)
+    gain = mat(mat1, mat2)
     stride = 2
     while stride < count:
         more = stride * 2 < count
@@ -65,7 +70,7 @@
             got_gain = shift_down(gain, axis, stride, count)
         carry = carry + dot(gain, got)
         if more:
-            gain = dot(gain, got_gain)
+            gain = mat(gain, got_gain)
         stride *= 2
     return carry
 
@@ -96,10 +101,10 @@
 
     phis = gates[:, 0, :, None] * transition[None]
     for i in range(1, hours):
-        phis = gates[:, i, :, None] * jnp.einsum("ab,sbc->sac", transition, phis, precision=precise)
+        phis = gates[:, i, :, None] * jnp.einsum("ab,sbc->sac", transition, phis, precision=product)
     block_phi = phis[0]
     for s in range(1, bands):
-        block_phi = dot(phis[s], block_phi)
+        block_phi = mat(phis[s], block_phi)
 
     above = halo(fields, bands)
     above, block_phi = lax.optimization_barrier((above, block_phi))

time: 164 us -> 160 us (0.976)
  matrix products: 50.4 us -> 46.4 us
    dot_general x55 -> x48, matrix products: 25.3 us -> 19.4 us  [dot(): return jnp.dot(a, b, precision=precise)]
    dot_general x7 -> x14, matrix products: 7.15 us -> 9 us  [the longest x7 4.67 us: mat(): return jnp.dot(a, b, precision=product)]
  transfers between devices with their start and end apart: 21 -> 21, of which waited for: 9 -> 9; matrix products, arithmetic and copies ran while one was open for 26% -> 25% of each run, Pallas kernels for 0% -> 0%
where the time goes in v4:
time: 160 us
  starting transfers between devices  52.8 us (33%)
  matrix products  46.4 us (29%)
  waiting for transfers between devices  31.4 us (20%)
  local copies, waits for them, and re-layouts  22.1 us (14%)
  other arithmetic  4.96 us (3%)
  between operations  2.08 us (1%)
    ppermute x12, starting transfers between devices, shift_down(): lax.ppermute(value, axis, [(i, i + steps) for i in range(count - steps)])  36.7 us
    ppermute x6, waiting for transfers between devices, shift_up(): lax.ppermute(value, axis, [(i + steps, i) for i in range(count - steps)])  24.1 us
    dot_general x48, matrix products, dot(): return jnp.dot(a, b, precision=precise)  19.4 us
    unnamed x136, local copies, waits for them, and re-layouts  16.1 us
    ppermute x6, starting transfers between devices, shift_up(): lax.ppermute(value, axis, [(i + steps, i) for i in range(count - steps)])  11.2 us
    conv_general_dilated x1, matrix products, conv_stride(): lax.conv_general_dilated(images, kernel, (2, 2), ((0, 0), (1, 1)), dimens...  9.38 us
    ppermute x12, waiting for transfers between devices, shift_down(): lax.ppermute(value, axis, [(i, i + steps) for i in range(count - steps)])  7.33 us
    dot_general x1, matrix products, encode(): jnp.einsum('shwc,hwcm->sm', encoded, obs_gain, preferred_element_type=jnp...  5.37 us
  transfers between devices with their start and end apart: 21, of which 9 were waited for; matrix products, arithmetic and copies ran while one was open for 25% of the time, Pallas kernels for 0%

profile of v4, /device:TPU:14, one launch (start us, length us, event | category | flops | bytes accessed | tf_op | source)
XLA Modules:
  0.0 159.7 jit_solution(14281255086388425817)
XLA Ops:
  0.7 1.6 slice.168
  2.3 0.8 copy.122
  3.1 4.6 %collective-permute-start = (bf16[32,8,3,256]{3,1,2,0:T(8,128)(2,1)}, bf16[32,8,3,256]{3,1,2,0:T(8,128)(2,1)}, u32[]{:S(2)}, u32[]{:S(2)}) collective-permute-start(bf16[32,8,3,256]{3,1,2,0:T(8,128)(2,1)} %copy.122), channel_id=1, source_target_pairs={{0,1},{1,2},{2,3},{4,5},{5,6},{6,7},{8,9},{9,10},{10,11},{12,13},{... | collective-permute-start | bytes 1179656 | tf_op jit(solution)/shard_map/ppermute | solution.py:20
  7.7 0.7 convert_dynamic-update-slice_fusion
  10.0 0.6 fusion.21
  10.6 0.6 fusion.20
  12.5 0.6 fusion.17
  14.0 1.1 fusion.75
  15.2 0.8 bitcast_dynamic-update-slice_fusion.4
  15.9 1.3 constant_dynamic-update-slice_fusion.16
  17.9 1.0 convolution_bitcast_fusion
  21.0 1.1 fusion.149
  22.1 0.7 fusion.79
  22.8 5.1 %copy.88 = bf16[32,8,8,256]{0,1,3,2:T(8,128)(2,1)} copy(bf16[32,8,8,256]{3,2,1,0:T(8,128)(2,1)} %param.7) | data formatting | bytes 2097152 | tf_op args[0]
  28.5 1.8 %bitcast_dynamic-update-slice_fusion = (f32[256,2048]{1,0:T(8,128)}, f32[2048,256]{1,0:T(8,128)}) fusion(f32[4,256,256]{1,2,0:T(8,128)S(1)} %convolution_bitcast_fusion, f32[2048,256]{1,0:T(8,128)} %fusion.79, f32[2,256,256]{1,2,0:T(8,128)} %copy-done.2), kind=kLoop, calls=%fused_computation.84 | loop fusion | bytes 1048576
  30.3 2.9 %copy.87 = bf16[32,8,3,256]{0,1,3,2:T(8,128)(2,1)} copy(bf16[32,8,3,256]{3,1,2,0:T(8,128)(2,1)} %collective-permute-done) | data formatting | bytes 786432 | tf_op jit(solution)/shard_map/optimization_barrier | solution.py:110
  33.2 9.4 %fusion.4 = f32[32,2,64,128]{3,0,2,1:T(8,128)} fusion(bf16[128,64,3,3]{0,1,3,2:T(8,128)(2,1)S(1)} %copy-done, pred[5]{0:T(512)(128)(4,1)} %compare_and_fusion, bf16[64,8,3,3]{0,1,3,2:T(8,128)(2,1)} %param.8, bf16[32,8,8,256]{0,1,3,2:T(8,128)(2,1)} %copy.88, bf16[32,8,3,256]{0,1,3,2:T(8,128)(2,1)} %copy.87), kind=kOutput, calls=%fused_computation.5 | convolution fusion | flops 799834112 | bytes 3695621 | tf_op jit(solution)/shard_map/conv_general_dilated | solution.py:28
  42.6 5.4 %convolution_bitcast_fusion.3 = f32[32,256]{1,0:T(8,128)S(1)} fusion(bf16[2,64,128,256]{3,2,1,0:T(8,128)(2,1)} %param.10, f32[32,2,64,128]{3,0,2,1:T(8,128)} %fusion.4), kind=kOutput, calls=%fused_computation.33 | convolution fusion | flops 271056896 | bytes 10518528 | tf_op jit(solution)/shard_map/shwc,hwcm->sm/dot_general | solution.py:50
  48.0 0.8 collective-permute-start.2
  48.9 1.3 collective-permute-start.3
  50.1 2.8 %collective-permute-start.1 = (f32[32,256]{1,0:T(8,128)S(1)}, f32[32,256]{1,0:T(8,128)S(1)}, u32[]{:S(2)}, u32[]{:S(2)}) collective-permute-start(f32[32,256]{1,0:T(8,128)S(1)} %convolution_bitcast_fusion.3), channel_id=1, source_target_pairs={{0,2},{1,3},{2,0},{3,1},{4,6},{5,7},{6,4},{7,5},{8,10},{9,11},{10,... | collective-permute-start | bytes 98312 | tf_op jit(solution)/shard_map/ppermute | solution.py:54
  53.0 0.9 fusion.84
  53.9 1.9 %collective-permute-start.5 = (f32[256,256]{1,0:T(8,128)S(1)}, f32[256,256]{1,0:T(8,128)S(1)}, u32[]{:S(2)}, u32[]{:S(2)}) collective-permute-start(f32[256,256]{1,0:T(8,128)S(1)} %copy-done.14), channel_id=1, source_target_pairs={{0,4},{4,8},{8,12},{12,16},{16,20},{20,24},{24,28},{28,32},{32,36}... | collective-permute-start | bytes 786440 | tf_op jit(solution)/shard_map/ppermute | solution.py:20
  55.8 3.4 %collective-permute-start.7 = (f32[256,256]{1,0:T(8,128)S(1)}, f32[256,256]{1,0:T(8,128)S(1)}, u32[]{:S(2)}, u32[]{:S(2)}) collective-permute-start(f32[256,256]{1,0:T(8,128)S(1)} %copy-done.14), channel_id=1, source_target_pairs={{0,8},{4,12},{8,16},{12,20},{16,24},{20,28},{24,32},{28,36},{32,40... | collective-permute-start | bytes 786440 | tf_op jit(solution)/shard_map/ppermute | solution.py:20
  63.0 3.4 %collective-permute-start.6 = (f32[256]{0:T(256)S(1)}, f32[256]{0:T(256)S(1)}, u32[]{:S(2)}, u32[]{:S(2)}) collective-permute-start(f32[256]{0:T(256)S(1)} %add.157), channel_id=1, source_target_pairs={{0,8},{4,12},{8,16},{12,20},{16,24},{20,28},{24,32},{28,36},{32,40... | collective-permute-start | bytes 3080 | tf_op jit(solution)/shard_map/ppermute | solution.py:20
  66.4 0.9 fusion.82
  67.3 2.9 %collective-permute-start.4 = (f32[256]{0:T(256)S(1)}, f32[256]{0:T(256)S(1)}, u32[]{:S(2)}, u32[]{:S(2)}) collective-permute-start(f32[256]{0:T(256)S(1)} %add.157), channel_id=1, source_target_pairs={{0,4},{4,8},{8,12},{12,16},{16,20},{20,24},{24,28},{28,32},{32,36}... | collective-permute-start | bytes 3080 | tf_op jit(solution)/shard_map/ppermute | solution.py:20
  70.5 1.7 %collective-permute-done.4 = f32[256]{0:T(256)S(1)} collective-permute-done((f32[256]{0:T(256)S(1)}, f32[256]{0:T(256)S(1)}, u32[]{:S(2)}, u32[]{:S(2)}) %collective-permute-start.4) | collective-permute-done | bytes 1056 | tf_op jit(solution)/shard_map/ppermute | solution.py:20
  72.2 5.6 %collective-permute-start.8 = (f32[256]{0:T(256)S(1)}, f32[256]{0:T(256)S(1)}, u32[]{:S(2)}, u32[]{:S(2)}) collective-permute-start(f32[256]{0:T(256)S(1)} %add.158), channel_id=1, source_target_pairs={{0,8},{4,12},{8,16},{12,20},{16,24},{20,28},{24,32},{28,36},{32,40... | collective-permute-start | bytes 3080 | tf_op jit(solution)/shard_map/ppermute | solution.py:20
  78.2 1.9 %collective-permute-start.9 = (f32[256,256]{1,0:T(8,128)S(1)}, f32[256,256]{1,0:T(8,128)S(1)}, u32[]{:S(2)}, u32[]{:S(2)}) collective-permute-start(f32[256,256]{1,0:T(8,128)S(1)} %fusion.133), channel_id=1, source_target_pairs={{0,8},{4,12},{8,16},{12,20},{16,24},{20,28},{24,32},{28,36},{32,40... | collective-permute-start | bytes 786440 | tf_op jit(solution)/shard_map/ppermute | solution.py:20
  80.1 0.9 fusion.80
  81.3 3.2 %collective-permute-start.10 = (f32[256]{0:T(256)S(1)}, f32[256]{0:T(256)S(1)}, u32[]{:S(2)}, u32[]{:S(2)}) collective-permute-start(f32[256]{0:T(256)S(1)} %add.159), channel_id=1, source_target_pairs={{0,16},{4,20},{8,24},{12,28},{16,32},{20,36},{24,40},{28,44},{32,4... | collective-permute-start | bytes 3080 | tf_op jit(solution)/shard_map/ppermute | solution.py:20
  84.4 2.0 %collective-permute-done.9 = f32[256,256]{1,0:T(8,128)S(1)} collective-permute-done((f32[256,256]{1,0:T(8,128)S(1)}, f32[256,256]{1,0:T(8,128)S(1)}, u32[]{:S(2)}, u32[]{:S(2)}) %collective-permute-start.9) | collective-permute-done | bytes 262176 | tf_op jit(solution)/shard_map/ppermute | solution.py:20
  86.7 2.9 %collective-permute-start.11 = (f32[256,256]{1,0:T(8,128)S(1)}, f32[256,256]{1,0:T(8,128)S(1)}, u32[]{:S(2)}, u32[]{:S(2)}) collective-permute-start(f32[256,256]{1,0:T(8,128)S(1)} %fusion.135), channel_id=1, source_target_pairs={{0,16},{4,20},{8,24},{12,28},{16,32},{20,36},{24,40},{28,44},{32,4... | collective-permute-start | bytes 786440 | tf_op jit(solution)/shard_map/ppermute | solution.py:20
  89.7 0.7 bitcast_dynamic-update-slice_fusion.1
  90.7 0.7 add.160
  91.4 2.1 %collective-permute-start.12 = (f32[256]{0:T(256)}, f32[256]{0:T(256)}, u32[]{:S(2)}, u32[]{:S(2)}) collective-permute-start(f32[256]{0:T(256)} %add.160), channel_id=1, source_target_pairs={{0,32},{4,36},{8,40},{12,44},{16,48},{20,52},{24,56},{28,60},{32,6... | collective-permute-start | bytes 3080 | tf_op jit(solution)/shard_map/ppermute | solution.py:20
  93.5 3.0 %collective-permute-done.11 = f32[256,256]{1,0:T(8,128)S(1)} collective-permute-done((f32[256,256]{1,0:T(8,128)S(1)}, f32[256,256]{1,0:T(8,128)S(1)}, u32[]{:S(2)}, u32[]{:S(2)}) %collective-permute-start.11) | collective-permute-done | bytes 262176 | tf_op jit(solution)/shard_map/ppermute | solution.py:20
  96.5 1.0 fusion.137
  97.5 3.4 %collective-permute-start.13 = (f32[256,256]{1,0:T(8,128)}, f32[256,256]{1,0:T(8,128)}, u32[]{:S(2)}, u32[]{:S(2)}) collective-permute-start(f32[256,256]{1,0:T(8,128)} %fusion.137), channel_id=1, source_target_pairs={{0,32},{4,36},{8,40},{12,44},{16,48},{20,52},{24,56},{28,60},{32,6... | collective-permute-start | bytes 786440 | tf_op jit(solution)/shard_map/ppermute | solution.py:20
  100.9 1.1 convolution_bitcast_fusion.2
  102.1 1.2 fusion.138
  103.4 0.8 add.161
  104.1 1.3 collective-permute-start.14
  105.4 0.6 collective-permute-done.13
  106.1 1.3 fusion.139
  107.9 0.7 add.163
  108.9 0.7 add.164
  113.1 1.3 fusion.15
  115.9 2.0 %collective-permute-start.16 = (f32[256]{0:T(256)S(1)}, f32[256]{0:T(256)S(1)}, u32[]{:S(2)}, u32[]{:S(2)}) collective-permute-start(f32[256]{0:T(256)S(1)} %select_add_fusion), channel_id=1, source_target_pairs={{8,0},{12,4},{16,8},{20,12},{24,16},{28,20},{32,24},{36,28},{40,32... | collective-permute-start | bytes 3080 | tf_op jit(solution)/shard_map/ppermute | solution.py:24
  118.0 0.8 fusion.78
  118.7 1.9 %collective-permute-start.15 = (f32[256]{0:T(256)S(1)}, f32[256]{0:T(256)S(1)}, u32[]{:S(2)}, u32[]{:S(2)}) collective-permute-start(f32[256]{0:T(256)S(1)} %select_add_fusion), channel_id=1, source_target_pairs={{4,0},{8,4},{12,8},{16,12},{20,16},{24,20},{28,24},{32,28},{36,32}... | collective-permute-start | bytes 3080 | tf_op jit(solution)/shard_map/ppermute | solution.py:24
  120.6 5.5 %collective-permute-done.16 = f32[256]{0:T(256)S(1)} collective-permute-done((f32[256]{0:T(256)S(1)}, f32[256]{0:T(256)S(1)}, u32[]{:S(2)}, u32[]{:S(2)}) %collective-permute-start.16) | collective-permute-done | bytes 1056 | tf_op jit(solution)/shard_map/ppermute | solution.py:24
  126.4 1.9 %collective-permute-start.17 = (f32[256]{0:T(256)S(1)}, f32[256]{0:T(256)S(1)}, u32[]{:S(2)}, u32[]{:S(2)}) collective-permute-start(f32[256]{0:T(256)S(1)} %add.179), channel_id=1, source_target_pairs={{8,0},{12,4},{16,8},{20,12},{24,16},{28,20},{32,24},{36,28},{40,32... | collective-permute-start | bytes 3080 | tf_op jit(solution)/shard_map/ppermute | solution.py:24
  128.4 0.8 constant_dynamic-update-slice_fusion.17
  129.2 4.9 %collective-permute-done.17 = f32[256]{0:T(256)S(1)} collective-permute-done((f32[256]{0:T(256)S(1)}, f32[256]{0:T(256)S(1)}, u32[]{:S(2)}, u32[]{:S(2)}) %collective-permute-start.17) | collective-permute-done | bytes 1056 | tf_op jit(solution)/shard_map/ppermute | solution.py:24
  134.3 2.0 %collective-permute-start.18 = (f32[256]{0:T(256)S(1)}, f32[256]{0:T(256)S(1)}, u32[]{:S(2)}, u32[]{:S(2)}) collective-permute-start(f32[256]{0:T(256)S(1)} %add.180), channel_id=1, source_target_pairs={{16,0},{20,4},{24,8},{28,12},{32,16},{36,20},{40,24},{44,28},{48,3... | collective-permute-start | bytes 3080 | tf_op jit(solution)/shard_map/ppermute | solution.py:24
  136.3 0.7 bitcast_dynamic-update-slice_fusion.3
  137.0 5.2 %collective-permute-done.18 = f32[256]{0:T(256)S(1)} collective-permute-done((f32[256]{0:T(256)S(1)}, f32[256]{0:T(256)S(1)}, u32[]{:S(2)}, u32[]{:S(2)}) %collective-permute-start.18) | collective-permute-done | bytes 1056 | tf_op jit(solution)/shard_map/ppermute | solution.py:24
  142.5 2.0 %collective-permute-start.19 = (f32[256]{0:T(256)S(1)}, f32[256]{0:T(256)S(1)}, u32[]{:S(2)}, u32[]{:S(2)}) collective-permute-start(f32[256]{0:T(256)S(1)} %add.181), channel_id=1, source_target_pairs={{32,0},{36,4},{40,8},{44,12},{48,16},{52,20},{56,24},{60,28},{64,3... | collective-permute-start | bytes 3080 | tf_op jit(solution)/shard_map/ppermute | solution.py:24
  144.5 3.5 %collective-permute-done.19 = f32[256]{0:T(256)S(1)} collective-permute-done((f32[256]{0:T(256)S(1)}, f32[256]{0:T(256)S(1)}, u32[]{:S(2)}, u32[]{:S(2)}) %collective-permute-start.19) | collective-permute-done | bytes 1056 | tf_op jit(solution)/shard_map/ppermute | solution.py:24
  148.3 1.3 collective-permute-start.20
  150.3 5.0 %collective-permute-done.20 = f32[256]{0:T(256)S(1)} collective-permute-done((f32[256]{0:T(256)S(1)}, f32[256]{0:T(256)S(1)}, u32[]{:S(2)}, u32[]{:S(2)}) %collective-permute-start.20) | collective-permute-done | bytes 1056 | tf_op jit(solution)/shard_map/ppermute | solution.py:24
  156.4 2.7 %fusion.12 = f32[1,8,256]{2,0,1:T(1,128)S(1)} fusion(f32[32,8,8,256]{3,2,1,0:T(8,128)} %bitcast.147, s32[]{:T(128)S(6)} %select_n.26, f32[1,256]{1,0:T(1,128)S(1)} %bitcast.448, f32[1,256]{1,0:T(1,128)S(1)} %bitcast.460, f32[1,256]{1,0:T(1,128)S(1)} %bitcast.445, f32[1,256]{1,0:T(1,128)S(1)} %bitcast.441), kind=kOutput, calls=%fused_computation.9 | convolution fusion | flops 6292224 | bytes 2109444 | tf_op jit(solution)/shard_map/dot_general | solution.py:12
  (222 shorter events, 20.8 us)
Async XLA Ops:
  0.6 32.6 %copy-start = (bf16[128,64,3,3]{0,1,3,2:T(8,128)(2,1)S(1)}, bf16[128,64,3,3]{0,1,3,2:T(8,128)(2,1)}, u32[]{:S(2)}) copy-start(bf16[128,64,3,3]{0,1,3,2:T(8,128)(2,1)} %param.9) | copy-start | bytes 442372
  0.7 7.9 %copy-start.54 = (f32[32,256]{1,0:T(8,128)S(1)}, f32[32,256]{1,0:T(8,128)}, u32[]{:S(2)}) copy-start(f32[32,256]{1,0:T(8,128)} %param.13) | copy-start | bytes 98308
  3.1 27.2 %collective-permute-start = (bf16[32,8,3,256]{3,1,2,0:T(8,128)(2,1)}, bf16[32,8,3,256]{3,1,2,0:T(8,128)(2,1)}, u32[]{:S(2)}, u32[]{:S(2)}) collective-permute-start(bf16[32,8,3,256]{3,1,2,0:T(8,128)(2,1)} %copy.122), channel_id=1, source_target_pairs={{0,1},{1,2},{2,3},{4,5},{5,6},{6,7},{8,9},{9,10},{10,11},{12,13},{... | collective-permute-start | bytes 1179656 | tf_op jit(solution)/shard_map/ppermute | solution.py:20
  42.6 11.3 %copy-start.14 = (f32[256,256]{1,0:T(8,128)S(1)}, f32[256,256]{1,0:T(8,128)}, u32[]{:S(2)}) copy-start(f32[256,256]{1,0:T(8,128)} %fusion.75) | copy-start | bytes 786436
  42.6 16.7 %copy-start.34 = (f32[4,1,256]{2,1,0:T(1,128)S(1)}, f32[4,1,256]{2,1,0:T(1,128)}, u32[]{:S(2)}) copy-start(f32[4,1,256]{2,1,0:T(1,128)} %copy-done.33) | copy-start | bytes 12292
  42.6 17.1 %copy-start.31 = (f32[4,1,256]{2,1,0:T(1,128)S(1)}, f32[4,1,256]{2,1,0:T(1,128)}, u32[]{:S(2)}) copy-start(f32[4,1,256]{2,1,0:T(1,128)} %copy-done.30) | copy-start | bytes 12292
  42.6 17.4 %copy-start.28 = (f32[4,1,256]{2,1,0:T(1,128)S(1)}, f32[4,1,256]{2,1,0:T(1,128)}, u32[]{:S(2)}) copy-start(f32[4,1,256]{2,1,0:T(1,128)} %copy-done.27) | copy-start | bytes 12292
  48.0 12.3 %copy-start.25 = (f32[4,1,256]{2,1,0:T(1,128)S(1)}, f32[4,1,256]{2,1,0:T(1,128)}, u32[]{:S(2)}) copy-start(f32[4,1,256]{2,1,0:T(1,128)} %copy-done.24) | copy-start | bytes 12292
  48.0 12.7 %copy-start.22 = (f32[4,1,256]{2,1,0:T(1,128)S(1)}, f32[4,1,256]{2,1,0:T(1,128)}, u32[]{:S(2)}) copy-start(f32[4,1,256]{2,1,0:T(1,128)} %copy-done.21) | copy-start | bytes 12292
  48.0 13.0 %copy-start.19 = (f32[4,1,256]{2,1,0:T(1,128)S(1)}, f32[4,1,256]{2,1,0:T(1,128)}, u32[]{:S(2)}) copy-start(f32[4,1,256]{2,1,0:T(1,128)} %copy-done.18) | copy-start | bytes 12292
  48.0 13.3 %copy-start.16 = (f32[4,1,256]{2,1,0:T(1,128)S(1)}, f32[4,1,256]{2,1,0:T(1,128)}, u32[]{:S(2)}) copy-start(f32[4,1,256]{2,1,0:T(1,128)} %copy-done.15) | copy-start | bytes 12292
  48.0 11.1 %collective-permute-start.2 = (f32[32,256]{1,0:T(8,128)S(1)}, f32[32,256]{1,0:T(8,128)S(1)}, u32[]{:S(2)}, u32[]{:S(2)}) collective-permute-start(f32[32,256]{1,0:T(8,128)S(1)} %convolution_bitcast_fusion.3), channel_id=1, source_target_pairs={{0,3},{1,0},{2,1},{3,2},{4,7},{5,4},{6,5},{7,6},{8,11},{9,8},{10,9... | collective-permute-start | bytes 98312 | tf_op jit(solution)/shard_map/ppermute | solution.py:54
  48.9 10.3 %collective-permute-start.3 = (f32[32,256]{1,0:T(8,128)S(1)}, f32[32,256]{1,0:T(8,128)S(1)}, u32[]{:S(2)}, u32[]{:S(2)}) collective-permute-start(f32[32,256]{1,0:T(8,128)S(1)} %convolution_bitcast_fusion.3), channel_id=1, source_target_pairs={{0,1},{1,2},{2,3},{3,0},{4,5},{5,6},{6,7},{7,4},{8,9},{9,10},{10,1... | collective-permute-start | bytes 98312 | tf_op jit(solution)/shard_map/ppermute | solution.py:54
  50.1 9.1 %collective-permute-start.1 = (f32[32,256]{1,0:T(8,128)S(1)}, f32[32,256]{1,0:T(8,128)S(1)}, u32[]{:S(2)}, u32[]{:S(2)}) collective-permute-start(f32[32,256]{1,0:T(8,128)S(1)} %convolution_bitcast_fusion.3), channel_id=1, source_target_pairs={{0,2},{1,3},{2,0},{3,1},{4,6},{5,7},{6,4},{7,5},{8,10},{9,11},{10,... | collective-permute-start | bytes 98312 | tf_op jit(solution)/shard_map/ppermute | solution.py:54
  53.9 16.4 %collective-permute-start.5 = (f32[256,256]{1,0:T(8,128)S(1)}, f32[256,256]{1,0:T(8,128)S(1)}, u32[]{:S(2)}, u32[]{:S(2)}) collective-permute-start(f32[256,256]{1,0:T(8,128)S(1)} %copy-done.14), channel_id=1, source_target_pairs={{0,4},{4,8},{8,12},{12,16},{16,20},{20,24},{24,28},{28,32},{32,36}... | collective-permute-start | bytes 786440 | tf_op jit(solution)/shard_map/ppermute | solution.py:20
  55.8 22.0 %collective-permute-start.7 = (f32[256,256]{1,0:T(8,128)S(1)}, f32[256,256]{1,0:T(8,128)S(1)}, u32[]{:S(2)}, u32[]{:S(2)}) collective-permute-start(f32[256,256]{1,0:T(8,128)S(1)} %copy-done.14), channel_id=1, source_target_pairs={{0,8},{4,12},{8,16},{12,20},{16,24},{20,28},{24,32},{28,36},{32,40... | collective-permute-start | bytes 786440 | tf_op jit(solution)/shard_map/ppermute | solution.py:20
  59.3 18.8 %copy-start.36 = (f32[4,1,256]{2,1,0:T(1,128)}, f32[4,1,256]{2,1,0:T(1,128)S(1)}, u32[]{:S(2)}) copy-start(f32[4,1,256]{2,1,0:T(1,128)S(1)} %get-tuple-element.16) | copy-start | bytes 12292
  59.3 18.8 %copy-start.38 = (f32[4,1,256]{2,1,0:T(1,128)}, f32[4,1,256]{2,1,0:T(1,128)S(1)}, u32[]{:S(2)}) copy-start(f32[4,1,256]{2,1,0:T(1,128)S(1)} %get-tuple-element.17) | copy-start | bytes 12292
  59.3 18.8 %copy-start.40 = (f32[4,1,256]{2,1,0:T(1,128)}, f32[4,1,256]{2,1,0:T(1,128)S(1)}, u32[]{:S(2)}) copy-start(f32[4,1,256]{2,1,0:T(1,128)S(1)} %get-tuple-element.18) | copy-start | bytes 12292
  59.3 18.8 %copy-start.42 = (f32[4,1,256]{2,1,0:T(1,128)}, f32[4,1,256]{2,1,0:T(1,128)S(1)}, u32[]{:S(2)}) copy-start(f32[4,1,256]{2,1,0:T(1,128)S(1)} %get-tuple-element.19) | copy-start | bytes 12292
  59.3 18.8 %copy-start.44 = (f32[4,1,256]{2,1,0:T(1,128)}, f32[4,1,256]{2,1,0:T(1,128)S(1)}, u32[]{:S(2)}) copy-start(f32[4,1,256]{2,1,0:T(1,128)S(1)} %get-tuple-element.20) | copy-start | bytes 12292
  59.3 18.8 %copy-start.46 = (f32[4,1,256]{2,1,0:T(1,128)}, f32[4,1,256]{2,1,0:T(1,128)S(1)}, u32[]{:S(2)}) copy-start(f32[4,1,256]{2,1,0:T(1,128)S(1)} %get-tuple-element.21) | copy-start | bytes 12292
  59.3 18.8 %copy-start.48 = (f32[4,1,256]{2,1,0:T(1,128)}, f32[4,1,256]{2,1,0:T(1,128)S(1)}, u32[]{:S(2)}) copy-start(f32[4,1,256]{2,1,0:T(1,128)S(1)} %get-tuple-element.22) | copy-start | bytes 12292
  59.3 18.8 %copy-start.50 = (f32[4,1,256]{2,1,0:T(1,128)}, f32[4,1,256]{2,1,0:T(1,128)S(1)}, u32[]{:S(2)}) copy-start(f32[4,1,256]{2,1,0:T(1,128)S(1)} %get-tuple-element.23) | copy-start | bytes 12292
  62.5 17.6 %copy-start.55 = (f32[1,256]{1,0:T(1,128)}, f32[1,256]{1,0:T(1,128)S(1)}, u32[]{:S(2)}) copy-start(f32[1,256]{1,0:T(1,128)S(1)} %get-tuple-element.34) | copy-start | bytes 3076
  62.5 17.6 %copy-start.57 = (f32[1,256]{1,0:T(1,128)}, f32[1,256]{1,0:T(1,128)S(1)}, u32[]{:S(2)}) copy-start(f32[1,256]{1,0:T(1,128)S(1)} %get-tuple-element.35) | copy-start | bytes 3076
  62.8 26.9 %copy-start.3 = (f32[2,256,256]{1,2,0:T(8,128)S(1)}, f32[2,256,256]{1,2,0:T(8,128)}, u32[]{:S(2)}) copy-start(f32[2,256,256]{1,2,0:T(8,128)} %copy-done.2) | copy-start | bytes 1572868
  63.0 7.2 %collective-permute-start.6 = (f32[256]{0:T(256)S(1)}, f32[256]{0:T(256)S(1)}, u32[]{:S(2)}, u32[]{:S(2)}) collective-permute-start(f32[256]{0:T(256)S(1)} %add.157), channel_id=1, source_target_pairs={{0,8},{4,12},{8,16},{12,20},{16,24},{20,28},{24,32},{28,36},{32,40... | collective-permute-start | bytes 3080 | tf_op jit(solution)/shard_map/ppermute | solution.py:20
  67.3 4.9 %collective-permute-start.4 = (f32[256]{0:T(256)S(1)}, f32[256]{0:T(256)S(1)}, u32[]{:S(2)}, u32[]{:S(2)}) collective-permute-start(f32[256]{0:T(256)S(1)} %add.157), channel_id=1, source_target_pairs={{0,4},{4,8},{8,12},{12,16},{16,20},{20,24},{24,28},{28,32},{32,36}... | collective-permute-start | bytes 3080 | tf_op jit(solution)/shard_map/ppermute | solution.py:20
  72.2 28.7 %copy-start.10 = (f32[256,256]{1,0:T(8,128)S(1)}, f32[256,256]{1,0:T(8,128)}, u32[]{:S(2)}) copy-start(f32[256,256]{1,0:T(8,128)} %param.12) | copy-start | bytes 786436
  72.2 8.8 %collective-permute-start.8 = (f32[256]{0:T(256)S(1)}, f32[256]{0:T(256)S(1)}, u32[]{:S(2)}, u32[]{:S(2)}) collective-permute-start(f32[256]{0:T(256)S(1)} %add.158), channel_id=1, source_target_pairs={{0,8},{4,12},{8,16},{12,20},{16,24},{20,28},{24,32},{28,36},{32,40... | collective-permute-start | bytes 3080 | tf_op jit(solution)/shard_map/ppermute | solution.py:20
  78.2 8.3 %collective-permute-start.9 = (f32[256,256]{1,0:T(8,128)S(1)}, f32[256,256]{1,0:T(8,128)S(1)}, u32[]{:S(2)}, u32[]{:S(2)}) collective-permute-start(f32[256,256]{1,0:T(8,128)S(1)} %fusion.133), channel_id=1, source_target_pairs={{0,8},{4,12},{8,16},{12,20},{16,24},{20,28},{24,32},{28,36},{32,40... | collective-permute-start | bytes 786440 | tf_op jit(solution)/shard_map/ppermute | solution.py:20
  81.3 9.2 %collective-permute-start.10 = (f32[256]{0:T(256)S(1)}, f32[256]{0:T(256)S(1)}, u32[]{:S(2)}, u32[]{:S(2)}) collective-permute-start(f32[256]{0:T(256)S(1)} %add.159), channel_id=1, source_target_pairs={{0,16},{4,20},{8,24},{12,28},{16,32},{20,36},{24,40},{28,44},{32,4... | collective-permute-start | bytes 3080 | tf_op jit(solution)/shard_map/ppermute | solution.py:20
  86.7 9.8 %collective-permute-start.11 = (f32[256,256]{1,0:T(8,128)S(1)}, f32[256,256]{1,0:T(8,128)S(1)}, u32[]{:S(2)}, u32[]{:S(2)}) collective-permute-start(f32[256,256]{1,0:T(8,128)S(1)} %fusion.135), channel_id=1, source_target_pairs={{0,16},{4,20},{8,24},{12,28},{16,32},{20,36},{24,40},{28,44},{32,4... | collective-permute-start | bytes 786440 | tf_op jit(solution)/shard_map/ppermute | solution.py:20
  91.4 10.8 %collective-permute-start.12 = (f32[256]{0:T(256)}, f32[256]{0:T(256)}, u32[]{:S(2)}, u32[]{:S(2)}) collective-permute-start(f32[256]{0:T(256)} %add.160), channel_id=1, source_target_pairs={{0,32},{4,36},{8,40},{12,44},{16,48},{20,52},{24,56},{28,60},{32,6... | collective-permute-start | bytes 3080 | tf_op jit(solution)/shard_map/ppermute | solution.py:20
  97.5 8.6 %collective-permute-start.13 = (f32[256,256]{1,0:T(8,128)}, f32[256,256]{1,0:T(8,128)}, u32[]{:S(2)}, u32[]{:S(2)}) collective-permute-start(f32[256,256]{1,0:T(8,128)} %fusion.137), channel_id=1, source_target_pairs={{0,32},{4,36},{8,40},{12,44},{16,48},{20,52},{24,56},{28,60},{32,6... | collective-permute-start | bytes 786440 | tf_op jit(solution)/shard_map/ppermute | solution.py:20
  102.0 7.8 %copy-start.56 = (f32[1,256]{1,0:T(1,128)S(1)}, f32[1,256]{1,0:T(1,128)}, u32[]{:S(2)}) copy-start(f32[1,256]{1,0:T(1,128)} %copy-done.55) | copy-start | bytes 3076
  102.0 7.9 %copy-start.51 = (f32[4,1,256]{2,1,0:T(1,128)S(1)}, f32[4,1,256]{2,1,0:T(1,128)}, u32[]{:S(2)}) copy-start(f32[4,1,256]{2,1,0:T(1,128)} %copy-done.50) | copy-start | bytes 12292
  102.0 7.9 %copy-start.53 = (f32[4,1,256]{2,1,0:T(1,128)S(1)}, f32[4,1,256]{2,1,0:T(1,128)}, u32[]{:S(2)}) copy-start(f32[4,1,256]{2,1,0:T(1,128)} %copy-done.52) | copy-start | bytes 12292
  102.0 8.2 %copy-start.35 = (f32[4,1,256]{2,1,0:T(1,128)S(1)}, f32[4,1,256]{2,1,0:T(1,128)}, u32[]{:S(2)}) copy-start(f32[4,1,256]{2,1,0:T(1,128)} %copy-done.33) | copy-start | bytes 12292
  102.0 8.2 %copy-start.49 = (f32[4,1,256]{2,1,0:T(1,128)S(1)}, f32[4,1,256]{2,1,0:T(1,128)}, u32[]{:S(2)}) copy-start(f32[4,1,256]{2,1,0:T(1,128)} %copy-done.48) | copy-start | bytes 12292
  102.0 8.6 %copy-start.32 = (f32[4,1,256]{2,1,0:T(1,128)S(1)}, f32[4,1,256]{2,1,0:T(1,128)}, u32[]{:S(2)}) copy-start(f32[4,1,256]{2,1,0:T(1,128)} %copy-done.30) | copy-start | bytes 12292
  102.0 8.6 %copy-start.47 = (f32[4,1,256]{2,1,0:T(1,128)S(1)}, f32[4,1,256]{2,1,0:T(1,128)}, u32[]{:S(2)}) copy-start(f32[4,1,256]{2,1,0:T(1,128)} %copy-done.46) | copy-start | bytes 12292
  102.0 8.9 %copy-start.29 = (f32[4,1,256]{2,1,0:T(1,128)S(1)}, f32[4,1,256]{2,1,0:T(1,128)}, u32[]{:S(2)}) copy-start(f32[4,1,256]{2,1,0:T(1,128)} %copy-done.27) | copy-start | bytes 12292
  102.0 8.9 %copy-start.45 = (f32[4,1,256]{2,1,0:T(1,128)S(1)}, f32[4,1,256]{2,1,0:T(1,128)}, u32[]{:S(2)}) copy-start(f32[4,1,256]{2,1,0:T(1,128)} %copy-done.44) | copy-start | bytes 12292
  102.0 9.2 %copy-start.26 = (f32[4,1,256]{2,1,0:T(1,128)S(1)}, f32[4,1,256]{2,1,0:T(1,128)}, u32[]{:S(2)}) copy-start(f32[4,1,256]{2,1,0:T(1,128)} %copy-done.24) | copy-start | bytes 12292
  102.0 9.2 %copy-start.43 = (f32[4,1,256]{2,1,0:T(1,128)S(1)}, f32[4,1,256]{2,1,0:T(1,128)}, u32[]{:S(2)}) copy-start(f32[4,1,256]{2,1,0:T(1,128)} %copy-done.42) | copy-start | bytes 12292
  102.1 9.5 %copy-start.23 = (f32[4,1,256]{2,1,0:T(1,128)S(1)}, f32[4,1,256]{2,1,0:T(1,128)}, u32[]{:S(2)}) copy-start(f32[4,1,256]{2,1,0:T(1,128)} %copy-done.21) | copy-start | bytes 12292
  102.1 9.5 %copy-start.41 = (f32[4,1,256]{2,1,0:T(1,128)S(1)}, f32[4,1,256]{2,1,0:T(1,128)}, u32[]{:S(2)}) copy-start(f32[4,1,256]{2,1,0:T(1,128)} %copy-done.40) | copy-start | bytes 12292
  102.1 9.9 %copy-start.20 = (f32[4,1,256]{2,1,0:T(1,128)S(1)}, f32[4,1,256]{2,1,0:T(1,128)}, u32[]{:S(2)}) copy-start(f32[4,1,256]{2,1,0:T(1,128)} %copy-done.18) | copy-start | bytes 12292
  102.1 9.9 %copy-start.39 = (f32[4,1,256]{2,1,0:T(1,128)S(1)}, f32[4,1,256]{2,1,0:T(1,128)}, u32[]{:S(2)}) copy-start(f32[4,1,256]{2,1,0:T(1,128)} %copy-done.38) | copy-start | bytes 12292
  102.1 10.2 %copy-start.17 = (f32[4,1,256]{2,1,0:T(1,128)S(1)}, f32[4,1,256]{2,1,0:T(1,128)}, u32[]{:S(2)}) copy-start(f32[4,1,256]{2,1,0:T(1,128)} %copy-done.15) | copy-start | bytes 12292
  102.1 10.2 %copy-start.37 = (f32[4,1,256]{2,1,0:T(1,128)S(1)}, f32[4,1,256]{2,1,0:T(1,128)}, u32[]{:S(2)}) copy-start(f32[4,1,256]{2,1,0:T(1,128)} %copy-done.36) | copy-start | bytes 12292
  103.4 9.3 %copy-start.13 = (f32[256,256,1]{1,0,2:T(8,128)S(1)}, f32[256,256,1]{1,0,2:T(8,128)}, u32[]{:S(2)}) copy-start(f32[256,256,1]{1,0,2:T(8,128)} %convolution_bitcast_fusion.2) | copy-start | bytes 786436
  104.1 3.2 %collective-permute-start.14 = (f32[256]{0:T(256)S(1)}, f32[256]{0:T(256)S(1)}, u32[]{:S(2)}, u32[]{:S(2)}) collective-permute-start(f32[256]{0:T(256)S(1)} %add.161), channel_id=1, source_target_pairs={{0,64},{4,68},{8,72},{12,76},{16,80},{20,84},{24,88},{28,92},{32,9... | collective-permute-start | bytes 3080 | tf_op jit(solution)/shard_map/ppermute | solution.py:20
  113.1 20.9 %copy-start.8 = (f32[256,256]{1,0:T(8,128)S(1)}, f32[256,256]{1,0:T(8,128)}, u32[]{:S(2)}) copy-start(f32[256,256]{1,0:T(8,128)} %copy-done.7) | copy-start | bytes 786436
  114.4 27.8 %copy-start.6 = (f32[256,256]{1,0:T(8,128)S(1)}, f32[256,256]{1,0:T(8,128)}, u32[]{:S(2)}) copy-start(f32[256,256]{1,0:T(8,128)} %copy-done.5) | copy-start | bytes 786436
  114.4 40.9 %copy-start.12 = (f32[256,256]{1,0:T(8,128)S(1)}, f32[256,256]{1,0:T(8,128)}, u32[]{:S(2)}) copy-start(f32[256,256]{1,0:T(8,128)} %fusion.149) | copy-start | bytes 786436
  115.9 10.2 %collective-permute-start.16 = (f32[256]{0:T(256)S(1)}, f32[256]{0:T(256)S(1)}, u32[]{:S(2)}, u32[]{:S(2)}) collective-permute-start(f32[256]{0:T(256)S(1)} %select_add_fusion), channel_id=1, source_target_pairs={{8,0},{12,4},{16,8},{20,12},{24,16},{28,20},{32,24},{36,28},{40,32... | collective-permute-start | bytes 3080 | tf_op jit(solution)/shard_map/ppermute | solution.py:24
  118.7 7.7 %collective-permute-start.15 = (f32[256]{0:T(256)S(1)}, f32[256]{0:T(256)S(1)}, u32[]{:S(2)}, u32[]{:S(2)}) collective-permute-start(f32[256]{0:T(256)S(1)} %select_add_fusion), channel_id=1, source_target_pairs={{4,0},{8,4},{12,8},{16,12},{20,16},{24,20},{28,24},{32,28},{36,32}... | collective-permute-start | bytes 3080 | tf_op jit(solution)/shard_map/ppermute | solution.py:24
  126.4 7.6 %collective-permute-start.17 = (f32[256]{0:T(256)S(1)}, f32[256]{0:T(256)S(1)}, u32[]{:S(2)}, u32[]{:S(2)}) collective-permute-start(f32[256]{0:T(256)S(1)} %add.179), channel_id=1, source_target_pairs={{8,0},{12,4},{16,8},{20,12},{24,16},{28,20},{32,24},{36,28},{40,32... | collective-permute-start | bytes 3080 | tf_op jit(solution)/shard_map/ppermute | solution.py:24
  134.3 7.9 %collective-permute-start.18 = (f32[256]{0:T(256)S(1)}, f32[256]{0:T(256)S(1)}, u32[]{:S(2)}, u32[]{:S(2)}) collective-permute-start(f32[256]{0:T(256)S(1)} %add.180), channel_id=1, source_target_pairs={{16,0},{20,4},{24,8},{28,12},{32,16},{36,20},{40,24},{44,28},{48,3... | collective-permute-start | bytes 3080 | tf_op jit(solution)/shard_map/ppermute | solution.py:24
  142.5 5.5 %collective-permute-start.19 = (f32[256]{0:T(256)S(1)}, f32[256]{0:T(256)S(1)}, u32[]{:S(2)}, u32[]{:S(2)}) collective-permute-start(f32[256]{0:T(256)S(1)} %add.181), channel_id=1, source_target_pairs={{32,0},{36,4},{40,8},{44,12},{48,16},{52,20},{56,24},{60,28},{64,3... | collective-permute-start | bytes 3080 | tf_op jit(solution)/shard_map/ppermute | solution.py:24
  148.3 7.0 %collective-permute-start.20 = (f32[256]{0:T(256)S(1)}, f32[256]{0:T(256)S(1)}, u32[]{:S(2)}, u32[]{:S(2)}) collective-permute-start(f32[256]{0:T(256)S(1)} %add.182), channel_id=1, source_target_pairs={{64,0},{68,4},{72,8},{76,12},{80,16},{84,20},{88,24},{92,28},{96,3... | collective-permute-start | bytes 3080 | tf_op jit(solution)/shard_map/ppermute | solution.py:24
  (15 other events, 42.2 us)

commit v5 on v3

--- a/solution.py
+++ b/solution.py
@@ -51,10 +51,11 @@
 
 
 def exclusive_scan(mats, vecs, axis, count):
-    mat1 = shift_down(mats, axis, 1, count)
-    mat2 = shift_down(mats, axis, 2, count)
-    vec1 = shift_down(vecs, axis, 1, count)
-    vec2 = shift_down(vecs, axis, 2, count)
+    joint = jnp.concatenate([mats, vecs[None, :]], axis=0)
+    got1 = shift_down(joint, axis, 1, count)
+    got2 = shift_down(joint, axis, 2, count)
+    mat1, vec1 = got1[:-1], got1[-1]
+    mat2, vec2 = got2[:-1], got2[-1]
     carry = vec1 + dot(mat1, vec2)
     gain = dot(mat1, mat2)
     stride = 2

time: 164 us -> 167 us (1.018)
  waiting for transfers between devices: 31.5 us -> 39.9 us
  starting transfers between devices: 52.7 us -> 46.9 us
    ppermute x12 -> x10, waiting for transfers between devices: 7.56 us -> 13.9 us  [shift_down(): lax.ppermute(value, axis, [(i, i + steps) for i in range(count - steps)])]
    ppermute x12 -> x10, starting transfers between devices: 36.7 us -> 31 us  [shift_down(): lax.ppermute(value, axis, [(i, i + steps) for i in range(count - steps)])]
  transfers between devices with their start and end apart: 21 -> 19, of which waited for: 9 -> 11; matrix products, arithmetic and copies ran while one was open for 26% -> 24% of each run, Pallas kernels for 0% -> 0%
where the time goes in v5:
time: 167 us; the launch traced here: 166 us
  matrix products  50.5 us (30%)
  starting transfers between devices  46.9 us (28%)
  waiting for transfers between devices  39.9 us (24%)
  local copies, waits for them, and re-layouts  22.2 us (13%)
  other arithmetic  4.91 us (3%)
  between operations  2.04 us (1%)
    ppermute x10, starting transfers between devices, shift_down(): lax.ppermute(value, axis, [(i, i + steps) for i in range(count - steps)])  31 us
    dot_general x55, matrix products, dot(): return jnp.dot(a, b, precision=precise)  25.4 us
    ppermute x6, waiting for transfers between devices, shift_up(): lax.ppermute(value, axis, [(i + steps, i) for i in range(count - steps)])  24.5 us
    unnamed x136, local copies, waits for them, and re-layouts  16.2 us
    ppermute x10, waiting for transfers between devices, shift_down(): lax.ppermute(value, axis, [(i, i + steps) for i in range(count - steps)])  13.9 us
    ppermute x6, starting transfers between devices, shift_up(): lax.ppermute(value, axis, [(i + steps, i) for i in range(count - steps)])  11 us
    conv_general_dilated x1, matrix products, conv_stride(): lax.conv_general_dilated(images, kernel, (2, 2), ((0, 0), (1, 1)), dimens...  9.41 us
    dot_general x7, matrix products, per_device(): jnp.einsum('ab,sbc->sac', transition, phis, precision=precise)  7.15 us
  transfers between devices with their start and end apart: 19, of which 11 were waited for; matrix products, arithmetic and copies ran while one was open for 24% of the time, Pallas kernels for 0%

profile of v5, /device:TPU:14, one launch (start us, length us, event | category | flops | bytes accessed | tf_op | source)
XLA Modules:
  0.0 166.5 jit_solution(5498468332425139467)
XLA Ops:
  0.7 1.6 slice.170
  2.3 0.8 copy.115
  3.1 4.6 %collective-permute-start = (bf16[32,8,3,256]{3,1,2,0:T(8,128)(2,1)}, bf16[32,8,3,256]{3,1,2,0:T(8,128)(2,1)}, u32[]{:S(2)}, u32[]{:S(2)}) collective-permute-start(bf16[32,8,3,256]{3,1,2,0:T(8,128)(2,1)} %copy.115), channel_id=1, source_target_pairs={{0,1},{1,2},{2,3},{4,5},{5,6},{6,7},{8,9},{9,10},{10,11},{12,13},{... | collective-permute-start | bytes 1179656 | tf_op jit(solution)/shard_map/ppermute | solution.py:15
  8.7 1.0 fusion.23
  9.8 1.0 fusion.22
  10.8 1.0 fusion.21
  11.8 1.0 fusion.20
  12.9 1.0 fusion.19
  13.9 1.0 fusion.18
  15.0 1.0 fusion.17
  17.2 1.3 fusion.77
  18.6 0.8 bitcast_dynamic-update-slice_fusion.4
  19.4 1.3 constant_dynamic-update-slice_fusion.16
  21.3 1.0 convolution_bitcast_fusion
  22.3 0.8 fusion.61
  24.7 0.7 fusion.81
  25.4 5.2 %copy.88 = bf16[32,8,8,256]{0,1,3,2:T(8,128)(2,1)} copy(bf16[32,8,8,256]{3,2,1,0:T(8,128)(2,1)} %param.7) | data formatting | bytes 2097152 | tf_op args[0]
  31.1 1.8 %bitcast_dynamic-update-slice_fusion = (f32[256,2048]{1,0:T(8,128)}, f32[2048,256]{1,0:T(8,128)}) fusion(f32[4,256,256]{1,2,0:T(8,128)S(1)} %convolution_bitcast_fusion, f32[2048,256]{1,0:T(8,128)} %fusion.81, f32[2,256,256]{1,2,0:T(8,128)} %copy-done.2), kind=kLoop, calls=%fused_computation.87 | loop fusion | bytes 1048576
  32.9 2.9 %copy.87 = bf16[32,8,3,256]{0,1,3,2:T(8,128)(2,1)} copy(bf16[32,8,3,256]{3,1,2,0:T(8,128)(2,1)} %collective-permute-done) | data formatting | bytes 786432 | tf_op jit(solution)/shard_map/optimization_barrier | solution.py:106
  35.8 9.4 %fusion.4 = f32[32,2,64,128]{3,0,2,1:T(8,128)} fusion(bf16[128,64,3,3]{0,1,3,2:T(8,128)(2,1)S(1)} %copy-done, pred[5]{0:T(512)(128)(4,1)} %compare_and_fusion, bf16[64,8,3,3]{0,1,3,2:T(8,128)(2,1)} %param.8, bf16[32,8,8,256]{0,1,3,2:T(8,128)(2,1)} %copy.88, bf16[32,8,3,256]{0,1,3,2:T(8,128)(2,1)} %copy.87), kind=kOutput, calls=%fused_computation.5 | convolution fusion | flops 799834112 | bytes 3695621 | tf_op jit(solution)/shard_map/conv_general_dilated | solution.py:23
  45.3 5.3 %convolution_bitcast_fusion.3 = f32[32,256]{1,0:T(8,128)S(1)} fusion(bf16[2,64,128,256]{3,2,1,0:T(8,128)(2,1)} %param.10, f32[32,2,64,128]{3,0,2,1:T(8,128)} %fusion.4), kind=kOutput, calls=%fused_computation.33 | convolution fusion | flops 271056896 | bytes 10518528 | tf_op jit(solution)/shard_map/shwc,hwcm->sm/dot_general | solution.py:45
  50.7 0.8 collective-permute-start.2
  51.5 1.3 collective-permute-start.3
  52.8 2.8 %collective-permute-start.1 = (f32[32,256]{1,0:T(8,128)S(1)}, f32[32,256]{1,0:T(8,128)S(1)}, u32[]{:S(2)}, u32[]{:S(2)}) collective-permute-start(f32[32,256]{1,0:T(8,128)S(1)} %convolution_bitcast_fusion.3), channel_id=1, source_target_pairs={{0,2},{1,3},{2,0},{3,1},{4,6},{5,7},{6,4},{7,5},{8,10},{9,11},{10,... | collective-permute-start | bytes 98312 | tf_op jit(solution)/shard_map/ppermute | solution.py:49
  55.6 1.1 fusion.152
  56.7 1.5 collective-permute-done.1
  62.0 1.9 %collective-permute-start.4 = (f32[257,256]{1,0:T(8,128)S(1)}, f32[257,256]{1,0:T(8,128)S(1)}, u32[]{:S(2)}, u32[]{:S(2)}) collective-permute-start(f32[257,256]{1,0:T(8,128)S(1)} %pad_maximum_fusion), channel_id=1, source_target_pairs={{0,4},{4,8},{8,12},{12,16},{16,20},{20,24},{24,28},{28,32},{32,36}... | collective-permute-start | bytes 789512 | tf_op jit(solution)/shard_map/ppermute | solution.py:15
  63.9 3.4 %collective-permute-start.5 = (f32[257,256]{1,0:T(8,128)S(1)}, f32[257,256]{1,0:T(8,128)S(1)}, u32[]{:S(2)}, u32[]{:S(2)}) collective-permute-start(f32[257,256]{1,0:T(8,128)S(1)} %pad_maximum_fusion), channel_id=1, source_target_pairs={{0,8},{4,12},{8,16},{12,20},{16,24},{20,28},{24,32},{28,36},{32,40... | collective-permute-start | bytes 789512 | tf_op jit(solution)/shard_map/ppermute | solution.py:15
  67.4 0.9 fusion.86
  68.4 0.9 fusion.84
  69.2 0.9 collective-permute-done.4
  70.2 5.0 %collective-permute-done.5 = f32[257,256]{1,0:T(8,128)S(1)} collective-permute-done((f32[257,256]{1,0:T(8,128)S(1)}, f32[257,256]{1,0:T(8,128)S(1)}, u32[]{:S(2)}, u32[]{:S(2)}) %collective-permute-start.5) | collective-permute-done | bytes 263200 | tf_op jit(solution)/shard_map/ppermute | solution.py:15
  75.5 5.9 %collective-permute-start.6 = (f32[256]{0:T(256)S(1)}, f32[256]{0:T(256)S(1)}, u32[]{:S(2)}, u32[]{:S(2)}) collective-permute-start(f32[256]{0:T(256)S(1)} %add.158), channel_id=1, source_target_pairs={{0,8},{4,12},{8,16},{12,20},{16,24},{20,28},{24,32},{28,36},{32,40... | collective-permute-start | bytes 3080 | tf_op jit(solution)/shard_map/ppermute | solution.py:15
  81.8 1.9 %collective-permute-start.7 = (f32[256,256]{1,0:T(8,128)S(1)}, f32[256,256]{1,0:T(8,128)S(1)}, u32[]{:S(2)}, u32[]{:S(2)}) collective-permute-start(f32[256,256]{1,0:T(8,128)S(1)} %fusion.51), channel_id=1, source_target_pairs={{0,8},{4,12},{8,16},{12,20},{16,24},{20,28},{24,32},{28,36},{32,40... | collective-permute-start | bytes 786440 | tf_op jit(solution)/shard_map/ppermute | solution.py:15
  83.7 0.9 fusion.82
  84.8 3.4 %collective-permute-start.8 = (f32[256]{0:T(256)S(1)}, f32[256]{0:T(256)S(1)}, u32[]{:S(2)}, u32[]{:S(2)}) collective-permute-start(f32[256]{0:T(256)S(1)} %add.159), channel_id=1, source_target_pairs={{0,16},{4,20},{8,24},{12,28},{16,32},{20,36},{24,40},{28,44},{32,4... | collective-permute-start | bytes 3080 | tf_op jit(solution)/shard_map/ppermute | solution.py:15
  88.3 3.5 %collective-permute-done.7 = f32[256,256]{1,0:T(8,128)S(1)} collective-permute-done((f32[256,256]{1,0:T(8,128)S(1)}, f32[256,256]{1,0:T(8,128)S(1)}, u32[]{:S(2)}, u32[]{:S(2)}) %collective-permute-start.7) | collective-permute-done | bytes 262176 | tf_op jit(solution)/shard_map/ppermute | solution.py:15
  92.2 2.2 %collective-permute-start.9 = (f32[256,256]{1,0:T(8,128)S(1)}, f32[256,256]{1,0:T(8,128)S(1)}, u32[]{:S(2)}, u32[]{:S(2)}) collective-permute-start(f32[256,256]{1,0:T(8,128)S(1)} %fusion.138), channel_id=1, source_target_pairs={{0,16},{4,20},{8,24},{12,28},{16,32},{20,36},{24,40},{28,44},{32,4... | collective-permute-start | bytes 786440 | tf_op jit(solution)/shard_map/ppermute | solution.py:15
  94.4 0.8 bitcast_dynamic-update-slice_fusion.1
  96.1 3.2 %collective-permute-start.10 = (f32[256]{0:T(256)}, f32[256]{0:T(256)}, u32[]{:S(2)}, u32[]{:S(2)}) collective-permute-start(f32[256]{0:T(256)} %add.160), channel_id=1, source_target_pairs={{0,32},{4,36},{8,40},{12,44},{16,48},{20,52},{24,56},{28,60},{32,6... | collective-permute-start | bytes 3080 | tf_op jit(solution)/shard_map/ppermute | solution.py:15
  99.3 3.6 %collective-permute-done.9 = f32[256,256]{1,0:T(8,128)S(1)} collective-permute-done((f32[256,256]{1,0:T(8,128)S(1)}, f32[256,256]{1,0:T(8,128)S(1)}, u32[]{:S(2)}, u32[]{:S(2)}) %collective-permute-start.9) | collective-permute-done | bytes 262176 | tf_op jit(solution)/shard_map/ppermute | solution.py:15
  102.9 1.1 fusion.140
  104.0 3.2 %collective-permute-start.11 = (f32[256,256]{1,0:T(8,128)}, f32[256,256]{1,0:T(8,128)}, u32[]{:S(2)}, u32[]{:S(2)}) collective-permute-start(f32[256,256]{1,0:T(8,128)} %fusion.140), channel_id=1, source_target_pairs={{0,32},{4,36},{8,40},{12,44},{16,48},{20,52},{24,56},{28,60},{32,6... | collective-permute-start | bytes 786440 | tf_op jit(solution)/shard_map/ppermute | solution.py:15
  107.2 1.1 convolution_bitcast_fusion.2
  108.4 1.2 fusion.141
  109.6 0.8 add.161
  110.4 1.3 collective-permute-start.12
  111.7 0.9 collective-permute-done.11
  112.6 1.4 fusion.142
  119.7 1.3 fusion.15
  122.4 1.9 %collective-permute-start.14 = (f32[256]{0:T(256)S(1)}, f32[256]{0:T(256)S(1)}, u32[]{:S(2)}, u32[]{:S(2)}) collective-permute-start(f32[256]{0:T(256)S(1)} %select_add_fusion), channel_id=1, source_target_pairs={{8,0},{12,4},{16,8},{20,12},{24,16},{28,20},{32,24},{36,28},{40,32... | collective-permute-start | bytes 3080 | tf_op jit(solution)/shard_map/ppermute | solution.py:19
  124.4 0.8 fusion.80
  125.1 1.9 %collective-permute-start.13 = (f32[256]{0:T(256)S(1)}, f32[256]{0:T(256)S(1)}, u32[]{:S(2)}, u32[]{:S(2)}) collective-permute-start(f32[256]{0:T(256)S(1)} %select_add_fusion), channel_id=1, source_target_pairs={{4,0},{8,4},{12,8},{16,12},{20,16},{24,20},{28,24},{32,28},{36,32}... | collective-permute-start | bytes 3080 | tf_op jit(solution)/shard_map/ppermute | solution.py:19
  127.1 5.8 %collective-permute-done.14 = f32[256]{0:T(256)S(1)} collective-permute-done((f32[256]{0:T(256)S(1)}, f32[256]{0:T(256)S(1)}, u32[]{:S(2)}, u32[]{:S(2)}) %collective-permute-start.14) | collective-permute-done | bytes 1056 | tf_op jit(solution)/shard_map/ppermute | solution.py:19
  133.2 1.9 %collective-permute-start.15 = (f32[256]{0:T(256)S(1)}, f32[256]{0:T(256)S(1)}, u32[]{:S(2)}, u32[]{:S(2)}) collective-permute-start(f32[256]{0:T(256)S(1)} %add.179), channel_id=1, source_target_pairs={{8,0},{12,4},{16,8},{20,12},{24,16},{28,20},{32,24},{36,28},{40,32... | collective-permute-start | bytes 3080 | tf_op jit(solution)/shard_map/ppermute | solution.py:19
  135.1 0.7 constant_dynamic-update-slice_fusion.17
  135.9 4.9 %collective-permute-done.15 = f32[256]{0:T(256)S(1)} collective-permute-done((f32[256]{0:T(256)S(1)}, f32[256]{0:T(256)S(1)}, u32[]{:S(2)}, u32[]{:S(2)}) %collective-permute-start.15) | collective-permute-done | bytes 1056 | tf_op jit(solution)/shard_map/ppermute | solution.py:19
  141.0 2.0 %collective-permute-start.16 = (f32[256]{0:T(256)S(1)}, f32[256]{0:T(256)S(1)}, u32[]{:S(2)}, u32[]{:S(2)}) collective-permute-start(f32[256]{0:T(256)S(1)} %add.180), channel_id=1, source_target_pairs={{16,0},{20,4},{24,8},{28,12},{32,16},{36,20},{40,24},{44,28},{48,3... | collective-permute-start | bytes 3080 | tf_op jit(solution)/shard_map/ppermute | solution.py:19
  143.8 5.2 %collective-permute-done.16 = f32[256]{0:T(256)S(1)} collective-permute-done((f32[256]{0:T(256)S(1)}, f32[256]{0:T(256)S(1)}, u32[]{:S(2)}, u32[]{:S(2)}) %collective-permute-start.16) | collective-permute-done | bytes 1056 | tf_op jit(solution)/shard_map/ppermute | solution.py:19
  149.2 2.0 %collective-permute-start.17 = (f32[256]{0:T(256)S(1)}, f32[256]{0:T(256)S(1)}, u32[]{:S(2)}, u32[]{:S(2)}) collective-permute-start(f32[256]{0:T(256)S(1)} %add.181), channel_id=1, source_target_pairs={{32,0},{36,4},{40,8},{44,12},{48,16},{52,20},{56,24},{60,28},{64,3... | collective-permute-start | bytes 3080 | tf_op jit(solution)/shard_map/ppermute | solution.py:19
  151.2 3.5 %collective-permute-done.17 = f32[256]{0:T(256)S(1)} collective-permute-done((f32[256]{0:T(256)S(1)}, f32[256]{0:T(256)S(1)}, u32[]{:S(2)}, u32[]{:S(2)}) %collective-permute-start.17) | collective-permute-done | bytes 1056 | tf_op jit(solution)/shard_map/ppermute | solution.py:19
  155.0 1.3 collective-permute-start.18
  157.0 5.0 %collective-permute-done.18 = f32[256]{0:T(256)S(1)} collective-permute-done((f32[256]{0:T(256)S(1)}, f32[256]{0:T(256)S(1)}, u32[]{:S(2)}, u32[]{:S(2)}) %collective-permute-start.18) | collective-permute-done | bytes 1056 | tf_op jit(solution)/shard_map/ppermute | solution.py:19
  163.1 2.7 %fusion.12 = f32[1,8,256]{2,0,1:T(1,128)S(1)} fusion(f32[32,8,8,256]{3,2,1,0:T(8,128)} %bitcast.150, s32[]{:T(128)S(6)} %select_n.26, f32[1,256]{1,0:T(1,128)S(1)} %bitcast.449, f32[1,256]{1,0:T(1,128)S(1)} %bitcast.461, f32[1,256]{1,0:T(1,128)S(1)} %bitcast.446, f32[1,256]{1,0:T(1,128)S(1)} %bitcast.442), kind=kOutput, calls=%fused_computation.9 | convolution fusion | flops 6292224 | bytes 2109444 | tf_op jit(solution)/shard_map/dot_general | solution.py:11
  (220 shorter events, 21.9 us)
Async XLA Ops:
  0.6 35.2 %copy-start = (bf16[128,64,3,3]{0,1,3,2:T(8,128)(2,1)S(1)}, bf16[128,64,3,3]{0,1,3,2:T(8,128)(2,1)}, u32[]{:S(2)}) copy-start(bf16[128,64,3,3]{0,1,3,2:T(8,128)(2,1)} %param.9) | copy-start | bytes 442372
  0.6 7.8 %copy-start.1 = (f32[256,256]{1,0:T(8,128)S(1)}, f32[256,256]{1,0:T(8,128)}, u32[]{:S(2)}) copy-start(f32[256,256]{1,0:T(8,128)} %param.11) | copy-start | bytes 786436
  0.7 7.9 %copy-start.54 = (f32[32,256]{1,0:T(8,128)S(1)}, f32[32,256]{1,0:T(8,128)}, u32[]{:S(2)}) copy-start(f32[32,256]{1,0:T(8,128)} %param.13) | copy-start | bytes 98308
  3.1 29.8 %collective-permute-start = (bf16[32,8,3,256]{3,1,2,0:T(8,128)(2,1)}, bf16[32,8,3,256]{3,1,2,0:T(8,128)(2,1)}, u32[]{:S(2)}, u32[]{:S(2)}) collective-permute-start(bf16[32,8,3,256]{3,1,2,0:T(8,128)(2,1)} %copy.115), channel_id=1, source_target_pairs={{0,1},{1,2},{2,3},{4,5},{5,6},{6,7},{8,9},{9,10},{10,11},{12,13},{... | collective-permute-start | bytes 1179656 | tf_op jit(solution)/shard_map/ppermute | solution.py:15
  45.3 13.1 %copy-start.34 = (f32[4,1,256]{2,1,0:T(1,128)S(1)}, f32[4,1,256]{2,1,0:T(1,128)}, u32[]{:S(2)}) copy-start(f32[4,1,256]{2,1,0:T(1,128)} %copy-done.33) | copy-start | bytes 12292
  45.3 13.4 %copy-start.31 = (f32[4,1,256]{2,1,0:T(1,128)S(1)}, f32[4,1,256]{2,1,0:T(1,128)}, u32[]{:S(2)}) copy-start(f32[4,1,256]{2,1,0:T(1,128)} %copy-done.30) | copy-start | bytes 12292
  45.3 13.7 %copy-start.28 = (f32[4,1,256]{2,1,0:T(1,128)S(1)}, f32[4,1,256]{2,1,0:T(1,128)}, u32[]{:S(2)}) copy-start(f32[4,1,256]{2,1,0:T(1,128)} %copy-done.27) | copy-start | bytes 12292
  45.3 14.1 %copy-start.25 = (f32[4,1,256]{2,1,0:T(1,128)S(1)}, f32[4,1,256]{2,1,0:T(1,128)}, u32[]{:S(2)}) copy-start(f32[4,1,256]{2,1,0:T(1,128)} %copy-done.24) | copy-start | bytes 12292
  50.6 9.0 %copy-start.22 = (f32[4,1,256]{2,1,0:T(1,128)S(1)}, f32[4,1,256]{2,1,0:T(1,128)}, u32[]{:S(2)}) copy-start(f32[4,1,256]{2,1,0:T(1,128)} %copy-done.21) | copy-start | bytes 12292
  50.6 9.3 %copy-start.19 = (f32[4,1,256]{2,1,0:T(1,128)S(1)}, f32[4,1,256]{2,1,0:T(1,128)}, u32[]{:S(2)}) copy-start(f32[4,1,256]{2,1,0:T(1,128)} %copy-done.18) | copy-start | bytes 12292
  50.6 9.7 %copy-start.16 = (f32[4,1,256]{2,1,0:T(1,128)S(1)}, f32[4,1,256]{2,1,0:T(1,128)}, u32[]{:S(2)}) copy-start(f32[4,1,256]{2,1,0:T(1,128)} %copy-done.15) | copy-start | bytes 12292
  50.7 11.3 %copy-start.14 = (f32[256,256]{1,0:T(8,128)S(1)}, f32[256,256]{1,0:T(8,128)}, u32[]{:S(2)}) copy-start(f32[256,256]{1,0:T(8,128)} %fusion.77) | copy-start | bytes 786436
  50.7 6.0 %collective-permute-start.2 = (f32[32,256]{1,0:T(8,128)S(1)}, f32[32,256]{1,0:T(8,128)S(1)}, u32[]{:S(2)}, u32[]{:S(2)}) collective-permute-start(f32[32,256]{1,0:T(8,128)S(1)} %convolution_bitcast_fusion.3), channel_id=1, source_target_pairs={{0,3},{1,0},{2,1},{3,2},{4,7},{5,4},{6,5},{7,6},{8,11},{9,8},{10,9... | collective-permute-start | bytes 98312 | tf_op jit(solution)/shard_map/ppermute | solution.py:49
  51.5 5.2 %collective-permute-start.3 = (f32[32,256]{1,0:T(8,128)S(1)}, f32[32,256]{1,0:T(8,128)S(1)}, u32[]{:S(2)}, u32[]{:S(2)}) collective-permute-start(f32[32,256]{1,0:T(8,128)S(1)} %convolution_bitcast_fusion.3), channel_id=1, source_target_pairs={{0,1},{1,2},{2,3},{3,0},{4,5},{5,6},{6,7},{7,4},{8,9},{9,10},{10,1... | collective-permute-start | bytes 98312 | tf_op jit(solution)/shard_map/ppermute | solution.py:49
  52.8 5.4 %collective-permute-start.1 = (f32[32,256]{1,0:T(8,128)S(1)}, f32[32,256]{1,0:T(8,128)S(1)}, u32[]{:S(2)}, u32[]{:S(2)}) collective-permute-start(f32[32,256]{1,0:T(8,128)S(1)} %convolution_bitcast_fusion.3), channel_id=1, source_target_pairs={{0,2},{1,3},{2,0},{3,1},{4,6},{5,7},{6,4},{7,5},{8,10},{9,11},{10,... | collective-permute-start | bytes 98312 | tf_op jit(solution)/shard_map/ppermute | solution.py:49
  58.2 9.1 %copy-start.36 = (f32[4,1,256]{2,1,0:T(1,128)}, f32[4,1,256]{2,1,0:T(1,128)S(1)}, u32[]{:S(2)}) copy-start(f32[4,1,256]{2,1,0:T(1,128)S(1)} %get-tuple-element.16) | copy-start | bytes 12292
  58.2 9.1 %copy-start.38 = (f32[4,1,256]{2,1,0:T(1,128)}, f32[4,1,256]{2,1,0:T(1,128)S(1)}, u32[]{:S(2)}) copy-start(f32[4,1,256]{2,1,0:T(1,128)S(1)} %get-tuple-element.17) | copy-start | bytes 12292
  58.2 9.1 %copy-start.40 = (f32[4,1,256]{2,1,0:T(1,128)}, f32[4,1,256]{2,1,0:T(1,128)S(1)}, u32[]{:S(2)}) copy-start(f32[4,1,256]{2,1,0:T(1,128)S(1)} %get-tuple-element.18) | copy-start | bytes 12292
  58.3 9.1 %copy-start.42 = (f32[4,1,256]{2,1,0:T(1,128)}, f32[4,1,256]{2,1,0:T(1,128)S(1)}, u32[]{:S(2)}) copy-start(f32[4,1,256]{2,1,0:T(1,128)S(1)} %get-tuple-element.19) | copy-start | bytes 12292
  58.3 9.1 %copy-start.44 = (f32[4,1,256]{2,1,0:T(1,128)}, f32[4,1,256]{2,1,0:T(1,128)S(1)}, u32[]{:S(2)}) copy-start(f32[4,1,256]{2,1,0:T(1,128)S(1)} %get-tuple-element.20) | copy-start | bytes 12292
  58.3 9.1 %copy-start.46 = (f32[4,1,256]{2,1,0:T(1,128)}, f32[4,1,256]{2,1,0:T(1,128)S(1)}, u32[]{:S(2)}) copy-start(f32[4,1,256]{2,1,0:T(1,128)S(1)} %get-tuple-element.21) | copy-start | bytes 12292
  58.3 9.1 %copy-start.48 = (f32[4,1,256]{2,1,0:T(1,128)}, f32[4,1,256]{2,1,0:T(1,128)S(1)}, u32[]{:S(2)}) copy-start(f32[4,1,256]{2,1,0:T(1,128)S(1)} %get-tuple-element.22) | copy-start | bytes 12292
  58.3 9.1 %copy-start.50 = (f32[4,1,256]{2,1,0:T(1,128)}, f32[4,1,256]{2,1,0:T(1,128)S(1)}, u32[]{:S(2)}) copy-start(f32[4,1,256]{2,1,0:T(1,128)S(1)} %get-tuple-element.23) | copy-start | bytes 12292
  61.4 6.0 %copy-start.55 = (f32[1,256]{1,0:T(1,128)}, f32[1,256]{1,0:T(1,128)S(1)}, u32[]{:S(2)}) copy-start(f32[1,256]{1,0:T(1,128)S(1)} %get-tuple-element.34) | copy-start | bytes 3076
  61.4 6.0 %copy-start.57 = (f32[1,256]{1,0:T(1,128)}, f32[1,256]{1,0:T(1,128)S(1)}, u32[]{:S(2)}) copy-start(f32[1,256]{1,0:T(1,128)S(1)} %get-tuple-element.35) | copy-start | bytes 3076
  62.0 8.2 %collective-permute-start.4 = (f32[257,256]{1,0:T(8,128)S(1)}, f32[257,256]{1,0:T(8,128)S(1)}, u32[]{:S(2)}, u32[]{:S(2)}) collective-permute-start(f32[257,256]{1,0:T(8,128)S(1)} %pad_maximum_fusion), channel_id=1, source_target_pairs={{0,4},{4,8},{8,12},{12,16},{16,20},{20,24},{24,28},{28,32},{32,36}... | collective-permute-start | bytes 789512 | tf_op jit(solution)/shard_map/ppermute | solution.py:15
  63.9 11.2 %collective-permute-start.5 = (f32[257,256]{1,0:T(8,128)S(1)}, f32[257,256]{1,0:T(8,128)S(1)}, u32[]{:S(2)}, u32[]{:S(2)}) collective-permute-start(f32[257,256]{1,0:T(8,128)S(1)} %pad_maximum_fusion), channel_id=1, source_target_pairs={{0,8},{4,12},{8,16},{12,20},{16,24},{20,28},{24,32},{28,36},{32,40... | collective-permute-start | bytes 789512 | tf_op jit(solution)/shard_map/ppermute | solution.py:15
  68.4 26.0 %copy-start.3 = (f32[2,256,256]{1,2,0:T(8,128)S(1)}, f32[2,256,256]{1,2,0:T(8,128)}, u32[]{:S(2)}) copy-start(f32[2,256,256]{1,2,0:T(8,128)} %copy-done.2) | copy-start | bytes 1572868
  75.4 31.7 %copy-start.10 = (f32[256,256]{1,0:T(8,128)S(1)}, f32[256,256]{1,0:T(8,128)}, u32[]{:S(2)}) copy-start(f32[256,256]{1,0:T(8,128)} %param.12) | copy-start | bytes 786436
  75.5 9.0 %collective-permute-start.6 = (f32[256]{0:T(256)S(1)}, f32[256]{0:T(256)S(1)}, u32[]{:S(2)}, u32[]{:S(2)}) collective-permute-start(f32[256]{0:T(256)S(1)} %add.158), channel_id=1, source_target_pairs={{0,8},{4,12},{8,16},{12,20},{16,24},{20,28},{24,32},{28,36},{32,40... | collective-permute-start | bytes 3080 | tf_op jit(solution)/shard_map/ppermute | solution.py:15
  81.8 10.1 %collective-permute-start.7 = (f32[256,256]{1,0:T(8,128)S(1)}, f32[256,256]{1,0:T(8,128)S(1)}, u32[]{:S(2)}, u32[]{:S(2)}) collective-permute-start(f32[256,256]{1,0:T(8,128)S(1)} %fusion.51), channel_id=1, source_target_pairs={{0,8},{4,12},{8,16},{12,20},{16,24},{20,28},{24,32},{28,36},{32,40... | collective-permute-start | bytes 786440 | tf_op jit(solution)/shard_map/ppermute | solution.py:15
  84.8 10.4 %collective-permute-start.8 = (f32[256]{0:T(256)S(1)}, f32[256]{0:T(256)S(1)}, u32[]{:S(2)}, u32[]{:S(2)}) collective-permute-start(f32[256]{0:T(256)S(1)} %add.159), channel_id=1, source_target_pairs={{0,16},{4,20},{8,24},{12,28},{16,32},{20,36},{24,40},{28,44},{32,4... | collective-permute-start | bytes 3080 | tf_op jit(solution)/shard_map/ppermute | solution.py:15
  92.2 10.7 %collective-permute-start.9 = (f32[256,256]{1,0:T(8,128)S(1)}, f32[256,256]{1,0:T(8,128)S(1)}, u32[]{:S(2)}, u32[]{:S(2)}) collective-permute-start(f32[256,256]{1,0:T(8,128)S(1)} %fusion.138), channel_id=1, source_target_pairs={{0,16},{4,20},{8,24},{12,28},{16,32},{20,36},{24,40},{28,44},{32,4... | collective-permute-start | bytes 786440 | tf_op jit(solution)/shard_map/ppermute | solution.py:15
  96.1 12.3 %collective-permute-start.10 = (f32[256]{0:T(256)}, f32[256]{0:T(256)}, u32[]{:S(2)}, u32[]{:S(2)}) collective-permute-start(f32[256]{0:T(256)} %add.160), channel_id=1, source_target_pairs={{0,32},{4,36},{8,40},{12,44},{16,48},{20,52},{24,56},{28,60},{32,6... | collective-permute-start | bytes 3080 | tf_op jit(solution)/shard_map/ppermute | solution.py:15
  104.0 8.6 %collective-permute-start.11 = (f32[256,256]{1,0:T(8,128)}, f32[256,256]{1,0:T(8,128)}, u32[]{:S(2)}, u32[]{:S(2)}) collective-permute-start(f32[256,256]{1,0:T(8,128)} %fusion.140), channel_id=1, source_target_pairs={{0,32},{4,36},{8,40},{12,44},{16,48},{20,52},{24,56},{28,60},{32,6... | collective-permute-start | bytes 786440 | tf_op jit(solution)/shard_map/ppermute | solution.py:15
  108.2 8.1 %copy-start.56 = (f32[1,256]{1,0:T(1,128)S(1)}, f32[1,256]{1,0:T(1,128)}, u32[]{:S(2)}) copy-start(f32[1,256]{1,0:T(1,128)} %copy-done.55) | copy-start | bytes 3076
  108.2 8.2 %copy-start.51 = (f32[4,1,256]{2,1,0:T(1,128)S(1)}, f32[4,1,256]{2,1,0:T(1,128)}, u32[]{:S(2)}) copy-start(f32[4,1,256]{2,1,0:T(1,128)} %copy-done.50) | copy-start | bytes 12292
  108.3 8.2 %copy-start.53 = (f32[4,1,256]{2,1,0:T(1,128)S(1)}, f32[4,1,256]{2,1,0:T(1,128)}, u32[]{:S(2)}) copy-start(f32[4,1,256]{2,1,0:T(1,128)} %copy-done.52) | copy-start | bytes 12292
  108.3 8.5 %copy-start.35 = (f32[4,1,256]{2,1,0:T(1,128)S(1)}, f32[4,1,256]{2,1,0:T(1,128)}, u32[]{:S(2)}) copy-start(f32[4,1,256]{2,1,0:T(1,128)} %copy-done.33) | copy-start | bytes 12292
  108.3 8.5 %copy-start.49 = (f32[4,1,256]{2,1,0:T(1,128)S(1)}, f32[4,1,256]{2,1,0:T(1,128)}, u32[]{:S(2)}) copy-start(f32[4,1,256]{2,1,0:T(1,128)} %copy-done.48) | copy-start | bytes 12292
  108.3 8.8 %copy-start.32 = (f32[4,1,256]{2,1,0:T(1,128)S(1)}, f32[4,1,256]{2,1,0:T(1,128)}, u32[]{:S(2)}) copy-start(f32[4,1,256]{2,1,0:T(1,128)} %copy-done.30) | copy-start | bytes 12292
  108.3 8.8 %copy-start.47 = (f32[4,1,256]{2,1,0:T(1,128)S(1)}, f32[4,1,256]{2,1,0:T(1,128)}, u32[]{:S(2)}) copy-start(f32[4,1,256]{2,1,0:T(1,128)} %copy-done.46) | copy-start | bytes 12292
  108.3 9.2 %copy-start.29 = (f32[4,1,256]{2,1,0:T(1,128)S(1)}, f32[4,1,256]{2,1,0:T(1,128)}, u32[]{:S(2)}) copy-start(f32[4,1,256]{2,1,0:T(1,128)} %copy-done.27) | copy-start | bytes 12292
  108.3 9.2 %copy-start.45 = (f32[4,1,256]{2,1,0:T(1,128)S(1)}, f32[4,1,256]{2,1,0:T(1,128)}, u32[]{:S(2)}) copy-start(f32[4,1,256]{2,1,0:T(1,128)} %copy-done.44) | copy-start | bytes 12292
  108.3 9.5 %copy-start.26 = (f32[4,1,256]{2,1,0:T(1,128)S(1)}, f32[4,1,256]{2,1,0:T(1,128)}, u32[]{:S(2)}) copy-start(f32[4,1,256]{2,1,0:T(1,128)} %copy-done.24) | copy-start | bytes 12292
  108.3 9.5 %copy-start.43 = (f32[4,1,256]{2,1,0:T(1,128)S(1)}, f32[4,1,256]{2,1,0:T(1,128)}, u32[]{:S(2)}) copy-start(f32[4,1,256]{2,1,0:T(1,128)} %copy-done.42) | copy-start | bytes 12292
  108.3 9.8 %copy-start.23 = (f32[4,1,256]{2,1,0:T(1,128)S(1)}, f32[4,1,256]{2,1,0:T(1,128)}, u32[]{:S(2)}) copy-start(f32[4,1,256]{2,1,0:T(1,128)} %copy-done.21) | copy-start | bytes 12292
  108.3 9.8 %copy-start.41 = (f32[4,1,256]{2,1,0:T(1,128)S(1)}, f32[4,1,256]{2,1,0:T(1,128)}, u32[]{:S(2)}) copy-start(f32[4,1,256]{2,1,0:T(1,128)} %copy-done.40) | copy-start | bytes 12292
  108.3 10.1 %copy-start.20 = (f32[4,1,256]{2,1,0:T(1,128)S(1)}, f32[4,1,256]{2,1,0:T(1,128)}, u32[]{:S(2)}) copy-start(f32[4,1,256]{2,1,0:T(1,128)} %copy-done.18) | copy-start | bytes 12292
  108.4 10.1 %copy-start.39 = (f32[4,1,256]{2,1,0:T(1,128)S(1)}, f32[4,1,256]{2,1,0:T(1,128)}, u32[]{:S(2)}) copy-start(f32[4,1,256]{2,1,0:T(1,128)} %copy-done.38) | copy-start | bytes 12292
  108.4 10.5 %copy-start.17 = (f32[4,1,256]{2,1,0:T(1,128)S(1)}, f32[4,1,256]{2,1,0:T(1,128)}, u32[]{:S(2)}) copy-start(f32[4,1,256]{2,1,0:T(1,128)} %copy-done.15) | copy-start | bytes 12292
  108.4 10.5 %copy-start.37 = (f32[4,1,256]{2,1,0:T(1,128)S(1)}, f32[4,1,256]{2,1,0:T(1,128)}, u32[]{:S(2)}) copy-start(f32[4,1,256]{2,1,0:T(1,128)} %copy-done.36) | copy-start | bytes 12292
  109.6 9.6 %copy-start.13 = (f32[256,256,1]{1,0,2:T(8,128)S(1)}, f32[256,256,1]{1,0,2:T(8,128)}, u32[]{:S(2)}) copy-start(f32[256,256,1]{1,0,2:T(8,128)} %convolution_bitcast_fusion.2) | copy-start | bytes 786436
  110.4 3.6 %collective-permute-start.12 = (f32[256]{0:T(256)S(1)}, f32[256]{0:T(256)S(1)}, u32[]{:S(2)}, u32[]{:S(2)}) collective-permute-start(f32[256]{0:T(256)S(1)} %add.161), channel_id=1, source_target_pairs={{0,64},{4,68},{8,72},{12,76},{16,80},{20,84},{24,88},{28,92},{32,9... | collective-permute-start | bytes 3080 | tf_op jit(solution)/shard_map/ppermute | solution.py:15
  114.0 5.7 %copy-start.11 = (f32[2048,256]{1,0:T(8,128)S(1)}, f32[2048,256]{1,0:T(8,128)}, u32[]{:S(2)}) copy-start(f32[2048,256]{1,0:T(8,128)} %get-tuple-element.7) | copy-start | bytes 6291460
  119.7 21.1 %copy-start.8 = (f32[256,256]{1,0:T(8,128)S(1)}, f32[256,256]{1,0:T(8,128)}, u32[]{:S(2)}) copy-start(f32[256,256]{1,0:T(8,128)} %copy-done.7) | copy-start | bytes 786436
  121.0 28.0 %copy-start.6 = (f32[256,256]{1,0:T(8,128)S(1)}, f32[256,256]{1,0:T(8,128)}, u32[]{:S(2)}) copy-start(f32[256,256]{1,0:T(8,128)} %copy-done.5) | copy-start | bytes 786436
  121.0 41.1 %copy-start.12 = (f32[256,256]{1,0:T(8,128)S(1)}, f32[256,256]{1,0:T(8,128)}, u32[]{:S(2)}) copy-start(f32[256,256]{1,0:T(8,128)} %fusion.152) | copy-start | bytes 786436
  122.4 10.4 %collective-permute-start.14 = (f32[256]{0:T(256)S(1)}, f32[256]{0:T(256)S(1)}, u32[]{:S(2)}, u32[]{:S(2)}) collective-permute-start(f32[256]{0:T(256)S(1)} %select_add_fusion), channel_id=1, source_target_pairs={{8,0},{12,4},{16,8},{20,12},{24,16},{28,20},{32,24},{36,28},{40,32... | collective-permute-start | bytes 3080 | tf_op jit(solution)/shard_map/ppermute | solution.py:19
  125.1 8.0 %collective-permute-start.13 = (f32[256]{0:T(256)S(1)}, f32[256]{0:T(256)S(1)}, u32[]{:S(2)}, u32[]{:S(2)}) collective-permute-start(f32[256]{0:T(256)S(1)} %select_add_fusion), channel_id=1, source_target_pairs={{4,0},{8,4},{12,8},{16,12},{20,16},{24,20},{28,24},{32,28},{36,32}... | collective-permute-start | bytes 3080 | tf_op jit(solution)/shard_map/ppermute | solution.py:19
  133.2 7.6 %collective-permute-start.15 = (f32[256]{0:T(256)S(1)}, f32[256]{0:T(256)S(1)}, u32[]{:S(2)}, u32[]{:S(2)}) collective-permute-start(f32[256]{0:T(256)S(1)} %add.179), channel_id=1, source_target_pairs={{8,0},{12,4},{16,8},{20,12},{24,16},{28,20},{32,24},{36,28},{40,32... | collective-permute-start | bytes 3080 | tf_op jit(solution)/shard_map/ppermute | solution.py:19
  141.0 7.9 %collective-permute-start.16 = (f32[256]{0:T(256)S(1)}, f32[256]{0:T(256)S(1)}, u32[]{:S(2)}, u32[]{:S(2)}) collective-permute-start(f32[256]{0:T(256)S(1)} %add.180), channel_id=1, source_target_pairs={{16,0},{20,4},{24,8},{28,12},{32,16},{36,20},{40,24},{44,28},{48,3... | collective-permute-start | bytes 3080 | tf_op jit(solution)/shard_map/ppermute | solution.py:19
  149.2 5.5 %collective-permute-start.17 = (f32[256]{0:T(256)S(1)}, f32[256]{0:T(256)S(1)}, u32[]{:S(2)}, u32[]{:S(2)}) collective-permute-start(f32[256]{0:T(256)S(1)} %add.181), channel_id=1, source_target_pairs={{32,0},{36,4},{40,8},{44,12},{48,16},{52,20},{56,24},{60,28},{64,3... | collective-permute-start | bytes 3080 | tf_op jit(solution)/shard_map/ppermute | solution.py:19
  155.0 7.0 %collective-permute-start.18 = (f32[256]{0:T(256)S(1)}, f32[256]{0:T(256)S(1)}, u32[]{:S(2)}, u32[]{:S(2)}) collective-permute-start(f32[256]{0:T(256)S(1)} %add.182), channel_id=1, source_target_pairs={{64,0},{68,4},{72,8},{76,12},{80,16},{84,20},{88,24},{92,28},{96,3... | collective-permute-start | bytes 3080 | tf_op jit(solution)/shard_map/ppermute | solution.py:19
  (13 other events, 33.9 us)

commit v6 on v3

--- a/solution.py
+++ b/solution.py
@@ -74,12 +74,14 @@
     got1 = shift_up(heads, axis, 1, count)
     got2 = shift_up(heads, axis, 2, count)
     entering = got1 + dot(step_power, got2)
-    jump = dot(step_power, step_power)
+    got2, jump = lax.optimization_barrier((got2, step_power))
+    jump = dot(jump, jump)
     stride = 2
     while stride < count:
         got = shift_up(entering, axis, stride, count)
         entering = entering + dot(jump, got)
         if stride * 2 < count:
+            got, jump = lax.optimization_barrier((got, jump))
             jump = dot(jump, jump)
         stride *= 2
     return entering

time: 164 us -> 169 us (1.030)
  matrix products: 50.4 us -> 55.4 us
    dot_general x55, matrix products: 25.3 us -> 30.3 us  [dot(): return jnp.dot(a, b, precision=precise)]
    unnamed x136 -> x84, local copies, waits for them, and re-layouts: 16.1 us -> 14.5 us
  transfers between devices with their start and end apart: 21 -> 21, of which waited for: 9 -> 9; matrix products, arithmetic and copies ran while one was open for 26% -> 24% of each run, Pallas kernels for 0% -> 0%
where the time goes in v6:
time: 169 us; the launch traced here: 168 us
  matrix products  55.4 us (33%)
  starting transfers between devices  52.8 us (31%)
  waiting for transfers between devices  32 us (19%)
  local copies, waits for them, and re-layouts  20.6 us (12%)
  other arithmetic  5.59 us (3%)
  between operations  1.83 us (1%)
    ppermute x12, starting transfers between devices, shift_down(): lax.ppermute(value, axis, [(i, i + steps) for i in range(count - steps)])  36.6 us
    dot_general x55, matrix products, dot(): return jnp.dot(a, b, precision=precise)  30.3 us
    ppermute x6, waiting for transfers between devices, shift_up(): lax.ppermute(value, axis, [(i + steps, i) for i in range(count - steps)])  23.6 us
    unnamed x84, local copies, waits for them, and re-layouts  14.5 us
    ppermute x6, starting transfers between devices, shift_up(): lax.ppermute(value, axis, [(i + steps, i) for i in range(count - steps)])  11.3 us
    conv_general_dilated x1, matrix products, conv_stride(): lax.conv_general_dilated(images, kernel, (2, 2), ((0, 0), (1, 1)), dimens...  9.37 us
    ppermute x12, waiting for transfers between devices, shift_down(): lax.ppermute(value, axis, [(i, i + steps) for i in range(count - steps)])  8.4 us
    dot_general x7, matrix products, per_device(): jnp.einsum('ab,sbc->sac', transition, phis, precision=precise)  7.16 us
  transfers between devices with their start and end apart: 21, of which 9 were waited for; matrix products, arithmetic and copies ran while one was open for 24% of the time, Pallas kernels for 0%

profile of v6, /device:TPU:14, one launch (start us, length us, event | category | flops | bytes accessed | tf_op | source)
XLA Modules:
  0.0 168.2 jit_solution(15574411267743628223)
XLA Ops:
  0.7 1.6 slice.168
  2.3 0.8 copy.122
  3.1 4.6 %collective-permute-start = (bf16[32,8,3,256]{3,1,2,0:T(8,128)(2,1)}, bf16[32,8,3,256]{3,1,2,0:T(8,128)(2,1)}, u32[]{:S(2)}, u32[]{:S(2)}) collective-permute-start(bf16[32,8,3,256]{3,1,2,0:T(8,128)(2,1)} %copy.122), channel_id=1, source_target_pairs={{0,1},{1,2},{2,3},{4,5},{5,6},{6,7},{8,9},{9,10},{10,11},{12,13},{... | collective-permute-start | bytes 1179656 | tf_op jit(solution)/shard_map/ppermute | solution.py:15
  8.7 1.0 fusion.23
  9.7 1.0 fusion.22
  10.8 1.0 fusion.21
  11.8 1.0 fusion.20
  12.9 1.0 fusion.19
  13.9 1.0 fusion.18
  15.0 1.0 fusion.17
  17.2 1.3 fusion.75
  19.4 1.3 constant_dynamic-update-slice_fusion.16
  21.3 1.0 convolution_bitcast_fusion
  23.0 0.8 fusion.59
  23.7 0.9 bitcast_dynamic-update-slice_fusion
  25.0 0.8 fusion.84
  25.9 0.9 fusion.82
  26.8 5.1 %copy.88 = bf16[32,8,8,256]{0,1,3,2:T(8,128)(2,1)} copy(bf16[32,8,8,256]{3,2,1,0:T(8,128)(2,1)} %param.7) | data formatting | bytes 2097152 | tf_op args[0]
  32.4 0.9 fusion.80
  33.3 3.0 %copy.87 = bf16[32,8,3,256]{0,1,3,2:T(8,128)(2,1)} copy(bf16[32,8,3,256]{3,1,2,0:T(8,128)(2,1)} %collective-permute-done) | data formatting | bytes 786432 | tf_op jit(solution)/shard_map/optimization_barrier | solution.py:107
  36.2 9.4 %fusion.4 = f32[32,2,64,128]{3,0,2,1:T(8,128)} fusion(bf16[128,64,3,3]{0,1,3,2:T(8,128)(2,1)S(1)} %copy-done, pred[5]{0:T(512)(128)(4,1)} %compare_and_fusion, bf16[64,8,3,3]{0,1,3,2:T(8,128)(2,1)} %param.8, bf16[32,8,8,256]{0,1,3,2:T(8,128)(2,1)} %copy.88, bf16[32,8,3,256]{0,1,3,2:T(8,128)(2,1)} %copy.87), kind=kOutput, calls=%fused_computation.5 | convolution fusion | flops 799834112 | bytes 3695621 | tf_op jit(solution)/shard_map/conv_general_dilated | solution.py:23
  45.7 5.4 %convolution_bitcast_fusion.3 = f32[32,256]{1,0:T(8,128)S(1)} fusion(bf16[2,64,128,256]{3,2,1,0:T(8,128)(2,1)} %param.10, f32[32,2,64,128]{3,0,2,1:T(8,128)} %fusion.4), kind=kOutput, calls=%fused_computation.33 | convolution fusion | flops 271056896 | bytes 10518528 | tf_op jit(solution)/shard_map/shwc,hwcm->sm/dot_general | solution.py:45
  51.1 0.8 collective-permute-start.2
  51.9 1.3 collective-permute-start.3
  53.2 2.8 %collective-permute-start.1 = (f32[32,256]{1,0:T(8,128)S(1)}, f32[32,256]{1,0:T(8,128)S(1)}, u32[]{:S(2)}, u32[]{:S(2)}) collective-permute-start(f32[32,256]{1,0:T(8,128)S(1)} %convolution_bitcast_fusion.3), channel_id=1, source_target_pairs={{0,2},{1,3},{2,0},{3,1},{4,6},{5,7},{6,4},{7,5},{8,10},{9,11},{10,... | collective-permute-start | bytes 98312 | tf_op jit(solution)/shard_map/ppermute | solution.py:49
  56.8 1.9 %collective-permute-start.5 = (f32[256,256]{1,0:T(8,128)S(1)}, f32[256,256]{1,0:T(8,128)S(1)}, u32[]{:S(2)}, u32[]{:S(2)}) collective-permute-start(f32[256,256]{1,0:T(8,128)S(1)} %copy-done.5), channel_id=1, source_target_pairs={{0,4},{4,8},{8,12},{12,16},{16,20},{20,24},{24,28},{28,32},{32,36}... | collective-permute-start | bytes 786440 | tf_op jit(solution)/shard_map/ppermute | solution.py:15
  58.7 3.4 %collective-permute-start.7 = (f32[256,256]{1,0:T(8,128)S(1)}, f32[256,256]{1,0:T(8,128)S(1)}, u32[]{:S(2)}, u32[]{:S(2)}) collective-permute-start(f32[256,256]{1,0:T(8,128)S(1)} %copy-done.5), channel_id=1, source_target_pairs={{0,8},{4,12},{8,16},{12,20},{16,24},{20,28},{24,32},{28,36},{32,40... | collective-permute-start | bytes 786440 | tf_op jit(solution)/shard_map/ppermute | solution.py:15
  65.9 3.4 %collective-permute-start.6 = (f32[256]{0:T(256)S(1)}, f32[256]{0:T(256)S(1)}, u32[]{:S(2)}, u32[]{:S(2)}) collective-permute-start(f32[256]{0:T(256)S(1)} %add.157), channel_id=1, source_target_pairs={{0,8},{4,12},{8,16},{12,20},{16,24},{20,28},{24,32},{28,36},{32,40... | collective-permute-start | bytes 3080 | tf_op jit(solution)/shard_map/ppermute | solution.py:15
  70.1 2.9 %collective-permute-start.4 = (f32[256]{0:T(256)S(1)}, f32[256]{0:T(256)S(1)}, u32[]{:S(2)}, u32[]{:S(2)}) collective-permute-start(f32[256]{0:T(256)S(1)} %add.157), channel_id=1, source_target_pairs={{0,4},{4,8},{8,12},{12,16},{16,20},{20,24},{24,28},{28,32},{32,36}... | collective-permute-start | bytes 3080 | tf_op jit(solution)/shard_map/ppermute | solution.py:15
  73.3 1.7 collective-permute-done.4
  75.0 5.5 %collective-permute-start.8 = (f32[256]{0:T(256)S(1)}, f32[256]{0:T(256)S(1)}, u32[]{:S(2)}, u32[]{:S(2)}) collective-permute-start(f32[256]{0:T(256)S(1)} %add.158), channel_id=1, source_target_pairs={{0,8},{4,12},{8,16},{12,20},{16,24},{20,28},{24,32},{28,36},{32,40... | collective-permute-start | bytes 3080 | tf_op jit(solution)/shard_map/ppermute | solution.py:15
  81.0 1.9 %collective-permute-start.9 = (f32[256,256]{1,0:T(8,128)S(1)}, f32[256,256]{1,0:T(8,128)S(1)}, u32[]{:S(2)}, u32[]{:S(2)}) collective-permute-start(f32[256,256]{1,0:T(8,128)S(1)} %fusion.133), channel_id=1, source_target_pairs={{0,8},{4,12},{8,16},{12,20},{16,24},{20,28},{24,32},{28,36},{32,40... | collective-permute-start | bytes 786440 | tf_op jit(solution)/shard_map/ppermute | solution.py:15
  82.9 0.8 constant_dynamic-update-slice_fusion.17
  84.0 3.2 %collective-permute-start.10 = (f32[256]{0:T(256)S(1)}, f32[256]{0:T(256)S(1)}, u32[]{:S(2)}, u32[]{:S(2)}) collective-permute-start(f32[256]{0:T(256)S(1)} %add.159), channel_id=1, source_target_pairs={{0,16},{4,20},{8,24},{12,28},{16,32},{20,36},{24,40},{28,44},{32,4... | collective-permute-start | bytes 3080 | tf_op jit(solution)/shard_map/ppermute | solution.py:15
  87.1 2.1 %collective-permute-done.9 = f32[256,256]{1,0:T(8,128)S(1)} collective-permute-done((f32[256,256]{1,0:T(8,128)S(1)}, f32[256,256]{1,0:T(8,128)S(1)}, u32[]{:S(2)}, u32[]{:S(2)}) %collective-permute-start.9) | collective-permute-done | bytes 262176 | tf_op jit(solution)/shard_map/ppermute | solution.py:15
  89.6 3.0 %collective-permute-start.11 = (f32[256,256]{1,0:T(8,128)S(1)}, f32[256,256]{1,0:T(8,128)S(1)}, u32[]{:S(2)}, u32[]{:S(2)}) collective-permute-start(f32[256,256]{1,0:T(8,128)S(1)} %fusion.135), channel_id=1, source_target_pairs={{0,16},{4,20},{8,24},{12,28},{16,32},{20,36},{24,40},{28,44},{32,4... | collective-permute-start | bytes 786440 | tf_op jit(solution)/shard_map/ppermute | solution.py:15
  94.4 2.3 %collective-permute-start.12 = (f32[256]{0:T(256)}, f32[256]{0:T(256)}, u32[]{:S(2)}, u32[]{:S(2)}) collective-permute-start(f32[256]{0:T(256)} %add.160), channel_id=1, source_target_pairs={{0,32},{4,36},{8,40},{12,44},{16,48},{20,52},{24,56},{28,60},{32,6... | collective-permute-start | bytes 3080 | tf_op jit(solution)/shard_map/ppermute | solution.py:15
  96.6 2.8 %collective-permute-done.11 = f32[256,256]{1,0:T(8,128)S(1)} collective-permute-done((f32[256,256]{1,0:T(8,128)S(1)}, f32[256,256]{1,0:T(8,128)S(1)}, u32[]{:S(2)}, u32[]{:S(2)}) %collective-permute-start.11) | collective-permute-done | bytes 262176 | tf_op jit(solution)/shard_map/ppermute | solution.py:15
  99.8 3.2 %collective-permute-start.13 = (f32[256,256]{1,0:T(8,128)S(1)}, f32[256,256]{1,0:T(8,128)}, u32[]{:S(2)}, u32[]{:S(2)}) collective-permute-start(f32[256,256]{1,0:T(8,128)S(1)} %fusion.137), channel_id=1, source_target_pairs={{0,32},{4,36},{8,40},{12,44},{16,48},{20,52},{24,56},{28,60},{32,6... | collective-permute-start | bytes 786440 | tf_op jit(solution)/shard_map/ppermute | solution.py:15
  103.4 0.9 fusion.138
  105.1 1.3 collective-permute-start.14
  106.4 1.8 %collective-permute-done.13 = f32[256,256]{1,0:T(8,128)} collective-permute-done((f32[256,256]{1,0:T(8,128)S(1)}, f32[256,256]{1,0:T(8,128)}, u32[]{:S(2)}, u32[]{:S(2)}) %collective-permute-start.13) | collective-permute-done | bytes 262176 | tf_op jit(solution)/shard_map/ppermute | solution.py:15
  108.2 1.3 fusion.139
  112.6 1.0 constant_dynamic-update-slice_fusion.7
  113.6 1.1 constant_dynamic-update-slice_fusion.6
  114.6 1.0 constant_dynamic-update-slice_fusion.5
  115.7 1.0 constant_dynamic-update-slice_fusion.4
  116.7 1.0 constant_dynamic-update-slice_fusion.3
  117.7 1.0 constant_dynamic-update-slice_fusion.2
  118.7 1.0 constant_dynamic-update-slice_fusion.1
  119.7 1.0 constant_dynamic-update-slice_fusion
  121.2 2.9 %fusion.15 = f32[4,8,256]{2,0,1:T(4,128)S(1)} fusion(f32[4,8,2048]{2,0,1:T(4,128)S(1)} %constant_dynamic-update-slice_fusion.8, f32[2048,256]{1,0:T(8,128)} %get-tuple-element.15), kind=kOutput, calls=%fused_computation.12 | convolution fusion | flops 201326592 | bytes 2392064 | tf_op jit(solution)/shard_map/dot_general | solution.py:11
  125.6 2.1 %collective-permute-start.16 = (f32[256]{0:T(256)S(1)}, f32[256]{0:T(256)S(1)}, u32[]{:S(2)}, u32[]{:S(2)}) collective-permute-start(f32[256]{0:T(256)S(1)} %select_add_fusion), channel_id=1, source_target_pairs={{8,0},{12,4},{16,8},{20,12},{24,16},{28,20},{32,24},{36,28},{40,32... | collective-permute-start | bytes 3080 | tf_op jit(solution)/shard_map/ppermute | solution.py:19
  127.7 1.9 %collective-permute-start.15 = (f32[256]{0:T(256)S(1)}, f32[256]{0:T(256)S(1)}, u32[]{:S(2)}, u32[]{:S(2)}) collective-permute-start(f32[256]{0:T(256)S(1)} %select_add_fusion), channel_id=1, source_target_pairs={{4,0},{8,4},{12,8},{16,12},{20,16},{24,20},{28,24},{32,28},{36,32}... | collective-permute-start | bytes 3080 | tf_op jit(solution)/shard_map/ppermute | solution.py:19
  130.3 4.4 %collective-permute-done.16 = f32[256]{0:T(256)S(1)} collective-permute-done((f32[256]{0:T(256)S(1)}, f32[256]{0:T(256)S(1)}, u32[]{:S(2)}, u32[]{:S(2)}) %collective-permute-start.16) | collective-permute-done | bytes 1056 | tf_op jit(solution)/shard_map/ppermute | solution.py:19
  135.0 1.9 %collective-permute-start.17 = (f32[256]{0:T(256)S(1)}, f32[256]{0:T(256)S(1)}, u32[]{:S(2)}, u32[]{:S(2)}) collective-permute-start(f32[256]{0:T(256)S(1)} %add.179), channel_id=1, source_target_pairs={{8,0},{12,4},{16,8},{20,12},{24,16},{28,20},{32,24},{36,28},{40,32... | collective-permute-start | bytes 3080 | tf_op jit(solution)/shard_map/ppermute | solution.py:19
  137.3 5.3 %collective-permute-done.17 = f32[256]{0:T(256)S(1)} collective-permute-done((f32[256]{0:T(256)S(1)}, f32[256]{0:T(256)S(1)}, u32[]{:S(2)}, u32[]{:S(2)}) %collective-permute-start.17) | collective-permute-done | bytes 1056 | tf_op jit(solution)/shard_map/ppermute | solution.py:19
  142.8 2.0 %collective-permute-start.18 = (f32[256]{0:T(256)S(1)}, f32[256]{0:T(256)S(1)}, u32[]{:S(2)}, u32[]{:S(2)}) collective-permute-start(f32[256]{0:T(256)S(1)} %add.180), channel_id=1, source_target_pairs={{16,0},{20,4},{24,8},{28,12},{32,16},{36,20},{40,24},{44,28},{48,3... | collective-permute-start | bytes 3080 | tf_op jit(solution)/shard_map/ppermute | solution.py:19
  145.2 5.6 %collective-permute-done.18 = f32[256]{0:T(256)S(1)} collective-permute-done((f32[256]{0:T(256)S(1)}, f32[256]{0:T(256)S(1)}, u32[]{:S(2)}, u32[]{:S(2)}) %collective-permute-start.18) | collective-permute-done | bytes 1056 | tf_op jit(solution)/shard_map/ppermute | solution.py:19
  151.0 2.0 %collective-permute-start.19 = (f32[256]{0:T(256)S(1)}, f32[256]{0:T(256)S(1)}, u32[]{:S(2)}, u32[]{:S(2)}) collective-permute-start(f32[256]{0:T(256)S(1)} %add.181), channel_id=1, source_target_pairs={{32,0},{36,4},{40,8},{44,12},{48,16},{52,20},{56,24},{60,28},{64,3... | collective-permute-start | bytes 3080 | tf_op jit(solution)/shard_map/ppermute | solution.py:19
  153.4 3.2 %collective-permute-done.19 = f32[256]{0:T(256)S(1)} collective-permute-done((f32[256]{0:T(256)S(1)}, f32[256]{0:T(256)S(1)}, u32[]{:S(2)}, u32[]{:S(2)}) %collective-permute-start.19) | collective-permute-done | bytes 1056 | tf_op jit(solution)/shard_map/ppermute | solution.py:19
  156.8 1.3 collective-permute-start.20
  158.6 5.3 %collective-permute-done.20 = f32[256]{0:T(256)S(1)} collective-permute-done((f32[256]{0:T(256)S(1)}, f32[256]{0:T(256)S(1)}, u32[]{:S(2)}, u32[]{:S(2)}) %collective-permute-start.20) | collective-permute-done | bytes 1056 | tf_op jit(solution)/shard_map/ppermute | solution.py:19
  164.9 2.7 %fusion.12 = f32[1,8,256]{2,0,1:T(1,128)S(1)} fusion(f32[32,8,8,256]{3,2,1,0:T(8,128)} %bitcast.147, s32[]{:T(128)S(6)} %select_n.26, f32[1,256]{1,0:T(1,128)S(1)} %bitcast.448, f32[1,256]{1,0:T(1,128)S(1)} %bitcast.459, f32[1,256]{1,0:T(1,128)S(1)} %bitcast.445, f32[1,256]{1,0:T(1,128)S(1)} %bitcast.441), kind=kOutput, calls=%fused_computation.9 | convolution fusion | flops 6292224 | bytes 2109444 | tf_op jit(solution)/shard_map/dot_general | solution.py:11
  (170 shorter events, 24.6 us)
Async XLA Ops:
  0.6 35.6 %copy-start = (bf16[128,64,3,3]{0,1,3,2:T(8,128)(2,1)S(1)}, bf16[128,64,3,3]{0,1,3,2:T(8,128)(2,1)}, u32[]{:S(2)}) copy-start(bf16[128,64,3,3]{0,1,3,2:T(8,128)(2,1)} %param.9) | copy-start | bytes 442372
  0.6 7.7 %copy-start.1 = (f32[256,256]{1,0:T(8,128)S(1)}, f32[256,256]{1,0:T(8,128)}, u32[]{:S(2)}) copy-start(f32[256,256]{1,0:T(8,128)} %param.11) | copy-start | bytes 786436
  0.7 7.9 %copy-start.29 = (f32[32,256]{1,0:T(8,128)S(1)}, f32[32,256]{1,0:T(8,128)}, u32[]{:S(2)}) copy-start(f32[32,256]{1,0:T(8,128)} %param.13) | copy-start | bytes 98308
  3.1 30.2 %collective-permute-start = (bf16[32,8,3,256]{3,1,2,0:T(8,128)(2,1)}, bf16[32,8,3,256]{3,1,2,0:T(8,128)(2,1)}, u32[]{:S(2)}, u32[]{:S(2)}) collective-permute-start(bf16[32,8,3,256]{3,1,2,0:T(8,128)(2,1)} %copy.122), channel_id=1, source_target_pairs={{0,1},{1,2},{2,3},{4,5},{5,6},{6,7},{8,9},{9,10},{10,11},{12,13},{... | collective-permute-start | bytes 1179656 | tf_op jit(solution)/shard_map/ppermute | solution.py:15
  8.6 1.1 copy-start.6
  8.6 1.1 copy-start.16
  8.6 1.1 copy-start.18
  8.6 1.1 copy-start.28
  8.6 3.2 %copy-start.12 = (f32[4,1,256]{2,1,0:T(1,128)}, f32[4,1,256]{2,1,0:T(1,128)S(1)}, u32[]{:S(2)}) copy-start(f32[4,1,256]{2,1,0:T(1,128)S(1)} %get-tuple-element.35) | copy-start | bytes 12292
  8.6 3.2 %copy-start.14 = (f32[4,1,256]{2,1,0:T(1,128)}, f32[4,1,256]{2,1,0:T(1,128)S(1)}, u32[]{:S(2)}) copy-start(f32[4,1,256]{2,1,0:T(1,128)S(1)} %get-tuple-element.34) | copy-start | bytes 12292
  8.6 4.2 %copy-start.8 = (f32[4,1,256]{2,1,0:T(1,128)}, f32[4,1,256]{2,1,0:T(1,128)S(1)}, u32[]{:S(2)}) copy-start(f32[4,1,256]{2,1,0:T(1,128)S(1)} %get-tuple-element.37) | copy-start | bytes 12292
  8.6 4.2 %copy-start.10 = (f32[4,1,256]{2,1,0:T(1,128)}, f32[4,1,256]{2,1,0:T(1,128)S(1)}, u32[]{:S(2)}) copy-start(f32[4,1,256]{2,1,0:T(1,128)S(1)} %get-tuple-element.36) | copy-start | bytes 12292
  14.9 3.6 %copy-start.4 = (f32[256,256]{1,0:T(8,128)S(1)}, f32[256,256]{1,0:T(8,128)}, u32[]{:S(2)}) copy-start(f32[256,256]{1,0:T(8,128)} %param.12) | copy-start | bytes 786436
  21.3 3.8 %copy-start.2 = (f32[2,256,256]{1,2,0:T(8,128)}, f32[2,256,256]{1,2,0:T(8,128)S(1)}, u32[]{:S(2)}) copy-start(f32[2,256,256]{1,2,0:T(8,128)S(1)} %convolution_bitcast_fusion.1) | copy-start | bytes 1572868
  45.6 10.4 %copy-start.3 = (f32[2,256,256]{1,2,0:T(8,128)S(1)}, f32[2,256,256]{1,2,0:T(8,128)}, u32[]{:S(2)}) copy-start(f32[2,256,256]{1,2,0:T(8,128)} %copy-done.2) | copy-start | bytes 1572868
  45.6 11.2 %copy-start.5 = (f32[256,256]{1,0:T(8,128)S(1)}, f32[256,256]{1,0:T(8,128)}, u32[]{:S(2)}) copy-start(f32[256,256]{1,0:T(8,128)} %fusion.75) | copy-start | bytes 786436
  45.6 16.7 %copy-start.19 = (f32[4,1,256]{2,1,0:T(1,128)S(1)}, f32[4,1,256]{2,1,0:T(1,128)}, u32[]{:S(2)}) copy-start(f32[4,1,256]{2,1,0:T(1,128)} %copy-done.18) | copy-start | bytes 12292
  45.6 17.0 %copy-start.17 = (f32[4,1,256]{2,1,0:T(1,128)S(1)}, f32[4,1,256]{2,1,0:T(1,128)}, u32[]{:S(2)}) copy-start(f32[4,1,256]{2,1,0:T(1,128)} %copy-done.16) | copy-start | bytes 12292
  45.6 17.3 %copy-start.15 = (f32[4,1,256]{2,1,0:T(1,128)S(1)}, f32[4,1,256]{2,1,0:T(1,128)}, u32[]{:S(2)}) copy-start(f32[4,1,256]{2,1,0:T(1,128)} %copy-done.14) | copy-start | bytes 12292
  45.7 17.6 %copy-start.13 = (f32[4,1,256]{2,1,0:T(1,128)S(1)}, f32[4,1,256]{2,1,0:T(1,128)}, u32[]{:S(2)}) copy-start(f32[4,1,256]{2,1,0:T(1,128)} %copy-done.12) | copy-start | bytes 12292
  45.7 18.0 %copy-start.11 = (f32[4,1,256]{2,1,0:T(1,128)S(1)}, f32[4,1,256]{2,1,0:T(1,128)}, u32[]{:S(2)}) copy-start(f32[4,1,256]{2,1,0:T(1,128)} %copy-done.10) | copy-start | bytes 12292
  51.1 12.9 %copy-start.9 = (f32[4,1,256]{2,1,0:T(1,128)S(1)}, f32[4,1,256]{2,1,0:T(1,128)}, u32[]{:S(2)}) copy-start(f32[4,1,256]{2,1,0:T(1,128)} %copy-done.8) | copy-start | bytes 12292
  51.1 13.2 %copy-start.7 = (f32[4,1,256]{2,1,0:T(1,128)S(1)}, f32[4,1,256]{2,1,0:T(1,128)}, u32[]{:S(2)}) copy-start(f32[4,1,256]{2,1,0:T(1,128)} %copy-done.6) | copy-start | bytes 12292
  51.1 11.0 %collective-permute-start.2 = (f32[32,256]{1,0:T(8,128)S(1)}, f32[32,256]{1,0:T(8,128)S(1)}, u32[]{:S(2)}, u32[]{:S(2)}) collective-permute-start(f32[32,256]{1,0:T(8,128)S(1)} %convolution_bitcast_fusion.3), channel_id=1, source_target_pairs={{0,3},{1,0},{2,1},{3,2},{4,7},{5,4},{6,5},{7,6},{8,11},{9,8},{10,9... | collective-permute-start | bytes 98312 | tf_op jit(solution)/shard_map/ppermute | solution.py:49
  51.9 10.2 %collective-permute-start.3 = (f32[32,256]{1,0:T(8,128)S(1)}, f32[32,256]{1,0:T(8,128)S(1)}, u32[]{:S(2)}, u32[]{:S(2)}) collective-permute-start(f32[32,256]{1,0:T(8,128)S(1)} %convolution_bitcast_fusion.3), channel_id=1, source_target_pairs={{0,1},{1,2},{2,3},{3,0},{4,5},{5,6},{6,7},{7,4},{8,9},{9,10},{10,1... | collective-permute-start | bytes 98312 | tf_op jit(solution)/shard_map/ppermute | solution.py:49
  53.2 9.0 %collective-permute-start.1 = (f32[32,256]{1,0:T(8,128)S(1)}, f32[32,256]{1,0:T(8,128)S(1)}, u32[]{:S(2)}, u32[]{:S(2)}) collective-permute-start(f32[32,256]{1,0:T(8,128)S(1)} %convolution_bitcast_fusion.3), channel_id=1, source_target_pairs={{0,2},{1,3},{2,0},{3,1},{4,6},{5,7},{6,4},{7,5},{8,10},{9,11},{10,... | collective-permute-start | bytes 98312 | tf_op jit(solution)/shard_map/ppermute | solution.py:49
  56.8 16.3 %collective-permute-start.5 = (f32[256,256]{1,0:T(8,128)S(1)}, f32[256,256]{1,0:T(8,128)S(1)}, u32[]{:S(2)}, u32[]{:S(2)}) collective-permute-start(f32[256,256]{1,0:T(8,128)S(1)} %copy-done.5), channel_id=1, source_target_pairs={{0,4},{4,8},{8,12},{12,16},{16,20},{20,24},{24,28},{28,32},{32,36}... | collective-permute-start | bytes 786440 | tf_op jit(solution)/shard_map/ppermute | solution.py:15
  58.7 21.9 %collective-permute-start.7 = (f32[256,256]{1,0:T(8,128)S(1)}, f32[256,256]{1,0:T(8,128)S(1)}, u32[]{:S(2)}, u32[]{:S(2)}) collective-permute-start(f32[256,256]{1,0:T(8,128)S(1)} %copy-done.5), channel_id=1, source_target_pairs={{0,8},{4,12},{8,16},{12,20},{16,24},{20,28},{24,32},{28,36},{32,40... | collective-permute-start | bytes 786440 | tf_op jit(solution)/shard_map/ppermute | solution.py:15
  62.2 18.3 %copy-start.20 = (f32[4,1,256]{2,1,0:T(1,128)}, f32[4,1,256]{2,1,0:T(1,128)S(1)}, u32[]{:S(2)}) copy-start(f32[4,1,256]{2,1,0:T(1,128)S(1)} %get-tuple-element.24) | copy-start | bytes 12292
  62.2 18.3 %copy-start.21 = (f32[4,1,256]{2,1,0:T(1,128)}, f32[4,1,256]{2,1,0:T(1,128)S(1)}, u32[]{:S(2)}) copy-start(f32[4,1,256]{2,1,0:T(1,128)S(1)} %get-tuple-element.25) | copy-start | bytes 12292
  62.2 18.3 %copy-start.22 = (f32[4,1,256]{2,1,0:T(1,128)}, f32[4,1,256]{2,1,0:T(1,128)S(1)}, u32[]{:S(2)}) copy-start(f32[4,1,256]{2,1,0:T(1,128)S(1)} %get-tuple-element.26) | copy-start | bytes 12292
  62.2 18.3 %copy-start.23 = (f32[4,1,256]{2,1,0:T(1,128)}, f32[4,1,256]{2,1,0:T(1,128)S(1)}, u32[]{:S(2)}) copy-start(f32[4,1,256]{2,1,0:T(1,128)S(1)} %get-tuple-element.27) | copy-start | bytes 12292
  62.2 18.3 %copy-start.24 = (f32[4,1,256]{2,1,0:T(1,128)}, f32[4,1,256]{2,1,0:T(1,128)S(1)}, u32[]{:S(2)}) copy-start(f32[4,1,256]{2,1,0:T(1,128)S(1)} %get-tuple-element.28) | copy-start | bytes 12292
  62.3 18.3 %copy-start.25 = (f32[4,1,256]{2,1,0:T(1,128)}, f32[4,1,256]{2,1,0:T(1,128)S(1)}, u32[]{:S(2)}) copy-start(f32[4,1,256]{2,1,0:T(1,128)S(1)} %get-tuple-element.29) | copy-start | bytes 12292
  62.3 18.3 %copy-start.26 = (f32[4,1,256]{2,1,0:T(1,128)}, f32[4,1,256]{2,1,0:T(1,128)S(1)}, u32[]{:S(2)}) copy-start(f32[4,1,256]{2,1,0:T(1,128)S(1)} %get-tuple-element.30) | copy-start | bytes 12292
  62.3 18.3 %copy-start.27 = (f32[4,1,256]{2,1,0:T(1,128)}, f32[4,1,256]{2,1,0:T(1,128)S(1)}, u32[]{:S(2)}) copy-start(f32[4,1,256]{2,1,0:T(1,128)S(1)} %get-tuple-element.31) | copy-start | bytes 12292
  65.5 15.1 %copy-start.30 = (f32[1,256]{1,0:T(1,128)}, f32[1,256]{1,0:T(1,128)S(1)}, u32[]{:S(2)}) copy-start(f32[1,256]{1,0:T(1,128)S(1)} %get-tuple-element.42) | copy-start | bytes 3076
  65.5 15.1 %copy-start.31 = (f32[1,256]{1,0:T(1,128)}, f32[1,256]{1,0:T(1,128)S(1)}, u32[]{:S(2)}) copy-start(f32[1,256]{1,0:T(1,128)S(1)} %get-tuple-element.43) | copy-start | bytes 3076
  65.9 7.1 %collective-permute-start.6 = (f32[256]{0:T(256)S(1)}, f32[256]{0:T(256)S(1)}, u32[]{:S(2)}, u32[]{:S(2)}) collective-permute-start(f32[256]{0:T(256)S(1)} %add.157), channel_id=1, source_target_pairs={{0,8},{4,12},{8,16},{12,20},{16,24},{20,28},{24,32},{28,36},{32,40... | collective-permute-start | bytes 3080 | tf_op jit(solution)/shard_map/ppermute | solution.py:15
  70.1 4.9 %collective-permute-start.4 = (f32[256]{0:T(256)S(1)}, f32[256]{0:T(256)S(1)}, u32[]{:S(2)}, u32[]{:S(2)}) collective-permute-start(f32[256]{0:T(256)S(1)} %add.157), channel_id=1, source_target_pairs={{0,4},{4,8},{8,12},{12,16},{16,20},{20,24},{24,28},{28,32},{32,36}... | collective-permute-start | bytes 3080 | tf_op jit(solution)/shard_map/ppermute | solution.py:15
  75.0 8.7 %collective-permute-start.8 = (f32[256]{0:T(256)S(1)}, f32[256]{0:T(256)S(1)}, u32[]{:S(2)}, u32[]{:S(2)}) collective-permute-start(f32[256]{0:T(256)S(1)} %add.158), channel_id=1, source_target_pairs={{0,8},{4,12},{8,16},{12,20},{16,24},{20,28},{24,32},{28,36},{32,40... | collective-permute-start | bytes 3080 | tf_op jit(solution)/shard_map/ppermute | solution.py:15
  81.0 8.3 %collective-permute-start.9 = (f32[256,256]{1,0:T(8,128)S(1)}, f32[256,256]{1,0:T(8,128)S(1)}, u32[]{:S(2)}, u32[]{:S(2)}) collective-permute-start(f32[256,256]{1,0:T(8,128)S(1)} %fusion.133), channel_id=1, source_target_pairs={{0,8},{4,12},{8,16},{12,20},{16,24},{20,28},{24,32},{28,36},{32,40... | collective-permute-start | bytes 786440 | tf_op jit(solution)/shard_map/ppermute | solution.py:15
  84.0 9.5 %collective-permute-start.10 = (f32[256]{0:T(256)S(1)}, f32[256]{0:T(256)S(1)}, u32[]{:S(2)}, u32[]{:S(2)}) collective-permute-start(f32[256]{0:T(256)S(1)} %add.159), channel_id=1, source_target_pairs={{0,16},{4,20},{8,24},{12,28},{16,32},{20,36},{24,40},{28,44},{32,4... | collective-permute-start | bytes 3080 | tf_op jit(solution)/shard_map/ppermute | solution.py:15
  89.6 9.8 %collective-permute-start.11 = (f32[256,256]{1,0:T(8,128)S(1)}, f32[256,256]{1,0:T(8,128)S(1)}, u32[]{:S(2)}, u32[]{:S(2)}) collective-permute-start(f32[256,256]{1,0:T(8,128)S(1)} %fusion.135), channel_id=1, source_target_pairs={{0,16},{4,20},{8,24},{12,28},{16,32},{20,36},{24,40},{28,44},{32,4... | collective-permute-start | bytes 786440 | tf_op jit(solution)/shard_map/ppermute | solution.py:15
  94.4 9.0 %collective-permute-start.12 = (f32[256]{0:T(256)}, f32[256]{0:T(256)}, u32[]{:S(2)}, u32[]{:S(2)}) collective-permute-start(f32[256]{0:T(256)} %add.160), channel_id=1, source_target_pairs={{0,32},{4,36},{8,40},{12,44},{16,48},{20,52},{24,56},{28,60},{32,6... | collective-permute-start | bytes 3080 | tf_op jit(solution)/shard_map/ppermute | solution.py:15
  99.8 8.4 %collective-permute-start.13 = (f32[256,256]{1,0:T(8,128)S(1)}, f32[256,256]{1,0:T(8,128)}, u32[]{:S(2)}, u32[]{:S(2)}) collective-permute-start(f32[256,256]{1,0:T(8,128)S(1)} %fusion.137), channel_id=1, source_target_pairs={{0,32},{4,36},{8,40},{12,44},{16,48},{20,52},{24,56},{28,60},{32,6... | collective-permute-start | bytes 786440 | tf_op jit(solution)/shard_map/ppermute | solution.py:15
  105.1 4.4 %collective-permute-start.14 = (f32[256]{0:T(256)S(1)}, f32[256]{0:T(256)S(1)}, u32[]{:S(2)}, u32[]{:S(2)}) collective-permute-start(f32[256]{0:T(256)S(1)} %add.161), channel_id=1, source_target_pairs={{0,64},{4,68},{8,72},{12,76},{16,80},{20,84},{24,88},{28,92},{32,9... | collective-permute-start | bytes 3080 | tf_op jit(solution)/shard_map/ppermute | solution.py:15
  125.6 9.1 %collective-permute-start.16 = (f32[256]{0:T(256)S(1)}, f32[256]{0:T(256)S(1)}, u32[]{:S(2)}, u32[]{:S(2)}) collective-permute-start(f32[256]{0:T(256)S(1)} %select_add_fusion), channel_id=1, source_target_pairs={{8,0},{12,4},{16,8},{20,12},{24,16},{28,20},{32,24},{36,28},{40,32... | collective-permute-start | bytes 3080 | tf_op jit(solution)/shard_map/ppermute | solution.py:19
  127.7 7.2 %collective-permute-start.15 = (f32[256]{0:T(256)S(1)}, f32[256]{0:T(256)S(1)}, u32[]{:S(2)}, u32[]{:S(2)}) collective-permute-start(f32[256]{0:T(256)S(1)} %select_add_fusion), channel_id=1, source_target_pairs={{4,0},{8,4},{12,8},{16,12},{20,16},{24,20},{28,24},{32,28},{36,32}... | collective-permute-start | bytes 3080 | tf_op jit(solution)/shard_map/ppermute | solution.py:19
  135.0 7.6 %collective-permute-start.17 = (f32[256]{0:T(256)S(1)}, f32[256]{0:T(256)S(1)}, u32[]{:S(2)}, u32[]{:S(2)}) collective-permute-start(f32[256]{0:T(256)S(1)} %add.179), channel_id=1, source_target_pairs={{8,0},{12,4},{16,8},{20,12},{24,16},{28,20},{32,24},{36,28},{40,32... | collective-permute-start | bytes 3080 | tf_op jit(solution)/shard_map/ppermute | solution.py:19
  142.8 7.9 %collective-permute-start.18 = (f32[256]{0:T(256)S(1)}, f32[256]{0:T(256)S(1)}, u32[]{:S(2)}, u32[]{:S(2)}) collective-permute-start(f32[256]{0:T(256)S(1)} %add.180), channel_id=1, source_target_pairs={{16,0},{20,4},{24,8},{28,12},{32,16},{36,20},{40,24},{44,28},{48,3... | collective-permute-start | bytes 3080 | tf_op jit(solution)/shard_map/ppermute | solution.py:19
  151.0 5.5 %collective-permute-start.19 = (f32[256]{0:T(256)S(1)}, f32[256]{0:T(256)S(1)}, u32[]{:S(2)}, u32[]{:S(2)}) collective-permute-start(f32[256]{0:T(256)S(1)} %add.181), channel_id=1, source_target_pairs={{32,0},{36,4},{40,8},{44,12},{48,16},{52,20},{56,24},{60,28},{64,3... | collective-permute-start | bytes 3080 | tf_op jit(solution)/shard_map/ppermute | solution.py:19
  156.8 7.0 %collective-permute-start.20 = (f32[256]{0:T(256)S(1)}, f32[256]{0:T(256)S(1)}, u32[]{:S(2)}, u32[]{:S(2)}) collective-permute-start(f32[256]{0:T(256)S(1)} %add.182), channel_id=1, source_target_pairs={{64,0},{68,4},{72,8},{76,12},{80,16},{84,20},{88,24},{92,28},{96,3... | collective-permute-start | bytes 3080 | tf_op jit(solution)/shard_map/ppermute | solution.py:19

commit v7 on v3

--- a/solution.py
+++ b/solution.py
@@ -106,13 +106,12 @@
     partial = encode(fields, above, conv_in, conv_mid, obs_gain, bands)
     increments = sum_bands(partial, bands).reshape(bands, hours, modes)
 
-    state = increments[:, 0]
-    local = [state]
+    gate_cols = jnp.transpose(gates, (1, 2, 0))
+    step_cols = jnp.transpose(increments, (1, 2, 0))
+    state = step_cols[0]
     for i in range(1, hours):
-        state = gates[:, i] * dot(state, transition_t) + increments[:, i]
-        local.append(state)
-    local = jnp.stack(local, axis=1)
-    ends = local[:, -1]
+        state = gate_cols[i] * dot(transition, state) + step_cols[i]
+    ends = state.T
     block_sum = ends[0]
     for s in range(1, bands):
         block_sum = dot(phis[s], block_sum) + ends[s]
@@ -121,12 +120,12 @@
     starts = [carry]
     for s in range(bands - 1):
         starts.append(dot(phis[s], starts[-1]) + ends[s])
-    state = jnp.stack(starts)
+    state = jnp.stack(starts).T
     filtered = []
     for i in range(hours):
-        state = gates[:, i] * dot(state, transition_t) + increments[:, i]
+        state = gate_cols[i] * dot(transition, state) + step_cols[i]
         filtered.append(state)
-    filtered = jnp.stack(filtered, axis=1)
+    filtered = jnp.transpose(jnp.stack(filtered), (2, 0, 1))
 
     powers = [jnp.eye(modes, dtype=jnp.float32), back_gain]
     while len(powers) <= hours:

time: 164 us -> 164 us (level)
    unnamed x136 -> x72, local copies, waits for them, and re-layouts: 16.1 us -> 15.4 us
  transfers between devices with their start and end apart: 21 -> 21, of which waited for: 9 -> 9; matrix products, arithmetic and copies ran while one was open for 26% -> 27% of each run, Pallas kernels for 0% -> 0%
where the time goes in v7:
time: 164 us; the launch traced here: 163 us
  starting transfers between devices  52.7 us (32%)
  matrix products  51.3 us (31%)
  waiting for transfers between devices  31.4 us (19%)
  local copies, waits for them, and re-layouts  21.4 us (13%)
  other arithmetic  4.89 us (3%)
    ppermute x12, starting transfers between devices, shift_down(): lax.ppermute(value, axis, [(i, i + steps) for i in range(count - steps)])  36.7 us
    dot_general x55, matrix products, dot(): return jnp.dot(a, b, precision=precise)  26.1 us
    ppermute x6, waiting for transfers between devices, shift_up(): lax.ppermute(value, axis, [(i + steps, i) for i in range(count - steps)])  23.8 us
    unnamed x72, local copies, waits for them, and re-layouts  15.4 us
    ppermute x6, starting transfers between devices, shift_up(): lax.ppermute(value, axis, [(i + steps, i) for i in range(count - steps)])  11 us
    conv_general_dilated x1, matrix products, conv_stride(): lax.conv_general_dilated(images, kernel, (2, 2), ((0, 0), (1, 1)), dimens...  9.43 us
    ppermute x12, waiting for transfers between devices, shift_down(): lax.ppermute(value, axis, [(i, i + steps) for i in range(count - steps)])  7.67 us
    dot_general x7, matrix products, per_device(): jnp.einsum('ab,sbc->sac', transition, phis, precision=precise)  7.14 us
  transfers between devices with their start and end apart: 21, of which 9 were waited for; matrix products, arithmetic and copies ran while one was open for 27% of the time, Pallas kernels for 0%

profile of v7, /device:TPU:14, one launch (start us, length us, event | category | flops | bytes accessed | tf_op | source)
XLA Modules:
  0.0 163.2 jit_solution(6232258725360057322)
XLA Ops:
  0.7 1.6 slice.191
  2.3 0.8 copy.73
  3.1 4.6 %collective-permute-start = (bf16[32,8,3,256]{3,1,2,0:T(8,128)(2,1)}, bf16[32,8,3,256]{3,1,2,0:T(8,128)(2,1)}, u32[]{:S(2)}, u32[]{:S(2)}) collective-permute-start(bf16[32,8,3,256]{3,1,2,0:T(8,128)(2,1)} %copy.73), channel_id=1, source_target_pairs={{0,1},{1,2},{2,3},{4,5},{5,6},{6,7},{8,9},{9,10},{10,11},{12,13},{... | collective-permute-start | bytes 1179656 | tf_op jit(solution)/shard_map/ppermute | solution.py:15
  8.6 1.0 fusion.23
  9.6 1.0 fusion.22
  10.6 1.0 fusion.21
  11.7 1.0 fusion.20
  12.7 1.0 fusion.19
  13.7 1.0 fusion.18
  14.8 1.0 fusion.17
  17.0 1.3 fusion.93
  19.2 1.3 constant_dynamic-update-slice_fusion.15
  21.1 1.0 convolution_bitcast_fusion
  22.1 0.8 fusion.77
  24.4 1.1 fusion.167
  26.2 5.1 %copy.46 = bf16[32,8,8,256]{0,1,3,2:T(8,128)(2,1)} copy(bf16[32,8,8,256]{3,2,1,0:T(8,128)(2,1)} %param.7) | data formatting | bytes 2097152 | tf_op args[0]
  31.9 1.9 %bitcast_dynamic-update-slice_fusion = (f32[256,2048]{1,0:T(8,128)}, f32[2048,256]{1,0:T(8,128)}) fusion(f32[4,256,256]{1,2,0:T(8,128)S(1)} %convolution_bitcast_fusion, f32[2048,256]{1,0:T(8,128)} %fusion.97, f32[2,256,256]{1,2,0:T(8,128)} %copy-done.2), kind=kLoop, calls=%fused_computation.102 | loop fusion | bytes 1048576
  33.8 3.0 %copy.45 = bf16[32,8,3,256]{0,1,3,2:T(8,128)(2,1)} copy(bf16[32,8,3,256]{3,1,2,0:T(8,128)(2,1)} %collective-permute-done) | data formatting | bytes 786432 | tf_op jit(solution)/shard_map/optimization_barrier | solution.py:105
  36.7 9.4 %fusion.4 = f32[32,2,64,128]{3,0,2,1:T(8,128)} fusion(bf16[128,64,3,3]{0,1,3,2:T(8,128)(2,1)S(1)} %copy-done, pred[5]{0:T(512)(128)(4,1)} %compare_and_fusion, bf16[64,8,3,3]{0,1,3,2:T(8,128)(2,1)} %param.8, bf16[32,8,8,256]{0,1,3,2:T(8,128)(2,1)} %copy.46, bf16[32,8,3,256]{0,1,3,2:T(8,128)(2,1)} %copy.45), kind=kOutput, calls=%fused_computation.5 | convolution fusion | flops 799834112 | bytes 3695621 | tf_op jit(solution)/shard_map/conv_general_dilated | solution.py:23
  46.2 5.4 %convolution_bitcast_fusion.3 = f32[32,256]{1,0:T(8,128)S(1)} fusion(bf16[2,64,128,256]{3,2,1,0:T(8,128)(2,1)} %param.10, f32[32,2,64,128]{3,0,2,1:T(8,128)} %fusion.4), kind=kOutput, calls=%fused_computation.33 | convolution fusion | flops 271056896 | bytes 10518528 | tf_op jit(solution)/shard_map/shwc,hwcm->sm/dot_general | solution.py:45
  51.6 0.8 collective-permute-start.2
  52.4 1.3 collective-permute-start.3
  53.6 2.9 %collective-permute-start.1 = (f32[32,256]{1,0:T(8,128)S(1)}, f32[32,256]{1,0:T(8,128)S(1)}, u32[]{:S(2)}, u32[]{:S(2)}) collective-permute-start(f32[32,256]{1,0:T(8,128)S(1)} %convolution_bitcast_fusion.3), channel_id=1, source_target_pairs={{0,2},{1,3},{2,0},{3,1},{4,6},{5,7},{6,4},{7,5},{8,10},{9,11},{10,... | collective-permute-start | bytes 98312 | tf_op jit(solution)/shard_map/ppermute | solution.py:49
  56.5 0.9 fusion.102
  57.5 1.9 %collective-permute-start.5 = (f32[256,256]{1,0:T(8,128)S(1)}, f32[256,256]{1,0:T(8,128)S(1)}, u32[]{:S(2)}, u32[]{:S(2)}) collective-permute-start(f32[256,256]{1,0:T(8,128)S(1)} %copy-done.18), channel_id=1, source_target_pairs={{0,4},{4,8},{8,12},{12,16},{16,20},{20,24},{24,28},{28,32},{32,36}... | collective-permute-start | bytes 786440 | tf_op jit(solution)/shard_map/ppermute | solution.py:15
  59.4 3.4 %collective-permute-start.7 = (f32[256,256]{1,0:T(8,128)S(1)}, f32[256,256]{1,0:T(8,128)S(1)}, u32[]{:S(2)}, u32[]{:S(2)}) collective-permute-start(f32[256,256]{1,0:T(8,128)S(1)} %copy-done.18), channel_id=1, source_target_pairs={{0,8},{4,12},{8,16},{12,20},{16,24},{20,28},{24,32},{28,36},{32,40... | collective-permute-start | bytes 786440 | tf_op jit(solution)/shard_map/ppermute | solution.py:15
  66.5 3.4 %collective-permute-start.6 = (f32[256]{0:T(256)S(1)}, f32[256]{0:T(256)S(1)}, u32[]{:S(2)}, u32[]{:S(2)}) collective-permute-start(f32[256]{0:T(256)S(1)} %add.157), channel_id=1, source_target_pairs={{0,8},{4,12},{8,16},{12,20},{16,24},{20,28},{24,32},{28,36},{32,40... | collective-permute-start | bytes 3080 | tf_op jit(solution)/shard_map/ppermute | solution.py:15
  69.9 0.9 fusion.100
  70.8 2.9 %collective-permute-start.4 = (f32[256]{0:T(256)S(1)}, f32[256]{0:T(256)S(1)}, u32[]{:S(2)}, u32[]{:S(2)}) collective-permute-start(f32[256]{0:T(256)S(1)} %add.157), channel_id=1, source_target_pairs={{0,4},{4,8},{8,12},{12,16},{16,20},{20,24},{24,28},{28,32},{32,36}... | collective-permute-start | bytes 3080 | tf_op jit(solution)/shard_map/ppermute | solution.py:15
  74.0 1.7 %collective-permute-done.4 = f32[256]{0:T(256)S(1)} collective-permute-done((f32[256]{0:T(256)S(1)}, f32[256]{0:T(256)S(1)}, u32[]{:S(2)}, u32[]{:S(2)}) %collective-permute-start.4) | collective-permute-done | bytes 1056 | tf_op jit(solution)/shard_map/ppermute | solution.py:15
  75.7 5.8 %collective-permute-start.8 = (f32[256]{0:T(256)S(1)}, f32[256]{0:T(256)S(1)}, u32[]{:S(2)}, u32[]{:S(2)}) collective-permute-start(f32[256]{0:T(256)S(1)} %add.158), channel_id=1, source_target_pairs={{0,8},{4,12},{8,16},{12,20},{16,24},{20,28},{24,32},{28,36},{32,40... | collective-permute-start | bytes 3080 | tf_op jit(solution)/shard_map/ppermute | solution.py:15
  82.0 1.9 %collective-permute-start.9 = (f32[256,256]{1,0:T(8,128)S(1)}, f32[256,256]{1,0:T(8,128)S(1)}, u32[]{:S(2)}, u32[]{:S(2)}) collective-permute-start(f32[256,256]{1,0:T(8,128)S(1)} %fusion.151), channel_id=1, source_target_pairs={{0,8},{4,12},{8,16},{12,20},{16,24},{20,28},{24,32},{28,36},{32,40... | collective-permute-start | bytes 786440 | tf_op jit(solution)/shard_map/ppermute | solution.py:15
  83.9 0.9 fusion.98
  85.0 3.2 %collective-permute-start.10 = (f32[256]{0:T(256)S(1)}, f32[256]{0:T(256)S(1)}, u32[]{:S(2)}, u32[]{:S(2)}) collective-permute-start(f32[256]{0:T(256)S(1)} %add.159), channel_id=1, source_target_pairs={{0,16},{4,20},{8,24},{12,28},{16,32},{20,36},{24,40},{28,44},{32,4... | collective-permute-start | bytes 3080 | tf_op jit(solution)/shard_map/ppermute | solution.py:15
  88.2 2.0 %collective-permute-done.9 = f32[256,256]{1,0:T(8,128)S(1)} collective-permute-done((f32[256,256]{1,0:T(8,128)S(1)}, f32[256,256]{1,0:T(8,128)S(1)}, u32[]{:S(2)}, u32[]{:S(2)}) %collective-permute-start.9) | collective-permute-done | bytes 262176 | tf_op jit(solution)/shard_map/ppermute | solution.py:15
  90.6 2.9 %collective-permute-start.11 = (f32[256,256]{1,0:T(8,128)S(1)}, f32[256,256]{1,0:T(8,128)S(1)}, u32[]{:S(2)}, u32[]{:S(2)}) collective-permute-start(f32[256,256]{1,0:T(8,128)S(1)} %fusion.153), channel_id=1, source_target_pairs={{0,16},{4,20},{8,24},{12,28},{16,32},{20,36},{24,40},{28,44},{32,4... | collective-permute-start | bytes 786440 | tf_op jit(solution)/shard_map/ppermute | solution.py:15
  93.6 0.8 bitcast_dynamic-update-slice_fusion.1
  95.2 2.1 %collective-permute-start.12 = (f32[256]{0:T(256)}, f32[256]{0:T(256)}, u32[]{:S(2)}, u32[]{:S(2)}) collective-permute-start(f32[256]{0:T(256)} %add.160), channel_id=1, source_target_pairs={{0,32},{4,36},{8,40},{12,44},{16,48},{20,52},{24,56},{28,60},{32,6... | collective-permute-start | bytes 3080 | tf_op jit(solution)/shard_map/ppermute | solution.py:15
  97.4 3.0 %collective-permute-done.11 = f32[256,256]{1,0:T(8,128)S(1)} collective-permute-done((f32[256,256]{1,0:T(8,128)S(1)}, f32[256,256]{1,0:T(8,128)S(1)}, u32[]{:S(2)}, u32[]{:S(2)}) %collective-permute-start.11) | collective-permute-done | bytes 262176 | tf_op jit(solution)/shard_map/ppermute | solution.py:15
  100.4 1.1 fusion.155
  101.5 3.2 %collective-permute-start.13 = (f32[256,256]{1,0:T(8,128)}, f32[256,256]{1,0:T(8,128)}, u32[]{:S(2)}, u32[]{:S(2)}) collective-permute-start(f32[256,256]{1,0:T(8,128)} %fusion.155), channel_id=1, source_target_pairs={{0,32},{4,36},{8,40},{12,44},{16,48},{20,52},{24,56},{28,60},{32,6... | collective-permute-start | bytes 786440 | tf_op jit(solution)/shard_map/ppermute | solution.py:15
  104.7 1.1 convolution_bitcast_fusion.2
  105.8 1.2 fusion.156
  107.0 0.8 add.161
  107.8 1.3 collective-permute-start.14
  109.1 1.0 collective-permute-done.13
  110.0 1.4 fusion.157
  112.0 0.8 add.163
  117.1 1.3 fusion.15
  119.8 1.9 %collective-permute-start.16 = (f32[256]{0:T(256)S(1)}, f32[256]{0:T(256)S(1)}, u32[]{:S(2)}, u32[]{:S(2)}) collective-permute-start(f32[256]{0:T(256)S(1)} %select_add_fusion), channel_id=1, source_target_pairs={{8,0},{12,4},{16,8},{20,12},{24,16},{28,20},{32,24},{36,28},{40,32... | collective-permute-start | bytes 3080 | tf_op jit(solution)/shard_map/ppermute | solution.py:19
  121.8 0.8 fusion.96
  122.5 1.9 %collective-permute-start.15 = (f32[256]{0:T(256)S(1)}, f32[256]{0:T(256)S(1)}, u32[]{:S(2)}, u32[]{:S(2)}) collective-permute-start(f32[256]{0:T(256)S(1)} %select_add_fusion), channel_id=1, source_target_pairs={{4,0},{8,4},{12,8},{16,12},{20,16},{24,20},{28,24},{32,28},{36,32}... | collective-permute-start | bytes 3080 | tf_op jit(solution)/shard_map/ppermute | solution.py:19
  124.5 5.1 %collective-permute-done.16 = f32[256]{0:T(256)S(1)} collective-permute-done((f32[256]{0:T(256)S(1)}, f32[256]{0:T(256)S(1)}, u32[]{:S(2)}, u32[]{:S(2)}) %collective-permute-start.16) | collective-permute-done | bytes 1056 | tf_op jit(solution)/shard_map/ppermute | solution.py:19
  129.9 1.9 %collective-permute-start.17 = (f32[256]{0:T(256)S(1)}, f32[256]{0:T(256)S(1)}, u32[]{:S(2)}, u32[]{:S(2)}) collective-permute-start(f32[256]{0:T(256)S(1)} %add.179), channel_id=1, source_target_pairs={{8,0},{12,4},{16,8},{20,12},{24,16},{28,20},{32,24},{36,28},{40,32... | collective-permute-start | bytes 3080 | tf_op jit(solution)/shard_map/ppermute | solution.py:19
  131.9 0.8 constant_dynamic-update-slice_fusion.16
  132.6 4.9 %collective-permute-done.17 = f32[256]{0:T(256)S(1)} collective-permute-done((f32[256]{0:T(256)S(1)}, f32[256]{0:T(256)S(1)}, u32[]{:S(2)}, u32[]{:S(2)}) %collective-permute-start.17) | collective-permute-done | bytes 1056 | tf_op jit(solution)/shard_map/ppermute | solution.py:19
  137.8 2.0 %collective-permute-start.18 = (f32[256]{0:T(256)S(1)}, f32[256]{0:T(256)S(1)}, u32[]{:S(2)}, u32[]{:S(2)}) collective-permute-start(f32[256]{0:T(256)S(1)} %add.180), channel_id=1, source_target_pairs={{16,0},{20,4},{24,8},{28,12},{32,16},{36,20},{40,24},{44,28},{48,3... | collective-permute-start | bytes 3080 | tf_op jit(solution)/shard_map/ppermute | solution.py:19
  139.8 0.8 bitcast_dynamic-update-slice_fusion.3
  140.5 5.2 %collective-permute-done.18 = f32[256]{0:T(256)S(1)} collective-permute-done((f32[256]{0:T(256)S(1)}, f32[256]{0:T(256)S(1)}, u32[]{:S(2)}, u32[]{:S(2)}) %collective-permute-start.18) | collective-permute-done | bytes 1056 | tf_op jit(solution)/shard_map/ppermute | solution.py:19
  146.0 2.0 %collective-permute-start.19 = (f32[256]{0:T(256)S(1)}, f32[256]{0:T(256)S(1)}, u32[]{:S(2)}, u32[]{:S(2)}) collective-permute-start(f32[256]{0:T(256)S(1)} %add.181), channel_id=1, source_target_pairs={{32,0},{36,4},{40,8},{44,12},{48,16},{52,20},{56,24},{60,28},{64,3... | collective-permute-start | bytes 3080 | tf_op jit(solution)/shard_map/ppermute | solution.py:19
  148.0 3.5 %collective-permute-done.19 = f32[256]{0:T(256)S(1)} collective-permute-done((f32[256]{0:T(256)S(1)}, f32[256]{0:T(256)S(1)}, u32[]{:S(2)}, u32[]{:S(2)}) %collective-permute-start.19) | collective-permute-done | bytes 1056 | tf_op jit(solution)/shard_map/ppermute | solution.py:19
  151.8 1.3 collective-permute-start.20
  153.8 5.0 %collective-permute-done.20 = f32[256]{0:T(256)S(1)} collective-permute-done((f32[256]{0:T(256)S(1)}, f32[256]{0:T(256)S(1)}, u32[]{:S(2)}, u32[]{:S(2)}) %collective-permute-start.20) | collective-permute-done | bytes 1056 | tf_op jit(solution)/shard_map/ppermute | solution.py:19
  159.9 2.7 %fusion.12 = f32[1,8,256]{2,0,1:T(1,128)S(1)} fusion(f32[32,8,8,256]{3,2,1,0:T(8,128)} %bitcast.175, s32[]{:T(128)S(6)} %select_n.26, f32[1,256]{1,0:T(1,128)S(1)} %bitcast.607, f32[1,256]{1,0:T(1,128)S(1)} %bitcast.619, f32[1,256]{1,0:T(1,128)S(1)} %bitcast.604, f32[1,256]{1,0:T(1,128)S(1)} %bitcast.600), kind=kOutput, calls=%fused_computation.9 | convolution fusion | flops 6292224 | bytes 2109444 | tf_op jit(solution)/shard_map/dot_general | solution.py:11
  (155 shorter events, 21.7 us)
Async XLA Ops:
  0.6 36.1 %copy-start = (bf16[128,64,3,3]{0,1,3,2:T(8,128)(2,1)S(1)}, bf16[128,64,3,3]{0,1,3,2:T(8,128)(2,1)}, u32[]{:S(2)}) copy-start(bf16[128,64,3,3]{0,1,3,2:T(8,128)(2,1)} %param.9) | copy-start | bytes 442372
  0.6 7.7 %copy-start.1 = (f32[256,256]{1,0:T(8,128)S(1)}, f32[256,256]{1,0:T(8,128)}, u32[]{:S(2)}) copy-start(f32[256,256]{1,0:T(8,128)} %param.11) | copy-start | bytes 786436
  0.7 7.8 %copy-start.19 = (f32[32,256]{1,0:T(8,128)S(1)}, f32[32,256]{1,0:T(8,128)}, u32[]{:S(2)}) copy-start(f32[32,256]{1,0:T(8,128)} %param.13) | copy-start | bytes 98308
  3.1 30.7 %collective-permute-start = (bf16[32,8,3,256]{3,1,2,0:T(8,128)(2,1)}, bf16[32,8,3,256]{3,1,2,0:T(8,128)(2,1)}, u32[]{:S(2)}, u32[]{:S(2)}) collective-permute-start(bf16[32,8,3,256]{3,1,2,0:T(8,128)(2,1)} %copy.73), channel_id=1, source_target_pairs={{0,1},{1,2},{2,3},{4,5},{5,6},{6,7},{8,9},{9,10},{10,11},{12,13},{... | collective-permute-start | bytes 1179656 | tf_op jit(solution)/shard_map/ppermute | solution.py:15
  14.8 3.6 %copy-start.9 = (f32[256,256]{1,0:T(8,128)S(1)}, f32[256,256]{1,0:T(8,128)}, u32[]{:S(2)}) copy-start(f32[256,256]{1,0:T(8,128)} %param.12) | copy-start | bytes 786436
  21.1 4.4 %copy-start.2 = (f32[2,256,256]{1,2,0:T(8,128)}, f32[2,256,256]{1,2,0:T(8,128)S(1)}, u32[]{:S(2)}) copy-start(f32[2,256,256]{1,2,0:T(8,128)S(1)} %convolution_bitcast_fusion.1) | copy-start | bytes 1572868
  23.6 2.6 %copy-start.7 = (f32[256,256]{1,0:T(8,128)}, f32[256,256]{1,0:T(8,128)S(1)}, u32[]{:S(2)}) copy-start(f32[256,256]{1,0:T(8,128)S(1)} %fusion.161) | copy-start | bytes 786436
  24.0 2.2 %copy-start.5 = (f32[256,256]{1,0:T(8,128)}, f32[256,256]{1,0:T(8,128)S(1)}, u32[]{:S(2)}) copy-start(f32[256,256]{1,0:T(8,128)S(1)} %fusion.163) | copy-start | bytes 786436
  46.2 11.3 %copy-start.20 = (f32[32,256]{1,0:T(8,128)S(1)}, f32[32,256]{1,0:T(8,128)}, u32[]{:S(2)}) copy-start(f32[32,256]{1,0:T(8,128)} %param.13) | copy-start | bytes 98308
  46.2 11.3 %copy-start.18 = (f32[256,256]{1,0:T(8,128)S(1)}, f32[256,256]{1,0:T(8,128)}, u32[]{:S(2)}) copy-start(f32[256,256]{1,0:T(8,128)} %fusion.93) | copy-start | bytes 786436
  51.6 11.3 %collective-permute-start.2 = (f32[32,256]{1,0:T(8,128)S(1)}, f32[32,256]{1,0:T(8,128)S(1)}, u32[]{:S(2)}, u32[]{:S(2)}) collective-permute-start(f32[32,256]{1,0:T(8,128)S(1)} %convolution_bitcast_fusion.3), channel_id=1, source_target_pairs={{0,3},{1,0},{2,1},{3,2},{4,7},{5,4},{6,5},{7,6},{8,11},{9,8},{10,9... | collective-permute-start | bytes 98312 | tf_op jit(solution)/shard_map/ppermute | solution.py:49
  52.4 10.4 %collective-permute-start.3 = (f32[32,256]{1,0:T(8,128)S(1)}, f32[32,256]{1,0:T(8,128)S(1)}, u32[]{:S(2)}, u32[]{:S(2)}) collective-permute-start(f32[32,256]{1,0:T(8,128)S(1)} %convolution_bitcast_fusion.3), channel_id=1, source_target_pairs={{0,1},{1,2},{2,3},{3,0},{4,5},{5,6},{6,7},{7,4},{8,9},{9,10},{10,1... | collective-permute-start | bytes 98312 | tf_op jit(solution)/shard_map/ppermute | solution.py:49
  53.6 9.2 %collective-permute-start.1 = (f32[32,256]{1,0:T(8,128)S(1)}, f32[32,256]{1,0:T(8,128)S(1)}, u32[]{:S(2)}, u32[]{:S(2)}) collective-permute-start(f32[32,256]{1,0:T(8,128)S(1)} %convolution_bitcast_fusion.3), channel_id=1, source_target_pairs={{0,2},{1,3},{2,0},{3,1},{4,6},{5,7},{6,4},{7,5},{8,10},{9,11},{10,... | collective-permute-start | bytes 98312 | tf_op jit(solution)/shard_map/ppermute | solution.py:49
  57.5 24.5 %copy-start.14 = (f32[4,8,256]{2,0,1:T(4,128)}, f32[4,8,256]{2,0,1:T(4,128)S(1)}, u32[]{:S(2)}) copy-start(f32[4,8,256]{2,0,1:T(4,128)S(1)} %copy.93) | copy-start | bytes 98308
  57.5 16.3 %collective-permute-start.5 = (f32[256,256]{1,0:T(8,128)S(1)}, f32[256,256]{1,0:T(8,128)S(1)}, u32[]{:S(2)}, u32[]{:S(2)}) collective-permute-start(f32[256,256]{1,0:T(8,128)S(1)} %copy-done.18), channel_id=1, source_target_pairs={{0,4},{4,8},{8,12},{12,16},{16,20},{20,24},{24,28},{28,32},{32,36}... | collective-permute-start | bytes 786440 | tf_op jit(solution)/shard_map/ppermute | solution.py:15
  59.4 22.1 %collective-permute-start.7 = (f32[256,256]{1,0:T(8,128)S(1)}, f32[256,256]{1,0:T(8,128)S(1)}, u32[]{:S(2)}, u32[]{:S(2)}) collective-permute-start(f32[256,256]{1,0:T(8,128)S(1)} %copy-done.18), channel_id=1, source_target_pairs={{0,8},{4,12},{8,16},{12,20},{16,24},{20,28},{24,32},{28,36},{32,40... | collective-permute-start | bytes 786440 | tf_op jit(solution)/shard_map/ppermute | solution.py:15
  62.9 19.1 %copy-start.16 = (f32[4,8,256]{2,0,1:T(4,128)}, f32[4,8,256]{2,0,1:T(4,128)S(1)}, u32[]{:S(2)}) copy-start(f32[4,8,256]{2,0,1:T(4,128)S(1)} %copy.92) | copy-start | bytes 98308
  66.0 17.9 %copy-start.21 = (f32[1,256]{1,0:T(1,128)}, f32[1,256]{1,0:T(1,128)S(1)}, u32[]{:S(2)}) copy-start(f32[1,256]{1,0:T(1,128)S(1)} %get-tuple-element.26) | copy-start | bytes 3076
  66.0 17.9 %copy-start.23 = (f32[1,256]{1,0:T(1,128)}, f32[1,256]{1,0:T(1,128)S(1)}, u32[]{:S(2)}) copy-start(f32[1,256]{1,0:T(1,128)S(1)} %get-tuple-element.27) | copy-start | bytes 3076
  66.2 27.4 %copy-start.3 = (f32[2,256,256]{1,2,0:T(8,128)S(1)}, f32[2,256,256]{1,2,0:T(8,128)}, u32[]{:S(2)}) copy-start(f32[2,256,256]{1,2,0:T(8,128)} %copy-done.2) | copy-start | bytes 1572868
  66.5 7.3 %collective-permute-start.6 = (f32[256]{0:T(256)S(1)}, f32[256]{0:T(256)S(1)}, u32[]{:S(2)}, u32[]{:S(2)}) collective-permute-start(f32[256]{0:T(256)S(1)} %add.157), channel_id=1, source_target_pairs={{0,8},{4,12},{8,16},{12,20},{16,24},{20,28},{24,32},{28,36},{32,40... | collective-permute-start | bytes 3080 | tf_op jit(solution)/shard_map/ppermute | solution.py:15
  70.8 4.9 %collective-permute-start.4 = (f32[256]{0:T(256)S(1)}, f32[256]{0:T(256)S(1)}, u32[]{:S(2)}, u32[]{:S(2)}) collective-permute-start(f32[256]{0:T(256)S(1)} %add.157), channel_id=1, source_target_pairs={{0,4},{4,8},{8,12},{12,16},{16,20},{20,24},{24,28},{28,32},{32,36}... | collective-permute-start | bytes 3080 | tf_op jit(solution)/shard_map/ppermute | solution.py:15
  75.7 29.0 %copy-start.10 = (f32[256,256]{1,0:T(8,128)S(1)}, f32[256,256]{1,0:T(8,128)}, u32[]{:S(2)}) copy-start(f32[256,256]{1,0:T(8,128)} %param.12) | copy-start | bytes 786436
  75.7 9.1 %collective-permute-start.8 = (f32[256]{0:T(256)S(1)}, f32[256]{0:T(256)S(1)}, u32[]{:S(2)}, u32[]{:S(2)}) collective-permute-start(f32[256]{0:T(256)S(1)} %add.158), channel_id=1, source_target_pairs={{0,8},{4,12},{8,16},{12,20},{16,24},{20,28},{24,32},{28,36},{32,40... | collective-permute-start | bytes 3080 | tf_op jit(solution)/shard_map/ppermute | solution.py:15
  82.0 8.3 %collective-permute-start.9 = (f32[256,256]{1,0:T(8,128)S(1)}, f32[256,256]{1,0:T(8,128)S(1)}, u32[]{:S(2)}, u32[]{:S(2)}) collective-permute-start(f32[256,256]{1,0:T(8,128)S(1)} %fusion.151), channel_id=1, source_target_pairs={{0,8},{4,12},{8,16},{12,20},{16,24},{20,28},{24,32},{28,36},{32,40... | collective-permute-start | bytes 786440 | tf_op jit(solution)/shard_map/ppermute | solution.py:15
  85.0 9.3 %collective-permute-start.10 = (f32[256]{0:T(256)S(1)}, f32[256]{0:T(256)S(1)}, u32[]{:S(2)}, u32[]{:S(2)}) collective-permute-start(f32[256]{0:T(256)S(1)} %add.159), channel_id=1, source_target_pairs={{0,16},{4,20},{8,24},{12,28},{16,32},{20,36},{24,40},{28,44},{32,4... | collective-permute-start | bytes 3080 | tf_op jit(solution)/shard_map/ppermute | solution.py:15
  90.6 9.8 %collective-permute-start.11 = (f32[256,256]{1,0:T(8,128)S(1)}, f32[256,256]{1,0:T(8,128)S(1)}, u32[]{:S(2)}, u32[]{:S(2)}) collective-permute-start(f32[256,256]{1,0:T(8,128)S(1)} %fusion.153), channel_id=1, source_target_pairs={{0,16},{4,20},{8,24},{12,28},{16,32},{20,36},{24,40},{28,44},{32,4... | collective-permute-start | bytes 786440 | tf_op jit(solution)/shard_map/ppermute | solution.py:15
  95.2 10.5 %collective-permute-start.12 = (f32[256]{0:T(256)}, f32[256]{0:T(256)}, u32[]{:S(2)}, u32[]{:S(2)}) collective-permute-start(f32[256]{0:T(256)} %add.160), channel_id=1, source_target_pairs={{0,32},{4,36},{8,40},{12,44},{16,48},{20,52},{24,56},{28,60},{32,6... | collective-permute-start | bytes 3080 | tf_op jit(solution)/shard_map/ppermute | solution.py:15
  101.5 8.6 %collective-permute-start.13 = (f32[256,256]{1,0:T(8,128)}, f32[256,256]{1,0:T(8,128)}, u32[]{:S(2)}, u32[]{:S(2)}) collective-permute-start(f32[256,256]{1,0:T(8,128)} %fusion.155), channel_id=1, source_target_pairs={{0,32},{4,36},{8,40},{12,44},{16,48},{20,52},{24,56},{28,60},{32,6... | collective-permute-start | bytes 786440 | tf_op jit(solution)/shard_map/ppermute | solution.py:15
  105.7 8.1 %copy-start.22 = (f32[1,256]{1,0:T(1,128)S(1)}, f32[1,256]{1,0:T(1,128)}, u32[]{:S(2)}) copy-start(f32[1,256]{1,0:T(1,128)} %copy-done.21) | copy-start | bytes 3076
  105.7 8.2 %copy-start.15 = (f32[4,8,256]{2,0,1:T(4,128)S(1)}, f32[4,8,256]{2,0,1:T(4,128)}, u32[]{:S(2)}) copy-start(f32[4,8,256]{2,0,1:T(4,128)} %copy-done.14) | copy-start | bytes 98308
  105.7 8.2 %copy-start.17 = (f32[4,8,256]{2,0,1:T(4,128)S(1)}, f32[4,8,256]{2,0,1:T(4,128)}, u32[]{:S(2)}) copy-start(f32[4,8,256]{2,0,1:T(4,128)} %copy-done.16) | copy-start | bytes 98308
  107.0 9.6 %copy-start.13 = (f32[256,256,1]{1,0,2:T(8,128)S(1)}, f32[256,256,1]{1,0,2:T(8,128)}, u32[]{:S(2)}) copy-start(f32[256,256,1]{1,0,2:T(8,128)} %convolution_bitcast_fusion.2) | copy-start | bytes 786436
  107.8 3.7 %collective-permute-start.14 = (f32[256]{0:T(256)S(1)}, f32[256]{0:T(256)S(1)}, u32[]{:S(2)}, u32[]{:S(2)}) collective-permute-start(f32[256]{0:T(256)S(1)} %add.161), channel_id=1, source_target_pairs={{0,64},{4,68},{8,72},{12,76},{16,80},{20,84},{24,88},{28,92},{32,9... | collective-permute-start | bytes 3080 | tf_op jit(solution)/shard_map/ppermute | solution.py:15
  111.5 5.6 %copy-start.11 = (f32[2048,256]{1,0:T(8,128)S(1)}, f32[2048,256]{1,0:T(8,128)}, u32[]{:S(2)}) copy-start(f32[2048,256]{1,0:T(8,128)} %get-tuple-element.7) | copy-start | bytes 6291460
  116.9 4.8 %copy-start.4 = (f32[2,256,256]{1,2,0:T(8,128)S(1)}, f32[2,256,256]{1,2,0:T(8,128)}, u32[]{:S(2)}) copy-start(f32[2,256,256]{1,2,0:T(8,128)} %copy-done.2) | copy-start | bytes 1572868
  117.1 20.5 %copy-start.8 = (f32[256,256]{1,0:T(8,128)S(1)}, f32[256,256]{1,0:T(8,128)}, u32[]{:S(2)}) copy-start(f32[256,256]{1,0:T(8,128)} %copy-done.7) | copy-start | bytes 786436
  118.4 27.3 %copy-start.6 = (f32[256,256]{1,0:T(8,128)S(1)}, f32[256,256]{1,0:T(8,128)}, u32[]{:S(2)}) copy-start(f32[256,256]{1,0:T(8,128)} %copy-done.5) | copy-start | bytes 786436
  118.4 40.4 %copy-start.12 = (f32[256,256]{1,0:T(8,128)S(1)}, f32[256,256]{1,0:T(8,128)}, u32[]{:S(2)}) copy-start(f32[256,256]{1,0:T(8,128)} %fusion.167) | copy-start | bytes 786436
  119.8 9.8 %collective-permute-start.16 = (f32[256]{0:T(256)S(1)}, f32[256]{0:T(256)S(1)}, u32[]{:S(2)}, u32[]{:S(2)}) collective-permute-start(f32[256]{0:T(256)S(1)} %select_add_fusion), channel_id=1, source_target_pairs={{8,0},{12,4},{16,8},{20,12},{24,16},{28,20},{32,24},{36,28},{40,32... | collective-permute-start | bytes 3080 | tf_op jit(solution)/shard_map/ppermute | solution.py:19
  122.5 7.3 %collective-permute-start.15 = (f32[256]{0:T(256)S(1)}, f32[256]{0:T(256)S(1)}, u32[]{:S(2)}, u32[]{:S(2)}) collective-permute-start(f32[256]{0:T(256)S(1)} %select_add_fusion), channel_id=1, source_target_pairs={{4,0},{8,4},{12,8},{16,12},{20,16},{24,20},{28,24},{32,28},{36,32}... | collective-permute-start | bytes 3080 | tf_op jit(solution)/shard_map/ppermute | solution.py:19
  129.9 7.6 %collective-permute-start.17 = (f32[256]{0:T(256)S(1)}, f32[256]{0:T(256)S(1)}, u32[]{:S(2)}, u32[]{:S(2)}) collective-permute-start(f32[256]{0:T(256)S(1)} %add.179), channel_id=1, source_target_pairs={{8,0},{12,4},{16,8},{20,12},{24,16},{28,20},{32,24},{36,28},{40,32... | collective-permute-start | bytes 3080 | tf_op jit(solution)/shard_map/ppermute | solution.py:19
  137.8 7.9 %collective-permute-start.18 = (f32[256]{0:T(256)S(1)}, f32[256]{0:T(256)S(1)}, u32[]{:S(2)}, u32[]{:S(2)}) collective-permute-start(f32[256]{0:T(256)S(1)} %add.180), channel_id=1, source_target_pairs={{16,0},{20,4},{24,8},{28,12},{32,16},{36,20},{40,24},{44,28},{48,3... | collective-permute-start | bytes 3080 | tf_op jit(solution)/shard_map/ppermute | solution.py:19
  146.0 5.5 %collective-permute-start.19 = (f32[256]{0:T(256)S(1)}, f32[256]{0:T(256)S(1)}, u32[]{:S(2)}, u32[]{:S(2)}) collective-permute-start(f32[256]{0:T(256)S(1)} %add.181), channel_id=1, source_target_pairs={{32,0},{36,4},{40,8},{44,12},{48,16},{52,20},{56,24},{60,28},{64,3... | collective-permute-start | bytes 3080 | tf_op jit(solution)/shard_map/ppermute | solution.py:19
  151.8 7.0 %collective-permute-start.20 = (f32[256]{0:T(256)S(1)}, f32[256]{0:T(256)S(1)}, u32[]{:S(2)}, u32[]{:S(2)}) collective-permute-start(f32[256]{0:T(256)S(1)} %add.182), channel_id=1, source_target_pairs={{64,0},{68,4},{72,8},{76,12},{80,16},{84,20},{88,24},{92,28},{96,3... | collective-permute-start | bytes 3080 | tf_op jit(solution)/shard_map/ppermute | solution.py:19

commit v8 on v7

--- a/solution.py
+++ b/solution.py
@@ -96,7 +96,7 @@
 
     phis = gates[:, 0, :, None] * transition[None]
     for i in range(1, hours):
-        phis = gates[:, i, :, None] * jnp.einsum("ab,sbc->sac", transition, phis, precision=precise)
+        phis = gates[:, i, :, None] * jnp.einsum("ab,sbc->sac", transition, phis, precision=lax.Precision.HIGH)
     block_phi = phis[0]
     for s in range(1, bands):
         block_phi = dot(phis[s], block_phi)

time: 164 us -> 161 us (0.982)
  matrix products: 51.3 us -> 48.3 us
    dot_general x7, matrix products: 7.14 us -> 4.32 us  [per_device(): jnp.einsum('ab,sbc->sac', transition, phis, precision=lax.Precision.HIGH)]
  transfers between devices with their start and end apart: 21 -> 21, of which waited for: 9 -> 9; matrix products, arithmetic and copies ran while one was open for 27% -> 26% of each run, Pallas kernels for 0% -> 0%
where the time goes in v8:
time: 161 us; the launch traced here: 160 us
  starting transfers between devices  52.7 us (33%)
  matrix products  48.3 us (30%)
  waiting for transfers between devices  31.4 us (20%)
  local copies, waits for them, and re-layouts  21.4 us (13%)
  other arithmetic  4.89 us (3%)
    ppermute x12, starting transfers between devices, shift_down(): lax.ppermute(value, axis, [(i, i + steps) for i in range(count - steps)])  36.7 us
    dot_general x55, matrix products, dot(): return jnp.dot(a, b, precision=precise)  25.9 us
    ppermute x6, waiting for transfers between devices, shift_up(): lax.ppermute(value, axis, [(i + steps, i) for i in range(count - steps)])  23.9 us
    unnamed x72, local copies, waits for them, and re-layouts  15.4 us
    ppermute x6, starting transfers between devices, shift_up(): lax.ppermute(value, axis, [(i + steps, i) for i in range(count - steps)])  11.1 us
    conv_general_dilated x1, matrix products, conv_stride(): lax.conv_general_dilated(images, kernel, (2, 2), ((0, 0), (1, 1)), dimens...  9.43 us
    ppermute x12, waiting for transfers between devices, shift_down(): lax.ppermute(value, axis, [(i, i + steps) for i in range(count - steps)])  7.45 us
    dot_general x1, matrix products, encode(): jnp.einsum('shwc,hwcm->sm', encoded, obs_gain, preferred_element_type=jnp...  5.38 us
  transfers between devices with their start and end apart: 21, of which 9 were waited for; matrix products, arithmetic and copies ran while one was open for 26% of the time, Pallas kernels for 0%

profile of v8, /device:TPU:14, one launch (start us, length us, event | category | flops | bytes accessed | tf_op | source)
XLA Modules:
  0.0 160.2 jit_solution(10921636167400098701)
XLA Ops:
  0.7 1.6 slice.191
  2.3 0.8 copy.73
  3.1 4.6 %collective-permute-start = (bf16[32,8,3,256]{3,1,2,0:T(8,128)(2,1)}, bf16[32,8,3,256]{3,1,2,0:T(8,128)(2,1)}, u32[]{:S(2)}, u32[]{:S(2)}) collective-permute-start(bf16[32,8,3,256]{3,1,2,0:T(8,128)(2,1)} %copy.73), channel_id=1, source_target_pairs={{0,1},{1,2},{2,3},{4,5},{5,6},{6,7},{8,9},{9,10},{10,11},{12,13},{... | collective-permute-start | bytes 1179656 | tf_op jit(solution)/shard_map/ppermute | solution.py:15
  7.6 0.7 convert_dynamic-update-slice_fusion
  9.2 0.6 fusion.22
  10.5 0.6 fusion.20
  12.4 0.6 fusion.17
  14.2 1.3 fusion.93
  15.6 0.7 bitcast_dynamic-update-slice_fusion.4
  16.4 1.3 constant_dynamic-update-slice_fusion.15
  18.3 1.0 convolution_bitcast_fusion
  21.4 1.1 fusion.167
  22.5 0.7 fusion.97
  23.2 5.1 %copy.46 = bf16[32,8,8,256]{0,1,3,2:T(8,128)(2,1)} copy(bf16[32,8,8,256]{3,2,1,0:T(8,128)(2,1)} %param.7) | data formatting | bytes 2097152 | tf_op args[0]
  28.9 1.9 %bitcast_dynamic-update-slice_fusion = (f32[256,2048]{1,0:T(8,128)}, f32[2048,256]{1,0:T(8,128)}) fusion(f32[4,256,256]{1,2,0:T(8,128)S(1)} %convolution_bitcast_fusion, f32[2048,256]{1,0:T(8,128)} %fusion.97, f32[2,256,256]{1,2,0:T(8,128)} %copy-done.2), kind=kLoop, calls=%fused_computation.102 | loop fusion | bytes 1048576
  30.8 3.0 %copy.45 = bf16[32,8,3,256]{0,1,3,2:T(8,128)(2,1)} copy(bf16[32,8,3,256]{3,1,2,0:T(8,128)(2,1)} %collective-permute-done) | data formatting | bytes 786432 | tf_op jit(solution)/shard_map/optimization_barrier | solution.py:105
  33.7 9.4 %fusion.4 = f32[32,2,64,128]{3,0,2,1:T(8,128)} fusion(bf16[128,64,3,3]{0,1,3,2:T(8,128)(2,1)S(1)} %copy-done, pred[5]{0:T(512)(128)(4,1)} %compare_and_fusion, bf16[64,8,3,3]{0,1,3,2:T(8,128)(2,1)} %param.8, bf16[32,8,8,256]{0,1,3,2:T(8,128)(2,1)} %copy.46, bf16[32,8,3,256]{0,1,3,2:T(8,128)(2,1)} %copy.45), kind=kOutput, calls=%fused_computation.5 | convolution fusion | flops 799834112 | bytes 3695621 | tf_op jit(solution)/shard_map/conv_general_dilated | solution.py:23
  43.2 5.4 %convolution_bitcast_fusion.3 = f32[32,256]{1,0:T(8,128)S(1)} fusion(bf16[2,64,128,256]{3,2,1,0:T(8,128)(2,1)} %param.10, f32[32,2,64,128]{3,0,2,1:T(8,128)} %fusion.4), kind=kOutput, calls=%fused_computation.33 | convolution fusion | flops 271056896 | bytes 10518528 | tf_op jit(solution)/shard_map/shwc,hwcm->sm/dot_general | solution.py:45
  48.6 0.8 collective-permute-start.2
  49.4 1.3 collective-permute-start.3
  50.7 2.9 %collective-permute-start.1 = (f32[32,256]{1,0:T(8,128)S(1)}, f32[32,256]{1,0:T(8,128)S(1)}, u32[]{:S(2)}, u32[]{:S(2)}) collective-permute-start(f32[32,256]{1,0:T(8,128)S(1)} %convolution_bitcast_fusion.3), channel_id=1, source_target_pairs={{0,2},{1,3},{2,0},{3,1},{4,6},{5,7},{6,4},{7,5},{8,10},{9,11},{10,... | collective-permute-start | bytes 98312 | tf_op jit(solution)/shard_map/ppermute | solution.py:49
  53.5 0.9 fusion.102
  54.5 1.9 %collective-permute-start.5 = (f32[256,256]{1,0:T(8,128)S(1)}, f32[256,256]{1,0:T(8,128)S(1)}, u32[]{:S(2)}, u32[]{:S(2)}) collective-permute-start(f32[256,256]{1,0:T(8,128)S(1)} %copy-done.18), channel_id=1, source_target_pairs={{0,4},{4,8},{8,12},{12,16},{16,20},{20,24},{24,28},{28,32},{32,36}... | collective-permute-start | bytes 786440 | tf_op jit(solution)/shard_map/ppermute | solution.py:15
  56.4 3.4 %collective-permute-start.7 = (f32[256,256]{1,0:T(8,128)S(1)}, f32[256,256]{1,0:T(8,128)S(1)}, u32[]{:S(2)}, u32[]{:S(2)}) collective-permute-start(f32[256,256]{1,0:T(8,128)S(1)} %copy-done.18), channel_id=1, source_target_pairs={{0,8},{4,12},{8,16},{12,20},{16,24},{20,28},{24,32},{28,36},{32,40... | collective-permute-start | bytes 786440 | tf_op jit(solution)/shard_map/ppermute | solution.py:15
  63.5 3.4 %collective-permute-start.6 = (f32[256]{0:T(256)S(1)}, f32[256]{0:T(256)S(1)}, u32[]{:S(2)}, u32[]{:S(2)}) collective-permute-start(f32[256]{0:T(256)S(1)} %add.157), channel_id=1, source_target_pairs={{0,8},{4,12},{8,16},{12,20},{16,24},{20,28},{24,32},{28,36},{32,40... | collective-permute-start | bytes 3080 | tf_op jit(solution)/shard_map/ppermute | solution.py:15
  66.9 0.9 fusion.100
  67.8 2.9 %collective-permute-start.4 = (f32[256]{0:T(256)S(1)}, f32[256]{0:T(256)S(1)}, u32[]{:S(2)}, u32[]{:S(2)}) collective-permute-start(f32[256]{0:T(256)S(1)} %add.157), channel_id=1, source_target_pairs={{0,4},{4,8},{8,12},{12,16},{16,20},{20,24},{24,28},{28,32},{32,36}... | collective-permute-start | bytes 3080 | tf_op jit(solution)/shard_map/ppermute | solution.py:15
  71.0 1.7 %collective-permute-done.4 = f32[256]{0:T(256)S(1)} collective-permute-done((f32[256]{0:T(256)S(1)}, f32[256]{0:T(256)S(1)}, u32[]{:S(2)}, u32[]{:S(2)}) %collective-permute-start.4) | collective-permute-done | bytes 1056 | tf_op jit(solution)/shard_map/ppermute | solution.py:15
  72.7 5.6 %collective-permute-start.8 = (f32[256]{0:T(256)S(1)}, f32[256]{0:T(256)S(1)}, u32[]{:S(2)}, u32[]{:S(2)}) collective-permute-start(f32[256]{0:T(256)S(1)} %add.158), channel_id=1, source_target_pairs={{0,8},{4,12},{8,16},{12,20},{16,24},{20,28},{24,32},{28,36},{32,40... | collective-permute-start | bytes 3080 | tf_op jit(solution)/shard_map/ppermute | solution.py:15
  78.7 1.9 %collective-permute-start.9 = (f32[256,256]{1,0:T(8,128)S(1)}, f32[256,256]{1,0:T(8,128)S(1)}, u32[]{:S(2)}, u32[]{:S(2)}) collective-permute-start(f32[256,256]{1,0:T(8,128)S(1)} %fusion.151), channel_id=1, source_target_pairs={{0,8},{4,12},{8,16},{12,20},{16,24},{20,28},{24,32},{28,36},{32,40... | collective-permute-start | bytes 786440 | tf_op jit(solution)/shard_map/ppermute | solution.py:15
  80.7 0.9 fusion.98
  81.8 3.2 %collective-permute-start.10 = (f32[256]{0:T(256)S(1)}, f32[256]{0:T(256)S(1)}, u32[]{:S(2)}, u32[]{:S(2)}) collective-permute-start(f32[256]{0:T(256)S(1)} %add.159), channel_id=1, source_target_pairs={{0,16},{4,20},{8,24},{12,28},{16,32},{20,36},{24,40},{28,44},{32,4... | collective-permute-start | bytes 3080 | tf_op jit(solution)/shard_map/ppermute | solution.py:15
  85.0 2.0 %collective-permute-done.9 = f32[256,256]{1,0:T(8,128)S(1)} collective-permute-done((f32[256,256]{1,0:T(8,128)S(1)}, f32[256,256]{1,0:T(8,128)S(1)}, u32[]{:S(2)}, u32[]{:S(2)}) %collective-permute-start.9) | collective-permute-done | bytes 262176 | tf_op jit(solution)/shard_map/ppermute | solution.py:15
  87.4 2.9 %collective-permute-start.11 = (f32[256,256]{1,0:T(8,128)S(1)}, f32[256,256]{1,0:T(8,128)S(1)}, u32[]{:S(2)}, u32[]{:S(2)}) collective-permute-start(f32[256,256]{1,0:T(8,128)S(1)} %fusion.153), channel_id=1, source_target_pairs={{0,16},{4,20},{8,24},{12,28},{16,32},{20,36},{24,40},{28,44},{32,4... | collective-permute-start | bytes 786440 | tf_op jit(solution)/shard_map/ppermute | solution.py:15
  90.4 0.8 bitcast_dynamic-update-slice_fusion.1
  91.4 0.6 add.160
  92.0 2.1 %collective-permute-start.12 = (f32[256]{0:T(256)}, f32[256]{0:T(256)}, u32[]{:S(2)}, u32[]{:S(2)}) collective-permute-start(f32[256]{0:T(256)} %add.160), channel_id=1, source_target_pairs={{0,32},{4,36},{8,40},{12,44},{16,48},{20,52},{24,56},{28,60},{32,6... | collective-permute-start | bytes 3080 | tf_op jit(solution)/shard_map/ppermute | solution.py:15
  94.2 3.0 %collective-permute-done.11 = f32[256,256]{1,0:T(8,128)S(1)} collective-permute-done((f32[256,256]{1,0:T(8,128)S(1)}, f32[256,256]{1,0:T(8,128)S(1)}, u32[]{:S(2)}, u32[]{:S(2)}) %collective-permute-start.11) | collective-permute-done | bytes 262176 | tf_op jit(solution)/shard_map/ppermute | solution.py:15
  97.2 1.1 fusion.155
  98.3 3.4 %collective-permute-start.13 = (f32[256,256]{1,0:T(8,128)}, f32[256,256]{1,0:T(8,128)}, u32[]{:S(2)}, u32[]{:S(2)}) collective-permute-start(f32[256,256]{1,0:T(8,128)} %fusion.155), channel_id=1, source_target_pairs={{0,32},{4,36},{8,40},{12,44},{16,48},{20,52},{24,56},{28,60},{32,6... | collective-permute-start | bytes 786440 | tf_op jit(solution)/shard_map/ppermute | solution.py:15
  101.7 1.1 convolution_bitcast_fusion.2
  102.8 1.2 fusion.156
  104.0 0.8 add.161
  104.8 1.3 collective-permute-start.14
  106.1 0.8 collective-permute-done.13
  106.8 1.4 fusion.157
  108.8 0.8 add.163
  109.8 0.6 add.164
  113.9 1.3 fusion.15
  116.6 2.0 %collective-permute-start.16 = (f32[256]{0:T(256)S(1)}, f32[256]{0:T(256)S(1)}, u32[]{:S(2)}, u32[]{:S(2)}) collective-permute-start(f32[256]{0:T(256)S(1)} %select_add_fusion), channel_id=1, source_target_pairs={{8,0},{12,4},{16,8},{20,12},{24,16},{28,20},{32,24},{36,28},{40,32... | collective-permute-start | bytes 3080 | tf_op jit(solution)/shard_map/ppermute | solution.py:19
  118.6 0.8 fusion.96
  119.4 1.9 %collective-permute-start.15 = (f32[256]{0:T(256)S(1)}, f32[256]{0:T(256)S(1)}, u32[]{:S(2)}, u32[]{:S(2)}) collective-permute-start(f32[256]{0:T(256)S(1)} %select_add_fusion), channel_id=1, source_target_pairs={{4,0},{8,4},{12,8},{16,12},{20,16},{24,20},{28,24},{32,28},{36,32}... | collective-permute-start | bytes 3080 | tf_op jit(solution)/shard_map/ppermute | solution.py:19
  121.3 5.3 %collective-permute-done.16 = f32[256]{0:T(256)S(1)} collective-permute-done((f32[256]{0:T(256)S(1)}, f32[256]{0:T(256)S(1)}, u32[]{:S(2)}, u32[]{:S(2)}) %collective-permute-start.16) | collective-permute-done | bytes 1056 | tf_op jit(solution)/shard_map/ppermute | solution.py:19
  126.9 1.9 %collective-permute-start.17 = (f32[256]{0:T(256)S(1)}, f32[256]{0:T(256)S(1)}, u32[]{:S(2)}, u32[]{:S(2)}) collective-permute-start(f32[256]{0:T(256)S(1)} %add.179), channel_id=1, source_target_pairs={{8,0},{12,4},{16,8},{20,12},{24,16},{28,20},{32,24},{36,28},{40,32... | collective-permute-start | bytes 3080 | tf_op jit(solution)/shard_map/ppermute | solution.py:19
  128.9 0.8 constant_dynamic-update-slice_fusion.16
  129.6 4.9 %collective-permute-done.17 = f32[256]{0:T(256)S(1)} collective-permute-done((f32[256]{0:T(256)S(1)}, f32[256]{0:T(256)S(1)}, u32[]{:S(2)}, u32[]{:S(2)}) %collective-permute-start.17) | collective-permute-done | bytes 1056 | tf_op jit(solution)/shard_map/ppermute | solution.py:19
  134.8 2.0 %collective-permute-start.18 = (f32[256]{0:T(256)S(1)}, f32[256]{0:T(256)S(1)}, u32[]{:S(2)}, u32[]{:S(2)}) collective-permute-start(f32[256]{0:T(256)S(1)} %add.180), channel_id=1, source_target_pairs={{16,0},{20,4},{24,8},{28,12},{32,16},{36,20},{40,24},{44,28},{48,3... | collective-permute-start | bytes 3080 | tf_op jit(solution)/shard_map/ppermute | solution.py:19
  136.8 0.8 bitcast_dynamic-update-slice_fusion.3
  137.5 5.2 %collective-permute-done.18 = f32[256]{0:T(256)S(1)} collective-permute-done((f32[256]{0:T(256)S(1)}, f32[256]{0:T(256)S(1)}, u32[]{:S(2)}, u32[]{:S(2)}) %collective-permute-start.18) | collective-permute-done | bytes 1056 | tf_op jit(solution)/shard_map/ppermute | solution.py:19
  143.0 2.0 %collective-permute-start.19 = (f32[256]{0:T(256)S(1)}, f32[256]{0:T(256)S(1)}, u32[]{:S(2)}, u32[]{:S(2)}) collective-permute-start(f32[256]{0:T(256)S(1)} %add.181), channel_id=1, source_target_pairs={{32,0},{36,4},{40,8},{44,12},{48,16},{52,20},{56,24},{60,28},{64,3... | collective-permute-start | bytes 3080 | tf_op jit(solution)/shard_map/ppermute | solution.py:19
  145.0 3.5 %collective-permute-done.19 = f32[256]{0:T(256)S(1)} collective-permute-done((f32[256]{0:T(256)S(1)}, f32[256]{0:T(256)S(1)}, u32[]{:S(2)}, u32[]{:S(2)}) %collective-permute-start.19) | collective-permute-done | bytes 1056 | tf_op jit(solution)/shard_map/ppermute | solution.py:19
  148.8 1.3 collective-permute-start.20
  150.8 5.0 %collective-permute-done.20 = f32[256]{0:T(256)S(1)} collective-permute-done((f32[256]{0:T(256)S(1)}, f32[256]{0:T(256)S(1)}, u32[]{:S(2)}, u32[]{:S(2)}) %collective-permute-start.20) | collective-permute-done | bytes 1056 | tf_op jit(solution)/shard_map/ppermute | solution.py:19
  156.9 2.7 %fusion.12 = f32[1,8,256]{2,0,1:T(1,128)S(1)} fusion(f32[32,8,8,256]{3,2,1,0:T(8,128)} %bitcast.175, s32[]{:T(128)S(6)} %select_n.26, f32[1,256]{1,0:T(1,128)S(1)} %bitcast.607, f32[1,256]{1,0:T(1,128)S(1)} %bitcast.619, f32[1,256]{1,0:T(1,128)S(1)} %bitcast.604, f32[1,256]{1,0:T(1,128)S(1)} %bitcast.600), kind=kOutput, calls=%fused_computation.9 | convolution fusion | flops 6292224 | bytes 2109444 | tf_op jit(solution)/shard_map/dot_general | solution.py:11
  (155 shorter events, 21.3 us)
Async XLA Ops:
  0.6 33.1 %copy-start = (bf16[128,64,3,3]{0,1,3,2:T(8,128)(2,1)S(1)}, bf16[128,64,3,3]{0,1,3,2:T(8,128)(2,1)}, u32[]{:S(2)}) copy-start(bf16[128,64,3,3]{0,1,3,2:T(8,128)(2,1)} %param.9) | copy-start | bytes 442372
  0.6 7.7 %copy-start.1 = (f32[256,256]{1,0:T(8,128)S(1)}, f32[256,256]{1,0:T(8,128)}, u32[]{:S(2)}) copy-start(f32[256,256]{1,0:T(8,128)} %param.11) | copy-start | bytes 786436
  0.7 7.8 %copy-start.19 = (f32[32,256]{1,0:T(8,128)S(1)}, f32[32,256]{1,0:T(8,128)}, u32[]{:S(2)}) copy-start(f32[32,256]{1,0:T(8,128)} %param.13) | copy-start | bytes 98308
  3.1 27.7 %collective-permute-start = (bf16[32,8,3,256]{3,1,2,0:T(8,128)(2,1)}, bf16[32,8,3,256]{3,1,2,0:T(8,128)(2,1)}, u32[]{:S(2)}, u32[]{:S(2)}) collective-permute-start(bf16[32,8,3,256]{3,1,2,0:T(8,128)(2,1)} %copy.73), channel_id=1, source_target_pairs={{0,1},{1,2},{2,3},{4,5},{5,6},{6,7},{8,9},{9,10},{10,11},{12,13},{... | collective-permute-start | bytes 1179656 | tf_op jit(solution)/shard_map/ppermute | solution.py:15
  12.3 3.2 %copy-start.9 = (f32[256,256]{1,0:T(8,128)S(1)}, f32[256,256]{1,0:T(8,128)}, u32[]{:S(2)}) copy-start(f32[256,256]{1,0:T(8,128)} %param.12) | copy-start | bytes 786436
  18.3 4.2 %copy-start.2 = (f32[2,256,256]{1,2,0:T(8,128)}, f32[2,256,256]{1,2,0:T(8,128)S(1)}, u32[]{:S(2)}) copy-start(f32[2,256,256]{1,2,0:T(8,128)S(1)} %convolution_bitcast_fusion.1) | copy-start | bytes 1572868
  20.6 2.6 %copy-start.7 = (f32[256,256]{1,0:T(8,128)}, f32[256,256]{1,0:T(8,128)S(1)}, u32[]{:S(2)}) copy-start(f32[256,256]{1,0:T(8,128)S(1)} %fusion.161) | copy-start | bytes 786436
  21.0 2.2 %copy-start.5 = (f32[256,256]{1,0:T(8,128)}, f32[256,256]{1,0:T(8,128)S(1)}, u32[]{:S(2)}) copy-start(f32[256,256]{1,0:T(8,128)S(1)} %fusion.163) | copy-start | bytes 786436
  43.2 11.3 %copy-start.20 = (f32[32,256]{1,0:T(8,128)S(1)}, f32[32,256]{1,0:T(8,128)}, u32[]{:S(2)}) copy-start(f32[32,256]{1,0:T(8,128)} %param.13) | copy-start | bytes 98308
  43.2 11.3 %copy-start.18 = (f32[256,256]{1,0:T(8,128)S(1)}, f32[256,256]{1,0:T(8,128)}, u32[]{:S(2)}) copy-start(f32[256,256]{1,0:T(8,128)} %fusion.93) | copy-start | bytes 786436
  48.6 11.3 %collective-permute-start.2 = (f32[32,256]{1,0:T(8,128)S(1)}, f32[32,256]{1,0:T(8,128)S(1)}, u32[]{:S(2)}, u32[]{:S(2)}) collective-permute-start(f32[32,256]{1,0:T(8,128)S(1)} %convolution_bitcast_fusion.3), channel_id=1, source_target_pairs={{0,3},{1,0},{2,1},{3,2},{4,7},{5,4},{6,5},{7,6},{8,11},{9,8},{10,9... | collective-permute-start | bytes 98312 | tf_op jit(solution)/shard_map/ppermute | solution.py:49
  49.4 10.4 %collective-permute-start.3 = (f32[32,256]{1,0:T(8,128)S(1)}, f32[32,256]{1,0:T(8,128)S(1)}, u32[]{:S(2)}, u32[]{:S(2)}) collective-permute-start(f32[32,256]{1,0:T(8,128)S(1)} %convolution_bitcast_fusion.3), channel_id=1, source_target_pairs={{0,1},{1,2},{2,3},{3,0},{4,5},{5,6},{6,7},{7,4},{8,9},{9,10},{10,1... | collective-permute-start | bytes 98312 | tf_op jit(solution)/shard_map/ppermute | solution.py:49
  50.7 9.2 %collective-permute-start.1 = (f32[32,256]{1,0:T(8,128)S(1)}, f32[32,256]{1,0:T(8,128)S(1)}, u32[]{:S(2)}, u32[]{:S(2)}) collective-permute-start(f32[32,256]{1,0:T(8,128)S(1)} %convolution_bitcast_fusion.3), channel_id=1, source_target_pairs={{0,2},{1,3},{2,0},{3,1},{4,6},{5,7},{6,4},{7,5},{8,10},{9,11},{10,... | collective-permute-start | bytes 98312 | tf_op jit(solution)/shard_map/ppermute | solution.py:49
  54.5 24.3 %copy-start.14 = (f32[4,8,256]{2,0,1:T(4,128)}, f32[4,8,256]{2,0,1:T(4,128)S(1)}, u32[]{:S(2)}) copy-start(f32[4,8,256]{2,0,1:T(4,128)S(1)} %copy.93) | copy-start | bytes 98308
  54.5 16.3 %collective-permute-start.5 = (f32[256,256]{1,0:T(8,128)S(1)}, f32[256,256]{1,0:T(8,128)S(1)}, u32[]{:S(2)}, u32[]{:S(2)}) collective-permute-start(f32[256,256]{1,0:T(8,128)S(1)} %copy-done.18), channel_id=1, source_target_pairs={{0,4},{4,8},{8,12},{12,16},{16,20},{20,24},{24,28},{28,32},{32,36}... | collective-permute-start | bytes 786440 | tf_op jit(solution)/shard_map/ppermute | solution.py:15
  56.4 21.9 %collective-permute-start.7 = (f32[256,256]{1,0:T(8,128)S(1)}, f32[256,256]{1,0:T(8,128)S(1)}, u32[]{:S(2)}, u32[]{:S(2)}) collective-permute-start(f32[256,256]{1,0:T(8,128)S(1)} %copy-done.18), channel_id=1, source_target_pairs={{0,8},{4,12},{8,16},{12,20},{16,24},{20,28},{24,32},{28,36},{32,40... | collective-permute-start | bytes 786440 | tf_op jit(solution)/shard_map/ppermute | solution.py:15
  59.9 18.8 %copy-start.16 = (f32[4,8,256]{2,0,1:T(4,128)}, f32[4,8,256]{2,0,1:T(4,128)S(1)}, u32[]{:S(2)}) copy-start(f32[4,8,256]{2,0,1:T(4,128)S(1)} %copy.92) | copy-start | bytes 98308
  63.0 17.7 %copy-start.21 = (f32[1,256]{1,0:T(1,128)}, f32[1,256]{1,0:T(1,128)S(1)}, u32[]{:S(2)}) copy-start(f32[1,256]{1,0:T(1,128)S(1)} %get-tuple-element.26) | copy-start | bytes 3076
  63.0 17.7 %copy-start.23 = (f32[1,256]{1,0:T(1,128)}, f32[1,256]{1,0:T(1,128)S(1)}, u32[]{:S(2)}) copy-start(f32[1,256]{1,0:T(1,128)S(1)} %get-tuple-element.27) | copy-start | bytes 3076
  63.2 27.1 %copy-start.3 = (f32[2,256,256]{1,2,0:T(8,128)S(1)}, f32[2,256,256]{1,2,0:T(8,128)}, u32[]{:S(2)}) copy-start(f32[2,256,256]{1,2,0:T(8,128)} %copy-done.2) | copy-start | bytes 1572868
  63.5 7.3 %collective-permute-start.6 = (f32[256]{0:T(256)S(1)}, f32[256]{0:T(256)S(1)}, u32[]{:S(2)}, u32[]{:S(2)}) collective-permute-start(f32[256]{0:T(256)S(1)} %add.157), channel_id=1, source_target_pairs={{0,8},{4,12},{8,16},{12,20},{16,24},{20,28},{24,32},{28,36},{32,40... | collective-permute-start | bytes 3080 | tf_op jit(solution)/shard_map/ppermute | solution.py:15
  67.8 4.9 %collective-permute-start.4 = (f32[256]{0:T(256)S(1)}, f32[256]{0:T(256)S(1)}, u32[]{:S(2)}, u32[]{:S(2)}) collective-permute-start(f32[256]{0:T(256)S(1)} %add.157), channel_id=1, source_target_pairs={{0,4},{4,8},{8,12},{12,16},{16,20},{20,24},{24,28},{28,32},{32,36}... | collective-permute-start | bytes 3080 | tf_op jit(solution)/shard_map/ppermute | solution.py:15
  72.7 29.0 %copy-start.10 = (f32[256,256]{1,0:T(8,128)S(1)}, f32[256,256]{1,0:T(8,128)}, u32[]{:S(2)}) copy-start(f32[256,256]{1,0:T(8,128)} %param.12) | copy-start | bytes 786436
  72.7 8.9 %collective-permute-start.8 = (f32[256]{0:T(256)S(1)}, f32[256]{0:T(256)S(1)}, u32[]{:S(2)}, u32[]{:S(2)}) collective-permute-start(f32[256]{0:T(256)S(1)} %add.158), channel_id=1, source_target_pairs={{0,8},{4,12},{8,16},{12,20},{16,24},{20,28},{24,32},{28,36},{32,40... | collective-permute-start | bytes 3080 | tf_op jit(solution)/shard_map/ppermute | solution.py:15
  78.7 8.3 %collective-permute-start.9 = (f32[256,256]{1,0:T(8,128)S(1)}, f32[256,256]{1,0:T(8,128)S(1)}, u32[]{:S(2)}, u32[]{:S(2)}) collective-permute-start(f32[256,256]{1,0:T(8,128)S(1)} %fusion.151), channel_id=1, source_target_pairs={{0,8},{4,12},{8,16},{12,20},{16,24},{20,28},{24,32},{28,36},{32,40... | collective-permute-start | bytes 786440 | tf_op jit(solution)/shard_map/ppermute | solution.py:15
  81.8 9.3 %collective-permute-start.10 = (f32[256]{0:T(256)S(1)}, f32[256]{0:T(256)S(1)}, u32[]{:S(2)}, u32[]{:S(2)}) collective-permute-start(f32[256]{0:T(256)S(1)} %add.159), channel_id=1, source_target_pairs={{0,16},{4,20},{8,24},{12,28},{16,32},{20,36},{24,40},{28,44},{32,4... | collective-permute-start | bytes 3080 | tf_op jit(solution)/shard_map/ppermute | solution.py:15
  87.4 9.8 %collective-permute-start.11 = (f32[256,256]{1,0:T(8,128)S(1)}, f32[256,256]{1,0:T(8,128)S(1)}, u32[]{:S(2)}, u32[]{:S(2)}) collective-permute-start(f32[256,256]{1,0:T(8,128)S(1)} %fusion.153), channel_id=1, source_target_pairs={{0,16},{4,20},{8,24},{12,28},{16,32},{20,36},{24,40},{28,44},{32,4... | collective-permute-start | bytes 786440 | tf_op jit(solution)/shard_map/ppermute | solution.py:15
  92.0 10.7 %collective-permute-start.12 = (f32[256]{0:T(256)}, f32[256]{0:T(256)}, u32[]{:S(2)}, u32[]{:S(2)}) collective-permute-start(f32[256]{0:T(256)} %add.160), channel_id=1, source_target_pairs={{0,32},{4,36},{8,40},{12,44},{16,48},{20,52},{24,56},{28,60},{32,6... | collective-permute-start | bytes 3080 | tf_op jit(solution)/shard_map/ppermute | solution.py:15
  98.3 8.6 %collective-permute-start.13 = (f32[256,256]{1,0:T(8,128)}, f32[256,256]{1,0:T(8,128)}, u32[]{:S(2)}, u32[]{:S(2)}) collective-permute-start(f32[256,256]{1,0:T(8,128)} %fusion.155), channel_id=1, source_target_pairs={{0,32},{4,36},{8,40},{12,44},{16,48},{20,52},{24,56},{28,60},{32,6... | collective-permute-start | bytes 786440 | tf_op jit(solution)/shard_map/ppermute | solution.py:15
  102.7 7.9 %copy-start.22 = (f32[1,256]{1,0:T(1,128)S(1)}, f32[1,256]{1,0:T(1,128)}, u32[]{:S(2)}) copy-start(f32[1,256]{1,0:T(1,128)} %copy-done.21) | copy-start | bytes 3076
  102.7 7.9 %copy-start.15 = (f32[4,8,256]{2,0,1:T(4,128)S(1)}, f32[4,8,256]{2,0,1:T(4,128)}, u32[]{:S(2)}) copy-start(f32[4,8,256]{2,0,1:T(4,128)} %copy-done.14) | copy-start | bytes 98308
  102.8 7.9 %copy-start.17 = (f32[4,8,256]{2,0,1:T(4,128)S(1)}, f32[4,8,256]{2,0,1:T(4,128)}, u32[]{:S(2)}) copy-start(f32[4,8,256]{2,0,1:T(4,128)} %copy-done.16) | copy-start | bytes 98308
  104.0 9.3 %copy-start.13 = (f32[256,256,1]{1,0,2:T(8,128)S(1)}, f32[256,256,1]{1,0,2:T(8,128)}, u32[]{:S(2)}) copy-start(f32[256,256,1]{1,0,2:T(8,128)} %convolution_bitcast_fusion.2) | copy-start | bytes 786436
  104.8 3.5 %collective-permute-start.14 = (f32[256]{0:T(256)S(1)}, f32[256]{0:T(256)S(1)}, u32[]{:S(2)}, u32[]{:S(2)}) collective-permute-start(f32[256]{0:T(256)S(1)} %add.161), channel_id=1, source_target_pairs={{0,64},{4,68},{8,72},{12,76},{16,80},{20,84},{24,88},{28,92},{32,9... | collective-permute-start | bytes 3080 | tf_op jit(solution)/shard_map/ppermute | solution.py:15
  108.3 5.6 %copy-start.11 = (f32[2048,256]{1,0:T(8,128)S(1)}, f32[2048,256]{1,0:T(8,128)}, u32[]{:S(2)}) copy-start(f32[2048,256]{1,0:T(8,128)} %get-tuple-element.7) | copy-start | bytes 6291460
  113.7 4.9 %copy-start.4 = (f32[2,256,256]{1,2,0:T(8,128)S(1)}, f32[2,256,256]{1,2,0:T(8,128)}, u32[]{:S(2)}) copy-start(f32[2,256,256]{1,2,0:T(8,128)} %copy-done.2) | copy-start | bytes 1572868
  113.8 20.7 %copy-start.8 = (f32[256,256]{1,0:T(8,128)S(1)}, f32[256,256]{1,0:T(8,128)}, u32[]{:S(2)}) copy-start(f32[256,256]{1,0:T(8,128)} %copy-done.7) | copy-start | bytes 786436
  115.2 27.6 %copy-start.6 = (f32[256,256]{1,0:T(8,128)S(1)}, f32[256,256]{1,0:T(8,128)}, u32[]{:S(2)}) copy-start(f32[256,256]{1,0:T(8,128)} %copy-done.5) | copy-start | bytes 786436
  115.2 40.6 %copy-start.12 = (f32[256,256]{1,0:T(8,128)S(1)}, f32[256,256]{1,0:T(8,128)}, u32[]{:S(2)}) copy-start(f32[256,256]{1,0:T(8,128)} %fusion.167) | copy-start | bytes 786436
  116.6 10.0 %collective-permute-start.16 = (f32[256]{0:T(256)S(1)}, f32[256]{0:T(256)S(1)}, u32[]{:S(2)}, u32[]{:S(2)}) collective-permute-start(f32[256]{0:T(256)S(1)} %select_add_fusion), channel_id=1, source_target_pairs={{8,0},{12,4},{16,8},{20,12},{24,16},{28,20},{32,24},{36,28},{40,32... | collective-permute-start | bytes 3080 | tf_op jit(solution)/shard_map/ppermute | solution.py:19
  119.4 7.5 %collective-permute-start.15 = (f32[256]{0:T(256)S(1)}, f32[256]{0:T(256)S(1)}, u32[]{:S(2)}, u32[]{:S(2)}) collective-permute-start(f32[256]{0:T(256)S(1)} %select_add_fusion), channel_id=1, source_target_pairs={{4,0},{8,4},{12,8},{16,12},{20,16},{24,20},{28,24},{32,28},{36,32}... | collective-permute-start | bytes 3080 | tf_op jit(solution)/shard_map/ppermute | solution.py:19
  126.9 7.6 %collective-permute-start.17 = (f32[256]{0:T(256)S(1)}, f32[256]{0:T(256)S(1)}, u32[]{:S(2)}, u32[]{:S(2)}) collective-permute-start(f32[256]{0:T(256)S(1)} %add.179), channel_id=1, source_target_pairs={{8,0},{12,4},{16,8},{20,12},{24,16},{28,20},{32,24},{36,28},{40,32... | collective-permute-start | bytes 3080 | tf_op jit(solution)/shard_map/ppermute | solution.py:19
  134.8 7.9 %collective-permute-start.18 = (f32[256]{0:T(256)S(1)}, f32[256]{0:T(256)S(1)}, u32[]{:S(2)}, u32[]{:S(2)}) collective-permute-start(f32[256]{0:T(256)S(1)} %add.180), channel_id=1, source_target_pairs={{16,0},{20,4},{24,8},{28,12},{32,16},{36,20},{40,24},{44,28},{48,3... | collective-permute-start | bytes 3080 | tf_op jit(solution)/shard_map/ppermute | solution.py:19
  143.0 5.5 %collective-permute-start.19 = (f32[256]{0:T(256)S(1)}, f32[256]{0:T(256)S(1)}, u32[]{:S(2)}, u32[]{:S(2)}) collective-permute-start(f32[256]{0:T(256)S(1)} %add.181), channel_id=1, source_target_pairs={{32,0},{36,4},{40,8},{44,12},{48,16},{52,20},{56,24},{60,28},{64,3... | collective-permute-start | bytes 3080 | tf_op jit(solution)/shard_map/ppermute | solution.py:19
  148.8 7.0 %collective-permute-start.20 = (f32[256]{0:T(256)S(1)}, f32[256]{0:T(256)S(1)}, u32[]{:S(2)}, u32[]{:S(2)}) collective-permute-start(f32[256]{0:T(256)S(1)} %add.182), channel_id=1, source_target_pairs={{64,0},{68,4},{72,8},{76,12},{80,16},{84,20},{88,24},{92,28},{96,3... | collective-permute-start | bytes 3080 | tf_op jit(solution)/shard_map/ppermute | solution.py:19

commit v9 on v7

--- a/solution.py
+++ b/solution.py
@@ -135,11 +135,11 @@
     powers = powers[: hours + 1]
     step = powers[hours]
     joined_t = dot(back_gain, transition).T
-    stacked = jnp.concatenate([p.T for p in powers[:hours]], axis=0)
+    stacked = jnp.stack(powers[:hours])
     sources = filtered - jnp.einsum("sia,ab->sib", filtered, joined_t, precision=precise)
     padded = jnp.concatenate([sources, jnp.zeros_like(sources)], axis=1)
-    hankel = jnp.concatenate([padded[:, d : d + hours] for d in range(hours)], axis=2)
-    inner = dot(hankel.reshape(bands * hours, hours * modes), stacked).reshape(bands, hours, modes)
+    hankel = jnp.stack([padded[:, d : d + hours] for d in range(hours)], axis=2)
+    inner = jnp.einsum("sidb,dab->sia", hankel, stacked, precision=precise)
     heads = inner[:, 0]
     block_head = heads[bands - 1]
     for s in range(bands - 2, -1, -1):
@@ -160,8 +160,8 @@
     for s in range(bands - 1, 0, -1):
         inputs.insert(0, heads[s] + dot(step, inputs[0]))
     mine = lax.dynamic_index_in_dim(jnp.stack(inputs), band, 0, False)
-    tails = jnp.concatenate([powers[hours - i].T for i in range(hours)], axis=1)
-    smoothed = lax.dynamic_index_in_dim(inner, band, 0, False) + dot(mine[None, :], tails).reshape(hours, modes)
+    tails = jnp.stack([powers[hours - i] for i in range(hours)])
+    smoothed = lax.dynamic_index_in_dim(inner, band, 0, False) + jnp.einsum("iab,b->ia", tails, mine, precision=precise)
     return lax.dynamic_index_in_dim(filtered, band, 0, False), smoothed
 
 

time: 164 us -> 160 us (0.976)
  local copies, waits for them, and re-layouts: 21.4 us -> 16.9 us
  matrix products: 51.3 us -> 49.6 us
    dot_general x55 -> x53, matrix products: 26.1 us -> 19.4 us  [dot(): return jnp.dot(a, b, precision=precise)]
    dot_general x0 -> x2, matrix products: none -> 5.67 us  [the longest x1 2.88 us: per_device(): inner = jnp.einsum('sidb,dab->sia', hankel, stacked, precision=precise)]
    unnamed x72 -> x57, local copies, waits for them, and re-layouts: 15.4 us -> 9.97 us
    another operation x1 -> x4, local copies, waits for them, and re-layouts: 0.01 us -> 1.68 us  [the longest x1 0.94 us: per_device(): stacked = jnp.stack(powers[:hours])]
  transfers between devices with their start and end apart: 21 -> 21, of which waited for: 9 -> 9; matrix products, arithmetic and copies ran while one was open for 27% -> 22% of each run, Pallas kernels for 0% -> 0%
where the time goes in v9:
time: 160 us; the launch traced here: 159 us
  starting transfers between devices  53.1 us (33%)
  matrix products  49.6 us (31%)
  waiting for transfers between devices  33 us (21%)
  local copies, waits for them, and re-layouts  16.9 us (11%)
  other arithmetic  4.92 us (3%)
    ppermute x12, starting transfers between devices, shift_down(): lax.ppermute(value, axis, [(i, i + steps) for i in range(count - steps)])  36.8 us
    ppermute x6, waiting for transfers between devices, shift_up(): lax.ppermute(value, axis, [(i + steps, i) for i in range(count - steps)])  23.9 us
    dot_general x53, matrix products, dot(): return jnp.dot(a, b, precision=precise)  19.4 us
    ppermute x6, starting transfers between devices, shift_up(): lax.ppermute(value, axis, [(i + steps, i) for i in range(count - steps)])  11.4 us
    unnamed x57, local copies, waits for them, and re-layouts  9.97 us
    conv_general_dilated x1, matrix products, conv_stride(): lax.conv_general_dilated(images, kernel, (2, 2), ((0, 0), (1, 1)), dimens...  9.43 us
    ppermute x12, waiting for transfers between devices, shift_down(): lax.ppermute(value, axis, [(i, i + steps) for i in range(count - steps)])  9.07 us
    dot_general x7, matrix products, per_device(): jnp.einsum('ab,sbc->sac', transition, phis, precision=precise)  7.14 us
  transfers between devices with their start and end apart: 21, of which 9 were waited for; matrix products, arithmetic and copies ran while one was open for 22% of the time, Pallas kernels for 0%

profile of v9, /device:TPU:14, one launch (start us, length us, event | category | flops | bytes accessed | tf_op | source)
XLA Modules:
  0.0 159.0 jit_solution(17501297420587869380)
XLA Ops:
  0.7 1.6 %slice.193 = bf16[32,8,3,256]{3,2,1,0:T(4,128)(2,1)S(1)} slice(bf16[32,8,8,256]{3,2,1,0:T(8,128)(2,1)} %param.7), slice={[0:32], [0:8], [5:8], [0:256]} | slice | bytes 786432 | tf_op jit(solution)/shard_map/slice | solution.py:34
  2.3 0.8 copy.75
  3.1 4.6 %collective-permute-start = (bf16[32,8,3,256]{3,1,2,0:T(8,128)(2,1)}, bf16[32,8,3,256]{3,1,2,0:T(8,128)(2,1)}, u32[]{:S(2)}, u32[]{:S(2)}) collective-permute-start(bf16[32,8,3,256]{3,1,2,0:T(8,128)(2,1)} %copy.75), channel_id=1, source_target_pairs={{0,1},{1,2},{2,3},{4,5},{5,6},{6,7},{8,9},{9,10},{10,11},{12,13},{... | collective-permute-start | bytes 1179656 | tf_op jit(solution)/shard_map/ppermute | solution.py:15
  8.6 1.0 fusion.20
  9.7 1.0 fusion.19
  10.7 1.0 fusion.18
  11.7 1.0 fusion.17
  12.7 1.0 fusion.16
  13.8 1.0 fusion.15
  14.8 1.0 fusion.14
  16.4 1.3 fusion.99
  18.3 1.0 convolution_bitcast_fusion
  19.5 0.8 convert_dynamic-update-slice_fusion
  20.2 0.7 constant_dynamic-update-slice_fusion.18
  21.0 1.4 copy-done.4
  22.3 0.7 constant_dynamic-update-slice_fusion.16
  23.6 5.1 %copy.46 = bf16[32,8,8,256]{0,1,3,2:T(8,128)(2,1)} copy(bf16[32,8,8,256]{3,2,1,0:T(8,128)(2,1)} %param.7) | data formatting | bytes 2097152 | tf_op args[0]
  28.7 0.8 constant_dynamic-update-slice_fusion.15
  29.5 0.6 fusion.93
  30.1 2.9 %copy.45 = bf16[32,8,3,256]{0,1,3,2:T(8,128)(2,1)} copy(bf16[32,8,3,256]{3,1,2,0:T(8,128)(2,1)} %collective-permute-done) | data formatting | bytes 786432 | tf_op jit(solution)/shard_map/optimization_barrier | solution.py:105
  33.1 9.4 %fusion.4 = f32[32,2,64,128]{3,0,2,1:T(8,128)} fusion(bf16[128,64,3,3]{0,1,3,2:T(8,128)(2,1)S(1)} %copy-done, pred[5]{0:T(512)(128)(4,1)S(1)} %copy-done.16, bf16[64,8,3,3]{0,1,3,2:T(8,128)(2,1)S(1)} %copy-done.15, bf16[32,8,8,256]{0,1,3,2:T(8,128)(2,1)} %copy.46, bf16[32,8,3,256]{0,1,3,2:T(8,128)(2,1)} %copy.45), kind=kOutput, calls=%fused_computation.5 | convolution fusion | flops 799834112 | bytes 3695621 | tf_op jit(solution)/shard_map/conv_general_dilated | solution.py:23
  42.5 5.3 %convolution_bitcast_fusion.3 = f32[32,256]{1,0:T(8,128)S(1)} fusion(bf16[2,64,128,256]{3,2,1,0:T(8,128)(2,1)} %param.10, f32[32,2,64,128]{3,0,2,1:T(8,128)} %fusion.4), kind=kOutput, calls=%fused_computation.30 | convolution fusion | flops 271056896 | bytes 10518528 | tf_op jit(solution)/shard_map/shwc,hwcm->sm/dot_general | solution.py:45
  47.9 0.8 collective-permute-start.2
  48.7 1.3 collective-permute-start.3
  50.0 2.9 %collective-permute-start.1 = (f32[32,256]{1,0:T(8,128)S(1)}, f32[32,256]{1,0:T(8,128)S(1)}, u32[]{:S(2)}, u32[]{:S(2)}) collective-permute-start(f32[32,256]{1,0:T(8,128)S(1)} %convolution_bitcast_fusion.3), channel_id=1, source_target_pairs={{0,2},{1,3},{2,0},{3,1},{4,6},{5,7},{6,4},{7,5},{8,10},{9,11},{10,... | collective-permute-start | bytes 98312 | tf_op jit(solution)/shard_map/ppermute | solution.py:49
  52.8 0.9 slice_dynamic-update-slice_fusion
  53.8 1.9 %collective-permute-start.5 = (f32[256,256]{1,0:T(8,128)S(1)}, f32[256,256]{1,0:T(8,128)S(1)}, u32[]{:S(2)}, u32[]{:S(2)}) collective-permute-start(f32[256,256]{1,0:T(8,128)S(1)} %fusion.93), channel_id=1, source_target_pairs={{0,4},{4,8},{8,12},{12,16},{16,20},{20,24},{24,28},{28,32},{32,36}... | collective-permute-start | bytes 786440 | tf_op jit(solution)/shard_map/ppermute | solution.py:15
  55.7 3.4 %collective-permute-start.7 = (f32[256,256]{1,0:T(8,128)S(1)}, f32[256,256]{1,0:T(8,128)S(1)}, u32[]{:S(2)}, u32[]{:S(2)}) collective-permute-start(f32[256,256]{1,0:T(8,128)S(1)} %fusion.93), channel_id=1, source_target_pairs={{0,8},{4,12},{8,16},{12,20},{16,24},{20,28},{24,32},{28,36},{32,40... | collective-permute-start | bytes 786440 | tf_op jit(solution)/shard_map/ppermute | solution.py:15
  61.7 0.6 fusion.149
  62.8 3.4 %collective-permute-start.6 = (f32[256]{0:T(256)S(1)}, f32[256]{0:T(256)S(1)}, u32[]{:S(2)}, u32[]{:S(2)}) collective-permute-start(f32[256]{0:T(256)S(1)} %add.157), channel_id=1, source_target_pairs={{0,8},{4,12},{8,16},{12,20},{16,24},{20,28},{24,32},{28,36},{32,40... | collective-permute-start | bytes 3080 | tf_op jit(solution)/shard_map/ppermute | solution.py:15
  66.2 0.6 fusion.77
  66.8 2.9 %collective-permute-start.4 = (f32[256]{0:T(256)S(1)}, f32[256]{0:T(256)S(1)}, u32[]{:S(2)}, u32[]{:S(2)}) collective-permute-start(f32[256]{0:T(256)S(1)} %add.157), channel_id=1, source_target_pairs={{0,4},{4,8},{8,12},{12,16},{16,20},{20,24},{24,28},{28,32},{32,36}... | collective-permute-start | bytes 3080 | tf_op jit(solution)/shard_map/ppermute | solution.py:15
  70.1 1.6 %collective-permute-done.4 = f32[256]{0:T(256)S(1)} collective-permute-done((f32[256]{0:T(256)S(1)}, f32[256]{0:T(256)S(1)}, u32[]{:S(2)}, u32[]{:S(2)}) %collective-permute-start.4) | collective-permute-done | bytes 1056 | tf_op jit(solution)/shard_map/ppermute | solution.py:15
  71.8 5.6 %collective-permute-start.8 = (f32[256]{0:T(256)S(1)}, f32[256]{0:T(256)S(1)}, u32[]{:S(2)}, u32[]{:S(2)}) collective-permute-start(f32[256]{0:T(256)S(1)} %add.158), channel_id=1, source_target_pairs={{0,8},{4,12},{8,16},{12,20},{16,24},{20,28},{24,32},{28,36},{32,40... | collective-permute-start | bytes 3080 | tf_op jit(solution)/shard_map/ppermute | solution.py:15
  77.8 1.9 %collective-permute-start.9 = (f32[256,256]{1,0:T(8,128)S(1)}, f32[256,256]{1,0:T(8,128)S(1)}, u32[]{:S(2)}, u32[]{:S(2)}) collective-permute-start(f32[256,256]{1,0:T(8,128)S(1)} %fusion.151), channel_id=1, source_target_pairs={{0,8},{4,12},{8,16},{12,20},{16,24},{20,28},{24,32},{28,36},{32,40... | collective-permute-start | bytes 786440 | tf_op jit(solution)/shard_map/ppermute | solution.py:15
  80.4 3.4 %collective-permute-start.10 = (f32[256]{0:T(256)S(1)}, f32[256]{0:T(256)S(1)}, u32[]{:S(2)}, u32[]{:S(2)}) collective-permute-start(f32[256]{0:T(256)S(1)} %add.159), channel_id=1, source_target_pairs={{0,16},{4,20},{8,24},{12,28},{16,32},{20,36},{24,40},{28,44},{32,4... | collective-permute-start | bytes 3080 | tf_op jit(solution)/shard_map/ppermute | solution.py:15
  83.8 2.3 %collective-permute-done.9 = f32[256,256]{1,0:T(8,128)S(1)} collective-permute-done((f32[256,256]{1,0:T(8,128)S(1)}, f32[256,256]{1,0:T(8,128)S(1)}, u32[]{:S(2)}, u32[]{:S(2)}) %collective-permute-start.9) | collective-permute-done | bytes 262176 | tf_op jit(solution)/shard_map/ppermute | solution.py:15
  86.5 2.7 %collective-permute-start.11 = (f32[256,256]{1,0:T(8,128)S(1)}, f32[256,256]{1,0:T(8,128)S(1)}, u32[]{:S(2)}, u32[]{:S(2)}) collective-permute-start(f32[256,256]{1,0:T(8,128)S(1)} %fusion.153), channel_id=1, source_target_pairs={{0,16},{4,20},{8,24},{12,28},{16,32},{20,36},{24,40},{28,44},{32,4... | collective-permute-start | bytes 786440 | tf_op jit(solution)/shard_map/ppermute | solution.py:15
  89.8 0.6 add.160
  90.4 2.4 %collective-permute-start.12 = (f32[256]{0:T(256)}, f32[256]{0:T(256)}, u32[]{:S(2)}, u32[]{:S(2)}) collective-permute-start(f32[256]{0:T(256)} %add.160), channel_id=1, source_target_pairs={{0,32},{4,36},{8,40},{12,44},{16,48},{20,52},{24,56},{28,60},{32,6... | collective-permute-start | bytes 3080 | tf_op jit(solution)/shard_map/ppermute | solution.py:15
  92.9 3.4 %collective-permute-done.11 = f32[256,256]{1,0:T(8,128)S(1)} collective-permute-done((f32[256,256]{1,0:T(8,128)S(1)}, f32[256,256]{1,0:T(8,128)S(1)}, u32[]{:S(2)}, u32[]{:S(2)}) %collective-permute-start.11) | collective-permute-done | bytes 262176 | tf_op jit(solution)/shard_map/ppermute | solution.py:15
  96.6 3.2 %collective-permute-start.13 = (f32[256,256]{1,0:T(8,128)S(1)}, f32[256,256]{1,0:T(8,128)}, u32[]{:S(2)}, u32[]{:S(2)}) collective-permute-start(f32[256,256]{1,0:T(8,128)S(1)} %fusion.155), channel_id=1, source_target_pairs={{0,32},{4,36},{8,40},{12,44},{16,48},{20,52},{24,56},{28,60},{32,6... | collective-permute-start | bytes 786440 | tf_op jit(solution)/shard_map/ppermute | solution.py:15
  100.3 0.9 fusion.156
  101.2 0.7 add.161
  101.9 1.3 collective-permute-start.14
  103.2 1.8 %collective-permute-done.13 = f32[256,256]{1,0:T(8,128)} collective-permute-done((f32[256,256]{1,0:T(8,128)S(1)}, f32[256,256]{1,0:T(8,128)}, u32[]{:S(2)}, u32[]{:S(2)}) %collective-permute-start.13) | collective-permute-done | bytes 262176 | tf_op jit(solution)/shard_map/ppermute | solution.py:15
  105.0 1.3 fusion.157
  106.9 0.7 add.163
  107.8 0.7 add.164
  111.9 2.9 %fusion.21 = f32[4,8,256]{2,0,1:T(4,128)S(1)} fusion(f32[4,8,8,256]{3,0,1,2:T(4,128)S(1)} %constant_dynamic-update-slice_fusion.7, f32[8,256,256]{1,2,0:T(8,128)} %slice_dynamic-update-slice_fusion), kind=kOutput, calls=%fused_computation.31 | convolution fusion | flops 201326592 | bytes 2392064 | tf_op jit(solution)/shard_map/sidb,dab->sia/dot_general | solution.py:142
  116.2 2.3 %collective-permute-start.16 = (f32[256]{0:T(256)S(1)}, f32[256]{0:T(256)S(1)}, u32[]{:S(2)}, u32[]{:S(2)}) collective-permute-start(f32[256]{0:T(256)S(1)} %select_add_fusion), channel_id=1, source_target_pairs={{8,0},{12,4},{16,8},{20,12},{24,16},{28,20},{32,24},{36,28},{40,32... | collective-permute-start | bytes 3080 | tf_op jit(solution)/shard_map/ppermute | solution.py:19
  118.9 1.9 %collective-permute-start.15 = (f32[256]{0:T(256)S(1)}, f32[256]{0:T(256)S(1)}, u32[]{:S(2)}, u32[]{:S(2)}) collective-permute-start(f32[256]{0:T(256)S(1)} %select_add_fusion), channel_id=1, source_target_pairs={{4,0},{8,4},{12,8},{16,12},{20,16},{24,20},{28,24},{32,28},{36,32}... | collective-permute-start | bytes 3080 | tf_op jit(solution)/shard_map/ppermute | solution.py:19
  120.8 4.5 %collective-permute-done.16 = f32[256]{0:T(256)S(1)} collective-permute-done((f32[256]{0:T(256)S(1)}, f32[256]{0:T(256)S(1)}, u32[]{:S(2)}, u32[]{:S(2)}) %collective-permute-start.16) | collective-permute-done | bytes 1056 | tf_op jit(solution)/shard_map/ppermute | solution.py:19
  125.7 1.9 %collective-permute-start.17 = (f32[256]{0:T(256)S(1)}, f32[256]{0:T(256)S(1)}, u32[]{:S(2)}, u32[]{:S(2)}) collective-permute-start(f32[256]{0:T(256)S(1)} %add.179), channel_id=1, source_target_pairs={{8,0},{12,4},{16,8},{20,12},{24,16},{28,20},{32,24},{36,28},{40,32... | collective-permute-start | bytes 3080 | tf_op jit(solution)/shard_map/ppermute | solution.py:19
  128.0 5.3 %collective-permute-done.17 = f32[256]{0:T(256)S(1)} collective-permute-done((f32[256]{0:T(256)S(1)}, f32[256]{0:T(256)S(1)}, u32[]{:S(2)}, u32[]{:S(2)}) %collective-permute-start.17) | collective-permute-done | bytes 1056 | tf_op jit(solution)/shard_map/ppermute | solution.py:19
  133.5 2.0 %collective-permute-start.18 = (f32[256]{0:T(256)S(1)}, f32[256]{0:T(256)S(1)}, u32[]{:S(2)}, u32[]{:S(2)}) collective-permute-start(f32[256]{0:T(256)S(1)} %add.180), channel_id=1, source_target_pairs={{16,0},{20,4},{24,8},{28,12},{32,16},{36,20},{40,24},{44,28},{48,3... | collective-permute-start | bytes 3080 | tf_op jit(solution)/shard_map/ppermute | solution.py:19
  135.9 5.6 %collective-permute-done.18 = f32[256]{0:T(256)S(1)} collective-permute-done((f32[256]{0:T(256)S(1)}, f32[256]{0:T(256)S(1)}, u32[]{:S(2)}, u32[]{:S(2)}) %collective-permute-start.18) | collective-permute-done | bytes 1056 | tf_op jit(solution)/shard_map/ppermute | solution.py:19
  141.7 2.0 %collective-permute-start.19 = (f32[256]{0:T(256)S(1)}, f32[256]{0:T(256)S(1)}, u32[]{:S(2)}, u32[]{:S(2)}) collective-permute-start(f32[256]{0:T(256)S(1)} %add.181), channel_id=1, source_target_pairs={{32,0},{36,4},{40,8},{44,12},{48,16},{52,20},{56,24},{60,28},{64,3... | collective-permute-start | bytes 3080 | tf_op jit(solution)/shard_map/ppermute | solution.py:19
  143.7 3.5 %collective-permute-done.19 = f32[256]{0:T(256)S(1)} collective-permute-done((f32[256]{0:T(256)S(1)}, f32[256]{0:T(256)S(1)}, u32[]{:S(2)}, u32[]{:S(2)}) %collective-permute-start.19) | collective-permute-done | bytes 1056 | tf_op jit(solution)/shard_map/ppermute | solution.py:19
  147.5 1.3 collective-permute-start.20
  148.9 0.6 copy.91
  149.5 5.0 %collective-permute-done.20 = f32[256]{0:T(256)S(1)} collective-permute-done((f32[256]{0:T(256)S(1)}, f32[256]{0:T(256)S(1)}, u32[]{:S(2)}, u32[]{:S(2)}) %collective-permute-start.20) | collective-permute-done | bytes 1056 | tf_op jit(solution)/shard_map/ppermute | solution.py:19
  155.6 2.8 %fusion.127 = f32[1,8,256]{2,0,1:T(1,128)S(1)} fusion(f32[8,256,256]{1,2,0:T(8,128)} %copy-done.4, s32[]{:T(128)S(6)} %select_n.26, f32[1,256]{1,0:T(1,128)S(1)} %bitcast.601, f32[1,256]{1,0:T(1,128)S(1)} %bitcast.611, f32[1,256]{1,0:T(1,128)S(1)} %bitcast.596, f32[1,256]{1,0:T(1,128)S(1)} %bitcast.592), kind=kOutput, calls=%fused_computation.227 | convolution fusion | flops 6292224 | bytes 2109444 | tf_op jit(solution)/shard_map/iab,b->ia/dot_general | solution.py:164
  158.4 0.6 bitcast_add_fusion
  (141 shorter events, 17.7 us)
Async XLA Ops:
  0.6 32.5 %copy-start = (bf16[128,64,3,3]{0,1,3,2:T(8,128)(2,1)S(1)}, bf16[128,64,3,3]{0,1,3,2:T(8,128)(2,1)}, u32[]{:S(2)}) copy-start(bf16[128,64,3,3]{0,1,3,2:T(8,128)(2,1)} %param.9) | copy-start | bytes 442372
  0.6 7.0 %copy-start.2 = (f32[256,256]{1,0:T(8,128)S(1)}, f32[256,256]{1,0:T(8,128)}, u32[]{:S(2)}) copy-start(f32[256,256]{1,0:T(8,128)} %param.12) | copy-start | bytes 786436
  0.7 7.8 %copy-start.1 = (f32[256,256]{1,0:T(8,128)S(1)}, f32[256,256]{1,0:T(8,128)}, u32[]{:S(2)}) copy-start(f32[256,256]{1,0:T(8,128)} %param.11) | copy-start | bytes 786436
  0.7 7.9 %copy-start.10 = (f32[32,256]{1,0:T(8,128)S(1)}, f32[32,256]{1,0:T(8,128)}, u32[]{:S(2)}) copy-start(f32[32,256]{1,0:T(8,128)} %param.13) | copy-start | bytes 98308
  3.1 27.0 %collective-permute-start = (bf16[32,8,3,256]{3,1,2,0:T(8,128)(2,1)}, bf16[32,8,3,256]{3,1,2,0:T(8,128)(2,1)}, u32[]{:S(2)}, u32[]{:S(2)}) collective-permute-start(bf16[32,8,3,256]{3,1,2,0:T(8,128)(2,1)} %copy.75), channel_id=1, source_target_pairs={{0,1},{1,2},{2,3},{4,5},{5,6},{6,7},{8,9},{9,10},{10,11},{12,13},{... | collective-permute-start | bytes 1179656 | tf_op jit(solution)/shard_map/ppermute | solution.py:15
  21.0 1.4 copy-start.4
  23.6 6.0 %copy-start.5 = (f32[256,256]{1,0:T(8,128)S(1)}, f32[256,256]{1,0:T(8,128)}, u32[]{:S(2)}) copy-start(f32[256,256]{1,0:T(8,128)} %fusion.99) | copy-start | bytes 786436
  29.5 3.6 %copy-start.15 = (bf16[64,8,3,3]{0,1,3,2:T(8,128)(2,1)S(1)}, bf16[64,8,3,3]{0,1,3,2:T(8,128)(2,1)}, u32[]{:S(2)}) copy-start(bf16[64,8,3,3]{0,1,3,2:T(8,128)(2,1)} %param.8) | copy-start | bytes 27652
  29.5 3.6 %copy-start.16 = (pred[5]{0:T(512)(128)(4,1)S(1)}, pred[5]{0:T(512)(128)(4,1)}, u32[]{:S(2)}) copy-start(pred[5]{0:T(512)(128)(4,1)} %compare_and_fusion) | copy-start | bytes 19
  42.5 11.2 %copy-start.11 = (f32[32,256]{1,0:T(8,128)S(1)}, f32[32,256]{1,0:T(8,128)}, u32[]{:S(2)}) copy-start(f32[32,256]{1,0:T(8,128)} %param.13) | copy-start | bytes 98308
  47.9 11.3 %collective-permute-start.2 = (f32[32,256]{1,0:T(8,128)S(1)}, f32[32,256]{1,0:T(8,128)S(1)}, u32[]{:S(2)}, u32[]{:S(2)}) collective-permute-start(f32[32,256]{1,0:T(8,128)S(1)} %convolution_bitcast_fusion.3), channel_id=1, source_target_pairs={{0,3},{1,0},{2,1},{3,2},{4,7},{5,4},{6,5},{7,6},{8,11},{9,8},{10,9... | collective-permute-start | bytes 98312 | tf_op jit(solution)/shard_map/ppermute | solution.py:49
  48.7 10.4 %collective-permute-start.3 = (f32[32,256]{1,0:T(8,128)S(1)}, f32[32,256]{1,0:T(8,128)S(1)}, u32[]{:S(2)}, u32[]{:S(2)}) collective-permute-start(f32[32,256]{1,0:T(8,128)S(1)} %convolution_bitcast_fusion.3), channel_id=1, source_target_pairs={{0,1},{1,2},{2,3},{3,0},{4,5},{5,6},{6,7},{7,4},{8,9},{9,10},{10,1... | collective-permute-start | bytes 98312 | tf_op jit(solution)/shard_map/ppermute | solution.py:49
  50.0 9.2 %collective-permute-start.1 = (f32[32,256]{1,0:T(8,128)S(1)}, f32[32,256]{1,0:T(8,128)S(1)}, u32[]{:S(2)}, u32[]{:S(2)}) collective-permute-start(f32[32,256]{1,0:T(8,128)S(1)} %convolution_bitcast_fusion.3), channel_id=1, source_target_pairs={{0,2},{1,3},{2,0},{3,1},{4,6},{5,7},{6,4},{7,5},{8,10},{9,11},{10,... | collective-permute-start | bytes 98312 | tf_op jit(solution)/shard_map/ppermute | solution.py:49
  53.8 17.9 %copy-start.6 = (f32[4,8,256]{2,0,1:T(4,128)}, f32[4,8,256]{2,0,1:T(4,128)S(1)}, u32[]{:S(2)}) copy-start(f32[4,8,256]{2,0,1:T(4,128)S(1)} %copy.90) | copy-start | bytes 98308
  53.8 16.0 %collective-permute-start.5 = (f32[256,256]{1,0:T(8,128)S(1)}, f32[256,256]{1,0:T(8,128)S(1)}, u32[]{:S(2)}, u32[]{:S(2)}) collective-permute-start(f32[256,256]{1,0:T(8,128)S(1)} %fusion.93), channel_id=1, source_target_pairs={{0,4},{4,8},{8,12},{12,16},{16,20},{20,24},{24,28},{28,32},{32,36}... | collective-permute-start | bytes 786440 | tf_op jit(solution)/shard_map/ppermute | solution.py:15
  55.7 21.7 %collective-permute-start.7 = (f32[256,256]{1,0:T(8,128)S(1)}, f32[256,256]{1,0:T(8,128)S(1)}, u32[]{:S(2)}, u32[]{:S(2)}) collective-permute-start(f32[256,256]{1,0:T(8,128)S(1)} %fusion.93), channel_id=1, source_target_pairs={{0,8},{4,12},{8,16},{12,20},{16,24},{20,28},{24,32},{28,36},{32,40... | collective-permute-start | bytes 786440 | tf_op jit(solution)/shard_map/ppermute | solution.py:15
  59.2 12.5 %copy-start.8 = (f32[4,8,256]{2,0,1:T(4,128)}, f32[4,8,256]{2,0,1:T(4,128)S(1)}, u32[]{:S(2)}) copy-start(f32[4,8,256]{2,0,1:T(4,128)S(1)} %copy.89) | copy-start | bytes 98308
  62.3 9.4 %copy-start.12 = (f32[1,256]{1,0:T(1,128)}, f32[1,256]{1,0:T(1,128)S(1)}, u32[]{:S(2)}) copy-start(f32[1,256]{1,0:T(1,128)S(1)} %get-tuple-element.22) | copy-start | bytes 3076
  62.3 9.4 %copy-start.14 = (f32[1,256]{1,0:T(1,128)}, f32[1,256]{1,0:T(1,128)S(1)}, u32[]{:S(2)}) copy-start(f32[1,256]{1,0:T(1,128)S(1)} %get-tuple-element.23) | copy-start | bytes 3076
  62.8 7.0 %collective-permute-start.6 = (f32[256]{0:T(256)S(1)}, f32[256]{0:T(256)S(1)}, u32[]{:S(2)}, u32[]{:S(2)}) collective-permute-start(f32[256]{0:T(256)S(1)} %add.157), channel_id=1, source_target_pairs={{0,8},{4,12},{8,16},{12,20},{16,24},{20,28},{24,32},{28,36},{32,40... | collective-permute-start | bytes 3080 | tf_op jit(solution)/shard_map/ppermute | solution.py:15
  66.8 4.9 %collective-permute-start.4 = (f32[256]{0:T(256)S(1)}, f32[256]{0:T(256)S(1)}, u32[]{:S(2)}, u32[]{:S(2)}) collective-permute-start(f32[256]{0:T(256)S(1)} %add.157), channel_id=1, source_target_pairs={{0,4},{4,8},{8,12},{12,16},{16,20},{20,24},{24,28},{28,32},{32,36}... | collective-permute-start | bytes 3080 | tf_op jit(solution)/shard_map/ppermute | solution.py:15
  71.7 28.1 %copy-start.3 = (f32[256,256]{1,0:T(8,128)S(1)}, f32[256,256]{1,0:T(8,128)}, u32[]{:S(2)}) copy-start(f32[256,256]{1,0:T(8,128)} %param.12) | copy-start | bytes 786436
  71.8 8.4 %collective-permute-start.8 = (f32[256]{0:T(256)S(1)}, f32[256]{0:T(256)S(1)}, u32[]{:S(2)}, u32[]{:S(2)}) collective-permute-start(f32[256]{0:T(256)S(1)} %add.158), channel_id=1, source_target_pairs={{0,8},{4,12},{8,16},{12,20},{16,24},{20,28},{24,32},{28,36},{32,40... | collective-permute-start | bytes 3080 | tf_op jit(solution)/shard_map/ppermute | solution.py:15
  77.8 8.3 %collective-permute-start.9 = (f32[256,256]{1,0:T(8,128)S(1)}, f32[256,256]{1,0:T(8,128)S(1)}, u32[]{:S(2)}, u32[]{:S(2)}) collective-permute-start(f32[256,256]{1,0:T(8,128)S(1)} %fusion.151), channel_id=1, source_target_pairs={{0,8},{4,12},{8,16},{12,20},{16,24},{20,28},{24,32},{28,36},{32,40... | collective-permute-start | bytes 786440 | tf_op jit(solution)/shard_map/ppermute | solution.py:15
  80.4 9.1 %collective-permute-start.10 = (f32[256]{0:T(256)S(1)}, f32[256]{0:T(256)S(1)}, u32[]{:S(2)}, u32[]{:S(2)}) collective-permute-start(f32[256]{0:T(256)S(1)} %add.159), channel_id=1, source_target_pairs={{0,16},{4,20},{8,24},{12,28},{16,32},{20,36},{24,40},{28,44},{32,4... | collective-permute-start | bytes 3080 | tf_op jit(solution)/shard_map/ppermute | solution.py:15
  86.5 9.8 %collective-permute-start.11 = (f32[256,256]{1,0:T(8,128)S(1)}, f32[256,256]{1,0:T(8,128)S(1)}, u32[]{:S(2)}, u32[]{:S(2)}) collective-permute-start(f32[256,256]{1,0:T(8,128)S(1)} %fusion.153), channel_id=1, source_target_pairs={{0,16},{4,20},{8,24},{12,28},{16,32},{20,36},{24,40},{28,44},{32,4... | collective-permute-start | bytes 786440 | tf_op jit(solution)/shard_map/ppermute | solution.py:15
  90.4 9.8 %collective-permute-start.12 = (f32[256]{0:T(256)}, f32[256]{0:T(256)}, u32[]{:S(2)}, u32[]{:S(2)}) collective-permute-start(f32[256]{0:T(256)} %add.160), channel_id=1, source_target_pairs={{0,32},{4,36},{8,40},{12,44},{16,48},{20,52},{24,56},{28,60},{32,6... | collective-permute-start | bytes 3080 | tf_op jit(solution)/shard_map/ppermute | solution.py:15
  96.6 8.4 %collective-permute-start.13 = (f32[256,256]{1,0:T(8,128)S(1)}, f32[256,256]{1,0:T(8,128)}, u32[]{:S(2)}, u32[]{:S(2)}) collective-permute-start(f32[256,256]{1,0:T(8,128)S(1)} %fusion.155), channel_id=1, source_target_pairs={{0,32},{4,36},{8,40},{12,44},{16,48},{20,52},{24,56},{28,60},{32,6... | collective-permute-start | bytes 786440 | tf_op jit(solution)/shard_map/ppermute | solution.py:15
  100.2 8.5 %copy-start.13 = (f32[1,256]{1,0:T(1,128)S(1)}, f32[1,256]{1,0:T(1,128)}, u32[]{:S(2)}) copy-start(f32[1,256]{1,0:T(1,128)} %copy-done.12) | copy-start | bytes 3076
  100.2 8.6 %copy-start.7 = (f32[4,8,256]{2,0,1:T(4,128)S(1)}, f32[4,8,256]{2,0,1:T(4,128)}, u32[]{:S(2)}) copy-start(f32[4,8,256]{2,0,1:T(4,128)} %copy-done.6) | copy-start | bytes 98308
  100.2 8.6 %copy-start.9 = (f32[4,8,256]{2,0,1:T(4,128)S(1)}, f32[4,8,256]{2,0,1:T(4,128)}, u32[]{:S(2)}) copy-start(f32[4,8,256]{2,0,1:T(4,128)} %copy-done.8) | copy-start | bytes 98308
  101.9 4.4 %collective-permute-start.14 = (f32[256]{0:T(256)S(1)}, f32[256]{0:T(256)S(1)}, u32[]{:S(2)}, u32[]{:S(2)}) collective-permute-start(f32[256]{0:T(256)S(1)} %add.161), channel_id=1, source_target_pairs={{0,64},{4,68},{8,72},{12,76},{16,80},{20,84},{24,88},{28,92},{32,9... | collective-permute-start | bytes 3080 | tf_op jit(solution)/shard_map/ppermute | solution.py:15
  116.2 9.1 %collective-permute-start.16 = (f32[256]{0:T(256)S(1)}, f32[256]{0:T(256)S(1)}, u32[]{:S(2)}, u32[]{:S(2)}) collective-permute-start(f32[256]{0:T(256)S(1)} %select_add_fusion), channel_id=1, source_target_pairs={{8,0},{12,4},{16,8},{20,12},{24,16},{28,20},{32,24},{36,28},{40,32... | collective-permute-start | bytes 3080 | tf_op jit(solution)/shard_map/ppermute | solution.py:19
  118.9 6.7 %collective-permute-start.15 = (f32[256]{0:T(256)S(1)}, f32[256]{0:T(256)S(1)}, u32[]{:S(2)}, u32[]{:S(2)}) collective-permute-start(f32[256]{0:T(256)S(1)} %select_add_fusion), channel_id=1, source_target_pairs={{4,0},{8,4},{12,8},{16,12},{20,16},{24,20},{28,24},{32,28},{36,32}... | collective-permute-start | bytes 3080 | tf_op jit(solution)/shard_map/ppermute | solution.py:19
  125.7 7.6 %collective-permute-start.17 = (f32[256]{0:T(256)S(1)}, f32[256]{0:T(256)S(1)}, u32[]{:S(2)}, u32[]{:S(2)}) collective-permute-start(f32[256]{0:T(256)S(1)} %add.179), channel_id=1, source_target_pairs={{8,0},{12,4},{16,8},{20,12},{24,16},{28,20},{32,24},{36,28},{40,32... | collective-permute-start | bytes 3080 | tf_op jit(solution)/shard_map/ppermute | solution.py:19
  133.5 7.9 %collective-permute-start.18 = (f32[256]{0:T(256)S(1)}, f32[256]{0:T(256)S(1)}, u32[]{:S(2)}, u32[]{:S(2)}) collective-permute-start(f32[256]{0:T(256)S(1)} %add.180), channel_id=1, source_target_pairs={{16,0},{20,4},{24,8},{28,12},{32,16},{36,20},{40,24},{44,28},{48,3... | collective-permute-start | bytes 3080 | tf_op jit(solution)/shard_map/ppermute | solution.py:19
  141.7 5.5 %collective-permute-start.19 = (f32[256]{0:T(256)S(1)}, f32[256]{0:T(256)S(1)}, u32[]{:S(2)}, u32[]{:S(2)}) collective-permute-start(f32[256]{0:T(256)S(1)} %add.181), channel_id=1, source_target_pairs={{32,0},{36,4},{40,8},{44,12},{48,16},{52,20},{56,24},{60,28},{64,3... | collective-permute-start | bytes 3080 | tf_op jit(solution)/shard_map/ppermute | solution.py:19
  147.5 7.0 %collective-permute-start.20 = (f32[256]{0:T(256)S(1)}, f32[256]{0:T(256)S(1)}, u32[]{:S(2)}, u32[]{:S(2)}) collective-permute-start(f32[256]{0:T(256)S(1)} %add.182), channel_id=1, source_target_pairs={{64,0},{68,4},{72,8},{76,12},{80,16},{84,20},{88,24},{92,28},{96,3... | collective-permute-start | bytes 3080 | tf_op jit(solution)/shard_map/ppermute | solution.py:19

commit v10 on v9

--- a/solution.py
+++ b/solution.py
@@ -135,7 +135,8 @@
     powers = powers[: hours + 1]
     step = powers[hours]
     joined_t = dot(back_gain, transition).T
-    stacked = jnp.stack(powers[:hours])
+    every = jnp.stack(powers[: hours + 1])
+    stacked = every[:hours]
     sources = filtered - jnp.einsum("sia,ab->sib", filtered, joined_t, precision=precise)
     padded = jnp.concatenate([sources, jnp.zeros_like(sources)], axis=1)
     hankel = jnp.stack([padded[:, d : d + hours] for d in range(hours)], axis=2)
@@ -160,8 +161,8 @@
     for s in range(bands - 1, 0, -1):
         inputs.insert(0, heads[s] + dot(step, inputs[0]))
     mine = lax.dynamic_index_in_dim(jnp.stack(inputs), band, 0, False)
-    tails = jnp.stack([powers[hours - i] for i in range(hours)])
-    smoothed = lax.dynamic_index_in_dim(inner, band, 0, False) + jnp.einsum("iab,b->ia", tails, mine, precision=precise)
+    reached = jnp.einsum("jab,b->ja", every[1:], mine, precision=precise)[::-1]
+    smoothed = lax.dynamic_index_in_dim(inner, band, 0, False) + reached
     return lax.dynamic_index_in_dim(filtered, band, 0, False), smoothed
 
 

time: 160 us -> 157 us (0.981)
  local copies, waits for them, and re-layouts: 16.9 us -> 12.6 us
  matrix products: 49.6 us -> 51.5 us
    unnamed x57 -> x58, local copies, waits for them, and re-layouts: 9.97 us -> 6.64 us
    dot_general x3, matrix products: 2.15 us -> 4.83 us  [per_device(): jnp.einsum('ab,sbc->sac', top, jnp.stack(powers[1:]), precision=precise)]
    dot_general x53, matrix products: 19.4 us -> 21.9 us  [dot(): return jnp.dot(a, b, precision=precise)]
  transfers between devices with their start and end apart: 21 -> 21, of which waited for: 9 -> 9; matrix products, arithmetic and copies ran while one was open for 22% -> 23% of each run, Pallas kernels for 0% -> 0%
where the time goes in v10:
time: 157 us; the launch traced here: 156 us
  starting transfers between devices  52.8 us (34%)
  matrix products  51.5 us (33%)
  waiting for transfers between devices  32.7 us (21%)
  local copies, waits for them, and re-layouts  12.6 us (8%)
  other arithmetic  4.88 us (3%)
    ppermute x12, starting transfers between devices, shift_down(): lax.ppermute(value, axis, [(i, i + steps) for i in range(count - steps)])  36.7 us
    ppermute x6, waiting for transfers between devices, shift_up(): lax.ppermute(value, axis, [(i + steps, i) for i in range(count - steps)])  24.3 us
    dot_general x53, matrix products, dot(): return jnp.dot(a, b, precision=precise)  21.9 us
    ppermute x6, starting transfers between devices, shift_up(): lax.ppermute(value, axis, [(i + steps, i) for i in range(count - steps)])  11.2 us
    conv_general_dilated x1, matrix products, conv_stride(): lax.conv_general_dilated(images, kernel, (2, 2), ((0, 0), (1, 1)), dimens...  9.44 us
    ppermute x12, waiting for transfers between devices, shift_down(): lax.ppermute(value, axis, [(i, i + steps) for i in range(count - steps)])  8.4 us
    dot_general x7, matrix products, per_device(): jnp.einsum('ab,sbc->sac', transition, phis, precision=precise)  7.15 us
    unnamed x58, local copies, waits for them, and re-layouts  6.64 us
  transfers between devices with their start and end apart: 21, of which 9 were waited for; matrix products, arithmetic and copies ran while one was open for 23% of the time, Pallas kernels for 0%

profile of v10, /device:TPU:14, one launch (start us, length us, event | category | flops | bytes accessed | tf_op | source)
XLA Modules:
  0.0 156.0 jit_solution(3441415734863366625)
XLA Ops:
  0.7 1.6 %slice.198 = bf16[32,8,3,256]{3,2,1,0:T(4,128)(2,1)S(1)} slice(bf16[32,8,8,256]{3,2,1,0:T(8,128)(2,1)} %param.7), slice={[0:32], [0:8], [5:8], [0:256]} | slice | bytes 786432 | tf_op jit(solution)/shard_map/slice | solution.py:34
  2.3 0.8 copy.75
  3.1 4.6 %collective-permute-start = (bf16[32,8,3,256]{3,1,2,0:T(8,128)(2,1)}, bf16[32,8,3,256]{3,1,2,0:T(8,128)(2,1)}, u32[]{:S(2)}, u32[]{:S(2)}) collective-permute-start(bf16[32,8,3,256]{3,1,2,0:T(8,128)(2,1)} %copy.75), channel_id=1, source_target_pairs={{0,1},{1,2},{2,3},{4,5},{5,6},{6,7},{8,9},{9,10},{10,11},{12,13},{... | collective-permute-start | bytes 1179656 | tf_op jit(solution)/shard_map/ppermute | solution.py:15
  7.6 0.7 convert_dynamic-update-slice_fusion
  8.6 1.0 fusion.27
  9.6 1.0 fusion.26
  10.6 1.0 fusion.25
  11.7 1.0 fusion.24
  12.7 1.0 fusion.23
  13.7 1.0 fusion.22
  14.8 1.0 fusion.21
  17.2 0.7 constant_dynamic-update-slice_fusion.18
  17.9 1.3 constant_dynamic-update-slice_fusion.17
  19.2 1.3 fusion.83
  20.5 3.9 %copy.46 = bf16[32,8,8,256]{0,1,3,2:T(8,128)(2,1)} copy(bf16[32,8,8,256]{3,2,1,0:T(8,128)(2,1)S(1)} %copy-done.5) | data formatting | bytes 2097152 | tf_op args[0]
  24.4 1.5 constant_dynamic-update-slice_fusion.16
  25.9 2.9 %copy.45 = bf16[32,8,3,256]{0,1,3,2:T(8,128)(2,1)} copy(bf16[32,8,3,256]{3,1,2,0:T(8,128)(2,1)} %collective-permute-done) | data formatting | bytes 786432 | tf_op jit(solution)/shard_map/optimization_barrier | solution.py:105
  28.8 9.4 %fusion.4 = f32[32,2,64,128]{3,0,2,1:T(8,128)} fusion(bf16[128,64,3,3]{0,1,3,2:T(8,128)(2,1)S(1)} %copy-done, pred[5]{0:T(512)(128)(4,1)S(1)} %compare_and_fusion, bf16[64,8,3,3]{0,1,3,2:T(8,128)(2,1)S(1)} %copy-done.20, bf16[32,8,8,256]{0,1,3,2:T(8,128)(2,1)} %copy.46, bf16[32,8,3,256]{0,1,3,2:T(8,128)(2,1)} %copy.45), kind=kOutput, calls=%fused_computation.5 | convolution fusion | flops 799834112 | bytes 3695621 | tf_op jit(solution)/shard_map/conv_general_dilated | solution.py:23
  38.3 5.4 %convolution_bitcast_fusion.3 = f32[32,256]{1,0:T(8,128)S(1)} fusion(bf16[2,64,128,256]{3,2,1,0:T(8,128)(2,1)} %param.10, f32[32,2,64,128]{3,0,2,1:T(8,128)} %fusion.4), kind=kOutput, calls=%fused_computation.38 | convolution fusion | flops 271056896 | bytes 10518528 | tf_op jit(solution)/shard_map/shwc,hwcm->sm/dot_general | solution.py:45
  43.7 0.8 collective-permute-start.2
  44.5 1.3 collective-permute-start.3
  45.8 2.9 %collective-permute-start.1 = (f32[32,256]{1,0:T(8,128)S(1)}, f32[32,256]{1,0:T(8,128)S(1)}, u32[]{:S(2)}, u32[]{:S(2)}) collective-permute-start(f32[32,256]{1,0:T(8,128)S(1)} %convolution_bitcast_fusion.3), channel_id=1, source_target_pairs={{0,2},{1,3},{2,0},{3,1},{4,6},{5,7},{6,4},{7,5},{8,10},{9,11},{10,... | collective-permute-start | bytes 98312 | tf_op jit(solution)/shard_map/ppermute | solution.py:49
  48.7 2.0 %constant_dynamic-update-slice_fusion.15 = (f32[9,256,256]{1,2,0:T(8,128)}, f32[4,256,256]{1,2,0:T(8,128)S(1)}) fusion(f32[9,256,256]{1,2,0:T(8,128)} %get-tuple-element.40, f32[2,256,256]{1,2,0:T(8,128)S(1)} %copy-done.7, f32[1,256,256]{1,2,0:T(8,128)S(1)} %bitcast.552, f32[1,256,256]{1,2,0:T(8,128)S(1)} %bitcast.549), kind=kOutput, calls=%fused_computation.154 | convolution fusion | flops 805830656 | bytes 3407872 | tf_op jit(solution)/shard_map/ab,sbc->sac/dot_general | solution.py:133
  50.7 1.9 %collective-permute-start.5 = (f32[256,256]{1,0:T(8,128)S(1)}, f32[256,256]{1,0:T(8,128)S(1)}, u32[]{:S(2)}, u32[]{:S(2)}) collective-permute-start(f32[256,256]{1,0:T(8,128)S(1)} %copy-done.14), channel_id=1, source_target_pairs={{0,4},{4,8},{8,12},{12,16},{16,20},{20,24},{24,28},{28,32},{32,36}... | collective-permute-start | bytes 786440 | tf_op jit(solution)/shard_map/ppermute | solution.py:15
  52.6 3.4 %collective-permute-start.7 = (f32[256,256]{1,0:T(8,128)S(1)}, f32[256,256]{1,0:T(8,128)S(1)}, u32[]{:S(2)}, u32[]{:S(2)}) collective-permute-start(f32[256,256]{1,0:T(8,128)S(1)} %copy-done.14), channel_id=1, source_target_pairs={{0,8},{4,12},{8,16},{12,20},{16,24},{20,28},{24,32},{28,36},{32,40... | collective-permute-start | bytes 786440 | tf_op jit(solution)/shard_map/ppermute | solution.py:15
  58.6 0.6 fusion.137
  59.7 3.4 %collective-permute-start.6 = (f32[256]{0:T(256)S(1)}, f32[256]{0:T(256)S(1)}, u32[]{:S(2)}, u32[]{:S(2)}) collective-permute-start(f32[256]{0:T(256)S(1)} %add.157), channel_id=1, source_target_pairs={{0,8},{4,12},{8,16},{12,20},{16,24},{20,28},{24,32},{28,36},{32,40... | collective-permute-start | bytes 3080 | tf_op jit(solution)/shard_map/ppermute | solution.py:15
  63.8 2.9 %collective-permute-start.4 = (f32[256]{0:T(256)S(1)}, f32[256]{0:T(256)S(1)}, u32[]{:S(2)}, u32[]{:S(2)}) collective-permute-start(f32[256]{0:T(256)S(1)} %add.157), channel_id=1, source_target_pairs={{0,4},{4,8},{8,12},{12,16},{16,20},{20,24},{24,28},{28,32},{32,36}... | collective-permute-start | bytes 3080 | tf_op jit(solution)/shard_map/ppermute | solution.py:15
  67.0 1.7 %collective-permute-done.4 = f32[256]{0:T(256)S(1)} collective-permute-done((f32[256]{0:T(256)S(1)}, f32[256]{0:T(256)S(1)}, u32[]{:S(2)}, u32[]{:S(2)}) %collective-permute-start.4) | collective-permute-done | bytes 1056 | tf_op jit(solution)/shard_map/ppermute | solution.py:15
  68.6 5.7 %collective-permute-start.8 = (f32[256]{0:T(256)S(1)}, f32[256]{0:T(256)S(1)}, u32[]{:S(2)}, u32[]{:S(2)}) collective-permute-start(f32[256]{0:T(256)S(1)} %add.158), channel_id=1, source_target_pairs={{0,8},{4,12},{8,16},{12,20},{16,24},{20,28},{24,32},{28,36},{32,40... | collective-permute-start | bytes 3080 | tf_op jit(solution)/shard_map/ppermute | solution.py:15
  74.8 1.9 %collective-permute-start.9 = (f32[256,256]{1,0:T(8,128)S(1)}, f32[256,256]{1,0:T(8,128)S(1)}, u32[]{:S(2)}, u32[]{:S(2)}) collective-permute-start(f32[256,256]{1,0:T(8,128)S(1)} %fusion.139), channel_id=1, source_target_pairs={{0,8},{4,12},{8,16},{12,20},{16,24},{20,28},{24,32},{28,36},{32,40... | collective-permute-start | bytes 786440 | tf_op jit(solution)/shard_map/ppermute | solution.py:15
  77.4 3.2 %collective-permute-start.10 = (f32[256]{0:T(256)S(1)}, f32[256]{0:T(256)S(1)}, u32[]{:S(2)}, u32[]{:S(2)}) collective-permute-start(f32[256]{0:T(256)S(1)} %add.159), channel_id=1, source_target_pairs={{0,16},{4,20},{8,24},{12,28},{16,32},{20,36},{24,40},{28,44},{32,4... | collective-permute-start | bytes 3080 | tf_op jit(solution)/shard_map/ppermute | solution.py:15
  80.5 2.5 %collective-permute-done.9 = f32[256,256]{1,0:T(8,128)S(1)} collective-permute-done((f32[256,256]{1,0:T(8,128)S(1)}, f32[256,256]{1,0:T(8,128)S(1)}, u32[]{:S(2)}, u32[]{:S(2)}) %collective-permute-start.9) | collective-permute-done | bytes 262176 | tf_op jit(solution)/shard_map/ppermute | solution.py:15
  83.4 2.5 %collective-permute-start.11 = (f32[256,256]{1,0:T(8,128)S(1)}, f32[256,256]{1,0:T(8,128)S(1)}, u32[]{:S(2)}, u32[]{:S(2)}) collective-permute-start(f32[256,256]{1,0:T(8,128)S(1)} %fusion.141), channel_id=1, source_target_pairs={{0,16},{4,20},{8,24},{12,28},{16,32},{20,36},{24,40},{28,44},{32,4... | collective-permute-start | bytes 786440 | tf_op jit(solution)/shard_map/ppermute | solution.py:15
  86.6 0.6 add.160
  87.3 2.6 %collective-permute-start.12 = (f32[256]{0:T(256)}, f32[256]{0:T(256)}, u32[]{:S(2)}, u32[]{:S(2)}) collective-permute-start(f32[256]{0:T(256)} %add.160), channel_id=1, source_target_pairs={{0,32},{4,36},{8,40},{12,44},{16,48},{20,52},{24,56},{28,60},{32,6... | collective-permute-start | bytes 3080 | tf_op jit(solution)/shard_map/ppermute | solution.py:15
  89.8 3.4 %collective-permute-done.11 = f32[256,256]{1,0:T(8,128)S(1)} collective-permute-done((f32[256,256]{1,0:T(8,128)S(1)}, f32[256,256]{1,0:T(8,128)S(1)}, u32[]{:S(2)}, u32[]{:S(2)}) %collective-permute-start.11) | collective-permute-done | bytes 262176 | tf_op jit(solution)/shard_map/ppermute | solution.py:15
  93.2 1.1 fusion.143
  94.3 3.2 %collective-permute-start.13 = (f32[256,256]{1,0:T(8,128)}, f32[256,256]{1,0:T(8,128)}, u32[]{:S(2)}, u32[]{:S(2)}) collective-permute-start(f32[256,256]{1,0:T(8,128)} %fusion.143), channel_id=1, source_target_pairs={{0,32},{4,36},{8,40},{12,44},{16,48},{20,52},{24,56},{28,60},{32,6... | collective-permute-start | bytes 786440 | tf_op jit(solution)/shard_map/ppermute | solution.py:15
  97.5 1.1 convolution_bitcast_fusion.2
  98.5 1.3 fusion.144
  99.8 0.7 add.161
  100.6 1.4 collective-permute-start.14
  102.0 0.9 collective-permute-done.13
  102.8 1.4 fusion.145
  104.8 0.7 add.163
  105.8 0.7 add.164
  106.6 0.6 add.165
  107.3 0.9 constant_dynamic-update-slice_fusion.6
  111.1 1.3 fusion.28
  113.9 2.1 %collective-permute-start.16 = (f32[256]{0:T(256)S(1)}, f32[256]{0:T(256)S(1)}, u32[]{:S(2)}, u32[]{:S(2)}) collective-permute-start(f32[256]{0:T(256)S(1)} %select_add_fusion), channel_id=1, source_target_pairs={{8,0},{12,4},{16,8},{20,12},{24,16},{28,20},{32,24},{36,28},{40,32... | collective-permute-start | bytes 3080 | tf_op jit(solution)/shard_map/ppermute | solution.py:19
  116.3 1.9 %collective-permute-start.15 = (f32[256]{0:T(256)S(1)}, f32[256]{0:T(256)S(1)}, u32[]{:S(2)}, u32[]{:S(2)}) collective-permute-start(f32[256]{0:T(256)S(1)} %select_add_fusion), channel_id=1, source_target_pairs={{4,0},{8,4},{12,8},{16,12},{20,16},{24,20},{28,24},{32,28},{36,32}... | collective-permute-start | bytes 3080 | tf_op jit(solution)/shard_map/ppermute | solution.py:19
  118.2 5.6 %collective-permute-done.16 = f32[256]{0:T(256)S(1)} collective-permute-done((f32[256]{0:T(256)S(1)}, f32[256]{0:T(256)S(1)}, u32[]{:S(2)}, u32[]{:S(2)}) %collective-permute-start.16) | collective-permute-done | bytes 1056 | tf_op jit(solution)/shard_map/ppermute | solution.py:19
  124.2 1.9 %collective-permute-start.17 = (f32[256]{0:T(256)S(1)}, f32[256]{0:T(256)S(1)}, u32[]{:S(2)}, u32[]{:S(2)}) collective-permute-start(f32[256]{0:T(256)S(1)} %add.179), channel_id=1, source_target_pairs={{8,0},{12,4},{16,8},{20,12},{24,16},{28,20},{32,24},{36,28},{40,32... | collective-permute-start | bytes 3080 | tf_op jit(solution)/shard_map/ppermute | solution.py:19
  126.5 5.3 %collective-permute-done.17 = f32[256]{0:T(256)S(1)} collective-permute-done((f32[256]{0:T(256)S(1)}, f32[256]{0:T(256)S(1)}, u32[]{:S(2)}, u32[]{:S(2)}) %collective-permute-start.17) | collective-permute-done | bytes 1056 | tf_op jit(solution)/shard_map/ppermute | solution.py:19
  132.1 2.0 %collective-permute-start.18 = (f32[256]{0:T(256)S(1)}, f32[256]{0:T(256)S(1)}, u32[]{:S(2)}, u32[]{:S(2)}) collective-permute-start(f32[256]{0:T(256)S(1)} %add.180), channel_id=1, source_target_pairs={{16,0},{20,4},{24,8},{28,12},{32,16},{36,20},{40,24},{44,28},{48,3... | collective-permute-start | bytes 3080 | tf_op jit(solution)/shard_map/ppermute | solution.py:19
  134.4 5.6 %collective-permute-done.18 = f32[256]{0:T(256)S(1)} collective-permute-done((f32[256]{0:T(256)S(1)}, f32[256]{0:T(256)S(1)}, u32[]{:S(2)}, u32[]{:S(2)}) %collective-permute-start.18) | collective-permute-done | bytes 1056 | tf_op jit(solution)/shard_map/ppermute | solution.py:19
  140.2 2.0 %collective-permute-start.19 = (f32[256]{0:T(256)S(1)}, f32[256]{0:T(256)S(1)}, u32[]{:S(2)}, u32[]{:S(2)}) collective-permute-start(f32[256]{0:T(256)S(1)} %add.181), channel_id=1, source_target_pairs={{32,0},{36,4},{40,8},{44,12},{48,16},{52,20},{56,24},{60,28},{64,3... | collective-permute-start | bytes 3080 | tf_op jit(solution)/shard_map/ppermute | solution.py:19
  142.2 0.8 constant_dynamic-slice_fusion.1
  143.0 2.8 %collective-permute-done.19 = f32[256]{0:T(256)S(1)} collective-permute-done((f32[256]{0:T(256)S(1)}, f32[256]{0:T(256)S(1)}, u32[]{:S(2)}, u32[]{:S(2)}) %collective-permute-start.19) | collective-permute-done | bytes 1056 | tf_op jit(solution)/shard_map/ppermute | solution.py:19
  146.0 1.3 collective-permute-start.20
  148.0 5.0 %collective-permute-done.20 = f32[256]{0:T(256)S(1)} collective-permute-done((f32[256]{0:T(256)S(1)}, f32[256]{0:T(256)S(1)}, u32[]{:S(2)}, u32[]{:S(2)}) %collective-permute-start.20) | collective-permute-done | bytes 1056 | tf_op jit(solution)/shard_map/ppermute | solution.py:19
  154.2 1.2 fusion.13
  155.4 0.6 bitcast_add_fusion
  (142 shorter events, 16.7 us)
Async XLA Ops:
  0.6 28.2 %copy-start = (bf16[128,64,3,3]{0,1,3,2:T(8,128)(2,1)S(1)}, bf16[128,64,3,3]{0,1,3,2:T(8,128)(2,1)}, u32[]{:S(2)}) copy-start(bf16[128,64,3,3]{0,1,3,2:T(8,128)(2,1)} %param.9) | copy-start | bytes 442372
  0.6 7.7 %copy-start.1 = (f32[256,256]{1,0:T(8,128)S(1)}, f32[256,256]{1,0:T(8,128)}, u32[]{:S(2)}) copy-start(f32[256,256]{1,0:T(8,128)} %param.11) | copy-start | bytes 786436
  0.7 7.8 %copy-start.15 = (f32[32,256]{1,0:T(8,128)S(1)}, f32[32,256]{1,0:T(8,128)}, u32[]{:S(2)}) copy-start(f32[32,256]{1,0:T(8,128)} %param.13) | copy-start | bytes 98308
  3.1 22.9 %collective-permute-start = (bf16[32,8,3,256]{3,1,2,0:T(8,128)(2,1)}, bf16[32,8,3,256]{3,1,2,0:T(8,128)(2,1)}, u32[]{:S(2)}, u32[]{:S(2)}) collective-permute-start(bf16[32,8,3,256]{3,1,2,0:T(8,128)(2,1)} %copy.75), channel_id=1, source_target_pairs={{0,1},{1,2},{2,3},{4,5},{5,6},{6,7},{8,9},{9,10},{10,11},{12,13},{... | collective-permute-start | bytes 1179656 | tf_op jit(solution)/shard_map/ppermute | solution.py:15
  14.8 2.3 %copy-start.2 = (f32[256,256]{1,0:T(8,128)S(1)}, f32[256,256]{1,0:T(8,128)}, u32[]{:S(2)}) copy-start(f32[256,256]{1,0:T(8,128)} %param.12) | copy-start | bytes 786436
  15.8 4.7 %copy-start.5 = (bf16[32,8,8,256]{3,2,1,0:T(8,128)(2,1)S(1)}, bf16[32,8,8,256]{3,2,1,0:T(8,128)(2,1)}, u32[]{:S(2)}) copy-start(bf16[32,8,8,256]{3,2,1,0:T(8,128)(2,1)} %param.7) | copy-start | bytes 3145732
  19.2 29.5 %copy-start.3 = (f32[256,256]{1,0:T(8,128)}, f32[256,256]{1,0:T(8,128)S(1)}, u32[]{:S(2)}) copy-start(f32[256,256]{1,0:T(8,128)S(1)} %get-tuple-element.39) | copy-start | bytes 786436
  24.4 4.5 %copy-start.20 = (bf16[64,8,3,3]{0,1,3,2:T(8,128)(2,1)S(1)}, bf16[64,8,3,3]{0,1,3,2:T(8,128)(2,1)}, u32[]{:S(2)}) copy-start(bf16[64,8,3,3]{0,1,3,2:T(8,128)(2,1)} %param.8) | copy-start | bytes 27652
  38.3 10.4 %copy-start.7 = (f32[2,256,256]{1,2,0:T(8,128)S(1)}, f32[2,256,256]{1,2,0:T(8,128)}, u32[]{:S(2)}) copy-start(f32[2,256,256]{1,2,0:T(8,128)} %get-tuple-element.41) | copy-start | bytes 1572868
  43.7 7.0 %copy-start.16 = (f32[32,256]{1,0:T(8,128)S(1)}, f32[32,256]{1,0:T(8,128)}, u32[]{:S(2)}) copy-start(f32[32,256]{1,0:T(8,128)} %param.13) | copy-start | bytes 98308
  43.7 7.0 %copy-start.14 = (f32[256,256]{1,0:T(8,128)S(1)}, f32[256,256]{1,0:T(8,128)}, u32[]{:S(2)}) copy-start(f32[256,256]{1,0:T(8,128)} %fusion.83) | copy-start | bytes 786436
  43.7 12.3 %collective-permute-start.2 = (f32[32,256]{1,0:T(8,128)S(1)}, f32[32,256]{1,0:T(8,128)S(1)}, u32[]{:S(2)}, u32[]{:S(2)}) collective-permute-start(f32[32,256]{1,0:T(8,128)S(1)} %convolution_bitcast_fusion.3), channel_id=1, source_target_pairs={{0,3},{1,0},{2,1},{3,2},{4,7},{5,4},{6,5},{7,6},{8,11},{9,8},{10,9... | collective-permute-start | bytes 98312 | tf_op jit(solution)/shard_map/ppermute | solution.py:49
  44.5 11.5 %collective-permute-start.3 = (f32[32,256]{1,0:T(8,128)S(1)}, f32[32,256]{1,0:T(8,128)S(1)}, u32[]{:S(2)}, u32[]{:S(2)}) collective-permute-start(f32[32,256]{1,0:T(8,128)S(1)} %convolution_bitcast_fusion.3), channel_id=1, source_target_pairs={{0,1},{1,2},{2,3},{3,0},{4,5},{5,6},{6,7},{7,4},{8,9},{9,10},{10,1... | collective-permute-start | bytes 98312 | tf_op jit(solution)/shard_map/ppermute | solution.py:49
  45.8 10.2 %collective-permute-start.1 = (f32[32,256]{1,0:T(8,128)S(1)}, f32[32,256]{1,0:T(8,128)S(1)}, u32[]{:S(2)}, u32[]{:S(2)}) collective-permute-start(f32[32,256]{1,0:T(8,128)S(1)} %convolution_bitcast_fusion.3), channel_id=1, source_target_pairs={{0,2},{1,3},{2,0},{3,1},{4,6},{5,7},{6,4},{7,5},{8,10},{9,11},{10,... | collective-permute-start | bytes 98312 | tf_op jit(solution)/shard_map/ppermute | solution.py:49
  50.7 12.4 %copy-start.10 = (f32[4,8,256]{2,0,1:T(4,128)}, f32[4,8,256]{2,0,1:T(4,128)S(1)}, u32[]{:S(2)}) copy-start(f32[4,8,256]{2,0,1:T(4,128)S(1)} %copy.90) | copy-start | bytes 98308
  50.7 16.0 %collective-permute-start.5 = (f32[256,256]{1,0:T(8,128)S(1)}, f32[256,256]{1,0:T(8,128)S(1)}, u32[]{:S(2)}, u32[]{:S(2)}) collective-permute-start(f32[256,256]{1,0:T(8,128)S(1)} %copy-done.14), channel_id=1, source_target_pairs={{0,4},{4,8},{8,12},{12,16},{16,20},{20,24},{24,28},{28,32},{32,36}... | collective-permute-start | bytes 786440 | tf_op jit(solution)/shard_map/ppermute | solution.py:15
  52.6 21.8 %collective-permute-start.7 = (f32[256,256]{1,0:T(8,128)S(1)}, f32[256,256]{1,0:T(8,128)S(1)}, u32[]{:S(2)}, u32[]{:S(2)}) collective-permute-start(f32[256,256]{1,0:T(8,128)S(1)} %copy-done.14), channel_id=1, source_target_pairs={{0,8},{4,12},{8,16},{12,20},{16,24},{20,28},{24,32},{28,36},{32,40... | collective-permute-start | bytes 786440 | tf_op jit(solution)/shard_map/ppermute | solution.py:15
  56.1 7.0 %copy-start.12 = (f32[4,8,256]{2,0,1:T(4,128)}, f32[4,8,256]{2,0,1:T(4,128)S(1)}, u32[]{:S(2)}) copy-start(f32[4,8,256]{2,0,1:T(4,128)S(1)} %copy.89) | copy-start | bytes 98308
  59.2 3.9 %copy-start.18 = (f32[1,256]{1,0:T(1,128)}, f32[1,256]{1,0:T(1,128)S(1)}, u32[]{:S(2)}) copy-start(f32[1,256]{1,0:T(1,128)S(1)} %get-tuple-element.20) | copy-start | bytes 3076
  59.2 3.9 %copy-start.19 = (f32[1,256]{1,0:T(1,128)}, f32[1,256]{1,0:T(1,128)S(1)}, u32[]{:S(2)}) copy-start(f32[1,256]{1,0:T(1,128)S(1)} %get-tuple-element.21) | copy-start | bytes 3076
  59.7 7.0 %collective-permute-start.6 = (f32[256]{0:T(256)S(1)}, f32[256]{0:T(256)S(1)}, u32[]{:S(2)}, u32[]{:S(2)}) collective-permute-start(f32[256]{0:T(256)S(1)} %add.157), channel_id=1, source_target_pairs={{0,8},{4,12},{8,16},{12,20},{16,24},{20,28},{24,32},{28,36},{32,40... | collective-permute-start | bytes 3080 | tf_op jit(solution)/shard_map/ppermute | solution.py:15
  63.8 4.9 %collective-permute-start.4 = (f32[256]{0:T(256)S(1)}, f32[256]{0:T(256)S(1)}, u32[]{:S(2)}, u32[]{:S(2)}) collective-permute-start(f32[256]{0:T(256)S(1)} %add.157), channel_id=1, source_target_pairs={{0,4},{4,8},{8,12},{12,16},{16,20},{20,24},{24,28},{28,32},{32,36}... | collective-permute-start | bytes 3080 | tf_op jit(solution)/shard_map/ppermute | solution.py:15
  68.6 8.4 %collective-permute-start.8 = (f32[256]{0:T(256)S(1)}, f32[256]{0:T(256)S(1)}, u32[]{:S(2)}, u32[]{:S(2)}) collective-permute-start(f32[256]{0:T(256)S(1)} %add.158), channel_id=1, source_target_pairs={{0,8},{4,12},{8,16},{12,20},{16,24},{20,28},{24,32},{28,36},{32,40... | collective-permute-start | bytes 3080 | tf_op jit(solution)/shard_map/ppermute | solution.py:15
  74.8 8.3 %collective-permute-start.9 = (f32[256,256]{1,0:T(8,128)S(1)}, f32[256,256]{1,0:T(8,128)S(1)}, u32[]{:S(2)}, u32[]{:S(2)}) collective-permute-start(f32[256,256]{1,0:T(8,128)S(1)} %fusion.139), channel_id=1, source_target_pairs={{0,8},{4,12},{8,16},{12,20},{16,24},{20,28},{24,32},{28,36},{32,40... | collective-permute-start | bytes 786440 | tf_op jit(solution)/shard_map/ppermute | solution.py:15
  77.4 9.0 %collective-permute-start.10 = (f32[256]{0:T(256)S(1)}, f32[256]{0:T(256)S(1)}, u32[]{:S(2)}, u32[]{:S(2)}) collective-permute-start(f32[256]{0:T(256)S(1)} %add.159), channel_id=1, source_target_pairs={{0,16},{4,20},{8,24},{12,28},{16,32},{20,36},{24,40},{28,44},{32,4... | collective-permute-start | bytes 3080 | tf_op jit(solution)/shard_map/ppermute | solution.py:15
  83.4 9.8 %collective-permute-start.11 = (f32[256,256]{1,0:T(8,128)S(1)}, f32[256,256]{1,0:T(8,128)S(1)}, u32[]{:S(2)}, u32[]{:S(2)}) collective-permute-start(f32[256,256]{1,0:T(8,128)S(1)} %fusion.141), channel_id=1, source_target_pairs={{0,16},{4,20},{8,24},{12,28},{16,32},{20,36},{24,40},{28,44},{32,4... | collective-permute-start | bytes 786440 | tf_op jit(solution)/shard_map/ppermute | solution.py:15
  87.3 11.3 %collective-permute-start.12 = (f32[256]{0:T(256)}, f32[256]{0:T(256)}, u32[]{:S(2)}, u32[]{:S(2)}) collective-permute-start(f32[256]{0:T(256)} %add.160), channel_id=1, source_target_pairs={{0,32},{4,36},{8,40},{12,44},{16,48},{20,52},{24,56},{28,60},{32,6... | collective-permute-start | bytes 3080 | tf_op jit(solution)/shard_map/ppermute | solution.py:15
  94.3 8.6 %collective-permute-start.13 = (f32[256,256]{1,0:T(8,128)}, f32[256,256]{1,0:T(8,128)}, u32[]{:S(2)}, u32[]{:S(2)}) collective-permute-start(f32[256,256]{1,0:T(8,128)} %fusion.143), channel_id=1, source_target_pairs={{0,32},{4,36},{8,40},{12,44},{16,48},{20,52},{24,56},{28,60},{32,6... | collective-permute-start | bytes 786440 | tf_op jit(solution)/shard_map/ppermute | solution.py:15
  98.5 12.1 %copy-start.9 = (f32[256,256,1]{1,0,2:T(8,128)S(1)}, f32[256,256,1]{1,0,2:T(8,128)}, u32[]{:S(2)}) copy-start(f32[256,256,1]{1,0,2:T(8,128)} %convolution_bitcast_fusion.2) | copy-start | bytes 786436
  98.5 9.7 %copy-start.11 = (f32[4,8,256]{2,0,1:T(4,128)S(1)}, f32[4,8,256]{2,0,1:T(4,128)}, u32[]{:S(2)}) copy-start(f32[4,8,256]{2,0,1:T(4,128)} %copy-done.10) | copy-start | bytes 98308
  98.5 9.7 %copy-start.13 = (f32[4,8,256]{2,0,1:T(4,128)S(1)}, f32[4,8,256]{2,0,1:T(4,128)}, u32[]{:S(2)}) copy-start(f32[4,8,256]{2,0,1:T(4,128)} %copy-done.12) | copy-start | bytes 98308
  100.6 10.5 %copy-start.6 = (f32[9,256,256]{1,2,0:T(8,128)S(1)}, f32[9,256,256]{1,2,0:T(8,128)}, u32[]{:S(2)}) copy-start(f32[9,256,256]{1,2,0:T(8,128)} %get-tuple-element.42) | copy-start | bytes 7077892
  100.6 3.7 %collective-permute-start.14 = (f32[256]{0:T(256)S(1)}, f32[256]{0:T(256)S(1)}, u32[]{:S(2)}, u32[]{:S(2)}) collective-permute-start(f32[256]{0:T(256)S(1)} %add.161), channel_id=1, source_target_pairs={{0,64},{4,68},{8,72},{12,76},{16,80},{20,84},{24,88},{28,92},{32,9... | collective-permute-start | bytes 3080 | tf_op jit(solution)/shard_map/ppermute | solution.py:15
  110.6 5.7 %copy-start.17 = (f32[8,256,4]{1,2,0:T(4,128)}, f32[8,256,4]{1,2,0:T(4,128)S(1)}, u32[]{:S(2)}) copy-start(f32[8,256,4]{1,2,0:T(4,128)S(1)} %fusion.32) | copy-start | bytes 98308
  113.8 40.4 %copy-start.4 = (f32[256,256]{1,0:T(8,128)S(1)}, f32[256,256]{1,0:T(8,128)}, u32[]{:S(2)}) copy-start(f32[256,256]{1,0:T(8,128)} %copy-done.3) | copy-start | bytes 786436
  113.8 40.4 %copy-start.8 = (f32[2,256,256]{1,2,0:T(8,128)S(1)}, f32[2,256,256]{1,2,0:T(8,128)}, u32[]{:S(2)}) copy-start(f32[2,256,256]{1,2,0:T(8,128)} %get-tuple-element.41) | copy-start | bytes 1572868
  113.9 10.0 %collective-permute-start.16 = (f32[256]{0:T(256)S(1)}, f32[256]{0:T(256)S(1)}, u32[]{:S(2)}, u32[]{:S(2)}) collective-permute-start(f32[256]{0:T(256)S(1)} %select_add_fusion), channel_id=1, source_target_pairs={{8,0},{12,4},{16,8},{20,12},{24,16},{28,20},{32,24},{36,28},{40,32... | collective-permute-start | bytes 3080 | tf_op jit(solution)/shard_map/ppermute | solution.py:19
  116.3 7.8 %collective-permute-start.15 = (f32[256]{0:T(256)S(1)}, f32[256]{0:T(256)S(1)}, u32[]{:S(2)}, u32[]{:S(2)}) collective-permute-start(f32[256]{0:T(256)S(1)} %select_add_fusion), channel_id=1, source_target_pairs={{4,0},{8,4},{12,8},{16,12},{20,16},{24,20},{28,24},{32,28},{36,32}... | collective-permute-start | bytes 3080 | tf_op jit(solution)/shard_map/ppermute | solution.py:19
  124.2 7.6 %collective-permute-start.17 = (f32[256]{0:T(256)S(1)}, f32[256]{0:T(256)S(1)}, u32[]{:S(2)}, u32[]{:S(2)}) collective-permute-start(f32[256]{0:T(256)S(1)} %add.179), channel_id=1, source_target_pairs={{8,0},{12,4},{16,8},{20,12},{24,16},{28,20},{32,24},{36,28},{40,32... | collective-permute-start | bytes 3080 | tf_op jit(solution)/shard_map/ppermute | solution.py:19
  132.1 7.9 %collective-permute-start.18 = (f32[256]{0:T(256)S(1)}, f32[256]{0:T(256)S(1)}, u32[]{:S(2)}, u32[]{:S(2)}) collective-permute-start(f32[256]{0:T(256)S(1)} %add.180), channel_id=1, source_target_pairs={{16,0},{20,4},{24,8},{28,12},{32,16},{36,20},{40,24},{44,28},{48,3... | collective-permute-start | bytes 3080 | tf_op jit(solution)/shard_map/ppermute | solution.py:19
  140.2 5.5 %collective-permute-start.19 = (f32[256]{0:T(256)S(1)}, f32[256]{0:T(256)S(1)}, u32[]{:S(2)}, u32[]{:S(2)}) collective-permute-start(f32[256]{0:T(256)S(1)} %add.181), channel_id=1, source_target_pairs={{32,0},{36,4},{40,8},{44,12},{48,16},{52,20},{56,24},{60,28},{64,3... | collective-permute-start | bytes 3080 | tf_op jit(solution)/shard_map/ppermute | solution.py:19
  146.0 7.0 %collective-permute-start.20 = (f32[256]{0:T(256)S(1)}, f32[256]{0:T(256)S(1)}, u32[]{:S(2)}, u32[]{:S(2)}) collective-permute-start(f32[256]{0:T(256)S(1)} %add.182), channel_id=1, source_target_pairs={{64,0},{68,4},{72,8},{76,12},{80,16},{84,20},{88,24},{92,28},{96,3... | collective-permute-start | bytes 3080 | tf_op jit(solution)/shard_map/ppermute | solution.py:19

commit v11 on v10

--- a/solution.py
+++ b/solution.py
@@ -98,8 +98,11 @@
     for i in range(1, hours):
         phis = gates[:, i, :, None] * jnp.einsum("ab,sbc->sac", transition, phis, precision=precise)
     block_phi = phis[0]
+    leading = [jnp.eye(modes, dtype=jnp.float32), block_phi]
     for s in range(1, bands):
         block_phi = dot(phis[s], block_phi)
+        leading.append(block_phi)
+    leading = jnp.stack(leading[:bands])
 
     above = halo(fields, bands)
     above, block_phi = lax.optimization_barrier((above, block_phi))
@@ -116,11 +119,11 @@
     for s in range(1, bands):
         block_sum = dot(phis[s], block_sum) + ends[s]
 
+    offsets = [jnp.zeros_like(ends[0])]
+    for s in range(bands - 1):
+        offsets.append(dot(phis[s], offsets[-1]) + ends[s])
     carry = exclusive_scan(block_phi, block_sum, "tm", blocks)
-    starts = [carry]
-    for s in range(bands - 1):
-        starts.append(dot(phis[s], starts[-1]) + ends[s])
-    state = jnp.stack(starts).T
+    state = (jnp.einsum("sab,b->sa", leading, carry, precision=precise) + jnp.stack(offsets)).T
     filtered = []
     for i in range(hours):
         state = gate_cols[i] * dot(transition, state) + step_cols[i]

time: 157 us -> 162 us (1.032)
  local copies, waits for them, and re-layouts: 12.6 us -> 17.8 us
    dot_general x0 -> x2, local copies, waits for them, and re-layouts: none -> 3.58 us  [dot(): return jnp.dot(a, b, precision=precise)]
    unnamed x58 -> x62, local copies, waits for them, and re-layouts: 6.64 us -> 8.75 us
    add x3 -> x1, other arithmetic: 2.02 us -> 0.01 us  [per_device(): offsets.append(dot(phis[s], offsets[-1]) + ends[s])]
    dot_general x0 -> x1, matrix products: none -> 1.98 us  [per_device(): jnp.einsum('sab,b->sa', leading, carry, precision=precise)]
    dot_general x53, matrix products: 21.9 us -> 20.1 us  [dot(): return jnp.dot(a, b, precision=precise)]
    ppermute x12, waiting for transfers between devices: 8.4 us -> 6.71 us  [shift_down(): lax.ppermute(value, axis, [(i, i + steps) for i in range(count - steps)])]
  transfers between devices with their start and end apart: 21 -> 21, of which waited for: 9 -> 8; matrix products, arithmetic and copies ran while one was open for 23% -> 26% of each run, Pallas kernels for 0% -> 0%
where the time goes in v11:
time: 162 us; the launch traced here: 161 us
  starting transfers between devices  53.1 us (33%)
  matrix products  51.6 us (32%)
  waiting for transfers between devices  32.4 us (20%)
  local copies, waits for them, and re-layouts  17.8 us (11%)
  other arithmetic  4.63 us (3%)
    ppermute x12, starting transfers between devices, shift_down(): lax.ppermute(value, axis, [(i, i + steps) for i in range(count - steps)])  36.7 us
    ppermute x6, waiting for transfers between devices, shift_up(): lax.ppermute(value, axis, [(i + steps, i) for i in range(count - steps)])  25.7 us
    dot_general x53, matrix products, dot(): return jnp.dot(a, b, precision=precise)  20.1 us
    ppermute x6, starting transfers between devices, shift_up(): lax.ppermute(value, axis, [(i + steps, i) for i in range(count - steps)])  11.4 us
    conv_general_dilated x1, matrix products, conv_stride(): lax.conv_general_dilated(images, kernel, (2, 2), ((0, 0), (1, 1)), dimens...  9.43 us
    unnamed x62, local copies, waits for them, and re-layouts  8.75 us
    dot_general x7, matrix products, per_device(): jnp.einsum('ab,sbc->sac', transition, phis, precision=precise)  7.15 us
    ppermute x12, waiting for transfers between devices, shift_down(): lax.ppermute(value, axis, [(i, i + steps) for i in range(count - steps)])  6.71 us
  transfers between devices with their start and end apart: 21, of which 8 were waited for; matrix products, arithmetic and copies ran while one was open for 26% of the time, Pallas kernels for 0%

profile of v11, /device:TPU:14, one launch (start us, length us, event | category | flops | bytes accessed | tf_op | source)
XLA Modules:
  0.0 161.1 jit_solution(6301631245541708394)
XLA Ops:
  0.7 1.6 slice.199
  2.3 0.8 copy.84
  3.1 4.6 %collective-permute-start = (bf16[32,8,3,256]{3,1,2,0:T(8,128)(2,1)}, bf16[32,8,3,256]{3,1,2,0:T(8,128)(2,1)}, u32[]{:S(2)}, u32[]{:S(2)}) collective-permute-start(bf16[32,8,3,256]{3,1,2,0:T(8,128)(2,1)} %copy.84), channel_id=1, source_target_pairs={{0,1},{1,2},{2,3},{4,5},{5,6},{6,7},{8,9},{9,10},{10,11},{12,13},{... | collective-permute-start | bytes 1179656 | tf_op jit(solution)/shard_map/ppermute | solution.py:15
  7.6 0.7 fusion.109
  8.6 1.0 fusion.27
  9.6 1.0 fusion.26
  10.6 1.0 fusion.25
  11.7 1.0 fusion.24
  12.7 1.0 fusion.23
  13.7 1.0 fusion.22
  14.8 1.0 fusion.21
  16.4 0.7 copy-done.5
  17.1 0.6 fusion.101
  17.9 0.7 constant_dynamic-update-slice_fusion.18
  18.6 1.3 constant_dynamic-update-slice_fusion.17
  19.9 1.4 constant_dynamic-update-slice_fusion.16
  21.3 2.0 %constant_dynamic-update-slice_fusion.15 = (f32[9,256,256]{1,2,0:T(8,128)}, f32[4,256,256]{1,2,0:T(8,128)S(1)}) fusion(f32[9,256,256]{1,2,0:T(8,128)} %get-tuple-element.44, f32[2,256,256]{1,2,0:T(8,128)S(1)} %get-tuple-element.45, f32[1,256,256]{1,2,0:T(8,128)S(1)} %bitcast.562, f32[1,256,256]{1,2,0:T(8,128)S(1)} %bitcast.559), kind=kOutput, calls=%fused_computation.164 | convolution fusion | flops 805830656 | bytes 3407872 | tf_op jit(solution)/shard_map/ab,sbc->sac/dot_general | solution.py:136
  23.9 5.3 %copy.54 = bf16[32,8,8,256]{0,1,3,2:T(8,128)(2,1)} copy(bf16[32,8,8,256]{3,2,1,0:T(8,128)(2,1)} %param.7) | data formatting | bytes 2097152 | tf_op args[0]
  29.7 1.3 fusion.96
  31.0 2.9 %copy.53 = bf16[32,8,3,256]{0,1,3,2:T(8,128)(2,1)} copy(bf16[32,8,3,256]{3,1,2,0:T(8,128)(2,1)} %collective-permute-done) | data formatting | bytes 786432 | tf_op jit(solution)/shard_map/optimization_barrier | solution.py:108
  34.0 9.4 %fusion.4 = f32[32,2,64,128]{3,0,2,1:T(8,128)} fusion(bf16[128,64,3,3]{0,1,3,2:T(8,128)(2,1)S(1)} %copy-done, pred[5]{0:T(512)(128)(4,1)} %compare_and_fusion, bf16[64,8,3,3]{0,1,3,2:T(8,128)(2,1)} %param.8, bf16[32,8,8,256]{0,1,3,2:T(8,128)(2,1)} %copy.54, bf16[32,8,3,256]{0,1,3,2:T(8,128)(2,1)} %copy.53), kind=kOutput, calls=%fused_computation.5 | convolution fusion | flops 799834112 | bytes 3695621 | tf_op jit(solution)/shard_map/conv_general_dilated | solution.py:23
  43.4 5.4 %convolution_bitcast_fusion.3 = f32[32,256]{1,0:T(8,128)S(1)} fusion(bf16[2,64,128,256]{3,2,1,0:T(8,128)(2,1)} %param.10, f32[32,2,64,128]{3,0,2,1:T(8,128)} %fusion.4), kind=kOutput, calls=%fused_computation.38 | convolution fusion | flops 271056896 | bytes 10518528 | tf_op jit(solution)/shard_map/shwc,hwcm->sm/dot_general | solution.py:45
  48.8 0.8 collective-permute-start.2
  49.6 1.3 collective-permute-start.3
  50.9 2.9 %collective-permute-start.1 = (f32[32,256]{1,0:T(8,128)S(1)}, f32[32,256]{1,0:T(8,128)S(1)}, u32[]{:S(2)}, u32[]{:S(2)}) collective-permute-start(f32[32,256]{1,0:T(8,128)S(1)} %convolution_bitcast_fusion.3), channel_id=1, source_target_pairs={{0,2},{1,3},{2,0},{3,1},{4,6},{5,7},{6,4},{7,5},{8,10},{9,11},{10,... | collective-permute-start | bytes 98312 | tf_op jit(solution)/shard_map/ppermute | solution.py:49
  54.0 1.9 %collective-permute-start.5 = (f32[256,256]{1,0:T(8,128)S(1)}, f32[256,256]{1,0:T(8,128)S(1)}, u32[]{:S(2)}, u32[]{:S(2)}) collective-permute-start(f32[256,256]{1,0:T(8,128)S(1)} %copy-done.15), channel_id=1, source_target_pairs={{0,4},{4,8},{8,12},{12,16},{16,20},{20,24},{24,28},{28,32},{32,36}... | collective-permute-start | bytes 786440 | tf_op jit(solution)/shard_map/ppermute | solution.py:15
  55.9 3.4 %collective-permute-start.7 = (f32[256,256]{1,0:T(8,128)S(1)}, f32[256,256]{1,0:T(8,128)S(1)}, u32[]{:S(2)}, u32[]{:S(2)}) collective-permute-start(f32[256,256]{1,0:T(8,128)S(1)} %copy-done.15), channel_id=1, source_target_pairs={{0,8},{4,12},{8,16},{12,20},{16,24},{20,28},{24,32},{28,36},{32,40... | collective-permute-start | bytes 786440 | tf_op jit(solution)/shard_map/ppermute | solution.py:15
  62.7 0.6 fusion.156
  63.5 3.4 %collective-permute-start.6 = (f32[256]{0:T(256)S(1)}, f32[256]{0:T(256)S(1)}, u32[]{:S(2)}, u32[]{:S(2)}) collective-permute-start(f32[256]{0:T(256)S(1)} %add.160), channel_id=1, source_target_pairs={{0,8},{4,12},{8,16},{12,20},{16,24},{20,28},{24,32},{28,36},{32,40... | collective-permute-start | bytes 3080 | tf_op jit(solution)/shard_map/ppermute | solution.py:15
  67.4 2.9 %collective-permute-start.4 = (f32[256]{0:T(256)S(1)}, f32[256]{0:T(256)S(1)}, u32[]{:S(2)}, u32[]{:S(2)}) collective-permute-start(f32[256]{0:T(256)S(1)} %add.160), channel_id=1, source_target_pairs={{0,4},{4,8},{8,12},{12,16},{16,20},{20,24},{24,28},{28,32},{32,36}... | collective-permute-start | bytes 3080 | tf_op jit(solution)/shard_map/ppermute | solution.py:15
  70.6 1.6 %collective-permute-done.4 = f32[256]{0:T(256)S(1)} collective-permute-done((f32[256]{0:T(256)S(1)}, f32[256]{0:T(256)S(1)}, u32[]{:S(2)}, u32[]{:S(2)}) %collective-permute-start.4) | collective-permute-done | bytes 1056 | tf_op jit(solution)/shard_map/ppermute | solution.py:15
  72.2 5.5 %collective-permute-start.8 = (f32[256]{0:T(256)S(1)}, f32[256]{0:T(256)S(1)}, u32[]{:S(2)}, u32[]{:S(2)}) collective-permute-start(f32[256]{0:T(256)S(1)} %add.161), channel_id=1, source_target_pairs={{0,8},{4,12},{8,16},{12,20},{16,24},{20,28},{24,32},{28,36},{32,40... | collective-permute-start | bytes 3080 | tf_op jit(solution)/shard_map/ppermute | solution.py:15
  78.2 1.9 %collective-permute-start.9 = (f32[256,256]{1,0:T(8,128)S(1)}, f32[256,256]{1,0:T(8,128)S(1)}, u32[]{:S(2)}, u32[]{:S(2)}) collective-permute-start(f32[256,256]{1,0:T(8,128)S(1)} %fusion.159), channel_id=1, source_target_pairs={{0,8},{4,12},{8,16},{12,20},{16,24},{20,28},{24,32},{28,36},{32,40... | collective-permute-start | bytes 786440 | tf_op jit(solution)/shard_map/ppermute | solution.py:15
  80.8 3.3 %collective-permute-start.10 = (f32[256]{0:T(256)S(1)}, f32[256]{0:T(256)S(1)}, u32[]{:S(2)}, u32[]{:S(2)}) collective-permute-start(f32[256]{0:T(256)S(1)} %add.162), channel_id=1, source_target_pairs={{0,16},{4,20},{8,24},{12,28},{16,32},{20,36},{24,40},{28,44},{32,4... | collective-permute-start | bytes 3080 | tf_op jit(solution)/shard_map/ppermute | solution.py:15
  84.1 2.3 %collective-permute-done.9 = f32[256,256]{1,0:T(8,128)S(1)} collective-permute-done((f32[256,256]{1,0:T(8,128)S(1)}, f32[256,256]{1,0:T(8,128)S(1)}, u32[]{:S(2)}, u32[]{:S(2)}) %collective-permute-start.9) | collective-permute-done | bytes 262176 | tf_op jit(solution)/shard_map/ppermute | solution.py:15
  86.8 2.7 %collective-permute-start.11 = (f32[256,256]{1,0:T(8,128)S(1)}, f32[256,256]{1,0:T(8,128)S(1)}, u32[]{:S(2)}, u32[]{:S(2)}) collective-permute-start(f32[256,256]{1,0:T(8,128)S(1)} %fusion.161), channel_id=1, source_target_pairs={{0,16},{4,20},{8,24},{12,28},{16,32},{20,36},{24,40},{28,44},{32,4... | collective-permute-start | bytes 786440 | tf_op jit(solution)/shard_map/ppermute | solution.py:15
  89.5 1.1 convolution_bitcast_fusion.2
  91.4 2.4 %collective-permute-start.12 = (f32[256]{0:T(256)}, f32[256]{0:T(256)}, u32[]{:S(2)}, u32[]{:S(2)}) collective-permute-start(f32[256]{0:T(256)} %add.163), channel_id=1, source_target_pairs={{0,32},{4,36},{8,40},{12,44},{16,48},{20,52},{24,56},{28,60},{32,6... | collective-permute-start | bytes 3080 | tf_op jit(solution)/shard_map/ppermute | solution.py:15
  93.9 2.7 %collective-permute-done.11 = f32[256,256]{1,0:T(8,128)S(1)} collective-permute-done((f32[256,256]{1,0:T(8,128)S(1)}, f32[256,256]{1,0:T(8,128)S(1)}, u32[]{:S(2)}, u32[]{:S(2)}) %collective-permute-start.11) | collective-permute-done | bytes 262176 | tf_op jit(solution)/shard_map/ppermute | solution.py:15
  97.0 3.2 %collective-permute-start.13 = (f32[256,256]{1,0:T(8,128)S(1)}, f32[256,256]{1,0:T(8,128)}, u32[]{:S(2)}, u32[]{:S(2)}) collective-permute-start(f32[256,256]{1,0:T(8,128)S(1)} %fusion.163), channel_id=1, source_target_pairs={{0,32},{4,36},{8,40},{12,44},{16,48},{20,52},{24,56},{28,60},{32,6... | collective-permute-start | bytes 786440 | tf_op jit(solution)/shard_map/ppermute | solution.py:15
  100.2 0.7 fusion.94
  100.9 1.8 %copy.51 = f32[256,256]{0,1:T(8,128)} copy(f32[256,256]{1,0:T(8,128)} %copy-done.6) | data formatting | bytes 524288 | tf_op jit(solution)/shard_map/dot_general | solution.py:11
  102.7 1.8 %copy.50 = f32[256,256]{0,1:T(8,128)} copy(f32[256,256]{1,0:T(8,128)} %copy-done.5) | data formatting | bytes 524288 | tf_op jit(solution)/shard_map/dot_general | solution.py:11
  104.5 0.7 slice.234
  105.3 1.0 fusion.164
  106.3 0.7 add.164
  106.9 1.4 collective-permute-start.14
  108.4 1.3 fusion.165
  110.1 2.0 %fusion.62 = f32[1,4,256]{2,0,1:T(1,128)S(1)} fusion(f32[256,1,1]{0,1,2:T(1,128)S(1)} %bitcast.660, f32[1,256,256]{1,2,0:T(8,128)} %bitcast.594, f32[1,256,256]{1,2,0:T(8,128)} %bitcast.595, f32[1,256,256]{1,2,0:T(8,128)} %slice.234, f32[1,256,256]{1,2,0:T(8,128)} %fusion.94), kind=kOutput, calls=%fused_computation.88 | convolution fusion | flops 3932160 | bytes 1053696 | tf_op jit(solution)/shard_map/sab,b->sa/dot_general | solution.py:126
  115.2 1.3 fusion.28
  118.0 2.3 %collective-permute-start.16 = (f32[256]{0:T(256)S(1)}, f32[256]{0:T(256)S(1)}, u32[]{:S(2)}, u32[]{:S(2)}) collective-permute-start(f32[256]{0:T(256)S(1)} %select_add_fusion), channel_id=1, source_target_pairs={{8,0},{12,4},{16,8},{20,12},{24,16},{28,20},{32,24},{36,28},{40,32... | collective-permute-start | bytes 3080 | tf_op jit(solution)/shard_map/ppermute | solution.py:19
  120.7 1.9 %collective-permute-start.15 = (f32[256]{0:T(256)S(1)}, f32[256]{0:T(256)S(1)}, u32[]{:S(2)}, u32[]{:S(2)}) collective-permute-start(f32[256]{0:T(256)S(1)} %select_add_fusion), channel_id=1, source_target_pairs={{4,0},{8,4},{12,8},{16,12},{20,16},{24,20},{28,24},{32,28},{36,32}... | collective-permute-start | bytes 3080 | tf_op jit(solution)/shard_map/ppermute | solution.py:19
  122.6 6.3 %collective-permute-done.16 = f32[256]{0:T(256)S(1)} collective-permute-done((f32[256]{0:T(256)S(1)}, f32[256]{0:T(256)S(1)}, u32[]{:S(2)}, u32[]{:S(2)}) %collective-permute-start.16) | collective-permute-done | bytes 1056 | tf_op jit(solution)/shard_map/ppermute | solution.py:19
  129.3 1.9 %collective-permute-start.17 = (f32[256]{0:T(256)S(1)}, f32[256]{0:T(256)S(1)}, u32[]{:S(2)}, u32[]{:S(2)}) collective-permute-start(f32[256]{0:T(256)S(1)} %add.183), channel_id=1, source_target_pairs={{8,0},{12,4},{16,8},{20,12},{24,16},{28,20},{32,24},{36,28},{40,32... | collective-permute-start | bytes 3080 | tf_op jit(solution)/shard_map/ppermute | solution.py:19
  131.6 5.3 %collective-permute-done.17 = f32[256]{0:T(256)S(1)} collective-permute-done((f32[256]{0:T(256)S(1)}, f32[256]{0:T(256)S(1)}, u32[]{:S(2)}, u32[]{:S(2)}) %collective-permute-start.17) | collective-permute-done | bytes 1056 | tf_op jit(solution)/shard_map/ppermute | solution.py:19
  137.1 2.0 %collective-permute-start.18 = (f32[256]{0:T(256)S(1)}, f32[256]{0:T(256)S(1)}, u32[]{:S(2)}, u32[]{:S(2)}) collective-permute-start(f32[256]{0:T(256)S(1)} %add.184), channel_id=1, source_target_pairs={{16,0},{20,4},{24,8},{28,12},{32,16},{36,20},{40,24},{44,28},{48,3... | collective-permute-start | bytes 3080 | tf_op jit(solution)/shard_map/ppermute | solution.py:19
  139.5 5.6 %collective-permute-done.18 = f32[256]{0:T(256)S(1)} collective-permute-done((f32[256]{0:T(256)S(1)}, f32[256]{0:T(256)S(1)}, u32[]{:S(2)}, u32[]{:S(2)}) %collective-permute-start.18) | collective-permute-done | bytes 1056 | tf_op jit(solution)/shard_map/ppermute | solution.py:19
  145.3 2.0 %collective-permute-start.19 = (f32[256]{0:T(256)S(1)}, f32[256]{0:T(256)S(1)}, u32[]{:S(2)}, u32[]{:S(2)}) collective-permute-start(f32[256]{0:T(256)S(1)} %add.185), channel_id=1, source_target_pairs={{32,0},{36,4},{40,8},{44,12},{48,16},{52,20},{56,24},{60,28},{64,3... | collective-permute-start | bytes 3080 | tf_op jit(solution)/shard_map/ppermute | solution.py:19
  147.3 3.5 %collective-permute-done.19 = f32[256]{0:T(256)S(1)} collective-permute-done((f32[256]{0:T(256)S(1)}, f32[256]{0:T(256)S(1)}, u32[]{:S(2)}, u32[]{:S(2)}) %collective-permute-start.19) | collective-permute-done | bytes 1056 | tf_op jit(solution)/shard_map/ppermute | solution.py:19
  151.1 1.3 collective-permute-start.20
  152.5 0.6 copy.106
  153.1 5.0 %collective-permute-done.20 = f32[256]{0:T(256)S(1)} collective-permute-done((f32[256]{0:T(256)S(1)}, f32[256]{0:T(256)S(1)}, u32[]{:S(2)}, u32[]{:S(2)}) %collective-permute-start.20) | collective-permute-done | bytes 1056 | tf_op jit(solution)/shard_map/ppermute | solution.py:19
  159.3 1.2 fusion.13
  160.5 0.6 bitcast_add_fusion
  (150 shorter events, 17.3 us)
Async XLA Ops:
  0.6 33.3 %copy-start = (bf16[128,64,3,3]{0,1,3,2:T(8,128)(2,1)S(1)}, bf16[128,64,3,3]{0,1,3,2:T(8,128)(2,1)}, u32[]{:S(2)}) copy-start(bf16[128,64,3,3]{0,1,3,2:T(8,128)(2,1)} %param.9) | copy-start | bytes 442372
  0.6 7.7 %copy-start.1 = (f32[256,256]{1,0:T(8,128)S(1)}, f32[256,256]{1,0:T(8,128)}, u32[]{:S(2)}) copy-start(f32[256,256]{1,0:T(8,128)} %param.11) | copy-start | bytes 786436
  0.7 7.9 %copy-start.16 = (f32[32,256]{1,0:T(8,128)S(1)}, f32[32,256]{1,0:T(8,128)}, u32[]{:S(2)}) copy-start(f32[32,256]{1,0:T(8,128)} %param.13) | copy-start | bytes 98308
  3.1 27.9 %collective-permute-start = (bf16[32,8,3,256]{3,1,2,0:T(8,128)(2,1)}, bf16[32,8,3,256]{3,1,2,0:T(8,128)(2,1)}, u32[]{:S(2)}, u32[]{:S(2)}) collective-permute-start(bf16[32,8,3,256]{3,1,2,0:T(8,128)(2,1)} %copy.84), channel_id=1, source_target_pairs={{0,1},{1,2},{2,3},{4,5},{5,6},{6,7},{8,9},{9,10},{10,11},{12,13},{... | collective-permute-start | bytes 1179656 | tf_op jit(solution)/shard_map/ppermute | solution.py:15
  14.8 2.9 %copy-start.2 = (f32[256,256]{1,0:T(8,128)S(1)}, f32[256,256]{1,0:T(8,128)}, u32[]{:S(2)}) copy-start(f32[256,256]{1,0:T(8,128)} %param.12) | copy-start | bytes 786436
  16.4 0.7 copy-start.5
  17.7 12.0 %copy-start.6 = (f32[256,256]{1,0:T(8,128)}, f32[256,256]{1,0:T(8,128)S(1)}, u32[]{:S(2)}) copy-start(f32[256,256]{1,0:T(8,128)S(1)} %fusion.101) | copy-start | bytes 786436
  19.9 3.4 %copy-start.3 = (f32[256,256]{1,0:T(8,128)}, f32[256,256]{1,0:T(8,128)S(1)}, u32[]{:S(2)}) copy-start(f32[256,256]{1,0:T(8,128)S(1)} %get-tuple-element.43) | copy-start | bytes 786436
  21.3 2.0 %copy-start.8 = (f32[2,256,256]{1,2,0:T(8,128)}, f32[2,256,256]{1,2,0:T(8,128)S(1)}, u32[]{:S(2)}) copy-start(f32[2,256,256]{1,2,0:T(8,128)S(1)} %get-tuple-element.45) | copy-start | bytes 1572868
  43.4 10.6 %copy-start.17 = (f32[32,256]{1,0:T(8,128)S(1)}, f32[32,256]{1,0:T(8,128)}, u32[]{:S(2)}) copy-start(f32[32,256]{1,0:T(8,128)} %param.13) | copy-start | bytes 98308
  43.4 10.6 %copy-start.15 = (f32[256,256]{1,0:T(8,128)S(1)}, f32[256,256]{1,0:T(8,128)}, u32[]{:S(2)}) copy-start(f32[256,256]{1,0:T(8,128)} %fusion.96) | copy-start | bytes 786436
  48.8 10.6 %collective-permute-start.2 = (f32[32,256]{1,0:T(8,128)S(1)}, f32[32,256]{1,0:T(8,128)S(1)}, u32[]{:S(2)}, u32[]{:S(2)}) collective-permute-start(f32[32,256]{1,0:T(8,128)S(1)} %convolution_bitcast_fusion.3), channel_id=1, source_target_pairs={{0,3},{1,0},{2,1},{3,2},{4,7},{5,4},{6,5},{7,6},{8,11},{9,8},{10,9... | collective-permute-start | bytes 98312 | tf_op jit(solution)/shard_map/ppermute | solution.py:49
  49.6 9.8 %collective-permute-start.3 = (f32[32,256]{1,0:T(8,128)S(1)}, f32[32,256]{1,0:T(8,128)S(1)}, u32[]{:S(2)}, u32[]{:S(2)}) collective-permute-start(f32[32,256]{1,0:T(8,128)S(1)} %convolution_bitcast_fusion.3), channel_id=1, source_target_pairs={{0,1},{1,2},{2,3},{3,0},{4,5},{5,6},{6,7},{7,4},{8,9},{9,10},{10,1... | collective-permute-start | bytes 98312 | tf_op jit(solution)/shard_map/ppermute | solution.py:49
  50.9 8.5 %collective-permute-start.1 = (f32[32,256]{1,0:T(8,128)S(1)}, f32[32,256]{1,0:T(8,128)S(1)}, u32[]{:S(2)}, u32[]{:S(2)}) collective-permute-start(f32[32,256]{1,0:T(8,128)S(1)} %convolution_bitcast_fusion.3), channel_id=1, source_target_pairs={{0,2},{1,3},{2,0},{3,1},{4,6},{5,7},{6,4},{7,5},{8,10},{9,11},{10,... | collective-permute-start | bytes 98312 | tf_op jit(solution)/shard_map/ppermute | solution.py:49
  54.0 23.8 %copy-start.11 = (f32[4,8,256]{2,0,1:T(4,128)}, f32[4,8,256]{2,0,1:T(4,128)S(1)}, u32[]{:S(2)}) copy-start(f32[4,8,256]{2,0,1:T(4,128)S(1)} %copy.105) | copy-start | bytes 98308
  54.0 16.3 %collective-permute-start.5 = (f32[256,256]{1,0:T(8,128)S(1)}, f32[256,256]{1,0:T(8,128)S(1)}, u32[]{:S(2)}, u32[]{:S(2)}) collective-permute-start(f32[256,256]{1,0:T(8,128)S(1)} %copy-done.15), channel_id=1, source_target_pairs={{0,4},{4,8},{8,12},{12,16},{16,20},{20,24},{24,28},{28,32},{32,36}... | collective-permute-start | bytes 786440 | tf_op jit(solution)/shard_map/ppermute | solution.py:15
  55.9 21.9 %collective-permute-start.7 = (f32[256,256]{1,0:T(8,128)S(1)}, f32[256,256]{1,0:T(8,128)S(1)}, u32[]{:S(2)}, u32[]{:S(2)}) collective-permute-start(f32[256,256]{1,0:T(8,128)S(1)} %copy-done.15), channel_id=1, source_target_pairs={{0,8},{4,12},{8,16},{12,20},{16,24},{20,28},{24,32},{28,36},{32,40... | collective-permute-start | bytes 786440 | tf_op jit(solution)/shard_map/ppermute | solution.py:15
  59.4 18.4 %copy-start.13 = (f32[4,8,256]{2,0,1:T(4,128)}, f32[4,8,256]{2,0,1:T(4,128)S(1)}, u32[]{:S(2)}) copy-start(f32[4,8,256]{2,0,1:T(4,128)S(1)} %copy.104) | copy-start | bytes 98308
  62.0 15.8 %copy-start.18 = (f32[256]{0:T(256)}, f32[256]{0:T(256)S(1)}, u32[]{:S(2)}) copy-start(f32[256]{0:T(256)S(1)} %add.166) | copy-start | bytes 3076
  62.2 15.5 %copy-start.20 = (f32[256]{0:T(256)}, f32[256]{0:T(256)S(1)}, u32[]{:S(2)}) copy-start(f32[256]{0:T(256)S(1)} %get-tuple-element.25) | copy-start | bytes 3076
  63.5 6.8 %collective-permute-start.6 = (f32[256]{0:T(256)S(1)}, f32[256]{0:T(256)S(1)}, u32[]{:S(2)}, u32[]{:S(2)}) collective-permute-start(f32[256]{0:T(256)S(1)} %add.160), channel_id=1, source_target_pairs={{0,8},{4,12},{8,16},{12,20},{16,24},{20,28},{24,32},{28,36},{32,40... | collective-permute-start | bytes 3080 | tf_op jit(solution)/shard_map/ppermute | solution.py:15
  67.4 4.9 %collective-permute-start.4 = (f32[256]{0:T(256)S(1)}, f32[256]{0:T(256)S(1)}, u32[]{:S(2)}, u32[]{:S(2)}) collective-permute-start(f32[256]{0:T(256)S(1)} %add.160), channel_id=1, source_target_pairs={{0,4},{4,8},{8,12},{12,16},{16,20},{20,24},{24,28},{28,32},{32,36}... | collective-permute-start | bytes 3080 | tf_op jit(solution)/shard_map/ppermute | solution.py:15
  72.2 8.3 %collective-permute-start.8 = (f32[256]{0:T(256)S(1)}, f32[256]{0:T(256)S(1)}, u32[]{:S(2)}, u32[]{:S(2)}) collective-permute-start(f32[256]{0:T(256)S(1)} %add.161), channel_id=1, source_target_pairs={{0,8},{4,12},{8,16},{12,20},{16,24},{20,28},{24,32},{28,36},{32,40... | collective-permute-start | bytes 3080 | tf_op jit(solution)/shard_map/ppermute | solution.py:15
  78.2 8.3 %collective-permute-start.9 = (f32[256,256]{1,0:T(8,128)S(1)}, f32[256,256]{1,0:T(8,128)S(1)}, u32[]{:S(2)}, u32[]{:S(2)}) collective-permute-start(f32[256,256]{1,0:T(8,128)S(1)} %fusion.159), channel_id=1, source_target_pairs={{0,8},{4,12},{8,16},{12,20},{16,24},{20,28},{24,32},{28,36},{32,40... | collective-permute-start | bytes 786440 | tf_op jit(solution)/shard_map/ppermute | solution.py:15
  80.8 9.8 %collective-permute-start.10 = (f32[256]{0:T(256)S(1)}, f32[256]{0:T(256)S(1)}, u32[]{:S(2)}, u32[]{:S(2)}) collective-permute-start(f32[256]{0:T(256)S(1)} %add.162), channel_id=1, source_target_pairs={{0,16},{4,20},{8,24},{12,28},{16,32},{20,36},{24,40},{28,44},{32,4... | collective-permute-start | bytes 3080 | tf_op jit(solution)/shard_map/ppermute | solution.py:15
  86.8 9.8 %collective-permute-start.11 = (f32[256,256]{1,0:T(8,128)S(1)}, f32[256,256]{1,0:T(8,128)S(1)}, u32[]{:S(2)}, u32[]{:S(2)}) collective-permute-start(f32[256,256]{1,0:T(8,128)S(1)} %fusion.161), channel_id=1, source_target_pairs={{0,16},{4,20},{8,24},{12,28},{16,32},{20,36},{24,40},{28,44},{32,4... | collective-permute-start | bytes 786440 | tf_op jit(solution)/shard_map/ppermute | solution.py:15
  91.4 13.9 %collective-permute-start.12 = (f32[256]{0:T(256)}, f32[256]{0:T(256)}, u32[]{:S(2)}, u32[]{:S(2)}) collective-permute-start(f32[256]{0:T(256)} %add.163), channel_id=1, source_target_pairs={{0,32},{4,36},{8,40},{12,44},{16,48},{20,52},{24,56},{28,60},{32,6... | collective-permute-start | bytes 3080 | tf_op jit(solution)/shard_map/ppermute | solution.py:15
  97.0 11.4 %collective-permute-start.13 = (f32[256,256]{1,0:T(8,128)S(1)}, f32[256,256]{1,0:T(8,128)}, u32[]{:S(2)}, u32[]{:S(2)}) collective-permute-start(f32[256,256]{1,0:T(8,128)S(1)} %fusion.163), channel_id=1, source_target_pairs={{0,32},{4,36},{8,40},{12,44},{16,48},{20,52},{24,56},{28,60},{32,6... | collective-permute-start | bytes 786440 | tf_op jit(solution)/shard_map/ppermute | solution.py:15
  105.3 6.8 %copy-start.12 = (f32[4,8,256]{2,0,1:T(4,128)S(1)}, f32[4,8,256]{2,0,1:T(4,128)}, u32[]{:S(2)}) copy-start(f32[4,8,256]{2,0,1:T(4,128)} %copy-done.11) | copy-start | bytes 98308
  105.3 6.8 %copy-start.14 = (f32[4,8,256]{2,0,1:T(4,128)S(1)}, f32[4,8,256]{2,0,1:T(4,128)}, u32[]{:S(2)}) copy-start(f32[4,8,256]{2,0,1:T(4,128)} %copy-done.13) | copy-start | bytes 98308
  105.3 6.8 %copy-start.19 = (f32[256]{0:T(256)S(1)}, f32[256]{0:T(256)}, u32[]{:S(2)}) copy-start(f32[256]{0:T(256)} %copy-done.18) | copy-start | bytes 3076
  105.3 6.8 %copy-start.21 = (f32[256]{0:T(256)S(1)}, f32[256]{0:T(256)}, u32[]{:S(2)}) copy-start(f32[256]{0:T(256)} %copy-done.20) | copy-start | bytes 3076
  105.3 6.8 %copy-start.22 = (f32[256]{0:T(256)S(1)}, f32[256]{0:T(256)}, u32[]{:S(2)}) copy-start(f32[256]{0:T(256)} %get-tuple-element.23) | copy-start | bytes 3076
  106.9 7.8 %copy-start.10 = (f32[256,256,1]{1,0,2:T(8,128)S(1)}, f32[256,256,1]{1,0,2:T(8,128)}, u32[]{:S(2)}) copy-start(f32[256,256,1]{1,0,2:T(8,128)} %convolution_bitcast_fusion.2) | copy-start | bytes 786436
  106.9 2.8 %collective-permute-start.14 = (f32[256]{0:T(256)S(1)}, f32[256]{0:T(256)S(1)}, u32[]{:S(2)}, u32[]{:S(2)}) collective-permute-start(f32[256]{0:T(256)S(1)} %add.164), channel_id=1, source_target_pairs={{0,64},{4,68},{8,72},{12,76},{16,80},{20,84},{24,88},{28,92},{32,9... | collective-permute-start | bytes 3080 | tf_op jit(solution)/shard_map/ppermute | solution.py:15
  110.0 5.2 %copy-start.7 = (f32[9,256,256]{1,2,0:T(8,128)S(1)}, f32[9,256,256]{1,2,0:T(8,128)}, u32[]{:S(2)}) copy-start(f32[9,256,256]{1,2,0:T(8,128)} %get-tuple-element.46) | copy-start | bytes 7077892
  117.9 41.3 %copy-start.4 = (f32[256,256]{1,0:T(8,128)S(1)}, f32[256,256]{1,0:T(8,128)}, u32[]{:S(2)}) copy-start(f32[256,256]{1,0:T(8,128)} %copy-done.3) | copy-start | bytes 786436
  117.9 41.3 %copy-start.9 = (f32[2,256,256]{1,2,0:T(8,128)S(1)}, f32[2,256,256]{1,2,0:T(8,128)}, u32[]{:S(2)}) copy-start(f32[2,256,256]{1,2,0:T(8,128)} %copy-done.8) | copy-start | bytes 1572868
  118.0 11.0 %collective-permute-start.16 = (f32[256]{0:T(256)S(1)}, f32[256]{0:T(256)S(1)}, u32[]{:S(2)}, u32[]{:S(2)}) collective-permute-start(f32[256]{0:T(256)S(1)} %select_add_fusion), channel_id=1, source_target_pairs={{8,0},{12,4},{16,8},{20,12},{24,16},{28,20},{32,24},{36,28},{40,32... | collective-permute-start | bytes 3080 | tf_op jit(solution)/shard_map/ppermute | solution.py:19
  120.7 8.5 %collective-permute-start.15 = (f32[256]{0:T(256)S(1)}, f32[256]{0:T(256)S(1)}, u32[]{:S(2)}, u32[]{:S(2)}) collective-permute-start(f32[256]{0:T(256)S(1)} %select_add_fusion), channel_id=1, source_target_pairs={{4,0},{8,4},{12,8},{16,12},{20,16},{24,20},{28,24},{32,28},{36,32}... | collective-permute-start | bytes 3080 | tf_op jit(solution)/shard_map/ppermute | solution.py:19
  129.3 7.6 %collective-permute-start.17 = (f32[256]{0:T(256)S(1)}, f32[256]{0:T(256)S(1)}, u32[]{:S(2)}, u32[]{:S(2)}) collective-permute-start(f32[256]{0:T(256)S(1)} %add.183), channel_id=1, source_target_pairs={{8,0},{12,4},{16,8},{20,12},{24,16},{28,20},{32,24},{36,28},{40,32... | collective-permute-start | bytes 3080 | tf_op jit(solution)/shard_map/ppermute | solution.py:19
  137.1 7.9 %collective-permute-start.18 = (f32[256]{0:T(256)S(1)}, f32[256]{0:T(256)S(1)}, u32[]{:S(2)}, u32[]{:S(2)}) collective-permute-start(f32[256]{0:T(256)S(1)} %add.184), channel_id=1, source_target_pairs={{16,0},{20,4},{24,8},{28,12},{32,16},{36,20},{40,24},{44,28},{48,3... | collective-permute-start | bytes 3080 | tf_op jit(solution)/shard_map/ppermute | solution.py:19
  145.3 5.5 %collective-permute-start.19 = (f32[256]{0:T(256)S(1)}, f32[256]{0:T(256)S(1)}, u32[]{:S(2)}, u32[]{:S(2)}) collective-permute-start(f32[256]{0:T(256)S(1)} %add.185), channel_id=1, source_target_pairs={{32,0},{36,4},{40,8},{44,12},{48,16},{52,20},{56,24},{60,28},{64,3... | collective-permute-start | bytes 3080 | tf_op jit(solution)/shard_map/ppermute | solution.py:19
  151.1 7.0 %collective-permute-start.20 = (f32[256]{0:T(256)S(1)}, f32[256]{0:T(256)S(1)}, u32[]{:S(2)}, u32[]{:S(2)}) collective-permute-start(f32[256]{0:T(256)S(1)} %add.186), channel_id=1, source_target_pairs={{64,0},{68,4},{72,8},{76,12},{80,16},{84,20},{88,24},{92,28},{96,3... | collective-permute-start | bytes 3080 | tf_op jit(solution)/shard_map/ppermute | solution.py:19
